TPU v7x, 512 devices: a whole 4x8x8 slice. The times are simulated.
512 devices in a mesh: length: 16 (over z, core), girth: 32 (over x, y).
Axes of the slice: x: 4, y: 8, z: 8, core: 2. Of those that a mesh axis runs over, the one named last changes fastest.
Arguments:
- wave_amplitude: bfloat16 [6, 2048, 65536], P(None, 'length', 'girth'), may hold values from -6 to 6
- load_bank: bfloat16 [65536, 256], P('girth'), may hold values from -0.125 to 0.125
- freq_owner: int32 [1], replicated, may hold values from 0 to 31
- thickness_class: int32 [2048, 8192], P('length', 'girth'), may hold values from 0 to 7
- class_stiffness: float32 [8], replicated, may hold values from 0.5 to 4
- coupling: float32 [6, 6], replicated, may hold values from -0.15 to 2, as said below
- stress_map: float32 [4, 6], replicated, may hold values from -2.5 to 2.5
- psd_weight: float32 [1], replicated, may hold values from 0.5 to 2
- hotspot_tile: int32 [16, 1024], P('length', 'girth'), may hold values from 0 to 127
- hotspot_owner: int32 [16, 1024, 1], P('length', 'girth'), may hold values from 0 to 31; in each aligned block of 32 rows (0 to 31, 32 to 63, ..., all dimensions but the last counted through in order) at most 2 rows name the same one
- prior_moments: float32 [16, 32, 32, 2, 2, 256], P('length', 'girth'), may hold values from 0.1 to 1
Outputs:
- response: float32 [6, 2048, 8192], P(None, 'length', 'girth')
- hotspot_moments: float32 [16, 32, 32, 2, 2, 256], P('length', 'girth')
Inputs may be any that keep to these rules, and one draw needn't show every extreme that they name: `hotspot_owner`: in each device's list of 32 hotspots no owner is named more than 2 times, and in some lists an owner is named exactly 2 times. `coupling`: Symmetric; each diagonal entry is at least 1 and exceeds the sum of the magnitudes of the other entries of its row.
All inputs are finite; a program needn't handle non-finite values.
Results may differ from a plain program's by a relative error of at most 0.0003.
Values may be sent and summed in bfloat16 or wider, within the bound.
No kernel may reach another device: no remote copies, remote signals or barrier semaphores. Data moves between devices by JAX's collectives and lax.ppermute only.
A program may use at most 64 MiB of HBM per device.

v0:
```python
import math

import jax
import jax.numpy as jnp
from jax import lax
from jax.sharding import PartitionSpec as P

SWEEPS = 4
CAP = 2


def spread(block, axis, source):
    block = jnp.where(lax.axis_index(axis) == source, block, jnp.zeros_like(block))
    return lax.psum(block, axis)


def padded_2(block, sides, width):
    for axis, dim in sides:
        count = lax.axis_size(axis)
        forward = [(i, i + 1) for i in range(count - 1)]
        backward = [(target, source) for source, target in forward]
        low = lax.ppermute(
            lax.slice_in_dim(block, block.shape[dim] - width, None, axis=dim), axis, forward
        )
        high = lax.ppermute(lax.slice_in_dim(block, 0, width, axis=dim), axis, backward)
        block = jnp.concatenate([low, block, high], axis=dim)
    return block


def chebyshev_weight(sweep):
    return 1.0 / (1.0 + 0.9 * math.cos(math.pi * (2 * sweep + 1) / (2 * SWEEPS)))


def operate_padded(padded, stiffness, coupling):
    centre = padded[:, 1:-1, 1:-1]
    beside = padded[:, 2:, 1:-1] + padded[:, :-2, 1:-1] + padded[:, 1:-1, 2:] + padded[:, 1:-1, :-2]
    mixing = jnp.einsum("ab,bij->aij", coupling, centre, precision=lax.Precision.HIGHEST)
    return stiffness * (4.0 * centre - beside) + mixing


def square_pairs(values, axis_at):
    first = jnp.take(values, 0, axis=axis_at)
    second = jnp.take(values, 1, axis=axis_at)
    third = jnp.take(values, 2, axis=axis_at)
    fourth = jnp.take(values, 3, axis=axis_at)
    return jnp.stack(
        [first * first + second * second, third * third + fourth * fourth], axis=axis_at
    )


def on_device(
    wave_amplitude,
    load_bank,
    freq_owner,
    thickness_class,
    class_stiffness,
    coupling,
    stress_map,
    psd_weight,
    hotspot_tile,
    hotspot_owner,
    prior_moments,
):
    row_count = wave_amplitude.shape[1]
    girth_cells = load_bank.shape[1]
    mode_count = load_bank.shape[0]
    amplitude = wave_amplitude.reshape(6 * row_count, mode_count)
    root = freq_owner[0]
    factors = spread(load_bank, "girth", root)
    loading = jnp.dot(amplitude, factors, preferred_element_type=jnp.float32)
    loading = loading.reshape(6, row_count, girth_cells)
    stiffness = jnp.zeros((row_count, girth_cells), jnp.float32)
    for level in range(class_stiffness.shape[0]):
        stiffness = stiffness + jnp.where(thickness_class == level, class_stiffness[level], 0.0)
    coupling_diag = jnp.diagonal(coupling)[:, None, None]
    diagonal = 4.0 * stiffness[None] + coupling_diag
    motion = chebyshev_weight(0) * (loading / diagonal)
    for sweep in range(1, SWEEPS):
        padded = padded_2(motion, (("length", 1), ("girth", 2)), 1)
        applied = operate_padded(padded, stiffness, coupling)
        motion = motion + chebyshev_weight(sweep) * ((loading - applied) / diagonal)
    girth_count = lax.axis_size("girth")
    tile_ids = hotspot_tile[0]
    owner_ids = hotspot_owner[0, :, 0]
    listed = owner_ids.shape[0]
    positions = jnp.arange(listed, dtype=jnp.int32)
    matching = owner_ids[:, None] == owner_ids[None, :]
    earlier = positions[None, :] < positions[:, None]
    slot_rank = jnp.sum(jnp.logical_and(matching, earlier).astype(jnp.int32), axis=1)
    target = owner_ids * CAP + slot_rank
    stresses = stiffness[:, None, :] * jnp.einsum(
        "ka,aij->ikj", stress_map, motion, precision=lax.Precision.HIGHEST
    )
    stress_rows = jnp.take(stresses, tile_ids, axis=0)
    outbox = jnp.zeros((girth_count * CAP, 4, girth_cells), jnp.float32).at[target].set(stress_rows)
    outbox = outbox.reshape(girth_count, CAP, 4, girth_cells)
    received = lax.all_to_all(outbox, "girth", split_axis=0, concat_axis=0, tiled=True)
    hotspot_moments = prior_moments + (psd_weight[0] * square_pairs(received, 2))[None, None]
    return (motion, hotspot_moments)


def solution(mesh):
    return jax.shard_map(
        on_device,
        mesh=mesh,
        in_specs=(
            P(None, "length", "girth"),
            P("girth", None),
            P(),
            P("length", "girth"),
            P(),
            P(),
            P(),
            P(),
            P("length", "girth"),
            P("length", "girth", None),
            P("length", "girth", None, None, None, None),
        ),
        out_specs=(P(None, "length", "girth"), P("length", "girth", None, None, None, None)),
        check_vma=False,
    )
```

profile of v0, /device:TPU:264, one launch (start us, length us, event | category | flops | bytes accessed | tf_op | source)
XLA Modules:
  0.0 299.6 jit_solution(5316711973554912137)
XLA Ops:
  7.2 0.0 copy-start
  7.2 0.0 all-reduce.2.cloned.1.call-start
  8.0 1.0 broadcast_select_fusion
  9.1 0.0 all-reduce.2.cloned.1.call-update
  9.1 0.6 gather_fusion
  9.8 0.7 fusion.51
  10.5 5.3 %broadcast_multiply_fusion.1 = (f32[128,256]{1,0:T(8,128)S(1)}, f32[128,256]{1,0:T(8,128)S(1)}) fusion(f32[]{:T(128)} %bitcast.11, s32[128,256]{1,0:T(8,128)S(1)} %copy-done.6, f32[]{:T(128)} %bitcast.10, f32[]{:T(128)} %bitcast.9, f32[]{:T(128)} %bitcast.8, f32[]{:T(128)} %bitcast.7, f32[]{:T(128)} %bitcast.6, f32[]{:T(128)} %bitcast.5, f32[]{:T(128)} %bitcast.4), kind=kLoop, calls=%fused_computation.85 | loop fusion | flops 786432 | bytes 393248 | tf_op jit(solution)/shard_map/mul | solution.py:76
  15.7 156.9 %all-reduce.2.cloned.1.call-done = bf16[2048,256]{1,0:T(8,128)(2,1)} async-done(((bf16[2048,256]{1,0:T(8,128)(2,1)}), bf16[2048,256]{1,0:T(8,128)(2,1)}) %all-reduce.2.cloned.1.call-update) | async-done | bytes 1048592 | tf_op jit(solution)/shard_map/psum | solution.py:14
  172.7 3.1 %convolution_bitcast_fusion.3 = f32[768,256]{0,1:T(8,128)} fusion(bf16[2048,256]{1,0:T(8,128)(2,1)} %all-reduce.2.cloned.1.call-done, bf16[768,2048]{1,0:T(8,128)(2,1)S(1)} %bitcast.120), kind=kOutput, calls=%fused_computation.22 | convolution fusion | flops 805306368 | bytes 4980736 | tf_op jit(solution)/shard_map/dot_general | solution.py:70
  175.8 2.3 copy.53
  178.1 1.8 broadcast_multiply_fusion
  179.9 1.9 collective-permute-start
  181.8 2.4 collective-permute-start.1
  184.3 3.8 %collective-permute-done.1 = f32[6,1,256]{2,0,1:T(8,128)S(1)} collective-permute-done((f32[6,1,256]{2,0,1:T(8,128)S(1)}, f32[6,1,256]{2,0,1:T(8,128)S(1)}, u32[]{:S(2)}, u32[]{:S(2)}) %collective-permute-start.1) | collective-permute-done | bytes 6176 | tf_op jit(solution)/shard_map/ppermute | solution.py:22
  188.0 0.1 pad_maximum_fusion
  188.1 1.2 fusion.46
  189.3 1.3 copy.55
  190.6 3.4 %collective-permute-start.2 = (f32[6,130,1]{1,2,0:T(1,128)S(1)}, f32[6,130,1]{1,2,0:T(1,128)S(1)}, u32[]{:S(2)}, u32[]{:S(2)}) collective-permute-start(f32[6,130,1]{1,2,0:T(1,128)S(1)} %copy.55), channel_id=1, source_target_pairs={{1,0},{2,1},{3,2},{4,3},{5,4},{6,5},{7,6},{8,7},{9,8},{10,9},{11,1... | collective-permute-start | bytes 9368 | tf_op jit(solution)/shard_map/ppermute | solution.py:25
  194.0 1.3 copy.57
  195.3 2.4 collective-permute-start.3
  197.8 0.2 convert_reduce_fusion
  198.0 0.0 collective-permute-done.2
  198.0 1.2 copy.56
  199.2 1.7 collective-permute-done.3
  200.9 1.2 copy.58
  202.0 6.4 %fusion.11 = f32[6,128,256]{2,0,1:T(8,128)S(1)} fusion(f32[6,128,256]{2,0,1:T(8,128)} %copy-done.2, f32[6,128,256]{2,1,0:T(8,128)} %bitcast.122, f32[6,130,1]{2,0,1:T(8,128)} %copy.58, f32[6,1,256]{2,0,1:T(8,128)S(1)} %collective-permute-done, f32[6,1,256]{2,0,1:T(8,128)S(1)} %collective-permute-done.1, f32[6,130,1]{2,0,1:T(8,128)} %copy.56, ...), kind=kOutput, calls=%fused_computation.21 | convolution fusion | flops 18284544 | bytes 2640136 | tf_op jit(solution)/shard_map/ab,bij->aij/dot_general | solution.py:37
  208.4 1.9 collective-permute-start.4
  210.4 2.4 collective-permute-start.5
  212.8 3.7 %collective-permute-done.5 = f32[6,1,256]{2,0,1:T(8,128)S(1)} collective-permute-done((f32[6,1,256]{2,0,1:T(8,128)S(1)}, f32[6,1,256]{2,0,1:T(8,128)S(1)}, u32[]{:S(2)}, u32[]{:S(2)}) %collective-permute-start.5) | collective-permute-done | bytes 6176 | tf_op jit(solution)/shard_map/ppermute | solution.py:22
  216.6 0.1 pad_maximum_fusion.1
  216.7 1.2 fusion.45
  217.8 1.3 copy.60
  219.1 1.9 collective-permute-start.6
  221.1 1.3 copy.62
  222.4 3.9 %collective-permute-start.7 = (f32[6,130,1]{1,2,0:T(1,128)S(1)}, f32[6,130,1]{1,2,0:T(1,128)S(1)}, u32[]{:S(2)}, u32[]{:S(2)}) collective-permute-start(f32[6,130,1]{1,2,0:T(1,128)S(1)} %copy.62), channel_id=1, source_target_pairs={{0,1},{1,2},{2,3},{3,4},{4,5},{5,6},{6,7},{7,8},{8,9},{9,10},{10,1... | collective-permute-start | bytes 9368 | tf_op jit(solution)/shard_map/ppermute | solution.py:22
  226.4 1.2 copy.61
  227.6 0.4 collective-permute-done.7
  227.9 1.2 copy.63
  229.1 6.4 %fusion.7 = f32[6,128,256]{2,0,1:T(8,128)S(1)} fusion(f32[6,128,256]{2,0,1:T(8,128)} %copy-done.5, f32[6,128,256]{2,1,0:T(8,128)} %bitcast.123, f32[6,130,1]{2,0,1:T(8,128)} %copy.63, f32[6,1,256]{2,0,1:T(8,128)S(1)} %collective-permute-done.4, f32[6,1,256]{2,0,1:T(8,128)S(1)} %collective-permute-done.5, f32[6,130,1]{2,0,1:T(8,128)} %copy.61, ...), kind=kOutput, calls=%fused_computation.16 | convolution fusion | flops 18087936 | bytes 2640136 | tf_op jit(solution)/shard_map/ab,bij->aij/dot_general | solution.py:37
  235.5 1.9 collective-permute-start.8
  237.4 2.4 collective-permute-start.9
  239.9 3.7 %collective-permute-done.9 = f32[6,1,256]{2,0,1:T(8,128)S(1)} collective-permute-done((f32[6,1,256]{2,0,1:T(8,128)S(1)}, f32[6,1,256]{2,0,1:T(8,128)S(1)}, u32[]{:S(2)}, u32[]{:S(2)}) %collective-permute-start.9) | collective-permute-done | bytes 6176 | tf_op jit(solution)/shard_map/ppermute | solution.py:22
  243.6 0.1 pad_maximum_fusion.2
  243.7 1.2 fusion.44
  244.9 1.3 copy.65
  246.2 1.9 collective-permute-start.10
  248.1 1.3 copy.67
  249.4 4.1 %collective-permute-start.11 = (f32[6,130,1]{1,2,0:T(1,128)S(1)}, f32[6,130,1]{1,2,0:T(1,128)S(1)}, u32[]{:S(2)}, u32[]{:S(2)}) collective-permute-start(f32[6,130,1]{1,2,0:T(1,128)S(1)} %copy.67), channel_id=1, source_target_pairs={{0,1},{1,2},{2,3},{3,4},{4,5},{5,6},{6,7},{7,8},{8,9},{9,10},{10,1... | collective-permute-start | bytes 9368 | tf_op jit(solution)/shard_map/ppermute | solution.py:22
  253.6 0.0 collective-permute-done.10
  253.6 1.2 copy.66
  254.8 0.2 collective-permute-done.11
  255.0 1.2 copy.68
  256.1 6.4 %fusion.3 = f32[6,128,256]{2,0,1:T(8,128)S(1)} fusion(f32[6,128,256]{2,0,1:T(8,128)} %copy-done.4, f32[6,128,256]{2,1,0:T(8,128)} %bitcast.124, f32[6,130,1]{2,0,1:T(8,128)} %copy.68, f32[6,1,256]{2,0,1:T(8,128)S(1)} %collective-permute-done.8, f32[6,1,256]{2,0,1:T(8,128)S(1)} %collective-permute-done.9, f32[6,130,1]{2,0,1:T(8,128)} %copy.66, ...), kind=kOutput, calls=%fused_computation.11 | convolution fusion | flops 18087936 | bytes 2640136 | tf_op jit(solution)/shard_map/ab,bij->aij/dot_general | solution.py:37
  262.6 1.0 copy-done.3
  263.5 1.8 fusion.12
  265.4 1.7 gather_fusion.1
  267.1 0.1 broadcast_select_fusion.1
  267.2 1.5 scatter_fusion
  268.7 0.8 copy.70
  269.5 11.4 %all-to-all-start = ((f32[32,2,4,256]{3,1,2,0:T(2,128)}), f32[32,2,4,256]{3,1,2,0:T(2,128)S(1)}, u32[]{:S(2)}, u32[]{:S(2)}) async-start(f32[32,2,4,256]{3,1,2,0:T(2,128)} %copy.70), calls=%async_computation | async-start | bytes 524288 | tf_op jit(solution)/shard_map/all_to_all | solution.py:97
  281.5 0.0 copy-start.7
  281.6 2.4 copy.76
  284.0 7.9 %all-to-all-done = f32[32,2,4,256]{3,1,2,0:T(2,128)S(1)} async-done(((f32[32,2,4,256]{3,1,2,0:T(2,128)}), f32[32,2,4,256]{3,1,2,0:T(2,128)S(1)}, u32[]{:S(2)}, u32[]{:S(2)}) %all-to-all-start) | async-done | bytes 262176 | tf_op jit(solution)/shard_map/all_to_all | solution.py:97
  292.0 0.8 copy.77
  (37 shorter events, 0.2 us)
Async XLA Ops:
  7.2 165.5 %copy-start = (bf16[6,128,2048]{2,1,0:T(8,128)(2,1)S(1)}, bf16[6,128,2048]{2,1,0:T(8,128)(2,1)}, u32[]{:S(2)}) copy-start(bf16[6,128,2048]{2,1,0:T(8,128)(2,1)} %param.19) | copy-start | bytes 9437188
  7.2 165.5 %all-reduce.2.cloned.1.call-start = ((), (), s32[]{:S(2)}) async-start(), calls=%async_computation.1 | async-start | bytes 2097152 | tf_op jit(solution)/shard_map/psum | solution.py:14
  8.0 1.1 copy-start.1
  9.1 0.7 copy-start.8
  9.1 1.4 copy-start.6
  179.9 8.2 %copy-start.2 = (f32[6,128,256]{2,0,1:T(8,128)}, f32[6,128,256]{2,0,1:T(8,128)S(1)}, u32[]{:S(2)}) copy-start(f32[6,128,256]{2,0,1:T(8,128)S(1)} %broadcast_multiply_fusion) | copy-start | bytes 2359300
  179.9 4.3 %collective-permute-start = (f32[6,1,256]{2,0,1:T(8,128)S(1)}, f32[6,1,256]{2,0,1:T(8,128)S(1)}, u32[]{:S(2)}, u32[]{:S(2)}) collective-permute-start(f32[6,1,256]{2,0,1:T(8,128)S(1)} %get-tuple-element.71), channel_id=1, source_target_pairs={{32,0},{64,32},{96,64},{128,96},{160,128},{192,160},{224,192},{256... | collective-permute-start | bytes 18440 | tf_op jit(solution)/shard_map/ppermute | solution.py:25
  181.8 6.2 %collective-permute-start.1 = (f32[6,1,256]{2,0,1:T(8,128)S(1)}, f32[6,1,256]{2,0,1:T(8,128)S(1)}, u32[]{:S(2)}, u32[]{:S(2)}) collective-permute-start(f32[6,1,256]{2,0,1:T(8,128)S(1)} %get-tuple-element.70), channel_id=1, source_target_pairs={{0,32},{32,64},{64,96},{96,128},{128,160},{160,192},{192,224},{224... | collective-permute-start | bytes 18440 | tf_op jit(solution)/shard_map/ppermute | solution.py:22
  189.3 8.5 %copy-start.10 = (s32[1,32,1]{1,2,0:T(1,128)S(1)}, s32[1,32,1]{1,2,0:T(1,128)}, u32[]{:S(2)}) copy-start(s32[1,32,1]{1,2,0:T(1,128)} %param.28) | copy-start | bytes 388
  190.6 7.4 %collective-permute-start.2 = (f32[6,130,1]{1,2,0:T(1,128)S(1)}, f32[6,130,1]{1,2,0:T(1,128)S(1)}, u32[]{:S(2)}, u32[]{:S(2)}) collective-permute-start(f32[6,130,1]{1,2,0:T(1,128)S(1)} %copy.55), channel_id=1, source_target_pairs={{1,0},{2,1},{3,2},{4,3},{5,4},{6,5},{7,6},{8,7},{9,8},{10,9},{11,1... | collective-permute-start | bytes 9368 | tf_op jit(solution)/shard_map/ppermute | solution.py:25
  195.3 5.5 %collective-permute-start.3 = (f32[6,130,1]{1,2,0:T(1,128)S(1)}, f32[6,130,1]{1,2,0:T(1,128)S(1)}, u32[]{:S(2)}, u32[]{:S(2)}) collective-permute-start(f32[6,130,1]{1,2,0:T(1,128)S(1)} %copy.57), channel_id=1, source_target_pairs={{0,1},{1,2},{2,3},{3,4},{4,5},{5,6},{6,7},{7,8},{8,9},{9,10},{10,1... | collective-permute-start | bytes 9368 | tf_op jit(solution)/shard_map/ppermute | solution.py:22
  208.4 8.2 %copy-start.5 = (f32[6,128,256]{2,0,1:T(8,128)}, f32[6,128,256]{2,0,1:T(8,128)S(1)}, u32[]{:S(2)}) copy-start(f32[6,128,256]{2,0,1:T(8,128)S(1)} %fusion.11) | copy-start | bytes 2359300
  208.4 4.4 %collective-permute-start.4 = (f32[6,1,256]{2,0,1:T(8,128)S(1)}, f32[6,1,256]{2,0,1:T(8,128)S(1)}, u32[]{:S(2)}, u32[]{:S(2)}) collective-permute-start(f32[6,1,256]{2,0,1:T(8,128)S(1)} %get-tuple-element.69), channel_id=1, source_target_pairs={{32,0},{64,32},{96,64},{128,96},{160,128},{192,160},{224,192},{256... | collective-permute-start | bytes 18440 | tf_op jit(solution)/shard_map/ppermute | solution.py:25
  210.4 6.2 %collective-permute-start.5 = (f32[6,1,256]{2,0,1:T(8,128)S(1)}, f32[6,1,256]{2,0,1:T(8,128)S(1)}, u32[]{:S(2)}, u32[]{:S(2)}) collective-permute-start(f32[6,1,256]{2,0,1:T(8,128)S(1)} %get-tuple-element.68), channel_id=1, source_target_pairs={{0,32},{32,64},{64,96},{96,128},{128,160},{160,192},{192,224},{224... | collective-permute-start | bytes 18440 | tf_op jit(solution)/shard_map/ppermute | solution.py:22
  217.8 8.5 %copy-start.11 = (s32[1,32]{1,0:T(1,128)S(1)}, s32[1,32]{1,0:T(1,128)}, u32[]{:S(2)}) copy-start(s32[1,32]{1,0:T(1,128)} %param.27) | copy-start | bytes 388
  219.1 7.2 %collective-permute-start.6 = (f32[6,130,1]{1,2,0:T(1,128)S(1)}, f32[6,130,1]{1,2,0:T(1,128)S(1)}, u32[]{:S(2)}, u32[]{:S(2)}) collective-permute-start(f32[6,130,1]{1,2,0:T(1,128)S(1)} %copy.60), channel_id=1, source_target_pairs={{1,0},{2,1},{3,2},{4,3},{5,4},{6,5},{7,6},{8,7},{9,8},{10,9},{11,1... | collective-permute-start | bytes 9368 | tf_op jit(solution)/shard_map/ppermute | solution.py:25
  222.4 5.5 %collective-permute-start.7 = (f32[6,130,1]{1,2,0:T(1,128)S(1)}, f32[6,130,1]{1,2,0:T(1,128)S(1)}, u32[]{:S(2)}, u32[]{:S(2)}) collective-permute-start(f32[6,130,1]{1,2,0:T(1,128)S(1)} %copy.62), channel_id=1, source_target_pairs={{0,1},{1,2},{2,3},{3,4},{4,5},{5,6},{6,7},{7,8},{8,9},{9,10},{10,1... | collective-permute-start | bytes 9368 | tf_op jit(solution)/shard_map/ppermute | solution.py:22
  235.5 8.2 %copy-start.4 = (f32[6,128,256]{2,0,1:T(8,128)}, f32[6,128,256]{2,0,1:T(8,128)S(1)}, u32[]{:S(2)}) copy-start(f32[6,128,256]{2,0,1:T(8,128)S(1)} %fusion.7) | copy-start | bytes 2359300
  235.5 4.4 %collective-permute-start.8 = (f32[6,1,256]{2,0,1:T(8,128)S(1)}, f32[6,1,256]{2,0,1:T(8,128)S(1)}, u32[]{:S(2)}, u32[]{:S(2)}) collective-permute-start(f32[6,1,256]{2,0,1:T(8,128)S(1)} %get-tuple-element.67), channel_id=1, source_target_pairs={{32,0},{64,32},{96,64},{128,96},{160,128},{192,160},{224,192},{256... | collective-permute-start | bytes 18440 | tf_op jit(solution)/shard_map/ppermute | solution.py:25
  237.4 6.2 %collective-permute-start.9 = (f32[6,1,256]{2,0,1:T(8,128)S(1)}, f32[6,1,256]{2,0,1:T(8,128)S(1)}, u32[]{:S(2)}, u32[]{:S(2)}) collective-permute-start(f32[6,1,256]{2,0,1:T(8,128)S(1)} %get-tuple-element.66), channel_id=1, source_target_pairs={{0,32},{32,64},{64,96},{96,128},{128,160},{160,192},{192,224},{224... | collective-permute-start | bytes 18440 | tf_op jit(solution)/shard_map/ppermute | solution.py:22
  246.2 7.4 %collective-permute-start.10 = (f32[6,130,1]{1,2,0:T(1,128)S(1)}, f32[6,130,1]{1,2,0:T(1,128)S(1)}, u32[]{:S(2)}, u32[]{:S(2)}) collective-permute-start(f32[6,130,1]{1,2,0:T(1,128)S(1)} %copy.65), channel_id=1, source_target_pairs={{1,0},{2,1},{3,2},{4,3},{5,4},{6,5},{7,6},{8,7},{9,8},{10,9},{11,1... | collective-permute-start | bytes 9368 | tf_op jit(solution)/shard_map/ppermute | solution.py:25
  249.4 5.5 %collective-permute-start.11 = (f32[6,130,1]{1,2,0:T(1,128)S(1)}, f32[6,130,1]{1,2,0:T(1,128)S(1)}, u32[]{:S(2)}, u32[]{:S(2)}) collective-permute-start(f32[6,130,1]{1,2,0:T(1,128)S(1)} %copy.67), channel_id=1, source_target_pairs={{0,1},{1,2},{2,3},{3,4},{4,5},{5,6},{6,7},{7,8},{8,9},{9,10},{10,1... | collective-permute-start | bytes 9368 | tf_op jit(solution)/shard_map/ppermute | solution.py:22
  256.1 7.4 %copy-start.9 = (f32[4,6]{1,0:T(4,128)S(1)}, f32[4,6]{1,0:T(4,128)}, u32[]{:S(2)}) copy-start(f32[4,6]{1,0:T(4,128)} %param.25) | copy-start | bytes 292
  262.6 1.0 copy-start.3
  269.5 22.4 %all-to-all-start = ((f32[32,2,4,256]{3,1,2,0:T(2,128)}), f32[32,2,4,256]{3,1,2,0:T(2,128)S(1)}, u32[]{:S(2)}, u32[]{:S(2)}) async-start(f32[32,2,4,256]{3,1,2,0:T(2,128)} %copy.70), calls=%async_computation | async-start | bytes 524288 | tf_op jit(solution)/shard_map/all_to_all | solution.py:97
  281.5 10.4 %copy-start.7 = (f32[1,1,32,2,2,256]{5,4,3,2,1,0:T(2,128)S(1)}, f32[1,1,32,2,2,256]{5,4,3,2,1,0:T(2,128)}, u32[]{:S(2)}) copy-start(f32[1,1,32,2,2,256]{5,4,3,2,1,0:T(2,128)} %param.29) | copy-start | bytes 393220
Sparse Core Ops, SparseCore 0:
  11.5 161.1 all-reduce.1
where the time goes:
time: 301 us; the launch traced here: 300 us
  waiting for transfers between devices  178 us (59%)
  starting transfers between devices  42.1 us (14%)
  local copies, waits for them, and re-layouts  30.3 us (10%)
  matrix products  24.2 us (8%)
  between operations  15.9 us (5%)
  other arithmetic  8.78 us (3%)
    psum x1, waiting for transfers between devices, spread(): return lax.psum(block, axis)  157 us
    dot_general x3, matrix products, operate_padded(): jnp.einsum('ab,bij->aij', coupling, centre, precision=lax.Precision.HIGHEST)  19.2 us
    ppermute x6, starting transfers between devices, padded_2(): lax.ppermute(lax.slice_in_dim(block, block.shape[dim] - width, None, axis...  17.7 us
    ppermute x6, waiting for transfers between devices, padded_2(): lax.ppermute(lax.slice_in_dim(block, block.shape[dim] - width, None, axis...  13.5 us
    ppermute x6, starting transfers between devices, padded_2(): lax.ppermute(lax.slice_in_dim(block, 0, width, axis=dim), axis, backward)  13 us
    all_to_all x1, starting transfers between devices, on_device(): lax.all_to_all(outbox, 'girth', split_axis=0, concat_axis=0, tiled=True)  11.4 us
    all_to_all x1, waiting for transfers between devices, on_device(): lax.all_to_all(outbox, 'girth', split_axis=0, concat_axis=0, tiled=True)  7.93 us
    slice x6, local copies, waits for them, and re-layouts, padded_2(): lax.slice_in_dim(block, 0, width, axis=dim)  7.41 us
  transfers between devices with their start and end apart: 14, of which 8 were waited for; matrix products, arithmetic and copies ran while one was open for 6% of the time, Pallas kernels for 0%

commit v1 on v0

--- a/solution.py
+++ b/solution.py
@@ -9,9 +9,27 @@
 CAP = 2
 
 
-def spread(block, axis, source):
-    block = jnp.where(lax.axis_index(axis) == source, block, jnp.zeros_like(block))
-    return lax.psum(block, axis)
+def scatter_gather(block, axis, source):
+    count = lax.axis_size(axis)
+    rows = block.shape[0]
+    send = block.reshape(count, rows // count, block.shape[1])
+    got = lax.all_to_all(send, axis, 0, 0, tiled=True)
+    mine = lax.dynamic_index_in_dim(got, source, 0, keepdims=False)
+    send = jnp.broadcast_to(mine[None], (count,) + mine.shape)
+    full = lax.all_to_all(send, axis, 0, 0, tiled=True)
+    return full.reshape(rows, block.shape[1])
+
+
+def spread(block, axis, source, pair_axis):
+    core = lax.axis_index(pair_axis) % 2
+    half = block.shape[0] // 2
+    mine = lax.dynamic_slice_in_dim(block, core * half, half, 0)
+    got = scatter_gather(mine, axis, source)
+    pairs = [(i, i ^ 1) for i in range(lax.axis_size(pair_axis))]
+    other = lax.ppermute(got, pair_axis, pairs)
+    low = jnp.where(core == 0, got, other)
+    high = jnp.where(core == 0, other, got)
+    return jnp.concatenate([low, high], axis=0)
 
 
 def padded_2(block, sides, width):
@@ -66,7 +84,7 @@
     mode_count = load_bank.shape[0]
     amplitude = wave_amplitude.reshape(6 * row_count, mode_count)
     root = freq_owner[0]
-    factors = spread(load_bank, "girth", root)
+    factors = spread(load_bank, "girth", root, "length")
     loading = jnp.dot(amplitude, factors, preferred_element_type=jnp.float32)
     loading = loading.reshape(6, row_count, girth_cells)
     stiffness = jnp.zeros((row_count, girth_cells), jnp.float32)

time: 301 us -> 184 us (0.61)
  the two profiles are of different devices: /device:TPU:264 before, /device:TPU:201 now
where the time goes in v1:
time: 184 us; the launch traced here: 183 us
  starting transfers between devices  64.4 us (35%)
  local copies, waits for them, and re-layouts  33 us (18%)
  waiting for transfers between devices  29.7 us (16%)
  matrix products  23 us (12%)
  blocking collectives  21.5 us (12%)
  other arithmetic  8.95 us (5%)
  between operations  2.43 us (1%)
    ppermute x6, starting transfers between devices, padded_2(): lax.ppermute(lax.slice_in_dim(block, block.shape[dim] - width, None, axis...  28.2 us
    all_to_all x1, blocking collectives, scatter_gather(): full = lax.all_to_all(send, axis, 0, 0, tiled=True)  21.5 us
    dot_general x3, matrix products, operate_padded(): jnp.einsum('ab,bij->aij', coupling, centre, precision=lax.Precision.HIGHEST)  19.2 us
    all_to_all x1, waiting for transfers between devices, scatter_gather(): got = lax.all_to_all(send, axis, 0, 0, tiled=True)  15.4 us
    ppermute x6, starting transfers between devices, padded_2(): lax.ppermute(lax.slice_in_dim(block, 0, width, axis=dim), axis, backward)  11.5 us
    all_to_all x1, starting transfers between devices, on_device(): lax.all_to_all(outbox, 'girth', split_axis=0, concat_axis=0, tiled=True)  9.94 us
    all_to_all x1, starting transfers between devices, scatter_gather(): got = lax.all_to_all(send, axis, 0, 0, tiled=True)  9.66 us
    all_to_all x1, waiting for transfers between devices, on_device(): lax.all_to_all(outbox, 'girth', split_axis=0, concat_axis=0, tiled=True)  8.57 us
  transfers between devices with their start and end apart: 15, of which 5 were waited for; matrix products, arithmetic and copies ran while one was open for 9% of the time, Pallas kernels for 0%

profile of v1, /device:TPU:201, one launch (start us, length us, event | category | flops | bytes accessed | tf_op | source)
XLA Modules:
  0.0 183.0 jit_solution(13717690421401291161)
XLA Ops:
  0.6 0.0 copy-start
  0.7 2.0 %constant_dynamic-slice_fusion = bf16[1024,256]{1,0:T(8,128)(2,1)} fusion(bf16[2048,256]{1,0:T(8,128)(2,1)} %param.20, s32[]{:T(128)S(6)} %select_n.96), kind=kLoop, calls=%fused_computation.107 | loop fusion | bytes 1048580 | tf_op jit(solution)/shard_map/dynamic_slice | solution.py:26
  2.7 9.7 %all-to-all-start = ((bf16[32,32,256]{2,1,0:T(8,128)(2,1)}), bf16[32,32,256]{2,1,0:T(8,128)(2,1)}, u32[]{:S(2)}, u32[]{:S(2)}) async-start(bf16[32,32,256]{2,1,0:T(8,128)(2,1)} %bitcast.132), calls=%async_computation | async-start | bytes 1048576 | tf_op jit(solution)/shard_map/all_to_all | solution.py:16
  12.4 0.0 copy-start.1
  13.0 15.4 %all-to-all-done = bf16[32,32,256]{2,1,0:T(8,128)(2,1)} async-done(((bf16[32,32,256]{2,1,0:T(8,128)(2,1)}), bf16[32,32,256]{2,1,0:T(8,128)(2,1)}, u32[]{:S(2)}, u32[]{:S(2)}) %all-to-all-start) | async-done | bytes 524320 | tf_op jit(solution)/shard_map/all_to_all | solution.py:16
  28.4 0.7 dynamic-slice_bitcast_fusion
  29.2 21.5 %all_to_all.15 = bf16[32,32,256]{2,1,0:T(8,128)(2,1)} all-to-all(bf16[32,32,256]{2,1,0:T(8,128)(2,1)S(1)} %broadcast_in_dim.84), channel_id=1, replica_groups=mesh['length'=16,'girth'=32] {'girth'}, dimensions={0} | all-to-all | bytes 1048576 | tf_op jit(solution)/shard_map/all_to_all | solution.py:19
  50.7 5.1 %collective-permute-start = (bf16[1024,256]{1,0:T(8,128)(2,1)}, bf16[1024,256]{1,0:T(8,128)(2,1)}, u32[]{:S(2)}, u32[]{:S(2)}) collective-permute-start(bf16[1024,256]{1,0:T(8,128)(2,1)} %bitcast.3), channel_id=1, source_target_pairs={{0,32},{32,0},{64,96},{96,64},{128,160},{160,128},{192,224},{224,1... | collective-permute-start | bytes 1572872 | tf_op jit(solution)/shard_map/ppermute | solution.py:29
  55.8 0.6 gather_fusion
  56.5 0.7 fusion.55
  57.1 5.2 %broadcast_multiply_fusion.1 = (f32[128,256]{1,0:T(8,128)S(1)}, f32[128,256]{1,0:T(8,128)S(1)}) fusion(f32[]{:T(128)} %bitcast.14, s32[128,256]{1,0:T(8,128)S(1)} %copy-done.6, f32[]{:T(128)} %bitcast.13, f32[]{:T(128)} %bitcast.12, f32[]{:T(128)} %bitcast.11, f32[]{:T(128)} %bitcast.10, f32[]{:T(128)} %bitcast.9, f32[]{:T(128)} %bitcast.8, f32[]{:T(128)} %bitcast.7), kind=kLoop, calls=%fused_computation.89 | loop fusion | flops 786432 | bytes 393248 | tf_op jit(solution)/shard_map/mul | solution.py:94
  62.3 1.3 broadcast_select_fusion.1
  63.6 2.0 %convolution_bitcast_fusion.3 = f32[768,256]{0,1:T(8,128)} fusion(bf16[768,2048]{1,0:T(8,128)(2,1)S(1)} %bitcast.127, bf16[1024,256]{1,0:T(8,128)(2,1)S(1)} %get-tuple-element.73, bf16[1024,256]{1,0:T(8,128)(2,1)S(1)} %get-tuple-element.72), kind=kOutput, calls=%fused_computation.22 | convolution fusion | flops 807403520 | bytes 4980736 | tf_op jit(solution)/shard_map/dot_general | solution.py:88
  65.6 2.3 %copy.53 = f32[768,256]{1,0:T(8,128)} copy(f32[768,256]{0,1:T(8,128)} %convolution_bitcast_fusion.3) | data formatting | bytes 1572864 | tf_op jit(solution)/shard_map/dot_general | solution.py:88
  67.9 1.8 broadcast_multiply_fusion
  69.7 1.9 %collective-permute-start.1 = (f32[6,1,256]{2,0,1:T(8,128)S(1)}, f32[6,1,256]{2,0,1:T(8,128)S(1)}, u32[]{:S(2)}, u32[]{:S(2)}) collective-permute-start(f32[6,1,256]{2,0,1:T(8,128)S(1)} %get-tuple-element.71), channel_id=1, source_target_pairs={{32,0},{64,32},{96,64},{128,96},{160,128},{192,160},{224,192},{256... | collective-permute-start | bytes 18440 | tf_op jit(solution)/shard_map/ppermute | solution.py:43
  71.7 5.1 %collective-permute-start.2 = (f32[6,1,256]{2,0,1:T(8,128)S(1)}, f32[6,1,256]{2,0,1:T(8,128)S(1)}, u32[]{:S(2)}, u32[]{:S(2)}) collective-permute-start(f32[6,1,256]{2,0,1:T(8,128)S(1)} %get-tuple-element.70), channel_id=1, source_target_pairs={{0,32},{32,64},{64,96},{96,128},{128,160},{160,192},{192,224},{224... | collective-permute-start | bytes 18440 | tf_op jit(solution)/shard_map/ppermute | solution.py:40
  76.8 0.0 collective-permute-done.1
  76.8 0.8 collective-permute-done.2
  77.6 0.1 pad_maximum_fusion
  77.7 1.1 fusion.50
  78.8 1.3 copy.55
  80.1 1.9 %collective-permute-start.3 = (f32[6,130,1]{1,2,0:T(1,128)S(1)}, f32[6,130,1]{1,2,0:T(1,128)S(1)}, u32[]{:S(2)}, u32[]{:S(2)}) collective-permute-start(f32[6,130,1]{1,2,0:T(1,128)S(1)} %copy.55), channel_id=1, source_target_pairs={{1,0},{2,1},{3,2},{4,3},{5,4},{6,5},{7,6},{8,7},{9,8},{10,9},{11,1... | collective-permute-start | bytes 9368 | tf_op jit(solution)/shard_map/ppermute | solution.py:43
  82.1 1.3 copy.57
  83.4 3.4 %collective-permute-start.4 = (f32[6,130,1]{1,2,0:T(1,128)S(1)}, f32[6,130,1]{1,2,0:T(1,128)S(1)}, u32[]{:S(2)}, u32[]{:S(2)}) collective-permute-start(f32[6,130,1]{1,2,0:T(1,128)S(1)} %copy.57), channel_id=1, source_target_pairs={{0,1},{1,2},{2,3},{3,4},{4,5},{5,6},{6,7},{7,8},{8,9},{9,10},{10,1... | collective-permute-start | bytes 9368 | tf_op jit(solution)/shard_map/ppermute | solution.py:40
  86.7 0.2 convert_reduce_fusion
  86.9 1.2 copy.56
  88.1 1.2 copy.58
  89.3 6.4 %fusion.11 = f32[6,128,256]{2,0,1:T(8,128)S(1)} fusion(f32[6,128,256]{2,0,1:T(8,128)} %copy-done.2, f32[6,128,256]{2,1,0:T(8,128)} %bitcast.129, f32[6,130,1]{2,0,1:T(8,128)} %copy.58, f32[6,1,256]{2,0,1:T(8,128)S(1)} %collective-permute-done.1, f32[6,1,256]{2,0,1:T(8,128)S(1)} %collective-permute-done.2, f32[6,130,1]{2,0,1:T(8,128)} %copy.56, ...), kind=kOutput, calls=%fused_computation.21 | convolution fusion | flops 18284544 | bytes 2640136 | tf_op jit(solution)/shard_map/ab,bij->aij/dot_general | solution.py:55
  95.7 1.9 %collective-permute-start.5 = (f32[6,1,256]{2,0,1:T(8,128)S(1)}, f32[6,1,256]{2,0,1:T(8,128)S(1)}, u32[]{:S(2)}, u32[]{:S(2)}) collective-permute-start(f32[6,1,256]{2,0,1:T(8,128)S(1)} %get-tuple-element.69), channel_id=1, source_target_pairs={{32,0},{64,32},{96,64},{128,96},{160,128},{192,160},{224,192},{256... | collective-permute-start | bytes 18440 | tf_op jit(solution)/shard_map/ppermute | solution.py:43
  97.6 6.2 %collective-permute-start.6 = (f32[6,1,256]{2,0,1:T(8,128)S(1)}, f32[6,1,256]{2,0,1:T(8,128)S(1)}, u32[]{:S(2)}, u32[]{:S(2)}) collective-permute-start(f32[6,1,256]{2,0,1:T(8,128)S(1)} %get-tuple-element.68), channel_id=1, source_target_pairs={{0,32},{32,64},{64,96},{96,128},{128,160},{160,192},{192,224},{224... | collective-permute-start | bytes 18440 | tf_op jit(solution)/shard_map/ppermute | solution.py:40
  103.8 0.7 collective-permute-done.6
  104.6 0.1 pad_maximum_fusion.1
  104.7 1.1 fusion.49
  105.8 1.3 copy.60
  107.1 1.9 %collective-permute-start.7 = (f32[6,130,1]{1,2,0:T(1,128)S(1)}, f32[6,130,1]{1,2,0:T(1,128)S(1)}, u32[]{:S(2)}, u32[]{:S(2)}) collective-permute-start(f32[6,130,1]{1,2,0:T(1,128)S(1)} %copy.60), channel_id=1, source_target_pairs={{1,0},{2,1},{3,2},{4,3},{5,4},{6,5},{7,6},{8,7},{9,8},{10,9},{11,1... | collective-permute-start | bytes 9368 | tf_op jit(solution)/shard_map/ppermute | solution.py:43
  109.1 1.3 copy.62
  110.4 3.6 %collective-permute-start.8 = (f32[6,130,1]{1,2,0:T(1,128)S(1)}, f32[6,130,1]{1,2,0:T(1,128)S(1)}, u32[]{:S(2)}, u32[]{:S(2)}) collective-permute-start(f32[6,130,1]{1,2,0:T(1,128)S(1)} %copy.62), channel_id=1, source_target_pairs={{0,1},{1,2},{2,3},{3,4},{4,5},{5,6},{6,7},{7,8},{8,9},{9,10},{10,1... | collective-permute-start | bytes 9368 | tf_op jit(solution)/shard_map/ppermute | solution.py:40
  114.1 1.2 copy.61
  115.2 1.2 copy.63
  116.4 6.4 %fusion.7 = f32[6,128,256]{2,0,1:T(8,128)S(1)} fusion(f32[6,128,256]{2,0,1:T(8,128)} %copy-done.5, f32[6,128,256]{2,1,0:T(8,128)} %bitcast.130, f32[6,130,1]{2,0,1:T(8,128)} %copy.63, f32[6,1,256]{2,0,1:T(8,128)S(1)} %collective-permute-done.5, f32[6,1,256]{2,0,1:T(8,128)S(1)} %collective-permute-done.6, f32[6,130,1]{2,0,1:T(8,128)} %copy.61, ...), kind=kOutput, calls=%fused_computation.16 | convolution fusion | flops 18087936 | bytes 2640136 | tf_op jit(solution)/shard_map/ab,bij->aij/dot_general | solution.py:55
  122.9 6.1 %collective-permute-start.10 = (f32[6,1,256]{2,0,1:T(8,128)S(1)}, f32[6,1,256]{2,0,1:T(8,128)S(1)}, u32[]{:S(2)}, u32[]{:S(2)}) collective-permute-start(f32[6,1,256]{2,0,1:T(8,128)S(1)} %get-tuple-element.66), channel_id=1, source_target_pairs={{0,32},{32,64},{64,96},{96,128},{128,160},{160,192},{192,224},{224... | collective-permute-start | bytes 18440 | tf_op jit(solution)/shard_map/ppermute | solution.py:40
  128.9 1.9 %collective-permute-start.9 = (f32[6,1,256]{2,0,1:T(8,128)S(1)}, f32[6,1,256]{2,0,1:T(8,128)S(1)}, u32[]{:S(2)}, u32[]{:S(2)}) collective-permute-start(f32[6,1,256]{2,0,1:T(8,128)S(1)} %get-tuple-element.67), channel_id=1, source_target_pairs={{32,0},{64,32},{96,64},{128,96},{160,128},{192,160},{224,192},{256... | collective-permute-start | bytes 18440 | tf_op jit(solution)/shard_map/ppermute | solution.py:43
  130.9 4.2 %collective-permute-done.9 = f32[6,1,256]{2,0,1:T(8,128)S(1)} collective-permute-done((f32[6,1,256]{2,0,1:T(8,128)S(1)}, f32[6,1,256]{2,0,1:T(8,128)S(1)}, u32[]{:S(2)}, u32[]{:S(2)}) %collective-permute-start.9) | collective-permute-done | bytes 6176 | tf_op jit(solution)/shard_map/ppermute | solution.py:43
  135.1 0.1 pad_maximum_fusion.2
  135.2 1.1 fusion.48
  136.4 1.3 copy.65
  137.7 1.9 %collective-permute-start.11 = (f32[6,130,1]{1,2,0:T(1,128)S(1)}, f32[6,130,1]{1,2,0:T(1,128)S(1)}, u32[]{:S(2)}, u32[]{:S(2)}) collective-permute-start(f32[6,130,1]{1,2,0:T(1,128)S(1)} %copy.65), channel_id=1, source_target_pairs={{1,0},{2,1},{3,2},{4,3},{5,4},{6,5},{7,6},{8,7},{9,8},{10,9},{11,1... | collective-permute-start | bytes 9368 | tf_op jit(solution)/shard_map/ppermute | solution.py:43
  139.6 1.3 copy.67
  140.9 3.8 %collective-permute-start.12 = (f32[6,130,1]{1,2,0:T(1,128)S(1)}, f32[6,130,1]{1,2,0:T(1,128)S(1)}, u32[]{:S(2)}, u32[]{:S(2)}) collective-permute-start(f32[6,130,1]{1,2,0:T(1,128)S(1)} %copy.67), channel_id=1, source_target_pairs={{0,1},{1,2},{2,3},{3,4},{4,5},{5,6},{6,7},{7,8},{8,9},{9,10},{10,1... | collective-permute-start | bytes 9368 | tf_op jit(solution)/shard_map/ppermute | solution.py:40
  144.8 1.2 copy.66
  145.9 1.2 copy.68
  147.1 6.4 %fusion.3 = f32[6,128,256]{2,0,1:T(8,128)S(1)} fusion(f32[6,128,256]{2,0,1:T(8,128)} %copy-done.4, f32[6,128,256]{2,1,0:T(8,128)} %bitcast.131, f32[6,130,1]{2,0,1:T(8,128)} %copy.68, f32[6,1,256]{2,0,1:T(8,128)S(1)} %collective-permute-done.9, f32[6,1,256]{2,0,1:T(8,128)S(1)} %collective-permute-done.10, f32[6,130,1]{2,0,1:T(8,128)} %copy.66, ...), kind=kOutput, calls=%fused_computation.11 | convolution fusion | flops 18087936 | bytes 2640136 | tf_op jit(solution)/shard_map/ab,bij->aij/dot_general | solution.py:55
  153.6 1.0 copy-done.3
  154.5 1.8 %fusion.12 = f32[128,4,256]{2,1,0:T(4,128)} fusion(f32[6,128,256]{2,0,1:T(8,128)S(1)} %fusion.3, f32[128,256]{1,0:T(8,128)S(1)} %get-tuple-element.59, f32[4,6]{1,0:T(4,128)S(1)} %copy-done.9), kind=kOutput, calls=%fused_computation.24 | convolution fusion | flops 9568256 | bytes 1441888 | tf_op jit(solution)/shard_map/ka,aij->ikj/dot_general | solution.py:109
  156.4 1.7 gather_fusion.1
  158.0 0.1 broadcast_select_fusion.2
  158.2 1.5 scatter_fusion
  159.7 0.8 copy.70
  160.5 9.9 %all-to-all-start.2 = ((f32[32,2,4,256]{3,1,2,0:T(2,128)}), f32[32,2,4,256]{3,1,2,0:T(2,128)S(1)}, u32[]{:S(2)}, u32[]{:S(2)}) async-start(f32[32,2,4,256]{3,1,2,0:T(2,128)} %copy.70), calls=%async_computation.2 | async-start | bytes 524288 | tf_op jit(solution)/shard_map/all_to_all | solution.py:115
  171.1 0.0 copy-start.7
  171.1 2.4 %copy.76 = f32[6,128,256]{2,1,0:T(8,128)} copy(f32[6,128,256]{2,0,1:T(8,128)} %copy-done.3) | data formatting | bytes 1572864
  173.5 8.6 %all-to-all-done.2 = f32[32,2,4,256]{3,1,2,0:T(2,128)S(1)} async-done(((f32[32,2,4,256]{3,1,2,0:T(2,128)}), f32[32,2,4,256]{3,1,2,0:T(2,128)S(1)}, u32[]{:S(2)}, u32[]{:S(2)}) %all-to-all-start.2) | async-done | bytes 262176 | tf_op jit(solution)/shard_map/all_to_all | solution.py:115
  182.2 0.8 copy.77
  (42 shorter events, 0.3 us)
Async XLA Ops:
  0.6 63.0 %copy-start = (bf16[6,128,2048]{2,1,0:T(8,128)(2,1)S(1)}, bf16[6,128,2048]{2,1,0:T(8,128)(2,1)}, u32[]{:S(2)}) copy-start(bf16[6,128,2048]{2,1,0:T(8,128)(2,1)} %param.19) | copy-start | bytes 9437188
  2.7 25.7 %all-to-all-start = ((bf16[32,32,256]{2,1,0:T(8,128)(2,1)}), bf16[32,32,256]{2,1,0:T(8,128)(2,1)}, u32[]{:S(2)}, u32[]{:S(2)}) async-start(bf16[32,32,256]{2,1,0:T(8,128)(2,1)} %bitcast.132), calls=%async_computation | async-start | bytes 1048576 | tf_op jit(solution)/shard_map/all_to_all | solution.py:16
  12.4 43.4 %copy-start.1 = (f32[6,6]{1,0:T(8,128)S(1)}, f32[6,6]{1,0:T(8,128)}, u32[]{:S(2)}) copy-start(f32[6,6]{1,0:T(8,128)} %param.24) | copy-start | bytes 436
  29.1 27.3 %copy-start.8 = (f32[8]{0:T(128)S(1)}, f32[8]{0:T(128)}, u32[]{:S(2)}) copy-start(f32[8]{0:T(128)} %param.23) | copy-start | bytes 100
  29.1 28.0 %copy-start.6 = (s32[128,256]{1,0:T(8,128)S(1)}, s32[128,256]{1,0:T(8,128)}, u32[]{:S(2)}) copy-start(s32[128,256]{1,0:T(8,128)} %param.22) | copy-start | bytes 393220
  50.7 11.7 %collective-permute-start = (bf16[1024,256]{1,0:T(8,128)(2,1)}, bf16[1024,256]{1,0:T(8,128)(2,1)}, u32[]{:S(2)}, u32[]{:S(2)}) collective-permute-start(bf16[1024,256]{1,0:T(8,128)(2,1)} %bitcast.3), channel_id=1, source_target_pairs={{0,32},{32,0},{64,96},{96,64},{128,160},{160,128},{192,224},{224,1... | collective-permute-start | bytes 1572872 | tf_op jit(solution)/shard_map/ppermute | solution.py:29
  69.7 7.9 %copy-start.2 = (f32[6,128,256]{2,0,1:T(8,128)}, f32[6,128,256]{2,0,1:T(8,128)S(1)}, u32[]{:S(2)}) copy-start(f32[6,128,256]{2,0,1:T(8,128)S(1)} %broadcast_multiply_fusion) | copy-start | bytes 2359300
  69.7 7.0 %collective-permute-start.1 = (f32[6,1,256]{2,0,1:T(8,128)S(1)}, f32[6,1,256]{2,0,1:T(8,128)S(1)}, u32[]{:S(2)}, u32[]{:S(2)}) collective-permute-start(f32[6,1,256]{2,0,1:T(8,128)S(1)} %get-tuple-element.71), channel_id=1, source_target_pairs={{32,0},{64,32},{96,64},{128,96},{160,128},{192,160},{224,192},{256... | collective-permute-start | bytes 18440 | tf_op jit(solution)/shard_map/ppermute | solution.py:43
  71.7 5.9 %collective-permute-start.2 = (f32[6,1,256]{2,0,1:T(8,128)S(1)}, f32[6,1,256]{2,0,1:T(8,128)S(1)}, u32[]{:S(2)}, u32[]{:S(2)}) collective-permute-start(f32[6,1,256]{2,0,1:T(8,128)S(1)} %get-tuple-element.70), channel_id=1, source_target_pairs={{0,32},{32,64},{64,96},{96,128},{128,160},{160,192},{192,224},{224... | collective-permute-start | bytes 18440 | tf_op jit(solution)/shard_map/ppermute | solution.py:40
  78.8 7.9 %copy-start.10 = (s32[1,32,1]{1,2,0:T(1,128)S(1)}, s32[1,32,1]{1,2,0:T(1,128)}, u32[]{:S(2)}) copy-start(s32[1,32,1]{1,2,0:T(1,128)} %param.28) | copy-start | bytes 388
  80.1 6.8 %collective-permute-start.3 = (f32[6,130,1]{1,2,0:T(1,128)S(1)}, f32[6,130,1]{1,2,0:T(1,128)S(1)}, u32[]{:S(2)}, u32[]{:S(2)}) collective-permute-start(f32[6,130,1]{1,2,0:T(1,128)S(1)} %copy.55), channel_id=1, source_target_pairs={{1,0},{2,1},{3,2},{4,3},{5,4},{6,5},{7,6},{8,7},{9,8},{10,9},{11,1... | collective-permute-start | bytes 9368 | tf_op jit(solution)/shard_map/ppermute | solution.py:43
  83.4 4.7 %collective-permute-start.4 = (f32[6,130,1]{1,2,0:T(1,128)S(1)}, f32[6,130,1]{1,2,0:T(1,128)S(1)}, u32[]{:S(2)}, u32[]{:S(2)}) collective-permute-start(f32[6,130,1]{1,2,0:T(1,128)S(1)} %copy.57), channel_id=1, source_target_pairs={{0,1},{1,2},{2,3},{3,4},{4,5},{5,6},{6,7},{7,8},{8,9},{9,10},{10,1... | collective-permute-start | bytes 9368 | tf_op jit(solution)/shard_map/ppermute | solution.py:40
  95.7 9.0 %copy-start.5 = (f32[6,128,256]{2,0,1:T(8,128)}, f32[6,128,256]{2,0,1:T(8,128)S(1)}, u32[]{:S(2)}) copy-start(f32[6,128,256]{2,0,1:T(8,128)S(1)} %fusion.11) | copy-start | bytes 2359300
  95.7 8.1 %collective-permute-start.5 = (f32[6,1,256]{2,0,1:T(8,128)S(1)}, f32[6,1,256]{2,0,1:T(8,128)S(1)}, u32[]{:S(2)}, u32[]{:S(2)}) collective-permute-start(f32[6,1,256]{2,0,1:T(8,128)S(1)} %get-tuple-element.69), channel_id=1, source_target_pairs={{32,0},{64,32},{96,64},{128,96},{160,128},{192,160},{224,192},{256... | collective-permute-start | bytes 18440 | tf_op jit(solution)/shard_map/ppermute | solution.py:43
  97.6 7.0 %collective-permute-start.6 = (f32[6,1,256]{2,0,1:T(8,128)S(1)}, f32[6,1,256]{2,0,1:T(8,128)S(1)}, u32[]{:S(2)}, u32[]{:S(2)}) collective-permute-start(f32[6,1,256]{2,0,1:T(8,128)S(1)} %get-tuple-element.68), channel_id=1, source_target_pairs={{0,32},{32,64},{64,96},{96,128},{128,160},{160,192},{192,224},{224... | collective-permute-start | bytes 18440 | tf_op jit(solution)/shard_map/ppermute | solution.py:40
  105.8 8.2 %copy-start.11 = (s32[1,32]{1,0:T(1,128)S(1)}, s32[1,32]{1,0:T(1,128)}, u32[]{:S(2)}) copy-start(s32[1,32]{1,0:T(1,128)} %param.27) | copy-start | bytes 388
  107.1 6.9 %collective-permute-start.7 = (f32[6,130,1]{1,2,0:T(1,128)S(1)}, f32[6,130,1]{1,2,0:T(1,128)S(1)}, u32[]{:S(2)}, u32[]{:S(2)}) collective-permute-start(f32[6,130,1]{1,2,0:T(1,128)S(1)} %copy.60), channel_id=1, source_target_pairs={{1,0},{2,1},{3,2},{4,3},{5,4},{6,5},{7,6},{8,7},{9,8},{10,9},{11,1... | collective-permute-start | bytes 9368 | tf_op jit(solution)/shard_map/ppermute | solution.py:43
  110.4 4.9 %collective-permute-start.8 = (f32[6,130,1]{1,2,0:T(1,128)S(1)}, f32[6,130,1]{1,2,0:T(1,128)S(1)}, u32[]{:S(2)}, u32[]{:S(2)}) collective-permute-start(f32[6,130,1]{1,2,0:T(1,128)S(1)} %copy.62), channel_id=1, source_target_pairs={{0,1},{1,2},{2,3},{3,4},{4,5},{5,6},{6,7},{7,8},{8,9},{9,10},{10,1... | collective-permute-start | bytes 9368 | tf_op jit(solution)/shard_map/ppermute | solution.py:40
  122.8 12.4 %copy-start.4 = (f32[6,128,256]{2,0,1:T(8,128)}, f32[6,128,256]{2,0,1:T(8,128)S(1)}, u32[]{:S(2)}) copy-start(f32[6,128,256]{2,0,1:T(8,128)S(1)} %fusion.7) | copy-start | bytes 2359300
  122.9 8.0 %collective-permute-start.10 = (f32[6,1,256]{2,0,1:T(8,128)S(1)}, f32[6,1,256]{2,0,1:T(8,128)S(1)}, u32[]{:S(2)}, u32[]{:S(2)}) collective-permute-start(f32[6,1,256]{2,0,1:T(8,128)S(1)} %get-tuple-element.66), channel_id=1, source_target_pairs={{0,32},{32,64},{64,96},{96,128},{128,160},{160,192},{192,224},{224... | collective-permute-start | bytes 18440 | tf_op jit(solution)/shard_map/ppermute | solution.py:40
  128.9 6.2 %collective-permute-start.9 = (f32[6,1,256]{2,0,1:T(8,128)S(1)}, f32[6,1,256]{2,0,1:T(8,128)S(1)}, u32[]{:S(2)}, u32[]{:S(2)}) collective-permute-start(f32[6,1,256]{2,0,1:T(8,128)S(1)} %get-tuple-element.67), channel_id=1, source_target_pairs={{32,0},{64,32},{96,64},{128,96},{160,128},{192,160},{224,192},{256... | collective-permute-start | bytes 18440 | tf_op jit(solution)/shard_map/ppermute | solution.py:43
  137.7 7.1 %collective-permute-start.11 = (f32[6,130,1]{1,2,0:T(1,128)S(1)}, f32[6,130,1]{1,2,0:T(1,128)S(1)}, u32[]{:S(2)}, u32[]{:S(2)}) collective-permute-start(f32[6,130,1]{1,2,0:T(1,128)S(1)} %copy.65), channel_id=1, source_target_pairs={{1,0},{2,1},{3,2},{4,3},{5,4},{6,5},{7,6},{8,7},{9,8},{10,9},{11,1... | collective-permute-start | bytes 9368 | tf_op jit(solution)/shard_map/ppermute | solution.py:43
  140.9 5.0 %collective-permute-start.12 = (f32[6,130,1]{1,2,0:T(1,128)S(1)}, f32[6,130,1]{1,2,0:T(1,128)S(1)}, u32[]{:S(2)}, u32[]{:S(2)}) collective-permute-start(f32[6,130,1]{1,2,0:T(1,128)S(1)} %copy.67), channel_id=1, source_target_pairs={{0,1},{1,2},{2,3},{3,4},{4,5},{5,6},{6,7},{7,8},{8,9},{9,10},{10,1... | collective-permute-start | bytes 9368 | tf_op jit(solution)/shard_map/ppermute | solution.py:40
  147.1 7.4 %copy-start.9 = (f32[4,6]{1,0:T(4,128)S(1)}, f32[4,6]{1,0:T(4,128)}, u32[]{:S(2)}) copy-start(f32[4,6]{1,0:T(4,128)} %param.25) | copy-start | bytes 292
  153.5 1.0 copy-start.3
  160.5 21.6 %all-to-all-start.2 = ((f32[32,2,4,256]{3,1,2,0:T(2,128)}), f32[32,2,4,256]{3,1,2,0:T(2,128)S(1)}, u32[]{:S(2)}, u32[]{:S(2)}) async-start(f32[32,2,4,256]{3,1,2,0:T(2,128)} %copy.70), calls=%async_computation.2 | async-start | bytes 524288 | tf_op jit(solution)/shard_map/all_to_all | solution.py:115
  171.1 11.1 %copy-start.7 = (f32[1,1,32,2,2,256]{5,4,3,2,1,0:T(2,128)S(1)}, f32[1,1,32,2,2,256]{5,4,3,2,1,0:T(2,128)}, u32[]{:S(2)}) copy-start(f32[1,1,32,2,2,256]{5,4,3,2,1,0:T(2,128)} %param.29) | copy-start | bytes 393220

commit v2 on v1

--- a/solution.py
+++ b/solution.py
@@ -91,12 +91,19 @@
     for level in range(class_stiffness.shape[0]):
         stiffness = stiffness + jnp.where(thickness_class == level, class_stiffness[level], 0.0)
     coupling_diag = jnp.diagonal(coupling)[:, None, None]
-    diagonal = 4.0 * stiffness[None] + coupling_diag
-    motion = chebyshev_weight(0) * (loading / diagonal)
+    width = SWEEPS - 1
+    packed = jnp.concatenate([loading, stiffness[None]], axis=0)
+    packed = padded_2(packed, (("length", 1), ("girth", 2)), width)
+    loading_ext = packed[:6]
+    stiffness_ext = packed[6]
+    diagonal_ext = 4.0 * stiffness_ext[None] + coupling_diag
+    motion = chebyshev_weight(0) * (loading_ext / diagonal_ext)
     for sweep in range(1, SWEEPS):
-        padded = padded_2(motion, (("length", 1), ("girth", 2)), 1)
-        applied = operate_padded(padded, stiffness, coupling)
-        motion = motion + chebyshev_weight(sweep) * ((loading - applied) / diagonal)
+        applied = operate_padded(motion, stiffness_ext[1:-1, 1:-1], coupling)
+        loading_ext = loading_ext[:, 1:-1, 1:-1]
+        stiffness_ext = stiffness_ext[1:-1, 1:-1]
+        diagonal_ext = diagonal_ext[:, 1:-1, 1:-1]
+        motion = motion[:, 1:-1, 1:-1] + chebyshev_weight(sweep) * ((loading_ext - applied) / diagonal_ext)
     girth_count = lax.axis_size("girth")
     tile_ids = hotspot_tile[0]
     owner_ids = hotspot_owner[0, :, 0]
@@ -106,14 +113,16 @@
     earlier = positions[None, :] < positions[:, None]
     slot_rank = jnp.sum(jnp.logical_and(matching, earlier).astype(jnp.int32), axis=1)
     target = owner_ids * CAP + slot_rank
-    stresses = stiffness[:, None, :] * jnp.einsum(
-        "ka,aij->ikj", stress_map, motion, precision=lax.Precision.HIGHEST
+    stiffness_rows = jnp.take(stiffness, tile_ids, axis=0)
+    motion_rows = jnp.take(motion, tile_ids, axis=1)
+    stress_rows = stiffness_rows[:, None, :] * jnp.einsum(
+        "ka,aij->ikj", stress_map, motion_rows, precision=lax.Precision.HIGHEST
     )
-    stress_rows = jnp.take(stresses, tile_ids, axis=0)
-    outbox = jnp.zeros((girth_count * CAP, 4, girth_cells), jnp.float32).at[target].set(stress_rows)
-    outbox = outbox.reshape(girth_count, CAP, 4, girth_cells)
+    spectra = square_pairs(stress_rows, 1)
+    outbox = jnp.zeros((girth_count * CAP, 2, girth_cells), jnp.float32).at[target].set(spectra)
+    outbox = outbox.reshape(girth_count, CAP, 2, girth_cells)
     received = lax.all_to_all(outbox, "girth", split_axis=0, concat_axis=0, tiled=True)
-    hotspot_moments = prior_moments + (psd_weight[0] * square_pairs(received, 2))[None, None]
+    hotspot_moments = prior_moments + (psd_weight[0] * received)[None, None]
     return (motion, hotspot_moments)
 
 

time: 184 us -> 131 us (0.71)
  the two profiles are of different devices: /device:TPU:201 before, /device:TPU:192 now
where the time goes in v2:
time: 131 us; the launch traced here: 129 us
  waiting for transfers between devices  40.3 us (31%)
  starting transfers between devices  35.2 us (27%)
  local copies, waits for them, and re-layouts  25.9 us (20%)
  matrix products  13.7 us (10%)
  other arithmetic  11.7 us (9%)
  between operations  2.36 us (2%)
    all_to_all x1, waiting for transfers between devices, scatter_gather(): got = lax.all_to_all(send, axis, 0, 0, tiled=True)  16.2 us
    dot_general x3, matrix products, operate_padded(): jnp.einsum('ab,bij->aij', coupling, centre, precision=lax.Precision.HIGHEST)  11.3 us
    all_to_all x1, starting transfers between devices, scatter_gather(): got = lax.all_to_all(send, axis, 0, 0, tiled=True)  10.2 us
    all_to_all x1, waiting for transfers between devices, scatter_gather(): full = lax.all_to_all(send, axis, 0, 0, tiled=True)  9.97 us
    all_to_all x1, waiting for transfers between devices, on_device(): lax.all_to_all(outbox, 'girth', split_axis=0, concat_axis=0, tiled=True)  7.3 us
    all_to_all x1, starting transfers between devices, on_device(): lax.all_to_all(outbox, 'girth', split_axis=0, concat_axis=0, tiled=True)  6.17 us
    ppermute x2, starting transfers between devices, padded_2(): lax.ppermute(lax.slice_in_dim(block, block.shape[dim] - width, None, axis...  6.15 us
    all_to_all x1, starting transfers between devices, scatter_gather(): full = lax.all_to_all(send, axis, 0, 0, tiled=True)  5.74 us
  transfers between devices with their start and end apart: 8, of which 6 were waited for; matrix products, arithmetic and copies ran while one was open for 10% of the time, Pallas kernels for 0%

profile of v2, /device:TPU:192, one launch (start us, length us, event | category | flops | bytes accessed | tf_op | source)
XLA Modules:
  0.0 129.0 jit_solution(12319080433648699502)
XLA Ops:
  0.6 0.0 copy-start
  0.7 2.0 %constant_dynamic-slice_fusion = bf16[1024,256]{1,0:T(8,128)(2,1)} fusion(bf16[2048,256]{1,0:T(8,128)(2,1)} %param.20, s32[]{:T(128)S(6)} %select_n.106), kind=kLoop, calls=%fused_computation.94 | loop fusion | bytes 1048580 | tf_op jit(solution)/shard_map/dynamic_slice | solution.py:26
  2.7 10.2 %all-to-all-start = ((bf16[32,32,256]{2,1,0:T(8,128)(2,1)}), bf16[32,32,256]{2,1,0:T(8,128)(2,1)}, u32[]{:S(2)}, u32[]{:S(2)}) async-start(bf16[32,32,256]{2,1,0:T(8,128)(2,1)} %bitcast.113), calls=%async_computation | async-start | bytes 1048576 | tf_op jit(solution)/shard_map/all_to_all | solution.py:16
  13.6 16.2 %all-to-all-done = bf16[32,32,256]{2,1,0:T(8,128)(2,1)} async-done(((bf16[32,32,256]{2,1,0:T(8,128)(2,1)}), bf16[32,32,256]{2,1,0:T(8,128)(2,1)}, u32[]{:S(2)}, u32[]{:S(2)}) %all-to-all-start) | async-done | bytes 524320 | tf_op jit(solution)/shard_map/all_to_all | solution.py:16
  29.8 0.7 dynamic-slice_bitcast_fusion
  30.5 0.9 broadcast_in_dim.98
  31.3 5.7 %all-to-all-start.1 = ((bf16[32,32,256]{2,1,0:T(8,128)(2,1)}), bf16[32,32,256]{2,1,0:T(8,128)(2,1)}, u32[]{:S(2)}, u32[]{:S(2)}) async-start(bf16[32,32,256]{2,1,0:T(8,128)(2,1)} %broadcast_in_dim.98), calls=%async_computation.1 | async-start | bytes 1048576 | tf_op jit(solution)/shard_map/all_to_all | solution.py:19
  37.1 0.0 copy-done.9
  37.1 0.7 fusion.52
  37.8 5.1 %select_add_fusion = f32[128,256]{1,0:T(8,128)S(1)} fusion(s32[128,256]{1,0:T(8,128)S(1)} %copy-done.7, f32[]{:T(128)} %bitcast.14, f32[]{:T(128)} %bitcast.13, f32[]{:T(128)} %bitcast.12, f32[]{:T(128)} %bitcast.11, f32[]{:T(128)} %bitcast.10, f32[]{:T(128)} %bitcast.9, f32[]{:T(128)} %bitcast.8, f32[]{:T(128)} %bitcast.7), kind=kLoop, calls=%fused_computation.59 | loop fusion | flops 753664 | bytes 262176 | tf_op jit(solution)/shard_map/add | solution.py:92
  42.9 0.1 broadcast_in_dim.108
  43.0 0.6 gather_fusion.1
  43.6 10.0 %all-to-all-done.1 = bf16[32,32,256]{2,1,0:T(8,128)(2,1)} async-done(((bf16[32,32,256]{2,1,0:T(8,128)(2,1)}), bf16[32,32,256]{2,1,0:T(8,128)(2,1)}, u32[]{:S(2)}, u32[]{:S(2)}) %all-to-all-start.1) | async-done | bytes 524320 | tf_op jit(solution)/shard_map/all_to_all | solution.py:19
  53.6 1.9 %collective-permute-start = (bf16[1024,256]{1,0:T(8,128)(2,1)}, bf16[1024,256]{1,0:T(8,128)(2,1)S(1)}, u32[]{:S(2)}, u32[]{:S(2)}) collective-permute-start(bf16[1024,256]{1,0:T(8,128)(2,1)} %bitcast.3), channel_id=1, source_target_pairs={{0,32},{32,0},{64,96},{96,64},{128,160},{160,128},{192,224},{224,1... | collective-permute-start | bytes 1572872 | tf_op jit(solution)/shard_map/ppermute | solution.py:29
  55.5 0.2 convert_reduce_fusion
  55.7 0.1 broadcast_select_fusion.2
  55.8 1.8 %collective-permute-done = bf16[1024,256]{1,0:T(8,128)(2,1)S(1)} collective-permute-done((bf16[1024,256]{1,0:T(8,128)(2,1)}, bf16[1024,256]{1,0:T(8,128)(2,1)S(1)}, u32[]{:S(2)}, u32[]{:S(2)}) %collective-permute-start) | collective-permute-done | bytes 524320 | tf_op jit(solution)/shard_map/ppermute | solution.py:29
  57.6 1.1 broadcast_select_fusion.1
  58.7 1.9 %convolution_bitcast_fusion.1 = f32[768,256]{0,1:T(8,128)} fusion(bf16[768,2048]{1,0:T(8,128)(2,1)S(1)} %bitcast.110, bf16[1024,256]{1,0:T(8,128)(2,1)S(1)} %get-tuple-element.65, bf16[1024,256]{1,0:T(8,128)(2,1)S(1)} %get-tuple-element.64), kind=kOutput, calls=%fused_computation.36 | convolution fusion | flops 807403520 | bytes 4980736 | tf_op jit(solution)/shard_map/dot_general | solution.py:88
  60.7 2.3 %copy.39 = f32[768,256]{1,0:T(8,128)} copy(f32[768,256]{0,1:T(8,128)} %convolution_bitcast_fusion.1) | data formatting | bytes 1572864 | tf_op jit(solution)/shard_map/dot_general | solution.py:88
  63.0 1.6 %copy.40 = f32[6,128,256]{2,0,1:T(8,128)S(1)} copy(f32[6,128,256]{2,1,0:T(8,128)} %bitcast.111) | data formatting | bytes 1572864 | tf_op jit(solution)/shard_map/reshape | solution.py:89
  64.6 2.0 %collective-permute-start.1 = (f32[7,3,256]{2,0,1:T(8,128)S(1)}, f32[7,3,256]{2,0,1:T(8,128)S(1)}, u32[]{:S(2)}, u32[]{:S(2)}) collective-permute-start(f32[7,3,256]{2,0,1:T(8,128)S(1)} %get-tuple-element.60), channel_id=1, source_target_pairs={{0,32},{32,64},{64,96},{96,128},{128,160},{160,192},{192,224},{224... | collective-permute-start | bytes 64520 | tf_op jit(solution)/shard_map/ppermute | solution.py:40
  66.7 3.5 %collective-permute-start.2 = (f32[7,3,256]{2,0,1:T(8,128)S(1)}, f32[7,3,256]{2,0,1:T(8,128)S(1)}, u32[]{:S(2)}, u32[]{:S(2)}) collective-permute-start(f32[7,3,256]{2,0,1:T(8,128)S(1)} %get-tuple-element.61), channel_id=1, source_target_pairs={{32,0},{64,32},{96,64},{128,96},{160,128},{192,160},{224,192},{256... | collective-permute-start | bytes 64520 | tf_op jit(solution)/shard_map/ppermute | solution.py:43
  70.2 0.0 collective-permute-done.1
  70.2 2.6 %collective-permute-done.2 = f32[7,3,256]{2,0,1:T(8,128)S(1)} collective-permute-done((f32[7,3,256]{2,0,1:T(8,128)S(1)}, f32[7,3,256]{2,0,1:T(8,128)S(1)}, u32[]{:S(2)}, u32[]{:S(2)}) %collective-permute-start.2) | collective-permute-done | bytes 21536 | tf_op jit(solution)/shard_map/ppermute | solution.py:43
  72.8 0.2 pad_maximum_fusion.1
  73.0 0.0 copy-start.1
  73.1 1.1 fusion.50
  74.2 1.4 %copy.41 = f32[7,134,3]{1,0,2:T(8,128)S(1)} copy(f32[7,134,3]{2,0,1:T(8,128)} %get-tuple-element.62) | data formatting | bytes 22512 | tf_op jit(solution)/shard_map/slice | solution.py:41
  75.6 4.1 %collective-permute-start.3 = (f32[7,134,3]{1,0,2:T(8,128)S(1)}, f32[7,134,3]{1,0,2:T(8,128)S(1)}, u32[]{:S(2)}, u32[]{:S(2)}) collective-permute-start(f32[7,134,3]{1,0,2:T(8,128)S(1)} %copy.41), channel_id=1, source_target_pairs={{0,1},{1,2},{2,3},{3,4},{4,5},{5,6},{6,7},{7,8},{8,9},{9,10},{10,1... | collective-permute-start | bytes 33776 | tf_op jit(solution)/shard_map/ppermute | solution.py:40
  79.7 1.4 %copy.42 = f32[7,134,3]{1,0,2:T(8,128)S(1)} copy(f32[7,134,3]{2,0,1:T(8,128)} %get-tuple-element.63) | data formatting | bytes 22512 | tf_op jit(solution)/shard_map/slice | solution.py:43
  81.1 1.5 %collective-permute-start.4 = (f32[7,134,3]{1,0,2:T(8,128)S(1)}, f32[7,134,3]{1,0,2:T(8,128)S(1)}, u32[]{:S(2)}, u32[]{:S(2)}) collective-permute-start(f32[7,134,3]{1,0,2:T(8,128)S(1)} %copy.42), channel_id=1, source_target_pairs={{1,0},{2,1},{3,2},{4,3},{5,4},{6,5},{7,6},{8,7},{9,8},{10,9},{11,1... | collective-permute-start | bytes 33776 | tf_op jit(solution)/shard_map/ppermute | solution.py:43
  82.6 0.6 gather_fusion
  83.2 0.0 collective-permute-done.3
  83.2 1.2 copy.43
  84.4 2.4 %collective-permute-done.4 = f32[7,134,3]{1,0,2:T(8,128)S(1)} collective-permute-done((f32[7,134,3]{1,0,2:T(8,128)S(1)}, f32[7,134,3]{1,0,2:T(8,128)S(1)}, u32[]{:S(2)}, u32[]{:S(2)}) %collective-permute-start.4) | collective-permute-done | bytes 11288 | tf_op jit(solution)/shard_map/ppermute | solution.py:43
  86.8 1.2 copy.44
  88.0 2.7 %broadcast_multiply_fusion = (f32[1,134,262]{2,0,1:T(1,128)S(1)}, f32[1,134,262]{2,0,1:T(1,128)S(1)}) fusion(f32[7,134,3]{2,0,1:T(8,128)} %copy.44, f32[7,3,256]{2,0,1:T(8,128)S(1)} %collective-permute-done.2, f32[1,128,256]{2,0,1:T(1,128)S(1)} %broadcast_in_dim.108, f32[6,128,256]{2,0,1:T(8,128)} %copy-done.2, f32[7,3,256]{2,0,1:T(8,128)S(1)} %collective-permute-done.1, ...), kind=kLoop, calls=%fused_computation.61 | loop fusion | flops 210648 | bytes 1263888 | tf_op jit(solution)/shard_map/mul | solution.py:99
  90.7 0.0 copy-start.3
  90.7 0.0 copy-start.4
  90.7 0.1 slice.218
  90.8 0.1 slice.226
  91.0 0.1 slice.233
  91.1 0.8 copy-done.3
  91.9 0.1 copy-done.4
  92.0 1.1 pad_maximum_fusion
  93.1 0.4 fusion
  93.5 4.0 %fusion.2 = f32[6,132,260]{2,0,1:T(8,128)S(1)} fusion(f32[6,134,262]{2,0,1:T(8,128)S(1)} %get-tuple-element.67, f32[6,134,262]{2,0,1:T(8,128)S(1)} %get-tuple-element.66, f32[7,134,262]{2,0,1:T(8,128)S(1)} %pad_maximum_fusion, f32[132,260]{1,0:T(8,128)S(1)} %slice.218, f32[6,6]{1,0:T(8,128)S(1)} %copy-done.1), kind=kOutput, calls=%fused_computation.9 | convolution fusion | flops 17091360 | bytes 14012800 | tf_op jit(solution)/shard_map/ab,bij->aij/dot_general | solution.py:55
  97.5 3.9 %fusion.8 = f32[6,130,258]{2,0,1:T(8,128)S(1)} fusion(f32[6,134,262]{2,0,1:T(8,128)S(1)} %get-tuple-element.67, f32[6,132,260]{2,0,1:T(8,128)S(1)} %fusion.2, f32[7,134,262]{2,0,1:T(8,128)S(1)} %pad_maximum_fusion, f32[130,258]{1,0:T(8,128)S(1)} %slice.226, f32[6,6]{1,0:T(8,128)S(1)} %copy-done.1), kind=kOutput, calls=%fused_computation.19 | convolution fusion | flops 16702920 | bytes 13797472 | tf_op jit(solution)/shard_map/ab,bij->aij/dot_general | solution.py:55
  101.4 0.0 copy-done.6
  101.4 0.0 copy-start.10
  101.4 3.5 %fusion.22 = f32[6,128,256]{2,0,1:T(8,128)} fusion(f32[6,134,262]{2,0,1:T(8,128)S(1)} %get-tuple-element.67, f32[6,130,258]{2,0,1:T(8,128)S(1)} %fusion.8, f32[128,256]{1,0:T(8,128)S(1)} %slice.233, f32[6,128,256]{2,1,0:T(8,128)S(1)} %bitcast.112, f32[6,6]{1,0:T(8,128)S(1)} %copy-done.1), kind=kOutput, calls=%fused_computation.35 | convolution fusion | flops 16318464 | bytes 9048064 | tf_op jit(solution)/shard_map/ab,bij->aij/dot_general | solution.py:55
  104.9 1.8 %gather_fusion.2 = f32[32,6,256]{2,1,0:T(8,128)S(1)} fusion(f32[6,128,256]{2,0,1:T(8,128)} %fusion.22, s32[1024]{0:T(1024)S(1)} %pad_clamp_fusion), kind=kCustom, calls=%fused_computation.2 | custom fusion | bytes 393344 | tf_op jit(solution)/shard_map/jit(_take)/gather | solution.py:117
  106.7 0.0 copy-done.10
  106.7 0.4 fusion.23
  107.2 0.0 copy-start.8
  107.2 0.1 fusion.51
  107.3 0.1 copy.49
  107.4 0.7 broadcast_in_dim.109
  108.1 3.7 %scatter_fusion = f32[64,2,256]{2,1,0:T(2,128)} fusion(f32[64,2,256]{2,1,0:T(2,128)} %broadcast_in_dim.109, s32[32]{0:T(128)S(1)} %fusion.46, f32[32,2,256]{2,1,0:T(2,128)S(1)} %copy.49), kind=kCustom, calls=%fused_computation.3 | custom fusion | bytes 196736 | tf_op jit(solution)/shard_map/scatter | solution.py:122
  111.8 6.2 %all-to-all-start.2 = ((f32[32,2,2,256]{3,2,1,0:T(2,128)}), f32[32,2,2,256]{3,2,1,0:T(2,128)S(1)}, u32[]{:S(2)}, u32[]{:S(2)}) async-start(f32[32,2,2,256]{3,2,1,0:T(2,128)} %bitcast.36), calls=%async_computation.2 | async-start | bytes 262144 | tf_op jit(solution)/shard_map/all_to_all | solution.py:124
  118.7 2.4 %copy.50 = f32[6,128,256]{2,1,0:T(8,128)} copy(f32[6,128,256]{2,0,1:T(8,128)} %fusion.22) | data formatting | bytes 1572864
  121.0 7.3 %all-to-all-done.2 = f32[32,2,2,256]{3,2,1,0:T(2,128)S(1)} async-done(((f32[32,2,2,256]{3,2,1,0:T(2,128)}), f32[32,2,2,256]{3,2,1,0:T(2,128)S(1)}, u32[]{:S(2)}, u32[]{:S(2)}) %all-to-all-start.2) | async-done | bytes 131104 | tf_op jit(solution)/shard_map/all_to_all | solution.py:124
  128.3 0.7 bitcast_add_fusion
  (25 shorter events, 0.1 us)
Async XLA Ops:
  0.6 58.1 %copy-start = (bf16[6,128,2048]{2,1,0:T(8,128)(2,1)S(1)}, bf16[6,128,2048]{2,1,0:T(8,128)(2,1)}, u32[]{:S(2)}) copy-start(bf16[6,128,2048]{2,1,0:T(8,128)(2,1)} %param.19) | copy-start | bytes 9437188
  0.7 36.4 %copy-start.9 = (f32[8]{0:T(128)S(1)}, f32[8]{0:T(128)}, u32[]{:S(2)}) copy-start(f32[8]{0:T(128)} %param.23) | copy-start | bytes 100
  2.7 35.1 %copy-start.7 = (s32[128,256]{1,0:T(8,128)S(1)}, s32[128,256]{1,0:T(8,128)}, u32[]{:S(2)}) copy-start(s32[128,256]{1,0:T(8,128)} %param.22) | copy-start | bytes 393220
  2.7 40.3 %copy-start.11 = (s32[1,32]{1,0:T(1,128)S(1)}, s32[1,32]{1,0:T(1,128)}, u32[]{:S(2)}) copy-start(s32[1,32]{1,0:T(1,128)} %param.27) | copy-start | bytes 388
  2.7 52.8 %copy-start.12 = (s32[1,32,1]{1,2,0:T(1,128)S(1)}, s32[1,32,1]{1,2,0:T(1,128)}, u32[]{:S(2)}) copy-start(s32[1,32,1]{1,2,0:T(1,128)} %param.28) | copy-start | bytes 388
  2.7 27.1 %all-to-all-start = ((bf16[32,32,256]{2,1,0:T(8,128)(2,1)}), bf16[32,32,256]{2,1,0:T(8,128)(2,1)}, u32[]{:S(2)}, u32[]{:S(2)}) async-start(bf16[32,32,256]{2,1,0:T(8,128)(2,1)} %bitcast.113), calls=%async_computation | async-start | bytes 1048576 | tf_op jit(solution)/shard_map/all_to_all | solution.py:16
  31.3 22.3 %all-to-all-start.1 = ((bf16[32,32,256]{2,1,0:T(8,128)(2,1)}), bf16[32,32,256]{2,1,0:T(8,128)(2,1)}, u32[]{:S(2)}, u32[]{:S(2)}) async-start(bf16[32,32,256]{2,1,0:T(8,128)(2,1)} %broadcast_in_dim.98), calls=%async_computation.1 | async-start | bytes 1048576 | tf_op jit(solution)/shard_map/all_to_all | solution.py:19
  53.6 4.0 %collective-permute-start = (bf16[1024,256]{1,0:T(8,128)(2,1)}, bf16[1024,256]{1,0:T(8,128)(2,1)S(1)}, u32[]{:S(2)}, u32[]{:S(2)}) collective-permute-start(bf16[1024,256]{1,0:T(8,128)(2,1)} %bitcast.3), channel_id=1, source_target_pairs={{0,32},{32,0},{64,96},{96,64},{128,160},{160,128},{192,224},{224,1... | collective-permute-start | bytes 1572872 | tf_op jit(solution)/shard_map/ppermute | solution.py:29
  64.6 8.5 %copy-start.2 = (f32[6,128,256]{2,0,1:T(8,128)}, f32[6,128,256]{2,0,1:T(8,128)S(1)}, u32[]{:S(2)}) copy-start(f32[6,128,256]{2,0,1:T(8,128)S(1)} %copy.40) | copy-start | bytes 2359300
  64.6 5.6 %collective-permute-start.1 = (f32[7,3,256]{2,0,1:T(8,128)S(1)}, f32[7,3,256]{2,0,1:T(8,128)S(1)}, u32[]{:S(2)}, u32[]{:S(2)}) collective-permute-start(f32[7,3,256]{2,0,1:T(8,128)S(1)} %get-tuple-element.60), channel_id=1, source_target_pairs={{0,32},{32,64},{64,96},{96,128},{128,160},{160,192},{192,224},{224... | collective-permute-start | bytes 64520 | tf_op jit(solution)/shard_map/ppermute | solution.py:40
  66.7 6.2 %collective-permute-start.2 = (f32[7,3,256]{2,0,1:T(8,128)S(1)}, f32[7,3,256]{2,0,1:T(8,128)S(1)}, u32[]{:S(2)}, u32[]{:S(2)}) collective-permute-start(f32[7,3,256]{2,0,1:T(8,128)S(1)} %get-tuple-element.61), channel_id=1, source_target_pairs={{32,0},{64,32},{96,64},{128,96},{160,128},{192,160},{224,192},{256... | collective-permute-start | bytes 64520 | tf_op jit(solution)/shard_map/ppermute | solution.py:43
  73.0 9.5 %copy-start.1 = (f32[6,6]{1,0:T(8,128)S(1)}, f32[6,6]{1,0:T(8,128)}, u32[]{:S(2)}) copy-start(f32[6,6]{1,0:T(8,128)} %param.24) | copy-start | bytes 436
  75.6 7.7 %collective-permute-start.3 = (f32[7,134,3]{1,0,2:T(8,128)S(1)}, f32[7,134,3]{1,0,2:T(8,128)S(1)}, u32[]{:S(2)}, u32[]{:S(2)}) collective-permute-start(f32[7,134,3]{1,0,2:T(8,128)S(1)} %copy.41), channel_id=1, source_target_pairs={{0,1},{1,2},{2,3},{3,4},{4,5},{5,6},{6,7},{7,8},{8,9},{9,10},{10,1... | collective-permute-start | bytes 33776 | tf_op jit(solution)/shard_map/ppermute | solution.py:40
  81.1 5.7 %collective-permute-start.4 = (f32[7,134,3]{1,0,2:T(8,128)S(1)}, f32[7,134,3]{1,0,2:T(8,128)S(1)}, u32[]{:S(2)}, u32[]{:S(2)}) collective-permute-start(f32[7,134,3]{1,0,2:T(8,128)S(1)} %copy.42), channel_id=1, source_target_pairs={{1,0},{2,1},{3,2},{4,3},{5,4},{6,5},{7,6},{8,7},{9,8},{10,9},{11,1... | collective-permute-start | bytes 33776 | tf_op jit(solution)/shard_map/ppermute | solution.py:43
  88.0 3.1 %copy-start.5 = (f32[7,134,3]{2,0,1:T(8,128)S(1)}, f32[7,134,3]{2,0,1:T(8,128)}, u32[]{:S(2)}) copy-start(f32[7,134,3]{2,0,1:T(8,128)} %copy.44) | copy-start | bytes 33772
  90.7 1.2 copy-start.3
  90.7 1.4 %copy-start.4 = (f32[7,134,3]{2,0,1:T(8,128)S(1)}, f32[7,134,3]{2,0,1:T(8,128)}, u32[]{:S(2)}) copy-start(f32[7,134,3]{2,0,1:T(8,128)} %copy.43) | copy-start | bytes 33772
  97.5 3.9 %copy-start.6 = (f32[768,256]{1,0:T(8,128)S(1)}, f32[768,256]{1,0:T(8,128)}, u32[]{:S(2)}) copy-start(f32[768,256]{1,0:T(8,128)} %copy.39) | copy-start | bytes 2359300
  101.4 5.3 %copy-start.10 = (f32[4,6]{1,0:T(4,128)S(1)}, f32[4,6]{1,0:T(4,128)}, u32[]{:S(2)}) copy-start(f32[4,6]{1,0:T(4,128)} %param.25) | copy-start | bytes 292
  107.2 21.1 %copy-start.8 = (f32[1,1,32,2,2,256]{5,4,3,2,1,0:T(2,128)S(1)}, f32[1,1,32,2,2,256]{5,4,3,2,1,0:T(2,128)}, u32[]{:S(2)}) copy-start(f32[1,1,32,2,2,256]{5,4,3,2,1,0:T(2,128)} %param.29) | copy-start | bytes 393220
  111.8 16.5 %all-to-all-start.2 = ((f32[32,2,2,256]{3,2,1,0:T(2,128)}), f32[32,2,2,256]{3,2,1,0:T(2,128)S(1)}, u32[]{:S(2)}, u32[]{:S(2)}) async-start(f32[32,2,2,256]{3,2,1,0:T(2,128)} %bitcast.36), calls=%async_computation.2 | async-start | bytes 262144 | tf_op jit(solution)/shard_map/all_to_all | solution.py:124

commit v3 on v2

--- a/solution.py
+++ b/solution.py
@@ -82,18 +82,20 @@
     row_count = wave_amplitude.shape[1]
     girth_cells = load_bank.shape[1]
     mode_count = load_bank.shape[0]
-    amplitude = wave_amplitude.reshape(6 * row_count, mode_count)
+    width = SWEEPS - 1
     root = freq_owner[0]
-    factors = spread(load_bank, "girth", root, "length")
-    loading = jnp.dot(amplitude, factors, preferred_element_type=jnp.float32)
-    loading = loading.reshape(6, row_count, girth_cells)
     stiffness = jnp.zeros((row_count, girth_cells), jnp.float32)
     for level in range(class_stiffness.shape[0]):
         stiffness = stiffness + jnp.where(thickness_class == level, class_stiffness[level], 0.0)
+    amplitude_ext = padded_2(wave_amplitude, (("length", 1),), width)
+    stiffness_rows = padded_2(stiffness, (("length", 0),), width)
+    factors = spread(load_bank, "girth", root, "length")
+    ext_rows = row_count + 2 * width
+    loading = jnp.dot(amplitude_ext.reshape(6 * ext_rows, mode_count), factors, preferred_element_type=jnp.float32)
+    loading = loading.reshape(6, ext_rows, girth_cells)
     coupling_diag = jnp.diagonal(coupling)[:, None, None]
-    width = SWEEPS - 1
-    packed = jnp.concatenate([loading, stiffness[None]], axis=0)
-    packed = padded_2(packed, (("length", 1), ("girth", 2)), width)
+    packed = jnp.concatenate([loading, stiffness_rows[None]], axis=0)
+    packed = padded_2(packed, (("girth", 2),), width)
     loading_ext = packed[:6]
     stiffness_ext = packed[6]
     diagonal_ext = 4.0 * stiffness_ext[None] + coupling_diag
@@ -113,13 +115,17 @@
     earlier = positions[None, :] < positions[:, None]
     slot_rank = jnp.sum(jnp.logical_and(matching, earlier).astype(jnp.int32), axis=1)
     target = owner_ids * CAP + slot_rank
-    stiffness_rows = jnp.take(stiffness, tile_ids, axis=0)
-    motion_rows = jnp.take(motion, tile_ids, axis=1)
-    stress_rows = stiffness_rows[:, None, :] * jnp.einsum(
-        "ka,aij->ikj", stress_map, motion_rows, precision=lax.Precision.HIGHEST
+    slots = jnp.arange(girth_count * CAP, dtype=jnp.int32)
+    hit = target[None, :] == slots[:, None]
+    filled = jnp.any(hit, axis=1)
+    slot_row = jnp.sum(jnp.where(hit, tile_ids[None, :], 0), axis=1)
+    stiffness_at = jnp.take(stiffness, slot_row, axis=0)
+    motion_at = jnp.take(motion, slot_row, axis=1)
+    stress_rows = stiffness_at[:, None, :] * jnp.einsum(
+        "ka,aij->ikj", stress_map, motion_at, precision=lax.Precision.HIGHEST
     )
     spectra = square_pairs(stress_rows, 1)
-    outbox = jnp.zeros((girth_count * CAP, 2, girth_cells), jnp.float32).at[target].set(spectra)
+    outbox = jnp.where(filled[:, None, None], spectra, 0.0)
     outbox = outbox.reshape(girth_count, CAP, 2, girth_cells)
     received = lax.all_to_all(outbox, "girth", split_axis=0, concat_axis=0, tiled=True)
     hotspot_moments = prior_moments + (psd_weight[0] * received)[None, None]

time: 131 us -> 118 us (0.901)
  local copies, waits for them, and re-layouts: 25.9 us -> 13.5 us
  starting transfers between devices: 35.2 us -> 43.2 us
  waiting for transfers between devices: 40.3 us -> 33.6 us
  matrix products: 13.7 us -> 8.37 us
  other arithmetic: 11.7 us -> 16.2 us
    all_to_all x1, waiting for transfers between devices: 16.2 us -> 3.54 us  [scatter_gather(): got = lax.all_to_all(send, axis, 0, 0, tiled=True)]
    dot_general x3, matrix products: 11.3 us -> 4.71 us  [operate_padded(): jnp.einsum('ab,bij->aij', coupling, centre, precision=lax.Precision.HIGHEST)]
    ppermute x2 -> x3, waiting for transfers between devices: 0.01 us -> 6.38 us  [padded_2(): lax.ppermute(lax.slice_in_dim(block, block.shape[dim] - width, None, axis...]
    add x0 -> x6, other arithmetic: none -> 5.87 us  [the longest x3 5.7 us: on_device(): motion[:, 1:-1, 1:-1]]
    ppermute x2 -> x3, starting transfers between devices: 6.15 us -> 10.2 us  [padded_2(): lax.ppermute(lax.slice_in_dim(block, block.shape[dim] - width, None, axis...]
    scatter x1 -> x0, local copies, waits for them, and re-layouts: 3.75 us -> none  [on_device(): jnp.zeros((girth_count * CAP, 2, girth_cells), jnp.float32).at[target]]
    mul x1 -> x0, other arithmetic: 2.68 us -> none  [on_device(): diagonal_ext = 4.0 * stiffness_ext[None] + coupling_diag]
    all_to_all x1, waiting for transfers between devices: 7.3 us -> 9.8 us  [on_device(): lax.all_to_all(outbox, 'girth', split_axis=0, concat_axis=0, tiled=True)]
  transfers between devices with their start and end apart: 8 -> 10, of which waited for: 6 -> 5; matrix products, arithmetic and copies ran while one was open for 10% -> 11% of each run, Pallas kernels for 0% -> 0%
where the time goes in v3:
time: 118 us; the launch traced here: 117 us
  starting transfers between devices  43.2 us (37%)
  waiting for transfers between devices  33.6 us (28%)
  other arithmetic  16.2 us (14%)
  local copies, waits for them, and re-layouts  13.5 us (11%)
  matrix products  8.37 us (7%)
  between operations  2.39 us (2%)
    ppermute x3, starting transfers between devices, padded_2(): lax.ppermute(lax.slice_in_dim(block, block.shape[dim] - width, None, axis...  10.2 us
    all_to_all x1, waiting for transfers between devices, scatter_gather(): full = lax.all_to_all(send, axis, 0, 0, tiled=True)  9.99 us
    all_to_all x1, starting transfers between devices, scatter_gather(): got = lax.all_to_all(send, axis, 0, 0, tiled=True)  9.95 us
    all_to_all x1, waiting for transfers between devices, on_device(): lax.all_to_all(outbox, 'girth', split_axis=0, concat_axis=0, tiled=True)  9.8 us
    ppermute x3, starting transfers between devices, padded_2(): lax.ppermute(lax.slice_in_dim(block, 0, width, axis=dim), axis, backward)  7.08 us
    ppermute x3, waiting for transfers between devices, padded_2(): lax.ppermute(lax.slice_in_dim(block, block.shape[dim] - width, None, axis...  6.38 us
    all_to_all x1, starting transfers between devices, scatter_gather(): full = lax.all_to_all(send, axis, 0, 0, tiled=True)  6.27 us
    all_to_all x1, starting transfers between devices, on_device(): lax.all_to_all(outbox, 'girth', split_axis=0, concat_axis=0, tiled=True)  5.76 us
  transfers between devices with their start and end apart: 10, of which 5 were waited for; matrix products, arithmetic and copies ran while one was open for 11% of the time, Pallas kernels for 0%

profile of v3, /device:TPU:192, one launch (start us, length us, event | category | flops | bytes accessed | tf_op | source)
XLA Modules:
  0.0 117.3 jit_solution(3727478880364695428)
XLA Ops:
  0.6 0.0 copy-start
  0.7 1.2 %copy-done = bf16[2048,256]{1,0:T(8,128)(2,1)S(1)} copy-done((bf16[2048,256]{1,0:T(8,128)(2,1)S(1)}, bf16[2048,256]{1,0:T(8,128)(2,1)}, u32[]{:S(2)}) %copy-start) | copy-done | bytes 1048600
  1.9 0.8 constant_dynamic-slice_fusion
  2.7 9.9 %all-to-all-start = ((bf16[32,32,256]{2,1,0:T(8,128)(2,1)}), bf16[32,32,256]{2,1,0:T(8,128)(2,1)S(1)}, u32[]{:S(2)}, u32[]{:S(2)}) async-start(bf16[32,32,256]{2,1,0:T(8,128)(2,1)} %bitcast), calls=%async_computation | async-start | bytes 1048576 | tf_op jit(solution)/shard_map/all_to_all | solution.py:16
  12.7 0.0 copy-start.12
  12.7 0.0 copy-start.13
  12.7 1.1 fusion.52
  13.8 1.9 %collective-permute-start = (bf16[6,3,2048]{2,1,0:T(4,128)(2,1)S(1)}, bf16[6,3,2048]{2,1,0:T(4,128)(2,1)S(1)}, u32[]{:S(2)}, u32[]{:S(2)}) collective-permute-start(bf16[6,3,2048]{2,1,0:T(4,128)(2,1)S(1)} %get-tuple-element.52), channel_id=1, source_target_pairs={{0,32},{32,64},{64,96},{96,128},{128,160},{160,192},{192,224},{224... | collective-permute-start | bytes 221192 | tf_op jit(solution)/shard_map/ppermute | solution.py:40
  15.7 3.6 %collective-permute-start.1 = (bf16[6,3,2048]{2,1,0:T(4,128)(2,1)S(1)}, bf16[6,3,2048]{2,1,0:T(4,128)(2,1)S(1)}, u32[]{:S(2)}, u32[]{:S(2)}) collective-permute-start(bf16[6,3,2048]{2,1,0:T(4,128)(2,1)S(1)} %get-tuple-element.53), channel_id=1, source_target_pairs={{32,0},{64,32},{96,64},{128,96},{160,128},{192,160},{224,192},{256... | collective-permute-start | bytes 221192 | tf_op jit(solution)/shard_map/ppermute | solution.py:43
  20.0 0.7 fusion.55
  20.7 5.2 %select_add_fusion = f32[128,256]{1,0:T(8,128)S(1)} fusion(s32[128,256]{1,0:T(8,128)S(1)} %copy-done.3, f32[]{:T(128)} %bitcast.12, f32[]{:T(128)} %bitcast.11, f32[]{:T(128)} %bitcast.10, f32[]{:T(128)} %bitcast.9, f32[]{:T(128)} %bitcast.8, f32[]{:T(128)} %bitcast.7, f32[]{:T(128)} %bitcast.6, f32[]{:T(128)} %bitcast.5), kind=kLoop, calls=%fused_computation.69 | loop fusion | flops 753664 | bytes 262176 | tf_op jit(solution)/shard_map/add | solution.py:89
  26.0 3.5 %all-to-all-done = bf16[32,32,256]{2,1,0:T(8,128)(2,1)S(1)} async-done(((bf16[32,32,256]{2,1,0:T(8,128)(2,1)}), bf16[32,32,256]{2,1,0:T(8,128)(2,1)S(1)}, u32[]{:S(2)}, u32[]{:S(2)}) %all-to-all-start) | async-done | bytes 524320 | tf_op jit(solution)/shard_map/all_to_all | solution.py:16
  29.5 0.9 broadcast_in_dim.125
  30.4 6.3 %all-to-all-start.1 = ((bf16[32,32,256]{2,1,0:T(8,128)(2,1)}), bf16[32,32,256]{2,1,0:T(8,128)(2,1)S(1)}, u32[]{:S(2)}, u32[]{:S(2)}) async-start(bf16[32,32,256]{2,1,0:T(8,128)(2,1)} %broadcast_in_dim.125), calls=%async_computation.1 | async-start | bytes 1048576 | tf_op jit(solution)/shard_map/all_to_all | solution.py:19
  36.7 3.6 %collective-permute-start.3 = (f32[3,256]{1,0:T(4,128)S(1)}, f32[3,256]{1,0:T(4,128)S(1)}, u32[]{:S(2)}, u32[]{:S(2)}) collective-permute-start(f32[3,256]{1,0:T(4,128)S(1)} %get-tuple-element.64), channel_id=1, source_target_pairs={{0,32},{32,64},{64,96},{96,128},{128,160},{160,192},{192,224},{224... | collective-permute-start | bytes 9224 | tf_op jit(solution)/shard_map/ppermute | solution.py:40
  40.3 2.0 %collective-permute-start.4 = (f32[3,256]{1,0:T(4,128)S(1)}, f32[3,256]{1,0:T(4,128)S(1)}, u32[]{:S(2)}, u32[]{:S(2)}) collective-permute-start(f32[3,256]{1,0:T(4,128)S(1)} %get-tuple-element.65), channel_id=1, source_target_pairs={{32,0},{64,32},{96,64},{128,96},{160,128},{192,160},{224,192},{256... | collective-permute-start | bytes 9224 | tf_op jit(solution)/shard_map/ppermute | solution.py:43
  42.2 0.2 convert_reduce_fusion
  42.4 0.1 select_reduce_fusion
  42.6 10.0 %all-to-all-done.1 = bf16[32,32,256]{2,1,0:T(8,128)(2,1)S(1)} async-done(((bf16[32,32,256]{2,1,0:T(8,128)(2,1)}), bf16[32,32,256]{2,1,0:T(8,128)(2,1)S(1)}, u32[]{:S(2)}, u32[]{:S(2)}) %all-to-all-start.1) | async-done | bytes 524320 | tf_op jit(solution)/shard_map/all_to_all | solution.py:19
  52.6 4.0 %collective-permute-start.2 = (bf16[1024,256]{1,0:T(8,128)(2,1)S(1)}, bf16[1024,256]{1,0:T(8,128)(2,1)S(1)}, u32[]{:S(2)}, u32[]{:S(2)}) collective-permute-start(bf16[1024,256]{1,0:T(8,128)(2,1)S(1)} %bitcast.83), channel_id=1, source_target_pairs={{0,32},{32,0},{64,96},{96,64},{128,160},{160,128},{192,224},{224,1... | collective-permute-start | bytes 1572872 | tf_op jit(solution)/shard_map/ppermute | solution.py:29
  56.5 0.0 copy-start.7
  56.5 0.7 gather_fusion.1
  57.2 0.1 broadcast_select_fusion.2
  57.3 0.7 fusion.43
  58.0 0.0 collective-permute-done.2
  58.0 0.1 broadcast_select_fusion.1
  58.2 3.0 %fusion = f32[6,134,256]{2,1,0:T(8,128)S(1)} fusion(bf16[6,3,2048]{2,1,0:T(4,128)(2,1)S(1)} %collective-permute-done.1, bf16[6,128,2048]{2,1,0:T(8,128)(2,1)} %param.19, bf16[6,3,2048]{2,1,0:T(4,128)(2,1)S(1)} %collective-permute-done, bf16[1024,256]{1,0:T(8,128)(2,1)S(1)} %get-tuple-element.55, bf16[1024,256]{1,0:T(8,128)(2,1)S(1)} %get-tuple-element.54), kind=kOutput, calls=%fused_computation.3 | convolution fusion | flops 855031808 | bytes 5165056 | tf_op jit(solution)/shard_map/dot_general | solution.py:94
  61.2 0.0 copy-start.1
  61.2 1.0 fusion.36
  62.2 4.7 %collective-permute-start.5 = (f32[7,134,3]{2,1,0:T(8,128)}, f32[7,134,3]{2,1,0:T(8,128)S(1)}, u32[]{:S(2)}, u32[]{:S(2)}) collective-permute-start(f32[7,134,3]{2,1,0:T(8,128)} %get-tuple-element.56), channel_id=1, source_target_pairs={{0,1},{1,2},{2,3},{3,4},{4,5},{5,6},{6,7},{7,8},{8,9},{9,10},{10,1... | collective-permute-start | bytes 33776 | tf_op jit(solution)/shard_map/ppermute | solution.py:40
  66.9 1.5 %collective-permute-start.6 = (f32[7,134,3]{2,1,0:T(8,128)S(1)}, f32[7,134,3]{2,1,0:T(8,128)S(1)}, u32[]{:S(2)}, u32[]{:S(2)}) collective-permute-start(f32[7,134,3]{2,1,0:T(8,128)S(1)} %get-tuple-element.57), channel_id=1, source_target_pairs={{1,0},{2,1},{3,2},{4,3},{5,4},{6,5},{7,6},{8,7},{9,8},{10,9},{11,1... | collective-permute-start | bytes 33776 | tf_op jit(solution)/shard_map/ppermute | solution.py:43
  68.3 0.6 or_bitcast_fusion
  68.9 1.4 %broadcast_in_dim.136 = pred[32,2]{1,0:T(8,128)(4,1)} reshape(pred[64]{0:T(512)(128)(4,1)} %fusion.43) | data formatting | bytes 128 | tf_op jit(solution)/shard_map/jit(_where)/broadcast_in_dim | solution.py:128
  70.3 1.4 %gather_fusion = f32[6]{0:T(128)} fusion(f32[6,6]{1,0:T(8,128)S(1)} %copy-done.1, s32[6]{0:T(128)} %or_bitcast_fusion), kind=kCustom, calls=%fused_computation | custom fusion | bytes 96 | tf_op jit(solution)/shard_map/jit(diagonal)/cond/branch_0_fun/gather | solution.py:96
  71.7 6.4 %collective-permute-done.5 = f32[7,134,3]{2,1,0:T(8,128)S(1)} collective-permute-done((f32[7,134,3]{2,1,0:T(8,128)}, f32[7,134,3]{2,1,0:T(8,128)S(1)}, u32[]{:S(2)}, u32[]{:S(2)}) %collective-permute-start.5) | collective-permute-done | bytes 11288 | tf_op jit(solution)/shard_map/ppermute | solution.py:40
  78.1 3.8 %collective-permute-done.6 = f32[7,134,3]{2,1,0:T(8,128)S(1)} collective-permute-done((f32[7,134,3]{2,1,0:T(8,128)S(1)}, f32[7,134,3]{2,1,0:T(8,128)S(1)}, u32[]{:S(2)}, u32[]{:S(2)}) %collective-permute-start.6) | collective-permute-done | bytes 11288 | tf_op jit(solution)/shard_map/ppermute | solution.py:43
  81.9 0.1 multiply_bitcast_fusion
  82.0 0.1 slice.231
  82.2 0.1 slice.239
  82.3 0.1 slice.247
  82.4 0.6 pad_maximum_fusion
  83.0 0.1 copy-done.11
  83.1 0.3 fusion.22
  83.3 0.5 slice.229
  83.8 1.6 %fusion.6 = f32[132,260,6]{1,2,0:T(8,128)S(1)} fusion(f32[6,132,260]{2,1,0:T(8,128)S(1)} %slice.229, f32[6,6]{1,0:T(8,128)S(1)} %copy-done.1), kind=kOutput, calls=%fused_computation.9 | convolution fusion | flops 14826240 | bytes 1647504 | tf_op jit(solution)/shard_map/ab,bij->aij/dot_general | solution.py:55
  85.4 2.1 %fusion.17 = f32[6,132,260]{2,1,0:T(8,128)S(1)} fusion(f32[6,134,262]{2,1,0:T(8,128)S(1)} %get-tuple-element.63, f32[6,134,262]{2,1,0:T(8,128)S(1)} %get-tuple-element.62, f32[7,134,262]{2,1,0:T(8,128)S(1)} %pad_maximum_fusion, f32[132,260,6]{1,2,0:T(8,128)S(1)} %fusion.6, f32[132,260]{1,0:T(8,128)S(1)} %slice.231), kind=kLoop, calls=%fused_computation.26 | loop fusion | flops 2265120 | bytes 7550400 | tf_op jit(solution)/shard_map/add | solution.py:108
  87.6 0.5 slice.237
  88.0 1.6 %fusion.8 = f32[130,258,6]{1,2,0:T(8,128)S(1)} fusion(f32[6,130,258]{2,1,0:T(8,128)S(1)} %slice.237, f32[6,6]{1,0:T(8,128)S(1)} %copy-done.1), kind=kOutput, calls=%fused_computation.11 | convolution fusion | flops 14489280 | bytes 1610064 | tf_op jit(solution)/shard_map/ab,bij->aij/dot_general | solution.py:55
  89.7 2.1 %fusion.11 = f32[6,130,258]{2,1,0:T(8,128)S(1)} fusion(f32[6,134,262]{2,1,0:T(8,128)S(1)} %get-tuple-element.63, f32[6,132,260]{2,1,0:T(8,128)S(1)} %fusion.17, f32[7,134,262]{2,1,0:T(8,128)S(1)} %pad_maximum_fusion, f32[130,258,6]{1,2,0:T(8,128)S(1)} %fusion.8, f32[130,258]{1,0:T(8,128)S(1)} %slice.239), kind=kLoop, calls=%fused_computation.16 | loop fusion | flops 2213640 | bytes 7378800 | tf_op jit(solution)/shard_map/add | solution.py:108
  91.8 0.3 slice.245
  92.1 1.4 %fusion.26 = f32[128,256,6]{1,2,0:T(8,128)S(1)} fusion(f32[6,128,256]{2,1,0:T(8,128)S(1)} %slice.245, f32[6,6]{1,0:T(8,128)S(1)} %copy-done.1), kind=kOutput, calls=%fused_computation.41 | convolution fusion | flops 14155776 | bytes 1573008 | tf_op jit(solution)/shard_map/ab,bij->aij/dot_general | solution.py:55
  93.5 1.4 %fusion.29 = f32[6,128,256]{2,1,0:T(8,128)S(1)} fusion(f32[6,134,262]{2,1,0:T(8,128)S(1)} %get-tuple-element.63, f32[6,130,258]{2,1,0:T(8,128)S(1)} %fusion.11, f32[6,134,256]{2,1,0:T(8,128)S(1)} %fusion, f32[128,256,6]{1,2,0:T(8,128)S(1)} %fusion.26, f32[128,256]{1,0:T(8,128)S(1)} %slice.247), kind=kLoop, calls=%fused_computation.47 | loop fusion | flops 2162688 | bytes 7208960 | tf_op jit(solution)/shard_map/add | solution.py:108
  95.0 0.0 copy-start.2
  95.0 1.5 %copy.41 = f32[6,128,256]{2,0,1:T(8,128)} copy(f32[6,128,256]{2,1,0:T(8,128)S(1)} %fusion.29) | data formatting | bytes 1572864 | tf_op jit(solution)/shard_map/add | solution.py:108
  96.5 1.9 %gather_fusion.2 = f32[64,6,256]{2,1,0:T(8,128)S(1)} fusion(f32[6,128,256]{2,0,1:T(8,128)} %copy.41, s32[1024]{0:T(1024)} %copy-done.7), kind=kCustom, calls=%fused_computation.2 | custom fusion | bytes 786688 | tf_op jit(solution)/shard_map/jit(_take)/gather | solution.py:123
  98.5 0.0 copy-start.4
  98.5 0.7 fusion.23
  99.1 0.2 fusion.53
  99.4 0.1 stack.12
  99.4 0.1 stack.13
  99.5 0.8 maximum_select_fusion
  100.3 5.8 %all-to-all-start.2 = ((f32[32,2,2,256]{3,2,1,0:T(2,128)}), f32[32,2,2,256]{3,2,1,0:T(2,128)S(1)}, u32[]{:S(2)}, u32[]{:S(2)}) async-start(f32[32,2,2,256]{3,2,1,0:T(2,128)} %maximum_select_fusion), calls=%async_computation.2 | async-start | bytes 262144 | tf_op jit(solution)/shard_map/all_to_all | solution.py:130
  106.7 9.8 %all-to-all-done.2 = f32[32,2,2,256]{3,2,1,0:T(2,128)S(1)} async-done(((f32[32,2,2,256]{3,2,1,0:T(2,128)}), f32[32,2,2,256]{3,2,1,0:T(2,128)S(1)}, u32[]{:S(2)}, u32[]{:S(2)}) %all-to-all-start.2) | async-done | bytes 131104 | tf_op jit(solution)/shard_map/all_to_all | solution.py:130
  116.5 0.7 bitcast_add_fusion
  (31 shorter events, 0.1 us)
Async XLA Ops:
  0.6 1.2 %copy-start = (bf16[2048,256]{1,0:T(8,128)(2,1)S(1)}, bf16[2048,256]{1,0:T(8,128)(2,1)}, u32[]{:S(2)}) copy-start(bf16[2048,256]{1,0:T(8,128)(2,1)} %param.20) | copy-start | bytes 3145732
  1.9 18.2 %copy-start.5 = (f32[8]{0:T(128)S(1)}, f32[8]{0:T(128)}, u32[]{:S(2)}) copy-start(f32[8]{0:T(128)} %param.23) | copy-start | bytes 100
  1.9 18.9 %copy-start.3 = (s32[128,256]{1,0:T(8,128)S(1)}, s32[128,256]{1,0:T(8,128)}, u32[]{:S(2)}) copy-start(s32[128,256]{1,0:T(8,128)} %param.22) | copy-start | bytes 393220
  2.7 26.8 %all-to-all-start = ((bf16[32,32,256]{2,1,0:T(8,128)(2,1)}), bf16[32,32,256]{2,1,0:T(8,128)(2,1)S(1)}, u32[]{:S(2)}, u32[]{:S(2)}) async-start(bf16[32,32,256]{2,1,0:T(8,128)(2,1)} %bitcast), calls=%async_computation | async-start | bytes 1048576 | tf_op jit(solution)/shard_map/all_to_all | solution.py:16
  12.7 29.6 %copy-start.12 = (s32[1,32,1]{1,2,0:T(1,128)S(1)}, s32[1,32,1]{1,2,0:T(1,128)}, u32[]{:S(2)}) copy-start(s32[1,32,1]{1,2,0:T(1,128)} %param.28) | copy-start | bytes 388
  12.7 29.8 %copy-start.13 = (s32[1,32]{1,0:T(1,128)S(1)}, s32[1,32]{1,0:T(1,128)}, u32[]{:S(2)}) copy-start(s32[1,32]{1,0:T(1,128)} %param.27) | copy-start | bytes 388
  13.8 44.4 %collective-permute-start = (bf16[6,3,2048]{2,1,0:T(4,128)(2,1)S(1)}, bf16[6,3,2048]{2,1,0:T(4,128)(2,1)S(1)}, u32[]{:S(2)}, u32[]{:S(2)}) collective-permute-start(bf16[6,3,2048]{2,1,0:T(4,128)(2,1)S(1)} %get-tuple-element.52), channel_id=1, source_target_pairs={{0,32},{32,64},{64,96},{96,128},{128,160},{160,192},{192,224},{224... | collective-permute-start | bytes 221192 | tf_op jit(solution)/shard_map/ppermute | solution.py:40
  15.7 42.4 %collective-permute-start.1 = (bf16[6,3,2048]{2,1,0:T(4,128)(2,1)S(1)}, bf16[6,3,2048]{2,1,0:T(4,128)(2,1)S(1)}, u32[]{:S(2)}, u32[]{:S(2)}) collective-permute-start(bf16[6,3,2048]{2,1,0:T(4,128)(2,1)S(1)} %get-tuple-element.53), channel_id=1, source_target_pairs={{32,0},{64,32},{96,64},{128,96},{160,128},{192,160},{224,192},{256... | collective-permute-start | bytes 221192 | tf_op jit(solution)/shard_map/ppermute | solution.py:43
  30.4 22.2 %all-to-all-start.1 = ((bf16[32,32,256]{2,1,0:T(8,128)(2,1)}), bf16[32,32,256]{2,1,0:T(8,128)(2,1)S(1)}, u32[]{:S(2)}, u32[]{:S(2)}) async-start(bf16[32,32,256]{2,1,0:T(8,128)(2,1)} %broadcast_in_dim.125), calls=%async_computation.1 | async-start | bytes 1048576 | tf_op jit(solution)/shard_map/all_to_all | solution.py:19
  36.7 21.3 %collective-permute-start.3 = (f32[3,256]{1,0:T(4,128)S(1)}, f32[3,256]{1,0:T(4,128)S(1)}, u32[]{:S(2)}, u32[]{:S(2)}) collective-permute-start(f32[3,256]{1,0:T(4,128)S(1)} %get-tuple-element.64), channel_id=1, source_target_pairs={{0,32},{32,64},{64,96},{96,128},{128,160},{160,192},{192,224},{224... | collective-permute-start | bytes 9224 | tf_op jit(solution)/shard_map/ppermute | solution.py:40
  40.3 17.7 %collective-permute-start.4 = (f32[3,256]{1,0:T(4,128)S(1)}, f32[3,256]{1,0:T(4,128)S(1)}, u32[]{:S(2)}, u32[]{:S(2)}) collective-permute-start(f32[3,256]{1,0:T(4,128)S(1)} %get-tuple-element.65), channel_id=1, source_target_pairs={{32,0},{64,32},{96,64},{128,96},{160,128},{192,160},{224,192},{256... | collective-permute-start | bytes 9224 | tf_op jit(solution)/shard_map/ppermute | solution.py:43
  42.6 15.6 %copy-start.9 = (pred[64]{0:T(512)(128)(4,1)}, pred[64]{0:T(512)(128)(4,1)S(1)}, u32[]{:S(2)}) copy-start(pred[64]{0:T(512)(128)(4,1)S(1)} %compare_and_fusion) | copy-start | bytes 196
  52.6 5.5 %collective-permute-start.2 = (bf16[1024,256]{1,0:T(8,128)(2,1)S(1)}, bf16[1024,256]{1,0:T(8,128)(2,1)S(1)}, u32[]{:S(2)}, u32[]{:S(2)}) collective-permute-start(bf16[1024,256]{1,0:T(8,128)(2,1)S(1)} %bitcast.83), channel_id=1, source_target_pairs={{0,32},{32,0},{64,96},{96,64},{128,160},{160,128},{192,224},{224,1... | collective-permute-start | bytes 1572872 | tf_op jit(solution)/shard_map/ppermute | solution.py:29
  56.5 1.6 %copy-start.7 = (s32[1024]{0:T(1024)}, s32[1024]{0:T(1024)S(1)}, u32[]{:S(2)}) copy-start(s32[1024]{0:T(1024)S(1)} %pad_clamp_fusion) | copy-start | bytes 12292
  61.2 9.1 %copy-start.1 = (f32[6,6]{1,0:T(8,128)S(1)}, f32[6,6]{1,0:T(8,128)}, u32[]{:S(2)}) copy-start(f32[6,6]{1,0:T(8,128)} %param.24) | copy-start | bytes 436
  62.2 15.9 %collective-permute-start.5 = (f32[7,134,3]{2,1,0:T(8,128)}, f32[7,134,3]{2,1,0:T(8,128)S(1)}, u32[]{:S(2)}, u32[]{:S(2)}) collective-permute-start(f32[7,134,3]{2,1,0:T(8,128)} %get-tuple-element.56), channel_id=1, source_target_pairs={{0,1},{1,2},{2,3},{3,4},{4,5},{5,6},{6,7},{7,8},{8,9},{9,10},{10,1... | collective-permute-start | bytes 33776 | tf_op jit(solution)/shard_map/ppermute | solution.py:40
  66.9 15.0 %collective-permute-start.6 = (f32[7,134,3]{2,1,0:T(8,128)S(1)}, f32[7,134,3]{2,1,0:T(8,128)S(1)}, u32[]{:S(2)}, u32[]{:S(2)}) collective-permute-start(f32[7,134,3]{2,1,0:T(8,128)S(1)} %get-tuple-element.57), channel_id=1, source_target_pairs={{1,0},{2,1},{3,2},{4,3},{5,4},{6,5},{7,6},{8,7},{9,8},{10,9},{11,1... | collective-permute-start | bytes 33776 | tf_op jit(solution)/shard_map/ppermute | solution.py:43
  82.4 0.7 copy-start.11
  95.0 3.5 %copy-start.2 = (f32[6,128,256]{2,1,0:T(8,128)}, f32[6,128,256]{2,1,0:T(8,128)S(1)}, u32[]{:S(2)}) copy-start(f32[6,128,256]{2,1,0:T(8,128)S(1)} %fusion.29) | copy-start | bytes 2359300
  95.0 3.5 %copy-start.8 = (f32[4,6]{1,0:T(4,128)S(1)}, f32[4,6]{1,0:T(4,128)}, u32[]{:S(2)}) copy-start(f32[4,6]{1,0:T(4,128)} %param.25) | copy-start | bytes 292
  95.0 3.5 %copy-start.10 = (pred[64]{0:T(512)(128)(4,1)S(1)}, pred[64]{0:T(512)(128)(4,1)}, u32[]{:S(2)}) copy-start(pred[64]{0:T(512)(128)(4,1)} %copy-done.9) | copy-start | bytes 196
  96.5 3.0 %copy-start.6 = (pred[32,2]{1,0:T(8,128)(4,1)S(1)}, pred[32,2]{1,0:T(8,128)(4,1)}, u32[]{:S(2)}) copy-start(pred[32,2]{1,0:T(8,128)(4,1)} %broadcast_in_dim.136) | copy-start | bytes 196
  98.5 18.1 %copy-start.4 = (f32[1,1,32,2,2,256]{5,4,3,2,1,0:T(2,128)S(1)}, f32[1,1,32,2,2,256]{5,4,3,2,1,0:T(2,128)}, u32[]{:S(2)}) copy-start(f32[1,1,32,2,2,256]{5,4,3,2,1,0:T(2,128)} %param.29) | copy-start | bytes 393220
  100.3 16.2 %all-to-all-start.2 = ((f32[32,2,2,256]{3,2,1,0:T(2,128)}), f32[32,2,2,256]{3,2,1,0:T(2,128)S(1)}, u32[]{:S(2)}, u32[]{:S(2)}) async-start(f32[32,2,2,256]{3,2,1,0:T(2,128)} %maximum_select_fusion), calls=%async_computation.2 | async-start | bytes 262144 | tf_op jit(solution)/shard_map/all_to_all | solution.py:130

commit v4 on v3

--- a/solution.py
+++ b/solution.py
@@ -43,6 +43,23 @@
         high = lax.ppermute(lax.slice_in_dim(block, 0, width, axis=dim), axis, backward)
         block = jnp.concatenate([low, block, high], axis=dim)
     return block
+
+
+def padded_last(block, axis, width):
+    count = lax.axis_size(axis)
+    forward = [(i, i + 1) for i in range(count - 1)]
+    backward = [(target, source) for source, target in forward]
+    lead, rows = block.shape[0], block.shape[1]
+
+    def pack(strip):
+        return jnp.swapaxes(strip, 1, 2).reshape(lead * width, rows)
+
+    def unpack(flat):
+        return jnp.swapaxes(flat.reshape(lead, width, rows), 1, 2)
+
+    low = unpack(lax.ppermute(pack(block[:, :, block.shape[2] - width :]), axis, forward))
+    high = unpack(lax.ppermute(pack(block[:, :, :width]), axis, backward))
+    return jnp.concatenate([low, block, high], axis=2)
 
 
 def chebyshev_weight(sweep):
@@ -95,7 +112,7 @@
     loading = loading.reshape(6, ext_rows, girth_cells)
     coupling_diag = jnp.diagonal(coupling)[:, None, None]
     packed = jnp.concatenate([loading, stiffness_rows[None]], axis=0)
-    packed = padded_2(packed, (("girth", 2),), width)
+    packed = padded_last(packed, "girth", width)
     loading_ext = packed[:6]
     stiffness_ext = packed[6]
     diagonal_ext = 4.0 * stiffness_ext[None] + coupling_diag
@@ -126,8 +143,9 @@
     )
     spectra = square_pairs(stress_rows, 1)
     outbox = jnp.where(filled[:, None, None], spectra, 0.0)
-    outbox = outbox.reshape(girth_count, CAP, 2, girth_cells)
+    outbox = outbox.reshape(girth_count, CAP * 2 * girth_cells // 128, 128)
     received = lax.all_to_all(outbox, "girth", split_axis=0, concat_axis=0, tiled=True)
+    received = received.reshape(girth_count, CAP, 2, girth_cells)
     hotspot_moments = prior_moments + (psd_weight[0] * received)[None, None]
     return (motion, hotspot_moments)
 

time: 118 us -> 109 us (0.924)
  waiting for transfers between devices: 33.6 us -> 27.2 us
  other arithmetic: 16.2 us -> 13.6 us
    ppermute x3 -> x2, waiting for transfers between devices: 6.38 us -> 0.01 us  [padded_2(): lax.ppermute(lax.slice_in_dim(block, block.shape[dim] - width, None, axis...]
    ppermute x0 -> x2, starting transfers between devices: none -> 6.14 us  [the longest x1 4.67 us: padded_last(): lax.ppermute(pack(block[:, :, block.shape[2] - width:]), axis, forward)]
    ppermute x3 -> x2, starting transfers between devices: 10.2 us -> 5.51 us  [padded_2(): lax.ppermute(lax.slice_in_dim(block, block.shape[dim] - width, None, axis...]
    ppermute x3 -> x2, waiting for transfers between devices: 3.83 us -> 0.01 us  [padded_2(): lax.ppermute(lax.slice_in_dim(block, 0, width, axis=dim), axis, backward)]
    ppermute x0 -> x2, waiting for transfers between devices: none -> 3.31 us  [the longest x1 3.31 us: padded_last(): high = unpack(lax.ppermute(pack(block[:, :, :width]), axis, backward))]
    ppermute x3 -> x2, starting transfers between devices: 7.08 us -> 5.61 us  [padded_2(): lax.ppermute(lax.slice_in_dim(block, 0, width, axis=dim), axis, backward)]
    broadcast_in_dim x1 -> x0, local copies, waits for them, and re-layouts: 1.39 us -> none  [on_device(): outbox = jnp.where(filled[:, None, None], spectra, 0.0)]
  transfers between devices with their start and end apart: 10 -> 10, of which waited for: 5 -> 5; matrix products, arithmetic and copies ran while one was open for 11% -> 10% of each run, Pallas kernels for 0% -> 0%
where the time goes in v4:
time: 109 us; the launch traced here: 108 us
  starting transfers between devices  43.2 us (40%)
  waiting for transfers between devices  27.2 us (25%)
  other arithmetic  13.6 us (12%)
  local copies, waits for them, and re-layouts  13.1 us (12%)
  matrix products  8.35 us (8%)
  between operations  2.41 us (2%)
    all_to_all x1, waiting for transfers between devices, scatter_gather(): full = lax.all_to_all(send, axis, 0, 0, tiled=True)  10 us
    all_to_all x1, starting transfers between devices, scatter_gather(): got = lax.all_to_all(send, axis, 0, 0, tiled=True)  9.95 us
    all_to_all x1, waiting for transfers between devices, on_device(): lax.all_to_all(outbox, 'girth', split_axis=0, concat_axis=0, tiled=True)  9.71 us
    all_to_all x1, starting transfers between devices, scatter_gather(): full = lax.all_to_all(send, axis, 0, 0, tiled=True)  6.27 us
    all_to_all x1, starting transfers between devices, on_device(): lax.all_to_all(outbox, 'girth', split_axis=0, concat_axis=0, tiled=True)  5.79 us
    add x3, other arithmetic, on_device(): motion[:, 1:-1, 1:-1]  5.74 us
    ppermute x2, starting transfers between devices, padded_2(): lax.ppermute(lax.slice_in_dim(block, 0, width, axis=dim), axis, backward)  5.61 us
    ppermute x2, starting transfers between devices, padded_2(): lax.ppermute(lax.slice_in_dim(block, block.shape[dim] - width, None, axis...  5.51 us
  transfers between devices with their start and end apart: 10, of which 5 were waited for; matrix products, arithmetic and copies ran while one was open for 10% of the time, Pallas kernels for 0%

profile of v4, /device:TPU:192, one launch (start us, length us, event | category | flops | bytes accessed | tf_op | source)
XLA Modules:
  0.0 107.9 jit_solution(17370646414125297694)
XLA Ops:
  0.6 0.0 copy-start
  0.7 1.2 %copy-done = bf16[2048,256]{1,0:T(8,128)(2,1)S(1)} copy-done((bf16[2048,256]{1,0:T(8,128)(2,1)S(1)}, bf16[2048,256]{1,0:T(8,128)(2,1)}, u32[]{:S(2)}) %copy-start) | copy-done | bytes 1048600
  1.9 0.8 constant_dynamic-slice_fusion
  2.7 9.9 %all-to-all-start = ((bf16[32,32,256]{2,1,0:T(8,128)(2,1)}), bf16[32,32,256]{2,1,0:T(8,128)(2,1)S(1)}, u32[]{:S(2)}, u32[]{:S(2)}) async-start(bf16[32,32,256]{2,1,0:T(8,128)(2,1)} %bitcast), calls=%async_computation | async-start | bytes 1048576 | tf_op jit(solution)/shard_map/all_to_all | solution.py:16
  12.7 0.0 copy-start.7
  12.7 0.0 copy-start.8
  12.7 1.1 %fusion.57 = (bf16[6,3,2048]{2,1,0:T(4,128)(2,1)S(1)}, bf16[6,3,2048]{2,1,0:T(4,128)(2,1)S(1)}) fusion(bf16[6,128,2048]{2,1,0:T(8,128)(2,1)} %param.19), kind=kLoop, calls=%fused_computation.105 | loop fusion | bytes 294912 | tf_op jit(solution)/shard_map/slice | solution.py:41
  13.8 1.9 %collective-permute-start = (bf16[6,3,2048]{2,1,0:T(4,128)(2,1)S(1)}, bf16[6,3,2048]{2,1,0:T(4,128)(2,1)S(1)}, u32[]{:S(2)}, u32[]{:S(2)}) collective-permute-start(bf16[6,3,2048]{2,1,0:T(4,128)(2,1)S(1)} %get-tuple-element.52), channel_id=1, source_target_pairs={{0,32},{32,64},{64,96},{96,128},{128,160},{160,192},{192,224},{224... | collective-permute-start | bytes 221192 | tf_op jit(solution)/shard_map/ppermute | solution.py:40
  15.7 3.6 %collective-permute-start.1 = (bf16[6,3,2048]{2,1,0:T(4,128)(2,1)S(1)}, bf16[6,3,2048]{2,1,0:T(4,128)(2,1)S(1)}, u32[]{:S(2)}, u32[]{:S(2)}) collective-permute-start(bf16[6,3,2048]{2,1,0:T(4,128)(2,1)S(1)} %get-tuple-element.53), channel_id=1, source_target_pairs={{32,0},{64,32},{96,64},{128,96},{160,128},{192,160},{224,192},{256... | collective-permute-start | bytes 221192 | tf_op jit(solution)/shard_map/ppermute | solution.py:43
  20.0 0.7 fusion.60
  20.7 5.2 %select_add_fusion = f32[128,256]{1,0:T(8,128)S(1)} fusion(s32[128,256]{1,0:T(8,128)S(1)} %copy-done.4, f32[]{:T(128)} %bitcast.12, f32[]{:T(128)} %bitcast.11, f32[]{:T(128)} %bitcast.10, f32[]{:T(128)} %bitcast.9, f32[]{:T(128)} %bitcast.8, f32[]{:T(128)} %bitcast.7, f32[]{:T(128)} %bitcast.6, f32[]{:T(128)} %bitcast.5), kind=kLoop, calls=%fused_computation.70 | loop fusion | flops 753664 | bytes 262176 | tf_op jit(solution)/shard_map/add | solution.py:106
  26.0 3.5 %all-to-all-done = bf16[32,32,256]{2,1,0:T(8,128)(2,1)S(1)} async-done(((bf16[32,32,256]{2,1,0:T(8,128)(2,1)}), bf16[32,32,256]{2,1,0:T(8,128)(2,1)S(1)}, u32[]{:S(2)}, u32[]{:S(2)}) %all-to-all-start) | async-done | bytes 524320 | tf_op jit(solution)/shard_map/all_to_all | solution.py:16
  29.5 0.9 broadcast_in_dim.121
  30.4 6.3 %all-to-all-start.1 = ((bf16[32,32,256]{2,1,0:T(8,128)(2,1)}), bf16[32,32,256]{2,1,0:T(8,128)(2,1)S(1)}, u32[]{:S(2)}, u32[]{:S(2)}) async-start(bf16[32,32,256]{2,1,0:T(8,128)(2,1)} %broadcast_in_dim.121), calls=%async_computation.1 | async-start | bytes 1048576 | tf_op jit(solution)/shard_map/all_to_all | solution.py:19
  36.7 3.6 %collective-permute-start.3 = (f32[3,256]{1,0:T(4,128)S(1)}, f32[3,256]{1,0:T(4,128)S(1)}, u32[]{:S(2)}, u32[]{:S(2)}) collective-permute-start(f32[3,256]{1,0:T(4,128)S(1)} %get-tuple-element.64), channel_id=1, source_target_pairs={{0,32},{32,64},{64,96},{96,128},{128,160},{160,192},{192,224},{224... | collective-permute-start | bytes 9224 | tf_op jit(solution)/shard_map/ppermute | solution.py:40
  40.3 2.0 %collective-permute-start.4 = (f32[3,256]{1,0:T(4,128)S(1)}, f32[3,256]{1,0:T(4,128)S(1)}, u32[]{:S(2)}, u32[]{:S(2)}) collective-permute-start(f32[3,256]{1,0:T(4,128)S(1)} %get-tuple-element.65), channel_id=1, source_target_pairs={{32,0},{64,32},{96,64},{128,96},{160,128},{192,160},{224,192},{256... | collective-permute-start | bytes 9224 | tf_op jit(solution)/shard_map/ppermute | solution.py:43
  42.3 0.2 convert_reduce_fusion
  42.4 0.1 select_reduce_fusion
  42.6 10.0 %all-to-all-done.1 = bf16[32,32,256]{2,1,0:T(8,128)(2,1)S(1)} async-done(((bf16[32,32,256]{2,1,0:T(8,128)(2,1)}), bf16[32,32,256]{2,1,0:T(8,128)(2,1)S(1)}, u32[]{:S(2)}, u32[]{:S(2)}) %all-to-all-start.1) | async-done | bytes 524320 | tf_op jit(solution)/shard_map/all_to_all | solution.py:19
  52.6 4.0 %collective-permute-start.2 = (bf16[1024,256]{1,0:T(8,128)(2,1)S(1)}, bf16[1024,256]{1,0:T(8,128)(2,1)S(1)}, u32[]{:S(2)}, u32[]{:S(2)}) collective-permute-start(bf16[1024,256]{1,0:T(8,128)(2,1)S(1)} %bitcast.101), channel_id=1, source_target_pairs={{0,32},{32,0},{64,96},{96,64},{128,160},{160,128},{192,224},{224,1... | collective-permute-start | bytes 1572872 | tf_op jit(solution)/shard_map/ppermute | solution.py:29
  56.5 0.7 gather_fusion.1
  57.2 0.1 broadcast_select_fusion.2
  57.3 0.1 fusion.48
  57.4 0.6 collective-permute-done.2
  58.0 0.1 broadcast_select_fusion.1
  58.2 3.0 %fusion = f32[6,134,256]{2,1,0:T(8,128)S(1)} fusion(bf16[6,3,2048]{2,1,0:T(4,128)(2,1)S(1)} %collective-permute-done.1, bf16[6,128,2048]{2,1,0:T(8,128)(2,1)} %param.19, bf16[6,3,2048]{2,1,0:T(4,128)(2,1)S(1)} %collective-permute-done, bf16[1024,256]{1,0:T(8,128)(2,1)S(1)} %get-tuple-element.55, bf16[1024,256]{1,0:T(8,128)(2,1)S(1)} %get-tuple-element.54), kind=kOutput, calls=%fused_computation.3 | convolution fusion | flops 855031808 | bytes 5165056 | tf_op jit(solution)/shard_map/dot_general | solution.py:111
  61.2 0.0 copy-start.1
  61.2 0.2 fusion.37
  61.4 0.3 copy.38
  61.7 4.7 %collective-permute-start.5 = (f32[21,134]{1,0:T(8,128)S(1)}, f32[21,134]{1,0:T(8,128)S(1)}, u32[]{:S(2)}, u32[]{:S(2)}) collective-permute-start(f32[21,134]{1,0:T(8,128)S(1)} %reshape.95), channel_id=1, source_target_pairs={{0,1},{1,2},{2,3},{3,4},{4,5},{5,6},{6,7},{7,8},{8,9},{9,10},{10,1... | collective-permute-start | bytes 33776 | tf_op jit(solution)/shard_map/ppermute | solution.py:60
  66.4 0.3 copy.40
  66.7 1.5 %collective-permute-start.6 = (f32[21,134]{1,0:T(8,128)S(1)}, f32[21,134]{1,0:T(8,128)S(1)}, u32[]{:S(2)}, u32[]{:S(2)}) collective-permute-start(f32[21,134]{1,0:T(8,128)S(1)} %reshape.97), channel_id=1, source_target_pairs={{1,0},{2,1},{3,2},{4,3},{5,4},{6,5},{7,6},{8,7},{9,8},{10,9},{11,1... | collective-permute-start | bytes 33776 | tf_op jit(solution)/shard_map/ppermute | solution.py:61
  68.2 0.6 gather_fusion
  68.9 0.2 copy.39
  69.1 3.3 %collective-permute-done.6 = f32[21,134]{1,0:T(8,128)S(1)} collective-permute-done((f32[21,134]{1,0:T(8,128)S(1)}, f32[21,134]{1,0:T(8,128)S(1)}, u32[]{:S(2)}, u32[]{:S(2)}) %collective-permute-start.6) | collective-permute-done | bytes 11288 | tf_op jit(solution)/shard_map/ppermute | solution.py:61
  72.5 0.2 copy.41
  72.7 0.1 multiply_bitcast_fusion
  72.9 0.6 pad_maximum_fusion
  73.4 0.1 slice.231
  73.6 0.1 slice.239
  73.7 0.1 slice.247
  73.8 0.2 fusion.22
  74.0 0.5 slice.229
  74.5 1.6 %fusion.6 = f32[132,260,6]{1,2,0:T(8,128)S(1)} fusion(f32[6,132,260]{2,1,0:T(8,128)S(1)} %slice.229, f32[6,6]{1,0:T(8,128)S(1)} %copy-done.1), kind=kOutput, calls=%fused_computation.9 | convolution fusion | flops 14826240 | bytes 1647504 | tf_op jit(solution)/shard_map/ab,bij->aij/dot_general | solution.py:72
  76.1 2.1 %fusion.17 = f32[6,132,260]{2,1,0:T(8,128)S(1)} fusion(f32[6,134,262]{2,1,0:T(8,128)S(1)} %get-tuple-element.63, f32[6,134,262]{2,1,0:T(8,128)S(1)} %get-tuple-element.62, f32[7,134,262]{2,1,0:T(8,128)S(1)} %pad_maximum_fusion, f32[132,260,6]{1,2,0:T(8,128)S(1)} %fusion.6, f32[132,260]{1,0:T(8,128)S(1)} %slice.231), kind=kLoop, calls=%fused_computation.26 | loop fusion | flops 2265120 | bytes 7550400 | tf_op jit(solution)/shard_map/add | solution.py:125
  78.3 0.5 slice.237
  78.7 1.6 %fusion.8 = f32[130,258,6]{1,2,0:T(8,128)S(1)} fusion(f32[6,130,258]{2,1,0:T(8,128)S(1)} %slice.237, f32[6,6]{1,0:T(8,128)S(1)} %copy-done.1), kind=kOutput, calls=%fused_computation.11 | convolution fusion | flops 14489280 | bytes 1610064 | tf_op jit(solution)/shard_map/ab,bij->aij/dot_general | solution.py:72
  80.4 2.2 %fusion.11 = f32[6,130,258]{2,1,0:T(8,128)S(1)} fusion(f32[6,134,262]{2,1,0:T(8,128)S(1)} %get-tuple-element.63, f32[6,132,260]{2,1,0:T(8,128)S(1)} %fusion.17, f32[7,134,262]{2,1,0:T(8,128)S(1)} %pad_maximum_fusion, f32[130,258,6]{1,2,0:T(8,128)S(1)} %fusion.8, f32[130,258]{1,0:T(8,128)S(1)} %slice.239), kind=kLoop, calls=%fused_computation.16 | loop fusion | flops 2213640 | bytes 7378800 | tf_op jit(solution)/shard_map/add | solution.py:125
  82.5 0.3 slice.245
  82.8 1.4 %fusion.26 = f32[128,256,6]{1,2,0:T(8,128)S(1)} fusion(f32[6,128,256]{2,1,0:T(8,128)S(1)} %slice.245, f32[6,6]{1,0:T(8,128)S(1)} %copy-done.1), kind=kOutput, calls=%fused_computation.41 | convolution fusion | flops 14155776 | bytes 1573008 | tf_op jit(solution)/shard_map/ab,bij->aij/dot_general | solution.py:72
  84.2 1.4 %fusion.29 = f32[6,128,256]{2,1,0:T(8,128)S(1)} fusion(f32[6,134,262]{2,1,0:T(8,128)S(1)} %get-tuple-element.63, f32[6,130,258]{2,1,0:T(8,128)S(1)} %fusion.11, f32[6,134,256]{2,1,0:T(8,128)S(1)} %fusion, f32[128,256,6]{1,2,0:T(8,128)S(1)} %fusion.26, f32[128,256]{1,0:T(8,128)S(1)} %slice.247), kind=kLoop, calls=%fused_computation.47 | loop fusion | flops 2162688 | bytes 7208960 | tf_op jit(solution)/shard_map/add | solution.py:125
  85.7 0.0 copy-start.2
  85.7 0.0 copy-start.6
  85.7 1.5 %copy.48 = f32[6,128,256]{2,0,1:T(8,128)} copy(f32[6,128,256]{2,1,0:T(8,128)S(1)} %fusion.29) | data formatting | bytes 1572864 | tf_op jit(solution)/shard_map/add | solution.py:125
  87.2 1.8 %gather_fusion.2 = f32[64,6,256]{2,1,0:T(8,128)S(1)} fusion(f32[6,128,256]{2,0,1:T(8,128)} %copy.48, s32[1024]{0:T(1024)S(1)} %pad_clamp_fusion), kind=kCustom, calls=%fused_computation.2 | custom fusion | bytes 786688 | tf_op jit(solution)/shard_map/jit(_take)/gather | solution.py:140
  89.0 0.7 fusion.23
  89.7 0.2 fusion.58
  89.9 0.1 maximum_select_fusion
  90.0 0.1 copy.52
  90.1 0.8 select_n.126
  90.9 5.8 %all-to-all-start.2 = ((f32[32,8,128]{2,1,0:T(8,128)}), f32[32,8,128]{2,1,0:T(8,128)S(1)}, u32[]{:S(2)}, u32[]{:S(2)}) async-start(f32[32,8,128]{2,1,0:T(8,128)} %select_n.126), calls=%async_computation.2 | async-start | bytes 262144 | tf_op jit(solution)/shard_map/all_to_all | solution.py:147
  97.3 9.7 %all-to-all-done.2 = f32[32,8,128]{2,1,0:T(8,128)S(1)} async-done(((f32[32,8,128]{2,1,0:T(8,128)}), f32[32,8,128]{2,1,0:T(8,128)S(1)}, u32[]{:S(2)}, u32[]{:S(2)}) %all-to-all-start.2) | async-done | bytes 131104 | tf_op jit(solution)/shard_map/all_to_all | solution.py:147
  107.1 0.1 mul.158
  107.2 0.7 add.177
  (30 shorter events, 0.2 us)
Async XLA Ops:
  0.6 1.2 %copy-start = (bf16[2048,256]{1,0:T(8,128)(2,1)S(1)}, bf16[2048,256]{1,0:T(8,128)(2,1)}, u32[]{:S(2)}) copy-start(bf16[2048,256]{1,0:T(8,128)(2,1)} %param.20) | copy-start | bytes 3145732
  1.9 18.2 %copy-start.5 = (f32[8]{0:T(128)S(1)}, f32[8]{0:T(128)}, u32[]{:S(2)}) copy-start(f32[8]{0:T(128)} %param.23) | copy-start | bytes 100
  1.9 18.9 %copy-start.4 = (s32[128,256]{1,0:T(8,128)S(1)}, s32[128,256]{1,0:T(8,128)}, u32[]{:S(2)}) copy-start(s32[128,256]{1,0:T(8,128)} %param.22) | copy-start | bytes 393220
  2.7 26.8 %all-to-all-start = ((bf16[32,32,256]{2,1,0:T(8,128)(2,1)}), bf16[32,32,256]{2,1,0:T(8,128)(2,1)S(1)}, u32[]{:S(2)}, u32[]{:S(2)}) async-start(bf16[32,32,256]{2,1,0:T(8,128)(2,1)} %bitcast), calls=%async_computation | async-start | bytes 1048576 | tf_op jit(solution)/shard_map/all_to_all | solution.py:16
  12.7 29.6 %copy-start.7 = (s32[1,32,1]{1,2,0:T(1,128)S(1)}, s32[1,32,1]{1,2,0:T(1,128)}, u32[]{:S(2)}) copy-start(s32[1,32,1]{1,2,0:T(1,128)} %param.28) | copy-start | bytes 388
  12.7 29.8 %copy-start.8 = (s32[1,32]{1,0:T(1,128)S(1)}, s32[1,32]{1,0:T(1,128)}, u32[]{:S(2)}) copy-start(s32[1,32]{1,0:T(1,128)} %param.27) | copy-start | bytes 388
  13.8 44.4 %collective-permute-start = (bf16[6,3,2048]{2,1,0:T(4,128)(2,1)S(1)}, bf16[6,3,2048]{2,1,0:T(4,128)(2,1)S(1)}, u32[]{:S(2)}, u32[]{:S(2)}) collective-permute-start(bf16[6,3,2048]{2,1,0:T(4,128)(2,1)S(1)} %get-tuple-element.52), channel_id=1, source_target_pairs={{0,32},{32,64},{64,96},{96,128},{128,160},{160,192},{192,224},{224... | collective-permute-start | bytes 221192 | tf_op jit(solution)/shard_map/ppermute | solution.py:40
  15.7 42.4 %collective-permute-start.1 = (bf16[6,3,2048]{2,1,0:T(4,128)(2,1)S(1)}, bf16[6,3,2048]{2,1,0:T(4,128)(2,1)S(1)}, u32[]{:S(2)}, u32[]{:S(2)}) collective-permute-start(bf16[6,3,2048]{2,1,0:T(4,128)(2,1)S(1)} %get-tuple-element.53), channel_id=1, source_target_pairs={{32,0},{64,32},{96,64},{128,96},{160,128},{192,160},{224,192},{256... | collective-permute-start | bytes 221192 | tf_op jit(solution)/shard_map/ppermute | solution.py:43
  30.4 22.2 %all-to-all-start.1 = ((bf16[32,32,256]{2,1,0:T(8,128)(2,1)}), bf16[32,32,256]{2,1,0:T(8,128)(2,1)S(1)}, u32[]{:S(2)}, u32[]{:S(2)}) async-start(bf16[32,32,256]{2,1,0:T(8,128)(2,1)} %broadcast_in_dim.121), calls=%async_computation.1 | async-start | bytes 1048576 | tf_op jit(solution)/shard_map/all_to_all | solution.py:19
  36.7 20.7 %collective-permute-start.3 = (f32[3,256]{1,0:T(4,128)S(1)}, f32[3,256]{1,0:T(4,128)S(1)}, u32[]{:S(2)}, u32[]{:S(2)}) collective-permute-start(f32[3,256]{1,0:T(4,128)S(1)} %get-tuple-element.64), channel_id=1, source_target_pairs={{0,32},{32,64},{64,96},{96,128},{128,160},{160,192},{192,224},{224... | collective-permute-start | bytes 9224 | tf_op jit(solution)/shard_map/ppermute | solution.py:40
  40.3 17.1 %collective-permute-start.4 = (f32[3,256]{1,0:T(4,128)S(1)}, f32[3,256]{1,0:T(4,128)S(1)}, u32[]{:S(2)}, u32[]{:S(2)}) collective-permute-start(f32[3,256]{1,0:T(4,128)S(1)} %get-tuple-element.65), channel_id=1, source_target_pairs={{32,0},{64,32},{96,64},{128,96},{160,128},{192,160},{224,192},{256... | collective-permute-start | bytes 9224 | tf_op jit(solution)/shard_map/ppermute | solution.py:43
  52.6 5.5 %collective-permute-start.2 = (bf16[1024,256]{1,0:T(8,128)(2,1)S(1)}, bf16[1024,256]{1,0:T(8,128)(2,1)S(1)}, u32[]{:S(2)}, u32[]{:S(2)}) collective-permute-start(bf16[1024,256]{1,0:T(8,128)(2,1)S(1)} %bitcast.101), channel_id=1, source_target_pairs={{0,32},{32,0},{64,96},{96,64},{128,160},{160,128},{192,224},{224,1... | collective-permute-start | bytes 1572872 | tf_op jit(solution)/shard_map/ppermute | solution.py:29
  61.2 7.0 %copy-start.1 = (f32[6,6]{1,0:T(8,128)S(1)}, f32[6,6]{1,0:T(8,128)}, u32[]{:S(2)}) copy-start(f32[6,6]{1,0:T(8,128)} %param.24) | copy-start | bytes 436
  61.7 7.2 %collective-permute-start.5 = (f32[21,134]{1,0:T(8,128)S(1)}, f32[21,134]{1,0:T(8,128)S(1)}, u32[]{:S(2)}, u32[]{:S(2)}) collective-permute-start(f32[21,134]{1,0:T(8,128)S(1)} %reshape.95), channel_id=1, source_target_pairs={{0,1},{1,2},{2,3},{3,4},{4,5},{5,6},{6,7},{7,8},{8,9},{9,10},{10,1... | collective-permute-start | bytes 33776 | tf_op jit(solution)/shard_map/ppermute | solution.py:60
  66.7 5.7 %collective-permute-start.6 = (f32[21,134]{1,0:T(8,128)S(1)}, f32[21,134]{1,0:T(8,128)S(1)}, u32[]{:S(2)}, u32[]{:S(2)}) collective-permute-start(f32[21,134]{1,0:T(8,128)S(1)} %reshape.97), channel_id=1, source_target_pairs={{1,0},{2,1},{3,2},{4,3},{5,4},{6,5},{7,6},{8,7},{9,8},{10,9},{11,1... | collective-permute-start | bytes 33776 | tf_op jit(solution)/shard_map/ppermute | solution.py:61
  85.7 3.3 %copy-start.2 = (f32[6,128,256]{2,1,0:T(8,128)}, f32[6,128,256]{2,1,0:T(8,128)S(1)}, u32[]{:S(2)}) copy-start(f32[6,128,256]{2,1,0:T(8,128)S(1)} %fusion.29) | copy-start | bytes 2359300
  85.7 3.3 %copy-start.6 = (f32[4,6]{1,0:T(4,128)S(1)}, f32[4,6]{1,0:T(4,128)}, u32[]{:S(2)}) copy-start(f32[4,6]{1,0:T(4,128)} %param.25) | copy-start | bytes 292
  89.7 17.5 %copy-start.3 = (f32[1,1,32,2,2,256]{5,4,3,2,1,0:T(2,128)S(1)}, f32[1,1,32,2,2,256]{5,4,3,2,1,0:T(2,128)}, u32[]{:S(2)}) copy-start(f32[1,1,32,2,2,256]{5,4,3,2,1,0:T(2,128)} %param.29) | copy-start | bytes 393220
  90.9 16.2 %all-to-all-start.2 = ((f32[32,8,128]{2,1,0:T(8,128)}), f32[32,8,128]{2,1,0:T(8,128)S(1)}, u32[]{:S(2)}, u32[]{:S(2)}) async-start(f32[32,8,128]{2,1,0:T(8,128)} %select_n.126), calls=%async_computation.2 | async-start | bytes 262144 | tf_op jit(solution)/shard_map/all_to_all | solution.py:147

commit v5 on v4

--- a/solution.py
+++ b/solution.py
@@ -69,8 +69,9 @@
 def operate_padded(padded, stiffness, coupling):
     centre = padded[:, 1:-1, 1:-1]
     beside = padded[:, 2:, 1:-1] + padded[:, :-2, 1:-1] + padded[:, 1:-1, 2:] + padded[:, 1:-1, :-2]
-    mixing = jnp.einsum("ab,bij->aij", coupling, centre, precision=lax.Precision.HIGHEST)
-    return stiffness * (4.0 * centre - beside) + mixing
+    fields = centre.shape[0]
+    mixing = [sum(coupling[a, b] * centre[b] for b in range(fields)) for a in range(fields)]
+    return stiffness * (4.0 * centre - beside) + jnp.stack(mixing)
 
 
 def square_pairs(values, axis_at):

time: 109 us -> 184 us (1.69)
  other arithmetic: 13.6 us -> 87.8 us
  matrix products: 8.35 us -> 3.67 us
  starting transfers between devices: 43.2 us -> 47.7 us
    unnamed x0 -> x15, other arithmetic: none -> 61.9 us
    another operation x0 -> x3, other arithmetic: none -> 12.7 us  [operate_padded(): return stiffness * (4.0 * centre - beside) + jnp.stack(mixing)]
    dot_general x3 -> x0, matrix products: 4.68 us -> none  [operate_padded(): jnp.einsum('ab,bij->aij', coupling, centre, precision=lax.Precision.HIGHEST)]
    all_to_all x1, waiting for transfers between devices: 10 us -> 13.5 us  [scatter_gather(): full = lax.all_to_all(send, axis, 0, 0, tiled=True)]
    all_to_all x1, waiting for transfers between devices: 3.54 us -> 0.01 us  [scatter_gather(): got = lax.all_to_all(send, axis, 0, 0, tiled=True)]
    all_to_all x1, starting transfers between devices: 6.27 us -> 9.78 us  [scatter_gather(): full = lax.all_to_all(send, axis, 0, 0, tiled=True)]
  transfers between devices with their start and end apart: 10 -> 10, of which waited for: 5 -> 4; matrix products, arithmetic and copies ran while one was open for 10% -> 6% of each run, Pallas kernels for 0% -> 0%
where the time goes in v5:
time: 184 us; the launch traced here: 182 us
  other arithmetic  87.8 us (48%)
  starting transfers between devices  47.7 us (26%)
  waiting for transfers between devices  27.2 us (15%)
  local copies, waits for them, and re-layouts  13.3 us (7%)
  matrix products  3.67 us (2%)
  between operations  2.48 us (1%)
    unnamed x15, other arithmetic  61.9 us
    all_to_all x1, waiting for transfers between devices, scatter_gather(): full = lax.all_to_all(send, axis, 0, 0, tiled=True)  13.5 us
    another operation x3, other arithmetic, operate_padded(): return stiffness * (4.0 * centre - beside) + jnp.stack(mixing)  12.7 us
    all_to_all x1, starting transfers between devices, scatter_gather(): got = lax.all_to_all(send, axis, 0, 0, tiled=True)  9.95 us
    all_to_all x1, starting transfers between devices, scatter_gather(): full = lax.all_to_all(send, axis, 0, 0, tiled=True)  9.78 us
    all_to_all x1, waiting for transfers between devices, on_device(): lax.all_to_all(outbox, 'girth', split_axis=0, concat_axis=0, tiled=True)  9.71 us
    all_to_all x1, starting transfers between devices, on_device(): lax.all_to_all(outbox, 'girth', split_axis=0, concat_axis=0, tiled=True)  5.96 us
    ppermute x2, starting transfers between devices, padded_2(): lax.ppermute(lax.slice_in_dim(block, block.shape[dim] - width, None, axis...  5.79 us
  transfers between devices with their start and end apart: 10, of which 4 were waited for; matrix products, arithmetic and copies ran while one was open for 6% of the time, Pallas kernels for 0%

profile of v5, /device:TPU:192, one launch (start us, length us, event | category | flops | bytes accessed | tf_op | source)
XLA Modules:
  0.0 182.2 jit_solution(15337666690056552506)
XLA Ops:
  0.7 1.2 copy-done
  1.9 0.8 constant_dynamic-slice_fusion
  2.7 9.9 %all-to-all-start = ((bf16[32,32,256]{2,1,0:T(8,128)(2,1)}), bf16[32,32,256]{2,1,0:T(8,128)(2,1)S(1)}, u32[]{:S(2)}, u32[]{:S(2)}) async-start(bf16[32,32,256]{2,1,0:T(8,128)(2,1)} %bitcast), calls=%async_computation | async-start | bytes 1048576 | tf_op jit(solution)/shard_map/all_to_all | solution.py:16
  12.7 1.1 fusion.48
  13.8 1.9 %collective-permute-start = (bf16[6,3,2048]{2,1,0:T(4,128)(2,1)S(1)}, bf16[6,3,2048]{2,1,0:T(4,128)(2,1)S(1)}, u32[]{:S(2)}, u32[]{:S(2)}) collective-permute-start(bf16[6,3,2048]{2,1,0:T(4,128)(2,1)S(1)} %get-tuple-element.52), channel_id=1, source_target_pairs={{0,32},{32,64},{64,96},{96,128},{128,160},{160,192},{192,224},{224... | collective-permute-start | bytes 221192 | tf_op jit(solution)/shard_map/ppermute | solution.py:40
  15.7 3.6 %collective-permute-start.1 = (bf16[6,3,2048]{2,1,0:T(4,128)(2,1)S(1)}, bf16[6,3,2048]{2,1,0:T(4,128)(2,1)S(1)}, u32[]{:S(2)}, u32[]{:S(2)}) collective-permute-start(bf16[6,3,2048]{2,1,0:T(4,128)(2,1)S(1)} %get-tuple-element.53), channel_id=1, source_target_pairs={{32,0},{64,32},{96,64},{128,96},{160,128},{192,160},{224,192},{256... | collective-permute-start | bytes 221192 | tf_op jit(solution)/shard_map/ppermute | solution.py:43
  19.4 0.7 fusion.53
  20.1 5.2 %select_add_fusion = f32[128,256]{1,0:T(8,128)S(1)} fusion(s32[128,256]{1,0:T(8,128)S(1)} %copy-done.4, f32[]{:T(128)} %bitcast.12, f32[]{:T(128)} %bitcast.11, f32[]{:T(128)} %bitcast.10, f32[]{:T(128)} %bitcast.9, f32[]{:T(128)} %bitcast.8, f32[]{:T(128)} %bitcast.7, f32[]{:T(128)} %bitcast.6, f32[]{:T(128)} %bitcast.5), kind=kLoop, calls=%fused_computation.82 | loop fusion | flops 753664 | bytes 262176 | tf_op jit(solution)/shard_map/add | solution.py:107
  25.3 3.9 %collective-permute-start.3 = (f32[3,256]{1,0:T(4,128)S(1)}, f32[3,256]{1,0:T(4,128)S(1)}, u32[]{:S(2)}, u32[]{:S(2)}) collective-permute-start(f32[3,256]{1,0:T(4,128)S(1)} %get-tuple-element.64), channel_id=1, source_target_pairs={{0,32},{32,64},{64,96},{96,128},{128,160},{160,192},{192,224},{224... | collective-permute-start | bytes 9224 | tf_op jit(solution)/shard_map/ppermute | solution.py:40
  29.2 1.9 %collective-permute-start.4 = (f32[3,256]{1,0:T(4,128)S(1)}, f32[3,256]{1,0:T(4,128)S(1)}, u32[]{:S(2)}, u32[]{:S(2)}) collective-permute-start(f32[3,256]{1,0:T(4,128)S(1)} %get-tuple-element.65), channel_id=1, source_target_pairs={{32,0},{64,32},{96,64},{128,96},{160,128},{192,160},{224,192},{256... | collective-permute-start | bytes 9224 | tf_op jit(solution)/shard_map/ppermute | solution.py:43
  31.8 0.9 broadcast_in_dim.121
  32.7 9.8 %all-to-all-start.1 = ((bf16[32,32,256]{2,1,0:T(8,128)(2,1)}), bf16[32,32,256]{2,1,0:T(8,128)(2,1)S(1)}, u32[]{:S(2)}, u32[]{:S(2)}) async-start(bf16[32,32,256]{2,1,0:T(8,128)(2,1)} %broadcast_in_dim.121), calls=%async_computation.1 | async-start | bytes 1048576 | tf_op jit(solution)/shard_map/all_to_all | solution.py:19
  42.5 0.2 convert_reduce_fusion
  42.8 0.7 gather_fusion.1
  43.5 0.7 fusion.51
  44.2 13.5 %all-to-all-done.1 = bf16[32,32,256]{2,1,0:T(8,128)(2,1)S(1)} async-done(((bf16[32,32,256]{2,1,0:T(8,128)(2,1)}), bf16[32,32,256]{2,1,0:T(8,128)(2,1)S(1)}, u32[]{:S(2)}, u32[]{:S(2)}) %all-to-all-start.1) | async-done | bytes 524320 | tf_op jit(solution)/shard_map/all_to_all | solution.py:19
  57.7 5.1 %collective-permute-start.2 = (bf16[1024,256]{1,0:T(8,128)(2,1)S(1)}, bf16[1024,256]{1,0:T(8,128)(2,1)S(1)}, u32[]{:S(2)}, u32[]{:S(2)}) collective-permute-start(bf16[1024,256]{1,0:T(8,128)(2,1)S(1)} %bitcast.124), channel_id=1, source_target_pairs={{0,32},{32,0},{64,96},{96,64},{128,160},{160,128},{192,224},{224,1... | collective-permute-start | bytes 1572872 | tf_op jit(solution)/shard_map/ppermute | solution.py:29
  63.0 0.7 fusion.52
  63.8 0.6 collective-permute-done.2
  64.4 0.1 broadcast_select_fusion.1
  64.5 3.0 %fusion = f32[6,134,256]{2,1,0:T(8,128)S(1)} fusion(bf16[6,3,2048]{2,1,0:T(4,128)(2,1)S(1)} %collective-permute-done.1, bf16[6,128,2048]{2,1,0:T(8,128)(2,1)} %param.19, bf16[6,3,2048]{2,1,0:T(4,128)(2,1)S(1)} %collective-permute-done, bf16[1024,256]{1,0:T(8,128)(2,1)S(1)} %get-tuple-element.55, bf16[1024,256]{1,0:T(8,128)(2,1)S(1)} %get-tuple-element.54), kind=kOutput, calls=%fused_computation.3 | convolution fusion | flops 855031808 | bytes 5165056 | tf_op jit(solution)/shard_map/dot_general | solution.py:112
  67.5 0.2 fusion.31
  67.7 0.3 copy.26
  68.0 4.1 %collective-permute-start.5 = (f32[21,134]{1,0:T(8,128)S(1)}, f32[21,134]{1,0:T(8,128)S(1)}, u32[]{:S(2)}, u32[]{:S(2)}) collective-permute-start(f32[21,134]{1,0:T(8,128)S(1)} %reshape.95), channel_id=1, source_target_pairs={{0,1},{1,2},{2,3},{3,4},{4,5},{5,6},{6,7},{7,8},{8,9},{9,10},{10,1... | collective-permute-start | bytes 33776 | tf_op jit(solution)/shard_map/ppermute | solution.py:60
  72.1 0.3 copy.28
  72.5 1.5 collective-permute-start.6
  74.0 0.6 gather_fusion
  74.6 0.2 copy.27
  74.9 3.3 %collective-permute-done.6 = f32[21,134]{1,0:T(8,128)S(1)} collective-permute-done((f32[21,134]{1,0:T(8,128)S(1)}, f32[21,134]{1,0:T(8,128)S(1)}, u32[]{:S(2)}, u32[]{:S(2)}) %collective-permute-start.6) | collective-permute-done | bytes 11288 | tf_op jit(solution)/shard_map/ppermute | solution.py:61
  78.2 0.2 copy.29
  78.4 0.1 multiply_bitcast_fusion
  78.6 0.6 pad_maximum_fusion
  79.2 0.1 slice.627
  79.3 0.1 slice.641
  79.5 0.2 fusion.18
  79.8 4.1 %add_dynamic-update-slice_fusion.11 = f32[6,132,260]{2,1,0:T(8,128)S(1)} fusion(f32[6,134,262]{2,1,0:T(8,128)S(1)} %get-tuple-element.62, f32[]{:T(128)} %bitcast.26, f32[]{:T(128)} %bitcast.25, f32[]{:T(128)} %bitcast.24, f32[]{:T(128)} %bitcast.23, f32[]{:T(128)} %bitcast.22, f32[]{:T(128)} %bitcast.21), kind=kLoop, calls=%fused_computation.72 | loop fusion | flops 377519 | bytes 1032600
  83.9 4.1 %add_dynamic-update-slice_fusion.10 = f32[6,132,260]{2,1,0:T(8,128)S(1)} fusion(f32[6,132,260]{2,1,0:T(8,128)S(1)} %add_dynamic-update-slice_fusion.11, f32[6,134,262]{2,1,0:T(8,128)S(1)} %get-tuple-element.62, f32[]{:T(128)} %bitcast.32, f32[]{:T(128)} %bitcast.31, f32[]{:T(128)} %bitcast.30, f32[]{:T(128)} %bitcast.29, f32[]{:T(128)} %bitcast.28, f32[]{:T(128)} %bitcast.27), kind=kLoop, calls=%fused_computation.71 | loop fusion | flops 377520 | bytes 1462296
  88.0 4.2 %add_dynamic-update-slice_fusion.9 = f32[6,132,260]{2,1,0:T(8,128)S(1)} fusion(f32[6,132,260]{2,1,0:T(8,128)S(1)} %add_dynamic-update-slice_fusion.10, f32[6,134,262]{2,1,0:T(8,128)S(1)} %get-tuple-element.62, f32[]{:T(128)} %bitcast.38, f32[]{:T(128)} %bitcast.37, f32[]{:T(128)} %bitcast.36, f32[]{:T(128)} %bitcast.35, f32[]{:T(128)} %bitcast.34, f32[]{:T(128)} %bitcast.33), kind=kLoop, calls=%fused_computation.70 | loop fusion | flops 377520 | bytes 1462296
  92.2 4.2 %add_dynamic-update-slice_fusion.8 = f32[6,132,260]{2,1,0:T(8,128)S(1)} fusion(f32[6,132,260]{2,1,0:T(8,128)S(1)} %add_dynamic-update-slice_fusion.9, f32[6,134,262]{2,1,0:T(8,128)S(1)} %get-tuple-element.62, f32[]{:T(128)} %bitcast.44, f32[]{:T(128)} %bitcast.43, f32[]{:T(128)} %bitcast.42, f32[]{:T(128)} %bitcast.41, f32[]{:T(128)} %bitcast.40, f32[]{:T(128)} %bitcast.39), kind=kLoop, calls=%fused_computation.69 | loop fusion | flops 377520 | bytes 1462296
  96.4 4.3 %add_dynamic-update-slice_fusion.7 = f32[6,132,260]{2,1,0:T(8,128)S(1)} fusion(f32[6,132,260]{2,1,0:T(8,128)S(1)} %add_dynamic-update-slice_fusion.8, f32[6,134,262]{2,1,0:T(8,128)S(1)} %get-tuple-element.62, f32[]{:T(128)} %bitcast.50, f32[]{:T(128)} %bitcast.49, f32[]{:T(128)} %bitcast.48, f32[]{:T(128)} %bitcast.47, f32[]{:T(128)} %bitcast.46, f32[]{:T(128)} %bitcast.45), kind=kLoop, calls=%fused_computation.68 | loop fusion | flops 377520 | bytes 1462296
  100.7 4.3 %add_dynamic-update-slice_fusion.6 = f32[6,132,260]{2,1,0:T(8,128)S(1)} fusion(f32[6,132,260]{2,1,0:T(8,128)S(1)} %add_dynamic-update-slice_fusion.7, f32[6,134,262]{2,1,0:T(8,128)S(1)} %get-tuple-element.62, f32[]{:T(128)} %bitcast.56, f32[]{:T(128)} %bitcast.55, f32[]{:T(128)} %bitcast.54, f32[]{:T(128)} %bitcast.53, f32[]{:T(128)} %bitcast.52, f32[]{:T(128)} %bitcast.51), kind=kLoop, calls=%fused_computation.67 | loop fusion | flops 377520 | bytes 1462296 | tf_op jit(solution)/shard_map/stack | solution.py:74
  105.0 2.1 %fusion.13 = f32[6,132,260]{2,1,0:T(8,128)S(1)} fusion(f32[6,134,262]{2,1,0:T(8,128)S(1)} %get-tuple-element.63, f32[6,132,260]{2,1,0:T(8,128)S(1)} %add_dynamic-update-slice_fusion.6, f32[6,134,262]{2,1,0:T(8,128)S(1)} %get-tuple-element.62, f32[7,134,262]{2,1,0:T(8,128)S(1)} %pad_maximum_fusion, f32[132,260]{1,0:T(8,128)S(1)} %slice.627), kind=kLoop, calls=%fused_computation.22 | loop fusion | flops 2265120 | bytes 7550400 | tf_op jit(solution)/shard_map/add | solution.py:126
  107.0 4.1 %add_dynamic-update-slice_fusion.5 = f32[6,130,258]{2,1,0:T(8,128)S(1)} fusion(f32[6,132,260]{2,1,0:T(8,128)S(1)} %fusion.13, f32[]{:T(128)} %bitcast.26, f32[]{:T(128)} %bitcast.25, f32[]{:T(128)} %bitcast.24, f32[]{:T(128)} %bitcast.23, f32[]{:T(128)} %bitcast.22, f32[]{:T(128)} %bitcast.21), kind=kLoop, calls=%fused_computation.66 | loop fusion | flops 368939 | bytes 1013880
  111.2 4.1 %add_dynamic-update-slice_fusion.4 = f32[6,130,258]{2,1,0:T(8,128)S(1)} fusion(f32[6,130,258]{2,1,0:T(8,128)S(1)} %add_dynamic-update-slice_fusion.5, f32[6,132,260]{2,1,0:T(8,128)S(1)} %fusion.13, f32[]{:T(128)} %bitcast.32, f32[]{:T(128)} %bitcast.31, f32[]{:T(128)} %bitcast.30, f32[]{:T(128)} %bitcast.29, f32[]{:T(128)} %bitcast.28, f32[]{:T(128)} %bitcast.27), kind=kLoop, calls=%fused_computation.65 | loop fusion | flops 368940 | bytes 1462296
  115.3 4.2 %add_dynamic-update-slice_fusion.3 = f32[6,130,258]{2,1,0:T(8,128)S(1)} fusion(f32[6,130,258]{2,1,0:T(8,128)S(1)} %add_dynamic-update-slice_fusion.4, f32[6,132,260]{2,1,0:T(8,128)S(1)} %fusion.13, f32[]{:T(128)} %bitcast.38, f32[]{:T(128)} %bitcast.37, f32[]{:T(128)} %bitcast.36, f32[]{:T(128)} %bitcast.35, f32[]{:T(128)} %bitcast.34, f32[]{:T(128)} %bitcast.33), kind=kLoop, calls=%fused_computation.64 | loop fusion | flops 368940 | bytes 1462296
  119.5 4.2 %add_dynamic-update-slice_fusion.2 = f32[6,130,258]{2,1,0:T(8,128)S(1)} fusion(f32[6,130,258]{2,1,0:T(8,128)S(1)} %add_dynamic-update-slice_fusion.3, f32[6,132,260]{2,1,0:T(8,128)S(1)} %fusion.13, f32[]{:T(128)} %bitcast.44, f32[]{:T(128)} %bitcast.43, f32[]{:T(128)} %bitcast.42, f32[]{:T(128)} %bitcast.41, f32[]{:T(128)} %bitcast.40, f32[]{:T(128)} %bitcast.39), kind=kLoop, calls=%fused_computation.63 | loop fusion | flops 368940 | bytes 1462296
  123.6 4.3 %add_dynamic-update-slice_fusion.1 = f32[6,130,258]{2,1,0:T(8,128)S(1)} fusion(f32[6,130,258]{2,1,0:T(8,128)S(1)} %add_dynamic-update-slice_fusion.2, f32[6,132,260]{2,1,0:T(8,128)S(1)} %fusion.13, f32[]{:T(128)} %bitcast.50, f32[]{:T(128)} %bitcast.49, f32[]{:T(128)} %bitcast.48, f32[]{:T(128)} %bitcast.47, f32[]{:T(128)} %bitcast.46, f32[]{:T(128)} %bitcast.45), kind=kLoop, calls=%fused_computation.62 | loop fusion | flops 368940 | bytes 1462296
  127.9 4.3 %add_dynamic-update-slice_fusion = f32[6,130,258]{2,1,0:T(8,128)S(1)} fusion(f32[6,130,258]{2,1,0:T(8,128)S(1)} %add_dynamic-update-slice_fusion.1, f32[6,132,260]{2,1,0:T(8,128)S(1)} %fusion.13, f32[]{:T(128)} %bitcast.56, f32[]{:T(128)} %bitcast.55, f32[]{:T(128)} %bitcast.54, f32[]{:T(128)} %bitcast.53, f32[]{:T(128)} %bitcast.52, f32[]{:T(128)} %bitcast.51), kind=kLoop, calls=%fused_computation.61 | loop fusion | flops 368940 | bytes 1462296 | tf_op jit(solution)/shard_map/stack | solution.py:74
  132.2 2.1 %fusion.7 = f32[6,130,258]{2,1,0:T(8,128)S(1)} fusion(f32[6,134,262]{2,1,0:T(8,128)S(1)} %get-tuple-element.63, f32[6,130,258]{2,1,0:T(8,128)S(1)} %add_dynamic-update-slice_fusion, f32[6,132,260]{2,1,0:T(8,128)S(1)} %fusion.13, f32[7,134,262]{2,1,0:T(8,128)S(1)} %pad_maximum_fusion, f32[130,258]{1,0:T(8,128)S(1)} %slice.641), kind=kLoop, calls=%fused_computation.12 | loop fusion | flops 2213640 | bytes 7378800 | tf_op jit(solution)/shard_map/add | solution.py:126
  134.3 4.0 %add_dynamic-update-slice_fusion.17 = f32[6,128,256]{2,1,0:T(8,128)S(1)} fusion(f32[6,130,258]{2,1,0:T(8,128)S(1)} %fusion.7, f32[]{:T(128)} %bitcast.26, f32[]{:T(128)} %bitcast.25, f32[]{:T(128)} %bitcast.24, f32[]{:T(128)} %bitcast.23, f32[]{:T(128)} %bitcast.22, f32[]{:T(128)} %bitcast.21), kind=kLoop, calls=%fused_computation.81 | loop fusion | flops 360447 | bytes 917528
  138.3 3.9 %add_dynamic-update-slice_fusion.16 = f32[6,128,256]{2,1,0:T(8,128)S(1)} fusion(f32[6,128,256]{2,1,0:T(8,128)S(1)} %add_dynamic-update-slice_fusion.17, f32[6,130,258]{2,1,0:T(8,128)S(1)} %fusion.7, f32[]{:T(128)} %bitcast.32, f32[]{:T(128)} %bitcast.31, f32[]{:T(128)} %bitcast.30, f32[]{:T(128)} %bitcast.29, f32[]{:T(128)} %bitcast.28, f32[]{:T(128)} %bitcast.27), kind=kLoop, calls=%fused_computation.80 | loop fusion | flops 360448 | bytes 917528
  142.2 4.3 %add_dynamic-update-slice_fusion.15 = f32[6,128,256]{2,1,0:T(8,128)S(1)} fusion(f32[6,128,256]{2,1,0:T(8,128)S(1)} %add_dynamic-update-slice_fusion.16, f32[6,130,258]{2,1,0:T(8,128)S(1)} %fusion.7, f32[]{:T(128)} %bitcast.38, f32[]{:T(128)} %bitcast.37, f32[]{:T(128)} %bitcast.36, f32[]{:T(128)} %bitcast.35, f32[]{:T(128)} %bitcast.34, f32[]{:T(128)} %bitcast.33), kind=kLoop, calls=%fused_computation.79 | loop fusion | flops 360448 | bytes 917528
  146.5 4.0 %add_dynamic-update-slice_fusion.14 = f32[6,128,256]{2,1,0:T(8,128)S(1)} fusion(f32[6,128,256]{2,1,0:T(8,128)S(1)} %add_dynamic-update-slice_fusion.15, f32[6,130,258]{2,1,0:T(8,128)S(1)} %fusion.7, f32[]{:T(128)} %bitcast.44, f32[]{:T(128)} %bitcast.43, f32[]{:T(128)} %bitcast.42, f32[]{:T(128)} %bitcast.41, f32[]{:T(128)} %bitcast.40, f32[]{:T(128)} %bitcast.39), kind=kLoop, calls=%fused_computation.78 | loop fusion | flops 360448 | bytes 917528
  150.4 4.1 %add_dynamic-update-slice_fusion.13 = f32[6,128,256]{2,1,0:T(8,128)S(1)} fusion(f32[6,128,256]{2,1,0:T(8,128)S(1)} %add_dynamic-update-slice_fusion.14, f32[6,130,258]{2,1,0:T(8,128)S(1)} %fusion.7, f32[]{:T(128)} %bitcast.50, f32[]{:T(128)} %bitcast.49, f32[]{:T(128)} %bitcast.48, f32[]{:T(128)} %bitcast.47, f32[]{:T(128)} %bitcast.46, f32[]{:T(128)} %bitcast.45), kind=kLoop, calls=%fused_computation.77 | loop fusion | flops 360448 | bytes 917528
  154.5 4.1 %add_dynamic-update-slice_fusion.12 = f32[6,128,256]{2,1,0:T(8,128)S(1)} fusion(f32[6,128,256]{2,1,0:T(8,128)S(1)} %add_dynamic-update-slice_fusion.13, f32[6,130,258]{2,1,0:T(8,128)S(1)} %fusion.7, f32[]{:T(128)} %bitcast.56, f32[]{:T(128)} %bitcast.55, f32[]{:T(128)} %bitcast.54, f32[]{:T(128)} %bitcast.53, f32[]{:T(128)} %bitcast.52, f32[]{:T(128)} %bitcast.51), kind=kLoop, calls=%fused_computation.76 | loop fusion | flops 360448 | bytes 917528 | tf_op jit(solution)/shard_map/stack | solution.py:74
  158.7 1.1 fusion.23
  159.8 1.5 copy.30
  161.3 1.8 gather_fusion.2
  163.1 0.7 fusion.19
  163.8 0.2 fusion.49
  164.2 0.8 select_n.126
  165.0 6.0 %all-to-all-start.2 = ((f32[32,8,128]{2,1,0:T(8,128)}), f32[32,8,128]{2,1,0:T(8,128)S(1)}, u32[]{:S(2)}, u32[]{:S(2)}) async-start(f32[32,8,128]{2,1,0:T(8,128)} %select_n.126), calls=%async_computation.2 | async-start | bytes 262144 | tf_op jit(solution)/shard_map/all_to_all | solution.py:148
  171.6 9.7 %all-to-all-done.2 = f32[32,8,128]{2,1,0:T(8,128)S(1)} async-done(((f32[32,8,128]{2,1,0:T(8,128)}), f32[32,8,128]{2,1,0:T(8,128)S(1)}, u32[]{:S(2)}, u32[]{:S(2)}) %all-to-all-start.2) | async-done | bytes 131104 | tf_op jit(solution)/shard_map/all_to_all | solution.py:148
  181.4 0.7 add.627
  (44 shorter events, 0.9 us)
Async XLA Ops:
  0.6 1.2 copy-start
  0.7 18.7 %copy-start.5 = (f32[8]{0:T(128)S(1)}, f32[8]{0:T(128)}, u32[]{:S(2)}) copy-start(f32[8]{0:T(128)} %param.23) | copy-start | bytes 100
  1.9 18.2 %copy-start.4 = (s32[128,256]{1,0:T(8,128)S(1)}, s32[128,256]{1,0:T(8,128)}, u32[]{:S(2)}) copy-start(s32[128,256]{1,0:T(8,128)} %param.22) | copy-start | bytes 393220
  2.7 29.1 %all-to-all-start = ((bf16[32,32,256]{2,1,0:T(8,128)(2,1)}), bf16[32,32,256]{2,1,0:T(8,128)(2,1)S(1)}, u32[]{:S(2)}, u32[]{:S(2)}) async-start(bf16[32,32,256]{2,1,0:T(8,128)(2,1)} %bitcast), calls=%async_computation | async-start | bytes 1048576 | tf_op jit(solution)/shard_map/all_to_all | solution.py:16
  12.6 29.8 %copy-start.7 = (s32[1,32,1]{1,2,0:T(1,128)S(1)}, s32[1,32,1]{1,2,0:T(1,128)}, u32[]{:S(2)}) copy-start(s32[1,32,1]{1,2,0:T(1,128)} %param.28) | copy-start | bytes 388
  12.7 30.0 %copy-start.8 = (s32[1,32]{1,0:T(1,128)S(1)}, s32[1,32]{1,0:T(1,128)}, u32[]{:S(2)}) copy-start(s32[1,32]{1,0:T(1,128)} %param.27) | copy-start | bytes 388
  13.8 50.7 %collective-permute-start = (bf16[6,3,2048]{2,1,0:T(4,128)(2,1)S(1)}, bf16[6,3,2048]{2,1,0:T(4,128)(2,1)S(1)}, u32[]{:S(2)}, u32[]{:S(2)}) collective-permute-start(bf16[6,3,2048]{2,1,0:T(4,128)(2,1)S(1)} %get-tuple-element.52), channel_id=1, source_target_pairs={{0,32},{32,64},{64,96},{96,128},{128,160},{160,192},{192,224},{224... | collective-permute-start | bytes 221192 | tf_op jit(solution)/shard_map/ppermute | solution.py:40
  15.7 48.8 %collective-permute-start.1 = (bf16[6,3,2048]{2,1,0:T(4,128)(2,1)S(1)}, bf16[6,3,2048]{2,1,0:T(4,128)(2,1)S(1)}, u32[]{:S(2)}, u32[]{:S(2)}) collective-permute-start(bf16[6,3,2048]{2,1,0:T(4,128)(2,1)S(1)} %get-tuple-element.53), channel_id=1, source_target_pairs={{32,0},{64,32},{96,64},{128,96},{160,128},{192,160},{224,192},{256... | collective-permute-start | bytes 221192 | tf_op jit(solution)/shard_map/ppermute | solution.py:43
  20.1 23.4 %copy-start.1 = (f32[6,6]{1,0:T(8,128)S(1)}, f32[6,6]{1,0:T(8,128)}, u32[]{:S(2)}) copy-start(f32[6,6]{1,0:T(8,128)} %param.24) | copy-start | bytes 436
  25.3 38.4 %collective-permute-start.3 = (f32[3,256]{1,0:T(4,128)S(1)}, f32[3,256]{1,0:T(4,128)S(1)}, u32[]{:S(2)}, u32[]{:S(2)}) collective-permute-start(f32[3,256]{1,0:T(4,128)S(1)} %get-tuple-element.64), channel_id=1, source_target_pairs={{0,32},{32,64},{64,96},{96,128},{128,160},{160,192},{192,224},{224... | collective-permute-start | bytes 9224 | tf_op jit(solution)/shard_map/ppermute | solution.py:40
  29.2 34.5 %collective-permute-start.4 = (f32[3,256]{1,0:T(4,128)S(1)}, f32[3,256]{1,0:T(4,128)S(1)}, u32[]{:S(2)}, u32[]{:S(2)}) collective-permute-start(f32[3,256]{1,0:T(4,128)S(1)} %get-tuple-element.65), channel_id=1, source_target_pairs={{32,0},{64,32},{96,64},{128,96},{160,128},{192,160},{224,192},{256... | collective-permute-start | bytes 9224 | tf_op jit(solution)/shard_map/ppermute | solution.py:43
  32.7 25.1 %all-to-all-start.1 = ((bf16[32,32,256]{2,1,0:T(8,128)(2,1)}), bf16[32,32,256]{2,1,0:T(8,128)(2,1)S(1)}, u32[]{:S(2)}, u32[]{:S(2)}) async-start(bf16[32,32,256]{2,1,0:T(8,128)(2,1)} %broadcast_in_dim.121), calls=%async_computation.1 | async-start | bytes 1048576 | tf_op jit(solution)/shard_map/all_to_all | solution.py:19
  57.7 6.6 %collective-permute-start.2 = (bf16[1024,256]{1,0:T(8,128)(2,1)S(1)}, bf16[1024,256]{1,0:T(8,128)(2,1)S(1)}, u32[]{:S(2)}, u32[]{:S(2)}) collective-permute-start(bf16[1024,256]{1,0:T(8,128)(2,1)S(1)} %bitcast.124), channel_id=1, source_target_pairs={{0,32},{32,0},{64,96},{96,64},{128,160},{160,128},{192,224},{224,1... | collective-permute-start | bytes 1572872 | tf_op jit(solution)/shard_map/ppermute | solution.py:29
  68.0 6.6 %collective-permute-start.5 = (f32[21,134]{1,0:T(8,128)S(1)}, f32[21,134]{1,0:T(8,128)S(1)}, u32[]{:S(2)}, u32[]{:S(2)}) collective-permute-start(f32[21,134]{1,0:T(8,128)S(1)} %reshape.95), channel_id=1, source_target_pairs={{0,1},{1,2},{2,3},{3,4},{4,5},{5,6},{6,7},{7,8},{8,9},{9,10},{10,1... | collective-permute-start | bytes 33776 | tf_op jit(solution)/shard_map/ppermute | solution.py:60
  72.5 5.7 %collective-permute-start.6 = (f32[21,134]{1,0:T(8,128)S(1)}, f32[21,134]{1,0:T(8,128)S(1)}, u32[]{:S(2)}, u32[]{:S(2)}) collective-permute-start(f32[21,134]{1,0:T(8,128)S(1)} %reshape.97), channel_id=1, source_target_pairs={{1,0},{2,1},{3,2},{4,3},{5,4},{6,5},{7,6},{8,7},{9,8},{10,9},{11,1... | collective-permute-start | bytes 33776 | tf_op jit(solution)/shard_map/ppermute | solution.py:61
  159.8 3.3 %copy-start.2 = (f32[6,128,256]{2,1,0:T(8,128)}, f32[6,128,256]{2,1,0:T(8,128)S(1)}, u32[]{:S(2)}) copy-start(f32[6,128,256]{2,1,0:T(8,128)S(1)} %fusion.23) | copy-start | bytes 2359300
  159.8 3.3 %copy-start.6 = (f32[4,6]{1,0:T(4,128)S(1)}, f32[4,6]{1,0:T(4,128)}, u32[]{:S(2)}) copy-start(f32[4,6]{1,0:T(4,128)} %param.25) | copy-start | bytes 292
  163.8 17.6 %copy-start.3 = (f32[1,1,32,2,2,256]{5,4,3,2,1,0:T(2,128)S(1)}, f32[1,1,32,2,2,256]{5,4,3,2,1,0:T(2,128)}, u32[]{:S(2)}) copy-start(f32[1,1,32,2,2,256]{5,4,3,2,1,0:T(2,128)} %param.29) | copy-start | bytes 393220
  165.0 16.3 %all-to-all-start.2 = ((f32[32,8,128]{2,1,0:T(8,128)}), f32[32,8,128]{2,1,0:T(8,128)S(1)}, u32[]{:S(2)}, u32[]{:S(2)}) async-start(f32[32,8,128]{2,1,0:T(8,128)} %select_n.126), calls=%async_computation.2 | async-start | bytes 262144 | tf_op jit(solution)/shard_map/all_to_all | solution.py:148

commit v6 on v4

--- a/solution.py
+++ b/solution.py
@@ -4,6 +4,8 @@
 import jax.numpy as jnp
 from jax import lax
 from jax.sharding import PartitionSpec as P
+from jax.experimental import pallas as pl
+from jax.experimental.pallas import tpu as pltpu
 
 SWEEPS = 4
 CAP = 2
@@ -60,6 +62,51 @@
     low = unpack(lax.ppermute(pack(block[:, :, block.shape[2] - width :]), axis, forward))
     high = unpack(lax.ppermute(pack(block[:, :, :width]), axis, backward))
     return jnp.concatenate([low, block, high], axis=2)
+
+
+def sweeps_kernel(coupling_ref, packed_ref, out_ref, motion_ref, next_ref):
+    fields = out_ref.shape[0]
+    rows, cols = packed_ref.shape[1], packed_ref.shape[2]
+    width = SWEEPS - 1
+    stiffness = packed_ref[fields]
+    for a in range(fields):
+        diagonal = 4.0 * stiffness + coupling_ref[a * fields + a]
+        motion_ref[a] = chebyshev_weight(0) * (packed_ref[a] / diagonal)
+    source, target = motion_ref, next_ref
+    for sweep in range(1, SWEEPS):
+        for a in range(fields):
+            centre = source[a]
+            beside = (
+                pltpu.roll(centre, rows - 1, 0)
+                + pltpu.roll(centre, 1, 0)
+                + pltpu.roll(centre, cols - 1, 1)
+                + pltpu.roll(centre, 1, 1)
+            )
+            mixing = coupling_ref[a * fields] * source[0]
+            for b in range(1, fields):
+                mixing = mixing + coupling_ref[a * fields + b] * source[b]
+            applied = stiffness * (4.0 * centre - beside) + mixing
+            diagonal = 4.0 * stiffness + coupling_ref[a * fields + a]
+            target[a] = centre + chebyshev_weight(sweep) * ((packed_ref[a] - applied) / diagonal)
+        source, target = target, source
+    out_rows, out_cols = out_ref.shape[1], out_ref.shape[2]
+    for a in range(fields):
+        moved = pltpu.roll(pltpu.roll(source[a], rows - width, 0), cols - width, 1)
+        out_ref[a] = moved[:out_rows, :out_cols]
+
+
+def run_sweeps(packed, coupling, out_rows, out_cols):
+    fields = packed.shape[0] - 1
+    return pl.pallas_call(
+        sweeps_kernel,
+        out_shape=jax.ShapeDtypeStruct((fields, out_rows, out_cols), jnp.float32),
+        in_specs=[
+            pl.BlockSpec(memory_space=pltpu.SMEM),
+            pl.BlockSpec(memory_space=pltpu.VMEM),
+        ],
+        out_specs=pl.BlockSpec(memory_space=pltpu.VMEM),
+        scratch_shapes=[pltpu.VMEM((fields,) + packed.shape[1:], jnp.float32)] * 2,
+    )(coupling.reshape(-1), packed)
 
 
 def chebyshev_weight(sweep):
@@ -113,16 +160,9 @@
     coupling_diag = jnp.diagonal(coupling)[:, None, None]
     packed = jnp.concatenate([loading, stiffness_rows[None]], axis=0)
     packed = padded_last(packed, "girth", width)
-    loading_ext = packed[:6]
-    stiffness_ext = packed[6]
-    diagonal_ext = 4.0 * stiffness_ext[None] + coupling_diag
-    motion = chebyshev_weight(0) * (loading_ext / diagonal_ext)
-    for sweep in range(1, SWEEPS):
-        applied = operate_padded(motion, stiffness_ext[1:-1, 1:-1], coupling)
-        loading_ext = loading_ext[:, 1:-1, 1:-1]
-        stiffness_ext = stiffness_ext[1:-1, 1:-1]
-        diagonal_ext = diagonal_ext[:, 1:-1, 1:-1]
-        motion = motion[:, 1:-1, 1:-1] + chebyshev_weight(sweep) * ((loading_ext - applied) / diagonal_ext)
+    ext_cols = packed.shape[2]
+    packed = jnp.pad(packed, ((0, 0), (0, -ext_rows % 8), (0, -ext_cols % 128)))
+    motion = run_sweeps(packed, coupling, row_count, girth_cells)
     girth_count = lax.axis_size("girth")
     tile_ids = hotspot_tile[0]
     owner_ids = hotspot_owner[0, :, 0]

time: 109 us -> 105 us (0.963)
  Pallas kernels: 0 us -> 6.92 us
  other arithmetic: 13.6 us -> 8.54 us
  matrix products: 8.35 us -> 3.67 us
  local copies, waits for them, and re-layouts: 13.1 us -> 10.5 us
  starting transfers between devices: 43.2 us -> 45 us
    pallas_call x0 -> x1, Pallas kernels: none -> 6.92 us  [run_sweeps(): pl.pallas_call(sweeps_kernel, out_shape=jax.ShapeDtypeStruct((fields, out...]
    add x4 -> x0, other arithmetic: 5.89 us -> none  [the longest x3 5.74 us: on_device(): motion[:, 1:-1, 1:-1]]
    dot_general x3 -> x0, matrix products: 4.68 us -> none  [operate_padded(): jnp.einsum('ab,bij->aij', coupling, centre, precision=lax.Precision.HIGHEST)]
    all_to_all x1, starting transfers between devices: 5.79 us -> 9.75 us  [on_device(): lax.all_to_all(outbox, 'girth', split_axis=0, concat_axis=0, tiled=True)]
    ppermute x1, waiting for transfers between devices: 3.31 us -> 0.01 us  [padded_last(): high = unpack(lax.ppermute(pack(block[:, :, :width]), axis, backward))]
    ppermute x1, starting transfers between devices: 3.95 us -> 2.01 us  [spread(): other = lax.ppermute(got, pair_axis, pairs)]
    pallas_call x0 -> x1, local copies, waits for them, and re-layouts: none -> 1.62 us  [run_sweeps(): pl.pallas_call(sweeps_kernel, out_shape=jax.ShapeDtypeStruct((fields, out...]
    slice x6 -> x0, local copies, waits for them, and re-layouts: 1.52 us -> none  [the longest x3 1.18 us: on_device(): motion[:, 1:-1, 1:-1]]
where the time goes in v6:
time: 105 us; the launch traced here: 104 us
  starting transfers between devices  45 us (43%)
  waiting for transfers between devices  26.9 us (26%)
  local copies, waits for them, and re-layouts  10.5 us (10%)
  other arithmetic  8.54 us (8%)
  Pallas kernels  6.92 us (7%)
  matrix products  3.67 us (3%)
  between operations  2.3 us (2%)
    all_to_all x1, starting transfers between devices, scatter_gather(): got = lax.all_to_all(send, axis, 0, 0, tiled=True)  10.1 us
    all_to_all x1, waiting for transfers between devices, scatter_gather(): full = lax.all_to_all(send, axis, 0, 0, tiled=True)  10 us
    all_to_all x1, starting transfers between devices, on_device(): lax.all_to_all(outbox, 'girth', split_axis=0, concat_axis=0, tiled=True)  9.75 us
    all_to_all x1, waiting for transfers between devices, on_device(): lax.all_to_all(outbox, 'girth', split_axis=0, concat_axis=0, tiled=True)  9.72 us
    pallas_call x1, Pallas kernels, run_sweeps(): pl.pallas_call(sweeps_kernel, out_shape=jax.ShapeDtypeStruct((fields, out...  6.92 us
    ppermute x2, starting transfers between devices, padded_2(): lax.ppermute(lax.slice_in_dim(block, 0, width, axis=dim), axis, backward)  6.15 us
    all_to_all x1, starting transfers between devices, scatter_gather(): full = lax.all_to_all(send, axis, 0, 0, tiled=True)  5.62 us
    add x1, other arithmetic, on_device(): stiffness + jnp.where(thickness_class == level, class_stiffness[level], 0.0)  5.18 us
  transfers between devices with their start and end apart: 10, of which 5 were waited for; matrix products, arithmetic and copies ran while one was open for 10% of the time, Pallas kernels for 0%

profile of v6, /device:TPU:192, one launch (start us, length us, event | category | flops | bytes accessed | tf_op | source)
XLA Modules:
  0.0 103.8 jit_solution(12084699774673221834)
XLA Ops:
  0.6 0.0 copy-start
  0.6 0.0 copy-start.3
  0.7 0.0 copy-start.2
  0.7 1.2 %copy-done = bf16[2048,256]{1,0:T(8,128)(2,1)S(1)} copy-done((bf16[2048,256]{1,0:T(8,128)(2,1)S(1)}, bf16[2048,256]{1,0:T(8,128)(2,1)}, u32[]{:S(2)}) %copy-start) | copy-done | bytes 1048600
  1.9 0.8 constant_dynamic-slice_fusion
  2.7 0.0 copy-start.6
  2.7 0.0 copy-start.7
  2.7 10.1 %all-to-all-start = ((bf16[32,32,256]{2,1,0:T(8,128)(2,1)}), bf16[32,32,256]{2,1,0:T(8,128)(2,1)S(1)}, u32[]{:S(2)}, u32[]{:S(2)}) async-start(bf16[32,32,256]{2,1,0:T(8,128)(2,1)} %bitcast), calls=%async_computation | async-start | bytes 1048576 | tf_op jit(solution)/shard_map/all_to_all | solution.py:18
  12.8 0.0 copy-done.3
  12.8 0.7 fusion.38
  13.5 0.0 copy-done.2
  13.5 5.2 %select_add_fusion = f32[128,256]{1,0:T(8,128)S(1)} fusion(s32[128,256]{1,0:T(8,128)S(1)} %copy-done.2, f32[]{:T(128)} %bitcast.12, f32[]{:T(128)} %bitcast.11, f32[]{:T(128)} %bitcast.10, f32[]{:T(128)} %bitcast.9, f32[]{:T(128)} %bitcast.8, f32[]{:T(128)} %bitcast.7, f32[]{:T(128)} %bitcast.6, f32[]{:T(128)} %bitcast.5), kind=kLoop, calls=%fused_computation.37 | loop fusion | flops 753664 | bytes 262176 | tf_op jit(solution)/shard_map/add | solution.py:153
  18.7 1.9 %collective-permute-start.3 = (f32[3,256]{1,0:T(4,128)S(1)}, f32[3,256]{1,0:T(4,128)S(1)}, u32[]{:S(2)}, u32[]{:S(2)}) collective-permute-start(f32[3,256]{1,0:T(4,128)S(1)} %get-tuple-element.60), channel_id=1, source_target_pairs={{0,32},{32,64},{64,96},{96,128},{128,160},{160,192},{192,224},{224... | collective-permute-start | bytes 9224 | tf_op jit(solution)/shard_map/ppermute | solution.py:42
  20.6 3.6 %collective-permute-start.4 = (f32[3,256]{1,0:T(4,128)S(1)}, f32[3,256]{1,0:T(4,128)S(1)}, u32[]{:S(2)}, u32[]{:S(2)}) collective-permute-start(f32[3,256]{1,0:T(4,128)S(1)} %get-tuple-element.61), channel_id=1, source_target_pairs={{32,0},{64,32},{96,64},{128,96},{160,128},{192,160},{224,192},{256... | collective-permute-start | bytes 9224 | tf_op jit(solution)/shard_map/ppermute | solution.py:45
  24.9 4.7 %all-to-all-done = bf16[32,32,256]{2,1,0:T(8,128)(2,1)S(1)} async-done(((bf16[32,32,256]{2,1,0:T(8,128)(2,1)}), bf16[32,32,256]{2,1,0:T(8,128)(2,1)S(1)}, u32[]{:S(2)}, u32[]{:S(2)}) %all-to-all-start) | async-done | bytes 524320 | tf_op jit(solution)/shard_map/all_to_all | solution.py:18
  29.6 0.9 broadcast_in_dim.113
  30.5 5.6 %all-to-all-start.1 = ((bf16[32,32,256]{2,1,0:T(8,128)(2,1)}), bf16[32,32,256]{2,1,0:T(8,128)(2,1)S(1)}, u32[]{:S(2)}, u32[]{:S(2)}) async-start(bf16[32,32,256]{2,1,0:T(8,128)(2,1)} %broadcast_in_dim.113), calls=%async_computation.1 | async-start | bytes 1048576 | tf_op jit(solution)/shard_map/all_to_all | solution.py:21
  36.1 1.1 %fusion.35 = (bf16[6,3,2048]{2,1,0:T(4,128)(2,1)S(1)}, bf16[6,3,2048]{2,1,0:T(4,128)(2,1)S(1)}) fusion(bf16[6,128,2048]{2,1,0:T(8,128)(2,1)} %param.19), kind=kLoop, calls=%fused_computation.68 | loop fusion | bytes 294912 | tf_op jit(solution)/shard_map/slice | solution.py:43
  37.2 3.1 %collective-permute-start = (bf16[6,3,2048]{2,1,0:T(4,128)(2,1)S(1)}, bf16[6,3,2048]{2,1,0:T(4,128)(2,1)S(1)}, u32[]{:S(2)}, u32[]{:S(2)}) collective-permute-start(bf16[6,3,2048]{2,1,0:T(4,128)(2,1)S(1)} %get-tuple-element.50), channel_id=1, source_target_pairs={{0,32},{32,64},{64,96},{96,128},{128,160},{160,192},{192,224},{224... | collective-permute-start | bytes 221192 | tf_op jit(solution)/shard_map/ppermute | solution.py:42
  40.3 2.5 %collective-permute-start.1 = (bf16[6,3,2048]{2,1,0:T(4,128)(2,1)S(1)}, bf16[6,3,2048]{2,1,0:T(4,128)(2,1)S(1)}, u32[]{:S(2)}, u32[]{:S(2)}) collective-permute-start(bf16[6,3,2048]{2,1,0:T(4,128)(2,1)S(1)} %get-tuple-element.51), channel_id=1, source_target_pairs={{32,0},{64,32},{96,64},{128,96},{160,128},{192,160},{224,192},{256... | collective-permute-start | bytes 221192 | tf_op jit(solution)/shard_map/ppermute | solution.py:45
  42.8 0.0 copy-done.6
  42.8 0.2 convert_reduce_fusion
  43.0 0.0 copy-done.7
  43.0 0.1 select_reduce_fusion
  43.1 0.7 gather_fusion
  43.8 10.0 %all-to-all-done.1 = bf16[32,32,256]{2,1,0:T(8,128)(2,1)S(1)} async-done(((bf16[32,32,256]{2,1,0:T(8,128)(2,1)}), bf16[32,32,256]{2,1,0:T(8,128)(2,1)S(1)}, u32[]{:S(2)}, u32[]{:S(2)}) %all-to-all-start.1) | async-done | bytes 524320 | tf_op jit(solution)/shard_map/all_to_all | solution.py:21
  53.8 2.0 %collective-permute-start.2 = (bf16[1024,256]{1,0:T(8,128)(2,1)S(1)}, bf16[1024,256]{1,0:T(8,128)(2,1)S(1)}, u32[]{:S(2)}, u32[]{:S(2)}) collective-permute-start(bf16[1024,256]{1,0:T(8,128)(2,1)S(1)} %bitcast.76), channel_id=1, source_target_pairs={{0,32},{32,0},{64,96},{96,64},{128,160},{160,128},{192,224},{224,1... | collective-permute-start | bytes 1572872 | tf_op jit(solution)/shard_map/ppermute | solution.py:31
  55.9 0.1 broadcast_select_fusion.2
  55.9 0.0 collective-permute-done.3
  55.9 0.0 collective-permute-done.4
  56.0 1.6 %collective-permute-done.2 = bf16[1024,256]{1,0:T(8,128)(2,1)S(1)} collective-permute-done((bf16[1024,256]{1,0:T(8,128)(2,1)S(1)}, bf16[1024,256]{1,0:T(8,128)(2,1)S(1)}, u32[]{:S(2)}, u32[]{:S(2)}) %collective-permute-start.2) | collective-permute-done | bytes 524320 | tf_op jit(solution)/shard_map/ppermute | solution.py:31
  57.6 0.1 broadcast_select_fusion.1
  57.7 0.0 collective-permute-done
  57.7 0.0 collective-permute-done.1
  57.7 3.0 %fusion = f32[6,134,256]{2,1,0:T(8,128)S(1)} fusion(bf16[6,3,2048]{2,1,0:T(4,128)(2,1)S(1)} %collective-permute-done.1, bf16[6,128,2048]{2,1,0:T(8,128)(2,1)} %param.19, bf16[6,3,2048]{2,1,0:T(4,128)(2,1)S(1)} %collective-permute-done, bf16[1024,256]{1,0:T(8,128)(2,1)S(1)} %get-tuple-element.53, bf16[1024,256]{1,0:T(8,128)(2,1)S(1)} %get-tuple-element.52), kind=kOutput, calls=%fused_computation.2 | convolution fusion | flops 855031808 | bytes 5165056 | tf_op jit(solution)/shard_map/dot_general | solution.py:158
  60.8 0.0 copy-start.4
  60.8 0.2 fusion.18
  61.0 0.3 copy.26
  61.3 0.3 copy.28
  61.6 1.3 %collective-permute-start.6 = (f32[21,134]{1,0:T(8,128)S(1)}, f32[21,134]{1,0:T(8,128)S(1)}, u32[]{:S(2)}, u32[]{:S(2)}) collective-permute-start(f32[21,134]{1,0:T(8,128)S(1)} %reshape.97), channel_id=1, source_target_pairs={{1,0},{2,1},{3,2},{4,3},{5,4},{6,5},{7,6},{8,7},{9,8},{10,9},{11,1... | collective-permute-start | bytes 33776 | tf_op jit(solution)/shard_map/ppermute | solution.py:63
  62.9 5.1 %collective-permute-start.5 = (f32[21,134]{1,0:T(8,128)S(1)}, f32[21,134]{1,0:T(8,128)S(1)}, u32[]{:S(2)}, u32[]{:S(2)}) collective-permute-start(f32[21,134]{1,0:T(8,128)S(1)} %reshape.95), channel_id=1, source_target_pairs={{0,1},{1,2},{2,3},{3,4},{4,5},{5,6},{6,7},{7,8},{8,9},{9,10},{10,1... | collective-permute-start | bytes 33776 | tf_op jit(solution)/shard_map/ppermute | solution.py:62
  68.0 0.1 fusion.29
  68.1 0.0 copy-done.4
  68.1 0.6 reshape.92.coupling_ref
  68.7 0.8 collective-permute-done.5
  69.6 0.2 copy.27
  69.8 0.0 collective-permute-done.6
  69.8 0.2 copy.29
  70.1 1.7 %select_maximum_fusion.packed_ref = f32[7,136,384]{2,1,0:T(8,128)} fusion(f32[7,134,3]{2,1,0:T(8,128)S(1)} %bitcast.78, f32[7,134,3]{2,1,0:T(8,128)S(1)} %bitcast.77, f32[1,134,256]{2,1,0:T(8,128)S(1)} %maximum_bitcast_fusion.2, f32[6,134,256]{2,1,0:T(8,128)S(1)} %fusion), kind=kLoop, calls=%fused_computation.8 | loop fusion | flops 5117952 | bytes 2445296 | tf_op jit(solution)/shard_map/concatenate | solution.py:64
  71.8 6.9 %shard_map.122 = f32[6,128,256]{2,1,0:T(8,128)} custom-call(f32[36]{0:T(128)} %reshape.92.coupling_ref, f32[7,136,384]{2,1,0:T(8,128)} %select_maximum_fusion.packed_ref), custom_call_target="tpu_custom_call" | custom-call | tf_op jit(solution)/shard_map/pallas_call | solution.py:100
  78.7 1.6 %copy.30 = f32[6,128,256]{2,0,1:T(8,128)S(1)} copy(f32[6,128,256]{2,1,0:T(8,128)} %shard_map.122) | data formatting | bytes 1572864 | tf_op jit(solution)/shard_map/pallas_call | solution.py:100
  80.3 0.6 gather_fusion.1
  81.0 0.0 copy-done.5
  81.0 0.7 fusion.12
  81.7 0.0 copy-start.1
  81.7 0.2 fusion.36
  81.9 0.1 maximum_select_fusion
  82.0 0.1 copy.34
  82.1 0.8 select_n.122
  82.8 9.7 %all-to-all-start.2 = ((f32[32,8,128]{2,1,0:T(8,128)}), f32[32,8,128]{2,1,0:T(8,128)S(1)}, u32[]{:S(2)}, u32[]{:S(2)}) async-start(f32[32,8,128]{2,1,0:T(8,128)} %select_n.122), calls=%async_computation.2 | async-start | bytes 262144 | tf_op jit(solution)/shard_map/all_to_all | solution.py:187
  93.2 9.7 %all-to-all-done.2 = f32[32,8,128]{2,1,0:T(8,128)S(1)} async-done(((f32[32,8,128]{2,1,0:T(8,128)}), f32[32,8,128]{2,1,0:T(8,128)S(1)}, u32[]{:S(2)}, u32[]{:S(2)}) %all-to-all-start.2) | async-done | bytes 131104 | tf_op jit(solution)/shard_map/all_to_all | solution.py:187
  103.0 0.1 mul.64
  103.1 0.0 copy-done.1
  103.1 0.7 add.96
  (14 shorter events, 0.2 us)
Async XLA Ops:
  0.6 1.2 %copy-start = (bf16[2048,256]{1,0:T(8,128)(2,1)S(1)}, bf16[2048,256]{1,0:T(8,128)(2,1)}, u32[]{:S(2)}) copy-start(bf16[2048,256]{1,0:T(8,128)(2,1)} %param.20) | copy-start | bytes 3145732
  0.6 12.1 %copy-start.3 = (f32[8]{0:T(128)S(1)}, f32[8]{0:T(128)}, u32[]{:S(2)}) copy-start(f32[8]{0:T(128)} %param.23) | copy-start | bytes 100
  0.7 12.8 %copy-start.2 = (s32[128,256]{1,0:T(8,128)S(1)}, s32[128,256]{1,0:T(8,128)}, u32[]{:S(2)}) copy-start(s32[128,256]{1,0:T(8,128)} %param.22) | copy-start | bytes 393220
  2.7 40.1 %copy-start.6 = (s32[1,32,1]{1,2,0:T(1,128)S(1)}, s32[1,32,1]{1,2,0:T(1,128)}, u32[]{:S(2)}) copy-start(s32[1,32,1]{1,2,0:T(1,128)} %param.28) | copy-start | bytes 388
  2.7 40.3 %copy-start.7 = (s32[1,32]{1,0:T(1,128)S(1)}, s32[1,32]{1,0:T(1,128)}, u32[]{:S(2)}) copy-start(s32[1,32]{1,0:T(1,128)} %param.27) | copy-start | bytes 388
  2.7 27.0 %all-to-all-start = ((bf16[32,32,256]{2,1,0:T(8,128)(2,1)}), bf16[32,32,256]{2,1,0:T(8,128)(2,1)S(1)}, u32[]{:S(2)}, u32[]{:S(2)}) async-start(bf16[32,32,256]{2,1,0:T(8,128)(2,1)} %bitcast), calls=%async_computation | async-start | bytes 1048576 | tf_op jit(solution)/shard_map/all_to_all | solution.py:18
  18.7 37.3 %collective-permute-start.3 = (f32[3,256]{1,0:T(4,128)S(1)}, f32[3,256]{1,0:T(4,128)S(1)}, u32[]{:S(2)}, u32[]{:S(2)}) collective-permute-start(f32[3,256]{1,0:T(4,128)S(1)} %get-tuple-element.60), channel_id=1, source_target_pairs={{0,32},{32,64},{64,96},{96,128},{128,160},{160,192},{192,224},{224... | collective-permute-start | bytes 9224 | tf_op jit(solution)/shard_map/ppermute | solution.py:42
  20.6 35.3 %collective-permute-start.4 = (f32[3,256]{1,0:T(4,128)S(1)}, f32[3,256]{1,0:T(4,128)S(1)}, u32[]{:S(2)}, u32[]{:S(2)}) collective-permute-start(f32[3,256]{1,0:T(4,128)S(1)} %get-tuple-element.61), channel_id=1, source_target_pairs={{32,0},{64,32},{96,64},{128,96},{160,128},{192,160},{224,192},{256... | collective-permute-start | bytes 9224 | tf_op jit(solution)/shard_map/ppermute | solution.py:45
  30.5 23.3 %all-to-all-start.1 = ((bf16[32,32,256]{2,1,0:T(8,128)(2,1)}), bf16[32,32,256]{2,1,0:T(8,128)(2,1)S(1)}, u32[]{:S(2)}, u32[]{:S(2)}) async-start(bf16[32,32,256]{2,1,0:T(8,128)(2,1)} %broadcast_in_dim.113), calls=%async_computation.1 | async-start | bytes 1048576 | tf_op jit(solution)/shard_map/all_to_all | solution.py:21
  37.2 20.5 %collective-permute-start = (bf16[6,3,2048]{2,1,0:T(4,128)(2,1)S(1)}, bf16[6,3,2048]{2,1,0:T(4,128)(2,1)S(1)}, u32[]{:S(2)}, u32[]{:S(2)}) collective-permute-start(bf16[6,3,2048]{2,1,0:T(4,128)(2,1)S(1)} %get-tuple-element.50), channel_id=1, source_target_pairs={{0,32},{32,64},{64,96},{96,128},{128,160},{160,192},{192,224},{224... | collective-permute-start | bytes 221192 | tf_op jit(solution)/shard_map/ppermute | solution.py:42
  40.3 17.4 %collective-permute-start.1 = (bf16[6,3,2048]{2,1,0:T(4,128)(2,1)S(1)}, bf16[6,3,2048]{2,1,0:T(4,128)(2,1)S(1)}, u32[]{:S(2)}, u32[]{:S(2)}) collective-permute-start(bf16[6,3,2048]{2,1,0:T(4,128)(2,1)S(1)} %get-tuple-element.51), channel_id=1, source_target_pairs={{32,0},{64,32},{96,64},{128,96},{160,128},{192,160},{224,192},{256... | collective-permute-start | bytes 221192 | tf_op jit(solution)/shard_map/ppermute | solution.py:45
  53.8 3.8 %collective-permute-start.2 = (bf16[1024,256]{1,0:T(8,128)(2,1)S(1)}, bf16[1024,256]{1,0:T(8,128)(2,1)S(1)}, u32[]{:S(2)}, u32[]{:S(2)}) collective-permute-start(bf16[1024,256]{1,0:T(8,128)(2,1)S(1)} %bitcast.76), channel_id=1, source_target_pairs={{0,32},{32,0},{64,96},{96,64},{128,160},{160,128},{192,224},{224,1... | collective-permute-start | bytes 1572872 | tf_op jit(solution)/shard_map/ppermute | solution.py:31
  60.8 7.4 %copy-start.4 = (f32[6,6]{1,0:T(8,128)S(1)}, f32[6,6]{1,0:T(8,128)}, u32[]{:S(2)}) copy-start(f32[6,6]{1,0:T(8,128)} %param.24) | copy-start | bytes 436
  61.6 8.2 %collective-permute-start.6 = (f32[21,134]{1,0:T(8,128)S(1)}, f32[21,134]{1,0:T(8,128)S(1)}, u32[]{:S(2)}, u32[]{:S(2)}) collective-permute-start(f32[21,134]{1,0:T(8,128)S(1)} %reshape.97), channel_id=1, source_target_pairs={{1,0},{2,1},{3,2},{4,3},{5,4},{6,5},{7,6},{8,7},{9,8},{10,9},{11,1... | collective-permute-start | bytes 33776 | tf_op jit(solution)/shard_map/ppermute | solution.py:63
  62.9 6.6 %collective-permute-start.5 = (f32[21,134]{1,0:T(8,128)S(1)}, f32[21,134]{1,0:T(8,128)S(1)}, u32[]{:S(2)}, u32[]{:S(2)}) collective-permute-start(f32[21,134]{1,0:T(8,128)S(1)} %reshape.95), channel_id=1, source_target_pairs={{0,1},{1,2},{2,3},{3,4},{4,5},{5,6},{6,7},{7,8},{8,9},{9,10},{10,1... | collective-permute-start | bytes 33776 | tf_op jit(solution)/shard_map/ppermute | solution.py:62
  78.7 2.3 %copy-start.5 = (f32[4,6]{1,0:T(4,128)S(1)}, f32[4,6]{1,0:T(4,128)}, u32[]{:S(2)}) copy-start(f32[4,6]{1,0:T(4,128)} %param.25) | copy-start | bytes 292
  81.7 21.4 %copy-start.1 = (f32[1,1,32,2,2,256]{5,4,3,2,1,0:T(2,128)S(1)}, f32[1,1,32,2,2,256]{5,4,3,2,1,0:T(2,128)}, u32[]{:S(2)}) copy-start(f32[1,1,32,2,2,256]{5,4,3,2,1,0:T(2,128)} %param.29) | copy-start | bytes 393220
  82.8 20.1 %all-to-all-start.2 = ((f32[32,8,128]{2,1,0:T(8,128)}), f32[32,8,128]{2,1,0:T(8,128)S(1)}, u32[]{:S(2)}, u32[]{:S(2)}) async-start(f32[32,8,128]{2,1,0:T(8,128)} %select_n.122), calls=%async_computation.2 | async-start | bytes 262144 | tf_op jit(solution)/shard_map/all_to_all | solution.py:187

commit v7 on v6

--- a/solution.py
+++ b/solution.py
@@ -64,14 +64,22 @@
     return jnp.concatenate([low, block, high], axis=2)
 
 
-def sweeps_kernel(coupling_ref, packed_ref, out_ref, motion_ref, next_ref):
+def sweeps_kernel(
+    rows_ref, coupling_ref, loading_ref, side_ref, stiff_ref, stiff_side_ref,
+    out_ref, picked_ref, load_scr, stiff_scr, motion_ref, next_ref,
+):
     fields = out_ref.shape[0]
-    rows, cols = packed_ref.shape[1], packed_ref.shape[2]
-    width = SWEEPS - 1
-    stiffness = packed_ref[fields]
+    cells = loading_ref.shape[2]
+    rows, cols = load_scr.shape[1], load_scr.shape[2]
+    stiff_scr[:, :cells] = stiff_ref[...]
+    stiff_scr[:, cells:] = stiff_side_ref[...]
     for a in range(fields):
-        diagonal = 4.0 * stiffness + coupling_ref[a * fields + a]
-        motion_ref[a] = chebyshev_weight(0) * (packed_ref[a] / diagonal)
+        load_scr[a, :, :cells] = loading_ref[a]
+        load_scr[a, :, cells:] = side_ref[a]
+    stiffness = stiff_scr[...]
+    for a in range(fields):
+        diagonal = 4.0 * stiffness + coupling_ref[a, a]
+        motion_ref[a] = chebyshev_weight(0) * (load_scr[a] / diagonal)
     source, target = motion_ref, next_ref
     for sweep in range(1, SWEEPS):
         for a in range(fields):
@@ -82,31 +90,72 @@
                 + pltpu.roll(centre, cols - 1, 1)
                 + pltpu.roll(centre, 1, 1)
             )
-            mixing = coupling_ref[a * fields] * source[0]
+            mixing = coupling_ref[a, 0] * source[0]
             for b in range(1, fields):
-                mixing = mixing + coupling_ref[a * fields + b] * source[b]
+                mixing = mixing + coupling_ref[a, b] * source[b]
             applied = stiffness * (4.0 * centre - beside) + mixing
-            diagonal = 4.0 * stiffness + coupling_ref[a * fields + a]
-            target[a] = centre + chebyshev_weight(sweep) * ((packed_ref[a] - applied) / diagonal)
+            diagonal = 4.0 * stiffness + coupling_ref[a, a]
+            target[a] = centre + chebyshev_weight(sweep) * ((load_scr[a] - applied) / diagonal)
         source, target = target, source
-    out_rows, out_cols = out_ref.shape[1], out_ref.shape[2]
+    out_rows = out_ref.shape[1]
     for a in range(fields):
-        moved = pltpu.roll(pltpu.roll(source[a], rows - width, 0), cols - width, 1)
-        out_ref[a] = moved[:out_rows, :out_cols]
-
-
-def run_sweeps(packed, coupling, out_rows, out_cols):
-    fields = packed.shape[0] - 1
+        out_ref[a] = source[a, :out_rows, :cells]
+    for slot in range(picked_ref.shape[1]):
+        row = rows_ref[slot]
+        for a in range(fields):
+            picked_ref[a, pl.ds(slot, 1), :] = source[a, pl.ds(row, 1), pl.ds(0, cells)]
+
+
+def run_sweeps(slot_row, coupling, loading, side, stiffness, stiffness_side, out_rows):
+    fields, rows, cells = loading.shape
+    cols = cells + side.shape[2]
+    smem = pl.BlockSpec(memory_space=pltpu.SMEM)
+    vmem = pl.BlockSpec(memory_space=pltpu.VMEM)
     return pl.pallas_call(
         sweeps_kernel,
-        out_shape=jax.ShapeDtypeStruct((fields, out_rows, out_cols), jnp.float32),
-        in_specs=[
-            pl.BlockSpec(memory_space=pltpu.SMEM),
-            pl.BlockSpec(memory_space=pltpu.VMEM),
+        out_shape=(
+            jax.ShapeDtypeStruct((fields, out_rows, cells), jnp.float32),
+            jax.ShapeDtypeStruct((fields, slot_row.shape[0], cells), jnp.float32),
+        ),
+        in_specs=[smem, smem, vmem, vmem, vmem, vmem],
+        out_specs=(vmem, vmem),
+        scratch_shapes=[
+            pltpu.VMEM((fields, rows, cols), jnp.float32),
+            pltpu.VMEM((rows, cols), jnp.float32),
+            pltpu.VMEM((fields, rows, cols), jnp.float32),
+            pltpu.VMEM((fields, rows, cols), jnp.float32),
         ],
-        out_specs=pl.BlockSpec(memory_space=pltpu.VMEM),
-        scratch_shapes=[pltpu.VMEM((fields,) + packed.shape[1:], jnp.float32)] * 2,
-    )(coupling.reshape(-1), packed)
+    )(slot_row, coupling, loading, side, stiffness, stiffness_side)
+
+
+def cyclic_rows(block, axis, dim, width, rows):
+    count = lax.axis_size(axis)
+    forward = [(i, i + 1) for i in range(count - 1)]
+    backward = [(target, source) for source, target in forward]
+    size = block.shape[dim]
+    before = lax.ppermute(lax.slice_in_dim(block, size - width, None, axis=dim), axis, forward)
+    after = lax.ppermute(lax.slice_in_dim(block, 0, width, axis=dim), axis, backward)
+    gap_shape = list(block.shape)
+    gap_shape[dim] = rows - size - 2 * width
+    return jnp.concatenate([block, after, jnp.zeros(gap_shape, block.dtype), before], axis=dim)
+
+
+def cyclic_side(block, axis, width, lanes):
+    count = lax.axis_size(axis)
+    forward = [(i, i + 1) for i in range(count - 1)]
+    backward = [(target, source) for source, target in forward]
+    lead, rows = block.shape[0], block.shape[1]
+
+    def pack(strip):
+        return jnp.swapaxes(strip, 1, 2).reshape(lead * width, rows)
+
+    def unpack(flat):
+        return jnp.swapaxes(flat.reshape(lead, width, rows), 1, 2)
+
+    before = unpack(lax.ppermute(pack(block[:, :, block.shape[2] - width :]), axis, forward))
+    after = unpack(lax.ppermute(pack(block[:, :, :width]), axis, backward))
+    gap = jnp.zeros((lead, rows, lanes - 2 * width), block.dtype)
+    return jnp.concatenate([after, gap, before], axis=2)
 
 
 def chebyshev_weight(sweep):
@@ -151,18 +200,10 @@
     stiffness = jnp.zeros((row_count, girth_cells), jnp.float32)
     for level in range(class_stiffness.shape[0]):
         stiffness = stiffness + jnp.where(thickness_class == level, class_stiffness[level], 0.0)
-    amplitude_ext = padded_2(wave_amplitude, (("length", 1),), width)
-    stiffness_rows = padded_2(stiffness, (("length", 0),), width)
-    factors = spread(load_bank, "girth", root, "length")
-    ext_rows = row_count + 2 * width
-    loading = jnp.dot(amplitude_ext.reshape(6 * ext_rows, mode_count), factors, preferred_element_type=jnp.float32)
-    loading = loading.reshape(6, ext_rows, girth_cells)
-    coupling_diag = jnp.diagonal(coupling)[:, None, None]
-    packed = jnp.concatenate([loading, stiffness_rows[None]], axis=0)
-    packed = padded_last(packed, "girth", width)
-    ext_cols = packed.shape[2]
-    packed = jnp.pad(packed, ((0, 0), (0, -ext_rows % 8), (0, -ext_cols % 128)))
-    motion = run_sweeps(packed, coupling, row_count, girth_cells)
+    ring_rows = -(-(row_count + 2 * width) // 8) * 8
+    amplitude_ext = cyclic_rows(wave_amplitude, "length", 1, width, ring_rows)
+    stiffness_ext = cyclic_rows(stiffness, "length", 0, width, ring_rows)
+    stiffness_side = cyclic_side(stiffness_ext[None], "girth", width, 128)[0]
     girth_count = lax.axis_size("girth")
     tile_ids = hotspot_tile[0]
     owner_ids = hotspot_owner[0, :, 0]
@@ -177,7 +218,13 @@
     filled = jnp.any(hit, axis=1)
     slot_row = jnp.sum(jnp.where(hit, tile_ids[None, :], 0), axis=1)
     stiffness_at = jnp.take(stiffness, slot_row, axis=0)
-    motion_at = jnp.take(motion, slot_row, axis=1)
+    factors = spread(load_bank, "girth", root, "length")
+    loading = jnp.dot(amplitude_ext.reshape(6 * ring_rows, mode_count), factors, preferred_element_type=jnp.float32)
+    loading = loading.reshape(6, ring_rows, girth_cells)
+    loading_side = cyclic_side(loading, "girth", width, 128)
+    motion, motion_at = run_sweeps(
+        slot_row, coupling, loading, loading_side, stiffness_ext, stiffness_side, row_count
+    )
     stress_rows = stiffness_at[:, None, :] * jnp.einsum(
         "ka,aij->ikj", stress_map, motion_at, precision=lax.Precision.HIGHEST
     )

time: 105 us -> 117 us (1.11)
  starting transfers between devices: 45 us -> 53.9 us
  other arithmetic: 8.54 us -> 11.4 us
  local copies, waits for them, and re-layouts: 10.5 us -> 8.94 us
    ppermute x6 -> x8, starting transfers between devices: 17.5 us -> 22.6 us  [the longest x2 8.64 us: cyclic_side(): lax.ppermute(pack(block[:, :, block.shape[2] - width:]), axis, forward)]
    all_to_all x1, waiting for transfers between devices: 4.73 us -> 0.01 us  [scatter_gather(): got = lax.all_to_all(send, axis, 0, 0, tiled=True)]
    all_to_all x1, starting transfers between devices: 5.62 us -> 9.79 us  [scatter_gather(): full = lax.all_to_all(send, axis, 0, 0, tiled=True)]
    all_to_all x1, waiting for transfers between devices: 10 us -> 14 us  [scatter_gather(): full = lax.all_to_all(send, axis, 0, 0, tiled=True)]
    all_to_all x1, starting transfers between devices: 9.75 us -> 6.53 us  [on_device(): lax.all_to_all(outbox, 'girth', split_axis=0, concat_axis=0, tiled=True)]
    ppermute x1, starting transfers between devices: 2.01 us -> 5.1 us  [spread(): other = lax.ppermute(got, pair_axis, pairs)]
    ppermute x6 -> x8, waiting for transfers between devices: 0.83 us -> 3.7 us  [the longest x2 3.68 us: cyclic_side(): after = unpack(lax.ppermute(pack(block[:, :, :width]), axis, backward))]
    ppermute x1, waiting for transfers between devices: 1.64 us -> 0.01 us  [spread(): other = lax.ppermute(got, pair_axis, pairs)]
  transfers between devices with their start and end apart: 10 -> 12, of which waited for: 5 -> 3; matrix products, arithmetic and copies ran while one was open for 10% -> 16% of each run, Pallas kernels for 0% -> 0%
where the time goes in v7:
time: 117 us; the launch traced here: 116 us
  starting transfers between devices  53.9 us (46%)
  waiting for transfers between devices  27.5 us (24%)
  other arithmetic  11.4 us (10%)
  local copies, waits for them, and re-layouts  8.94 us (8%)
  Pallas kernels  6.85 us (6%)
  matrix products  4.82 us (4%)
  between operations  2.33 us (2%)
    all_to_all x1, waiting for transfers between devices, scatter_gather(): full = lax.all_to_all(send, axis, 0, 0, tiled=True)  14 us
    all_to_all x1, starting transfers between devices, scatter_gather(): got = lax.all_to_all(send, axis, 0, 0, tiled=True)  9.95 us
    all_to_all x1, starting transfers between devices, scatter_gather(): full = lax.all_to_all(send, axis, 0, 0, tiled=True)  9.79 us
    all_to_all x1, waiting for transfers between devices, on_device(): lax.all_to_all(outbox, 'girth', split_axis=0, concat_axis=0, tiled=True)  9.76 us
    ppermute x2, starting transfers between devices, cyclic_side(): lax.ppermute(pack(block[:, :, block.shape[2] - width:]), axis, forward)  8.64 us
    pallas_call x1, Pallas kernels, run_sweeps(): pl.pallas_call(sweeps_kernel, out_shape=(jax.ShapeDtypeStruct((fields, ou...  6.85 us
    all_to_all x1, starting transfers between devices, on_device(): lax.all_to_all(outbox, 'girth', split_axis=0, concat_axis=0, tiled=True)  6.53 us
    ppermute x2, starting transfers between devices, cyclic_rows(): lax.ppermute(lax.slice_in_dim(block, size - width, None, axis=dim), axis,...  6.28 us
  transfers between devices with their start and end apart: 12, of which 3 were waited for; matrix products, arithmetic and copies ran while one was open for 16% of the time, Pallas kernels for 0%

profile of v7, /device:TPU:192, one launch (start us, length us, event | category | flops | bytes accessed | tf_op | source)
XLA Modules:
  0.0 115.7 jit_solution(9403792419563930801)
XLA Ops:
  0.6 0.0 copy-start
  0.7 1.2 %copy-done = bf16[2048,256]{1,0:T(8,128)(2,1)S(1)} copy-done((bf16[2048,256]{1,0:T(8,128)(2,1)S(1)}, bf16[2048,256]{1,0:T(8,128)(2,1)}, u32[]{:S(2)}) %copy-start) | copy-done | bytes 1048600
  1.9 0.8 constant_dynamic-slice_fusion
  2.7 9.9 %all-to-all-start = ((bf16[32,32,256]{2,1,0:T(8,128)(2,1)}), bf16[32,32,256]{2,1,0:T(8,128)(2,1)S(1)}, u32[]{:S(2)}, u32[]{:S(2)}) async-start(bf16[32,32,256]{2,1,0:T(8,128)(2,1)} %bitcast.2), calls=%async_computation | async-start | bytes 1048576 | tf_op jit(solution)/shard_map/all_to_all | solution.py:18
  12.6 1.6 %fusion.27 = (f32[1]{0:T(128)}, f32[1]{0:T(128)}, f32[1]{0:T(128)}, f32[1]{0:T(128)}, f32[1]{0:T(128)}, /*index=5*/f32[1]{0:T(128)}, f32[1]{0:T(128)}, f32[1]{0:T(128)}) fusion(f32[8]{0:T(128)} %param.23), kind=kLoop, calls=%fused_computation.58 | loop fusion | bytes 64 | tf_op jit(solution)/shard_map/slice | solution.py:202
  14.3 6.1 %select_add_fusion = f32[128,256]{1,0:T(8,128)S(1)} fusion(s32[128,256]{1,0:T(8,128)} %param.22, f32[]{:T(128)} %bitcast.18, f32[]{:T(128)} %bitcast.17, f32[]{:T(128)} %bitcast.16, f32[]{:T(128)} %bitcast.15, f32[]{:T(128)} %bitcast.14, f32[]{:T(128)} %bitcast.13, f32[]{:T(128)} %bitcast.12, f32[]{:T(128)} %bitcast.11), kind=kLoop, calls=%fused_computation.22 | loop fusion | flops 753664 | bytes 262176 | tf_op jit(solution)/shard_map/add | solution.py:202
  20.4 1.9 %collective-permute-start.5 = (f32[3,256]{1,0:T(4,128)S(1)}, f32[3,256]{1,0:T(4,128)S(1)}, u32[]{:S(2)}, u32[]{:S(2)}) collective-permute-start(f32[3,256]{1,0:T(4,128)S(1)} %get-tuple-element.66), channel_id=1, source_target_pairs={{32,0},{64,32},{96,64},{128,96},{160,128},{192,160},{224,192},{256... | collective-permute-start | bytes 9224 | tf_op jit(solution)/shard_map/ppermute | solution.py:137
  22.3 2.4 %collective-permute-start.6 = (f32[3,256]{1,0:T(4,128)S(1)}, f32[3,256]{1,0:T(4,128)S(1)}, u32[]{:S(2)}, u32[]{:S(2)}) collective-permute-start(f32[3,256]{1,0:T(4,128)S(1)} %get-tuple-element.67), channel_id=1, source_target_pairs={{0,32},{32,64},{64,96},{96,128},{128,160},{160,192},{192,224},{224... | collective-permute-start | bytes 9224 | tf_op jit(solution)/shard_map/ppermute | solution.py:136
  24.7 1.1 fusion.24
  25.8 3.2 %collective-permute-start = (bf16[6,3,2048]{2,1,0:T(4,128)(2,1)S(1)}, bf16[6,3,2048]{2,1,0:T(4,128)(2,1)S(1)}, u32[]{:S(2)}, u32[]{:S(2)}) collective-permute-start(bf16[6,3,2048]{2,1,0:T(4,128)(2,1)S(1)} %get-tuple-element.54), channel_id=1, source_target_pairs={{32,0},{64,32},{96,64},{128,96},{160,128},{192,160},{224,192},{256... | collective-permute-start | bytes 221192 | tf_op jit(solution)/shard_map/ppermute | solution.py:137
  29.0 3.9 %collective-permute-start.1 = (bf16[6,3,2048]{2,1,0:T(4,128)(2,1)S(1)}, bf16[6,3,2048]{2,1,0:T(4,128)(2,1)S(1)}, u32[]{:S(2)}, u32[]{:S(2)}) collective-permute-start(bf16[6,3,2048]{2,1,0:T(4,128)(2,1)S(1)} %get-tuple-element.55), channel_id=1, source_target_pairs={{0,32},{32,64},{64,96},{96,128},{128,160},{160,192},{192,224},{224... | collective-permute-start | bytes 221192 | tf_op jit(solution)/shard_map/ppermute | solution.py:136
  33.5 0.9 convert_reduce_fusion
  34.4 0.7 multiply_add_fusion
  35.1 0.0 all-to-all-done
  35.1 0.9 broadcast_in_dim.119
  36.0 9.8 %all-to-all-start.1 = ((bf16[32,32,256]{2,1,0:T(8,128)(2,1)}), bf16[32,32,256]{2,1,0:T(8,128)(2,1)S(1)}, u32[]{:S(2)}, u32[]{:S(2)}) async-start(bf16[32,32,256]{2,1,0:T(8,128)(2,1)} %broadcast_in_dim.119), calls=%async_computation.1 | async-start | bytes 1048576 | tf_op jit(solution)/shard_map/all_to_all | solution.py:21
  45.8 0.1 select_reduce_fusion.rows_ref
  45.9 0.7 gather_fusion
  46.6 0.1 broadcast_select_fusion.2
  46.6 0.1 fusion.19
  46.7 0.1 pad.15.clone
  46.8 0.1 pad.18.clone
  46.9 0.1 pad.24.clone
  47.0 14.0 %all-to-all-done.1 = bf16[32,32,256]{2,1,0:T(8,128)(2,1)S(1)} async-done(((bf16[32,32,256]{2,1,0:T(8,128)(2,1)}), bf16[32,32,256]{2,1,0:T(8,128)(2,1)S(1)}, u32[]{:S(2)}, u32[]{:S(2)}) %all-to-all-start.1) | async-done | bytes 524320 | tf_op jit(solution)/shard_map/all_to_all | solution.py:21
  61.0 5.1 %collective-permute-start.2 = (bf16[1024,256]{1,0:T(8,128)(2,1)S(1)}, bf16[1024,256]{1,0:T(8,128)(2,1)S(1)}, u32[]{:S(2)}, u32[]{:S(2)}) collective-permute-start(bf16[1024,256]{1,0:T(8,128)(2,1)S(1)} %bitcast.89), channel_id=1, source_target_pairs={{0,32},{32,0},{64,96},{96,64},{128,160},{160,128},{192,224},{224,1... | collective-permute-start | bytes 1572872 | tf_op jit(solution)/shard_map/ppermute | solution.py:31
  66.1 0.0 collective-permute-done.5
  66.1 0.0 collective-permute-done.6
  66.1 0.1 fusion.28
  66.2 0.1 slice_bitcast_fusion.3
  66.3 1.3 %collective-permute-start.7 = (f32[3,136]{0,1:T(8,128)S(1)}, f32[3,136]{0,1:T(8,128)S(1)}, u32[]{:S(2)}, u32[]{:S(2)}) collective-permute-start(f32[3,136]{0,1:T(8,128)S(1)} %get-tuple-element.64), channel_id=1, source_target_pairs={{1,0},{2,1},{3,2},{4,3},{5,4},{6,5},{7,6},{8,7},{9,8},{10,9},{11,1... | collective-permute-start | bytes 4904 | tf_op jit(solution)/shard_map/ppermute | solution.py:156
  67.6 4.7 %collective-permute-start.8 = (f32[3,136]{0,1:T(8,128)S(1)}, f32[3,136]{0,1:T(8,128)S(1)}, u32[]{:S(2)}, u32[]{:S(2)}) collective-permute-start(f32[3,136]{0,1:T(8,128)S(1)} %get-tuple-element.65), channel_id=1, source_target_pairs={{0,1},{1,2},{2,3},{3,4},{4,5},{5,6},{6,7},{7,8},{8,9},{9,10},{10,1... | collective-permute-start | bytes 4904 | tf_op jit(solution)/shard_map/ppermute | solution.py:155
  72.3 0.7 pad_maximum_fusion.1.stiff_ref
  73.1 0.0 collective-permute-done.2
  73.1 0.1 broadcast_select_fusion.1
  73.2 0.0 collective-permute-done
  73.2 0.0 collective-permute-done.1
  73.2 3.0 %fusion.loading_ref = f32[6,136,256]{2,1,0:T(8,128)S(1)} fusion(bf16[6,3,2048]{2,1,0:T(4,128)(2,1)S(1)} %collective-permute-done.1, bf16[6,3,2048]{2,1,0:T(4,128)(2,1)S(1)} %collective-permute-done, bf16[6,128,2048]{2,1,0:T(8,128)(2,1)} %param.19, bf16[136]{0:T(256)(128)(2,1)S(1)} %pad.24.clone, bf16[1024,256]{1,0:T(8,128)(2,1)S(1)} %get-tuple-element.57, ...), kind=kOutput, calls=%fused_computation.1 | convolution fusion | flops 871104512 | bytes 5177616 | tf_op jit(solution)/shard_map/dot_general | solution.py:222
  76.3 0.0 copy-start.3
  76.3 0.2 slice_bitcast_fusion.1
  76.5 0.3 copy.26
  76.8 0.3 copy.28
  77.0 3.9 %collective-permute-start.4 = (f32[18,136]{1,0:T(8,128)S(1)}, f32[18,136]{1,0:T(8,128)S(1)}, u32[]{:S(2)}, u32[]{:S(2)}) collective-permute-start(f32[18,136]{1,0:T(8,128)S(1)} %reshape.105), channel_id=1, source_target_pairs={{0,1},{1,2},{2,3},{3,4},{4,5},{5,6},{6,7},{7,8},{8,9},{9,10},{10,1... | collective-permute-start | bytes 29384 | tf_op jit(solution)/shard_map/ppermute | solution.py:155
  81.0 1.3 %collective-permute-start.3 = (f32[18,136]{1,0:T(8,128)S(1)}, f32[18,136]{1,0:T(8,128)S(1)}, u32[]{:S(2)}, u32[]{:S(2)}) collective-permute-start(f32[18,136]{1,0:T(8,128)S(1)} %reshape.103), channel_id=1, source_target_pairs={{1,0},{2,1},{3,2},{4,3},{5,4},{6,5},{7,6},{8,7},{9,8},{10,9},{11,1... | collective-permute-start | bytes 29384 | tf_op jit(solution)/shard_map/ppermute | solution.py:156
  82.3 0.0 collective-permute-done.7
  82.3 0.0 collective-permute-done.8
  82.3 0.7 maximum_bitcast_fusion.2.stiff_side_ref
  83.0 3.7 %collective-permute-done.3 = f32[18,136]{1,0:T(8,128)S(1)} collective-permute-done((f32[18,136]{1,0:T(8,128)S(1)}, f32[18,136]{1,0:T(8,128)S(1)}, u32[]{:S(2)}, u32[]{:S(2)}) %collective-permute-start.3) | collective-permute-done | bytes 9824 | tf_op jit(solution)/shard_map/ppermute | solution.py:156
  86.7 0.2 copy.27
  86.9 0.0 collective-permute-done.4
  87.0 0.2 copy.29
  87.2 0.0 copy-start.2
  87.2 1.0 pad_maximum_fusion.side_ref
  88.1 0.0 copy-done.1
  88.1 6.9 %shard_map.122 = (f32[6,128,256]{2,1,0:T(8,128)}, f32[6,64,256]{2,1,0:T(8,128)}) custom-call(s32[64]{0:T(128)} %copy-done.4, f32[6,6]{1,0:T(8,128)} %coupling_ref.1, f32[6,136,256]{2,1,0:T(8,128)} %copy-done.1, f32[6,136,128]{2,1,0:T(8,128)} %pad_maximum_fusion.side_ref, f32[136,256]{1,0:T(8,128)} %pad_maximum_fusion.1.stiff_ref, ...), custom_call_target="tpu_custom_call" | custom-call | tf_op jit(solution)/shard_map/pallas_call | solution.py:114
  95.0 0.0 copy-done.3
  95.0 1.8 %fusion.8 = f32[64,4,256]{2,1,0:T(4,128)S(1)} fusion(f32[6,64,256]{2,1,0:T(8,128)} %get-tuple-element.9, f32[64,256]{1,0:T(8,128)S(1)} %broadcast_select_fusion.2, f32[4,6]{1,0:T(4,128)S(1)} %copy-done.3), kind=kOutput, calls=%fused_computation.10 | convolution fusion | flops 4784128 | bytes 720992 | tf_op jit(solution)/shard_map/ka,aij->ikj/dot_general | solution.py:228
  96.8 0.2 fusion.25
  97.0 0.1 maximum_select_fusion
  97.1 0.1 copy.34
  97.2 0.8 select_n.115
  98.0 6.5 %all-to-all-start.2 = ((f32[32,8,128]{2,1,0:T(8,128)}), f32[32,8,128]{2,1,0:T(8,128)S(1)}, u32[]{:S(2)}, u32[]{:S(2)}) async-start(f32[32,8,128]{2,1,0:T(8,128)} %select_n.115), calls=%async_computation.2 | async-start | bytes 262144 | tf_op jit(solution)/shard_map/all_to_all | solution.py:234
  105.1 9.8 %all-to-all-done.2 = f32[32,8,128]{2,1,0:T(8,128)S(1)} async-done(((f32[32,8,128]{2,1,0:T(8,128)}), f32[32,8,128]{2,1,0:T(8,128)S(1)}, u32[]{:S(2)}, u32[]{:S(2)}) %all-to-all-start.2) | async-done | bytes 131104 | tf_op jit(solution)/shard_map/all_to_all | solution.py:234
  114.9 0.1 mul.64
  115.0 0.7 add.90
  (20 shorter events, 0.2 us)
Async XLA Ops:
  0.6 1.2 %copy-start = (bf16[2048,256]{1,0:T(8,128)(2,1)S(1)}, bf16[2048,256]{1,0:T(8,128)(2,1)}, u32[]{:S(2)}) copy-start(bf16[2048,256]{1,0:T(8,128)(2,1)} %param.20) | copy-start | bytes 3145732
  0.6 45.1 %copy-start.5 = (s32[1,32]{1,0:T(1,128)S(1)}, s32[1,32]{1,0:T(1,128)}, u32[]{:S(2)}) copy-start(s32[1,32]{1,0:T(1,128)} %param.27) | copy-start | bytes 388
  2.7 32.4 %all-to-all-start = ((bf16[32,32,256]{2,1,0:T(8,128)(2,1)}), bf16[32,32,256]{2,1,0:T(8,128)(2,1)S(1)}, u32[]{:S(2)}, u32[]{:S(2)}) async-start(bf16[32,32,256]{2,1,0:T(8,128)(2,1)} %bitcast.2), calls=%async_computation | async-start | bytes 1048576 | tf_op jit(solution)/shard_map/all_to_all | solution.py:18
  20.4 45.8 %collective-permute-start.5 = (f32[3,256]{1,0:T(4,128)S(1)}, f32[3,256]{1,0:T(4,128)S(1)}, u32[]{:S(2)}, u32[]{:S(2)}) collective-permute-start(f32[3,256]{1,0:T(4,128)S(1)} %get-tuple-element.66), channel_id=1, source_target_pairs={{32,0},{64,32},{96,64},{128,96},{160,128},{192,160},{224,192},{256... | collective-permute-start | bytes 9224 | tf_op jit(solution)/shard_map/ppermute | solution.py:137
  22.3 43.8 %collective-permute-start.6 = (f32[3,256]{1,0:T(4,128)S(1)}, f32[3,256]{1,0:T(4,128)S(1)}, u32[]{:S(2)}, u32[]{:S(2)}) collective-permute-start(f32[3,256]{1,0:T(4,128)S(1)} %get-tuple-element.67), channel_id=1, source_target_pairs={{0,32},{32,64},{64,96},{96,128},{128,160},{160,192},{192,224},{224... | collective-permute-start | bytes 9224 | tf_op jit(solution)/shard_map/ppermute | solution.py:136
  25.8 47.4 %collective-permute-start = (bf16[6,3,2048]{2,1,0:T(4,128)(2,1)S(1)}, bf16[6,3,2048]{2,1,0:T(4,128)(2,1)S(1)}, u32[]{:S(2)}, u32[]{:S(2)}) collective-permute-start(bf16[6,3,2048]{2,1,0:T(4,128)(2,1)S(1)} %get-tuple-element.54), channel_id=1, source_target_pairs={{32,0},{64,32},{96,64},{128,96},{160,128},{192,160},{224,192},{256... | collective-permute-start | bytes 221192 | tf_op jit(solution)/shard_map/ppermute | solution.py:137
  29.0 44.2 %collective-permute-start.1 = (bf16[6,3,2048]{2,1,0:T(4,128)(2,1)S(1)}, bf16[6,3,2048]{2,1,0:T(4,128)(2,1)S(1)}, u32[]{:S(2)}, u32[]{:S(2)}) collective-permute-start(bf16[6,3,2048]{2,1,0:T(4,128)(2,1)S(1)} %get-tuple-element.55), channel_id=1, source_target_pairs={{0,32},{32,64},{64,96},{96,128},{128,160},{160,192},{192,224},{224... | collective-permute-start | bytes 221192 | tf_op jit(solution)/shard_map/ppermute | solution.py:136
  36.0 25.1 %all-to-all-start.1 = ((bf16[32,32,256]{2,1,0:T(8,128)(2,1)}), bf16[32,32,256]{2,1,0:T(8,128)(2,1)S(1)}, u32[]{:S(2)}, u32[]{:S(2)}) async-start(bf16[32,32,256]{2,1,0:T(8,128)(2,1)} %broadcast_in_dim.119), calls=%async_computation.1 | async-start | bytes 1048576 | tf_op jit(solution)/shard_map/all_to_all | solution.py:21
  45.9 30.4 %copy-start.4 = (s32[64]{0:T(128)}, s32[64]{0:T(128)S(1)}, u32[]{:S(2)}) copy-start(s32[64]{0:T(128)S(1)} %select_reduce_fusion.rows_ref) | copy-start | bytes 772
  61.0 12.1 %collective-permute-start.2 = (bf16[1024,256]{1,0:T(8,128)(2,1)S(1)}, bf16[1024,256]{1,0:T(8,128)(2,1)S(1)}, u32[]{:S(2)}, u32[]{:S(2)}) collective-permute-start(bf16[1024,256]{1,0:T(8,128)(2,1)S(1)} %bitcast.89), channel_id=1, source_target_pairs={{0,32},{32,0},{64,96},{96,64},{128,160},{160,128},{192,224},{224,1... | collective-permute-start | bytes 1572872 | tf_op jit(solution)/shard_map/ppermute | solution.py:31
  66.3 16.0 %collective-permute-start.7 = (f32[3,136]{0,1:T(8,128)S(1)}, f32[3,136]{0,1:T(8,128)S(1)}, u32[]{:S(2)}, u32[]{:S(2)}) collective-permute-start(f32[3,136]{0,1:T(8,128)S(1)} %get-tuple-element.64), channel_id=1, source_target_pairs={{1,0},{2,1},{3,2},{4,3},{5,4},{6,5},{7,6},{8,7},{9,8},{10,9},{11,1... | collective-permute-start | bytes 4904 | tf_op jit(solution)/shard_map/ppermute | solution.py:156
  67.6 14.7 %collective-permute-start.8 = (f32[3,136]{0,1:T(8,128)S(1)}, f32[3,136]{0,1:T(8,128)S(1)}, u32[]{:S(2)}, u32[]{:S(2)}) collective-permute-start(f32[3,136]{0,1:T(8,128)S(1)} %get-tuple-element.65), channel_id=1, source_target_pairs={{0,1},{1,2},{2,3},{3,4},{4,5},{5,6},{6,7},{7,8},{8,9},{9,10},{10,1... | collective-permute-start | bytes 4904 | tf_op jit(solution)/shard_map/ppermute | solution.py:155
  76.3 11.9 %copy-start.1 = (f32[6,136,256]{2,1,0:T(8,128)}, f32[6,136,256]{2,1,0:T(8,128)S(1)}, u32[]{:S(2)}) copy-start(f32[6,136,256]{2,1,0:T(8,128)S(1)} %fusion.loading_ref) | copy-start | bytes 2506756
  76.3 18.7 %copy-start.3 = (f32[4,6]{1,0:T(4,128)S(1)}, f32[4,6]{1,0:T(4,128)}, u32[]{:S(2)}) copy-start(f32[4,6]{1,0:T(4,128)} %param.25) | copy-start | bytes 292
  77.0 9.9 %collective-permute-start.4 = (f32[18,136]{1,0:T(8,128)S(1)}, f32[18,136]{1,0:T(8,128)S(1)}, u32[]{:S(2)}, u32[]{:S(2)}) collective-permute-start(f32[18,136]{1,0:T(8,128)S(1)} %reshape.105), channel_id=1, source_target_pairs={{0,1},{1,2},{2,3},{3,4},{4,5},{5,6},{6,7},{7,8},{8,9},{9,10},{10,1... | collective-permute-start | bytes 29384 | tf_op jit(solution)/shard_map/ppermute | solution.py:155
  81.0 5.7 %collective-permute-start.3 = (f32[18,136]{1,0:T(8,128)S(1)}, f32[18,136]{1,0:T(8,128)S(1)}, u32[]{:S(2)}, u32[]{:S(2)}) collective-permute-start(f32[18,136]{1,0:T(8,128)S(1)} %reshape.103), channel_id=1, source_target_pairs={{1,0},{2,1},{3,2},{4,3},{5,4},{6,5},{7,6},{8,7},{9,8},{10,9},{11,1... | collective-permute-start | bytes 29384 | tf_op jit(solution)/shard_map/ppermute | solution.py:156
  87.2 27.8 %copy-start.2 = (f32[1,1,32,2,2,256]{5,4,3,2,1,0:T(2,128)S(1)}, f32[1,1,32,2,2,256]{5,4,3,2,1,0:T(2,128)}, u32[]{:S(2)}) copy-start(f32[1,1,32,2,2,256]{5,4,3,2,1,0:T(2,128)} %param.29) | copy-start | bytes 393220
  98.0 16.9 %all-to-all-start.2 = ((f32[32,8,128]{2,1,0:T(8,128)}), f32[32,8,128]{2,1,0:T(8,128)S(1)}, u32[]{:S(2)}, u32[]{:S(2)}) async-start(f32[32,8,128]{2,1,0:T(8,128)} %select_n.115), calls=%async_computation.2 | async-start | bytes 262144 | tf_op jit(solution)/shard_map/all_to_all | solution.py:234

commit v8 on v7

--- a/solution.py
+++ b/solution.py
@@ -65,14 +65,14 @@
 
 
 def sweeps_kernel(
-    rows_ref, coupling_ref, loading_ref, side_ref, stiff_ref, stiff_side_ref,
+    rows_ref, coupling_ref, loading_ref, side_ref, stiff_ref,
     out_ref, picked_ref, load_scr, stiff_scr, motion_ref, next_ref,
 ):
     fields = out_ref.shape[0]
     cells = loading_ref.shape[2]
     rows, cols = load_scr.shape[1], load_scr.shape[2]
     stiff_scr[:, :cells] = stiff_ref[...]
-    stiff_scr[:, cells:] = stiff_side_ref[...]
+    stiff_scr[:, cells:] = side_ref[fields]
     for a in range(fields):
         load_scr[a, :, :cells] = loading_ref[a]
         load_scr[a, :, cells:] = side_ref[a]
@@ -106,7 +106,7 @@
             picked_ref[a, pl.ds(slot, 1), :] = source[a, pl.ds(row, 1), pl.ds(0, cells)]
 
 
-def run_sweeps(slot_row, coupling, loading, side, stiffness, stiffness_side, out_rows):
+def run_sweeps(slot_row, coupling, loading, side, stiffness, out_rows):
     fields, rows, cells = loading.shape
     cols = cells + side.shape[2]
     smem = pl.BlockSpec(memory_space=pltpu.SMEM)
@@ -117,7 +117,7 @@
             jax.ShapeDtypeStruct((fields, out_rows, cells), jnp.float32),
             jax.ShapeDtypeStruct((fields, slot_row.shape[0], cells), jnp.float32),
         ),
-        in_specs=[smem, smem, vmem, vmem, vmem, vmem],
+        in_specs=[smem, smem, vmem, vmem, vmem],
         out_specs=(vmem, vmem),
         scratch_shapes=[
             pltpu.VMEM((fields, rows, cols), jnp.float32),
@@ -125,7 +125,7 @@
             pltpu.VMEM((fields, rows, cols), jnp.float32),
             pltpu.VMEM((fields, rows, cols), jnp.float32),
         ],
-    )(slot_row, coupling, loading, side, stiffness, stiffness_side)
+    )(slot_row, coupling, loading, side, stiffness)
 
 
 def cyclic_rows(block, axis, dim, width, rows):
@@ -140,21 +140,24 @@
     return jnp.concatenate([block, after, jnp.zeros(gap_shape, block.dtype), before], axis=dim)
 
 
-def cyclic_side(block, axis, width, lanes):
+def cyclic_side(blocks, axis, width, lanes):
     count = lax.axis_size(axis)
     forward = [(i, i + 1) for i in range(count - 1)]
     backward = [(target, source) for source, target in forward]
-    lead, rows = block.shape[0], block.shape[1]
-
-    def pack(strip):
+    lead = sum(block.shape[0] for block in blocks)
+    rows = blocks[0].shape[1]
+    size = blocks[0].shape[2]
+
+    def pack(start):
+        strip = jnp.concatenate([block[:, :, start : start + width] for block in blocks], axis=0)
         return jnp.swapaxes(strip, 1, 2).reshape(lead * width, rows)
 
     def unpack(flat):
         return jnp.swapaxes(flat.reshape(lead, width, rows), 1, 2)
 
-    before = unpack(lax.ppermute(pack(block[:, :, block.shape[2] - width :]), axis, forward))
-    after = unpack(lax.ppermute(pack(block[:, :, :width]), axis, backward))
-    gap = jnp.zeros((lead, rows, lanes - 2 * width), block.dtype)
+    before = unpack(lax.ppermute(pack(size - width), axis, forward))
+    after = unpack(lax.ppermute(pack(0), axis, backward))
+    gap = jnp.zeros((lead, rows, lanes - 2 * width), before.dtype)
     return jnp.concatenate([after, gap, before], axis=2)
 
 
@@ -203,7 +206,6 @@
     ring_rows = -(-(row_count + 2 * width) // 8) * 8
     amplitude_ext = cyclic_rows(wave_amplitude, "length", 1, width, ring_rows)
     stiffness_ext = cyclic_rows(stiffness, "length", 0, width, ring_rows)
-    stiffness_side = cyclic_side(stiffness_ext[None], "girth", width, 128)[0]
     girth_count = lax.axis_size("girth")
     tile_ids = hotspot_tile[0]
     owner_ids = hotspot_owner[0, :, 0]
@@ -221,10 +223,8 @@
     factors = spread(load_bank, "girth", root, "length")
     loading = jnp.dot(amplitude_ext.reshape(6 * ring_rows, mode_count), factors, preferred_element_type=jnp.float32)
     loading = loading.reshape(6, ring_rows, girth_cells)
-    loading_side = cyclic_side(loading, "girth", width, 128)
-    motion, motion_at = run_sweeps(
-        slot_row, coupling, loading, loading_side, stiffness_ext, stiffness_side, row_count
-    )
+    side = cyclic_side([loading, stiffness_ext[None]], "girth", width, 128)
+    motion, motion_at = run_sweeps(slot_row, coupling, loading, side, stiffness_ext, row_count)
     stress_rows = stiffness_at[:, None, :] * jnp.einsum(
         "ka,aij->ikj", stress_map, motion_at, precision=lax.Precision.HIGHEST
     )

time: 117 us -> 110 us (0.940)
  starting transfers between devices: 53.9 us -> 47.6 us
  other arithmetic: 11.4 us -> 9.96 us
    ppermute x4 -> x2, starting transfers between devices: 11.2 us -> 5.4 us  [the longest x1 4.11 us: cyclic_side(): before = unpack(lax.ppermute(pack(size - width), axis, forward))]
    ppermute x4 -> x2, waiting for transfers between devices: 3.68 us -> 3.68 us  [the longest x1 3.68 us: cyclic_side(): after = unpack(lax.ppermute(pack(0), axis, backward))]
  transfers between devices with their start and end apart: 12 -> 10, of which waited for: 3 -> 4; matrix products, arithmetic and copies ran while one was open for 16% -> 12% of each run, Pallas kernels for 0% -> 0%
where the time goes in v8:
time: 110 us; the launch traced here: 109 us
  starting transfers between devices  47.6 us (43%)
  waiting for transfers between devices  28.6 us (26%)
  other arithmetic  9.96 us (9%)
  local copies, waits for them, and re-layouts  9.3 us (8%)
  Pallas kernels  6.84 us (6%)
  matrix products  4.83 us (4%)
  between operations  2.34 us (2%)
    all_to_all x1, waiting for transfers between devices, scatter_gather(): full = lax.all_to_all(send, axis, 0, 0, tiled=True)  14.4 us
    all_to_all x1, starting transfers between devices, scatter_gather(): got = lax.all_to_all(send, axis, 0, 0, tiled=True)  9.95 us
    all_to_all x1, starting transfers between devices, scatter_gather(): full = lax.all_to_all(send, axis, 0, 0, tiled=True)  9.78 us
    all_to_all x1, waiting for transfers between devices, on_device(): lax.all_to_all(outbox, 'girth', split_axis=0, concat_axis=0, tiled=True)  9.71 us
    pallas_call x1, Pallas kernels, run_sweeps(): pl.pallas_call(sweeps_kernel, out_shape=(jax.ShapeDtypeStruct((fields, ou...  6.84 us
    ppermute x2, starting transfers between devices, cyclic_rows(): lax.ppermute(lax.slice_in_dim(block, size - width, None, axis=dim), axis,...  6.28 us
    add x1, other arithmetic, on_device(): stiffness + jnp.where(thickness_class == level, class_stiffness[level], 0.0)  5.97 us
    all_to_all x1, starting transfers between devices, on_device(): lax.all_to_all(outbox, 'girth', split_axis=0, concat_axis=0, tiled=True)  5.96 us
  transfers between devices with their start and end apart: 10, of which 4 were waited for; matrix products, arithmetic and copies ran while one was open for 12% of the time, Pallas kernels for 0%

profile of v8, /device:TPU:192, one launch (start us, length us, event | category | flops | bytes accessed | tf_op | source)
XLA Modules:
  0.0 109.4 jit_solution(13302842118705111160)
XLA Ops:
  0.6 0.0 copy-start
  0.6 0.0 copy-start.5
  0.7 0.0 copy-start.6
  0.7 1.2 %copy-done = bf16[2048,256]{1,0:T(8,128)(2,1)S(1)} copy-done((bf16[2048,256]{1,0:T(8,128)(2,1)S(1)}, bf16[2048,256]{1,0:T(8,128)(2,1)}, u32[]{:S(2)}) %copy-start) | copy-done | bytes 1048600
  1.9 0.8 constant_dynamic-slice_fusion
  2.7 10.0 %all-to-all-start = ((bf16[32,32,256]{2,1,0:T(8,128)(2,1)}), bf16[32,32,256]{2,1,0:T(8,128)(2,1)S(1)}, u32[]{:S(2)}, u32[]{:S(2)}) async-start(bf16[32,32,256]{2,1,0:T(8,128)(2,1)} %bitcast.2), calls=%async_computation | async-start | bytes 1048576 | tf_op jit(solution)/shard_map/all_to_all | solution.py:18
  12.6 1.6 %fusion.29 = (f32[1]{0:T(128)}, f32[1]{0:T(128)}, f32[1]{0:T(128)}, f32[1]{0:T(128)}, f32[1]{0:T(128)}, /*index=5*/f32[1]{0:T(128)}, f32[1]{0:T(128)}, f32[1]{0:T(128)}) fusion(f32[8]{0:T(128)} %param.23), kind=kLoop, calls=%fused_computation.57 | loop fusion | bytes 64 | tf_op jit(solution)/shard_map/slice | solution.py:205
  14.3 6.0 %select_add_fusion = f32[128,256]{1,0:T(8,128)S(1)} fusion(s32[128,256]{1,0:T(8,128)} %param.22, f32[]{:T(128)} %bitcast.14, f32[]{:T(128)} %bitcast.13, f32[]{:T(128)} %bitcast.12, f32[]{:T(128)} %bitcast.11, f32[]{:T(128)} %bitcast.10, f32[]{:T(128)} %bitcast.9, f32[]{:T(128)} %bitcast.8, f32[]{:T(128)} %bitcast.7), kind=kLoop, calls=%fused_computation.20 | loop fusion | flops 753664 | bytes 262176 | tf_op jit(solution)/shard_map/add | solution.py:205
  20.3 1.9 %collective-permute-start.3 = (f32[3,256]{1,0:T(4,128)S(1)}, f32[3,256]{1,0:T(4,128)S(1)}, u32[]{:S(2)}, u32[]{:S(2)}) collective-permute-start(f32[3,256]{1,0:T(4,128)S(1)} %get-tuple-element.66), channel_id=1, source_target_pairs={{32,0},{64,32},{96,64},{128,96},{160,128},{192,160},{224,192},{256... | collective-permute-start | bytes 9224 | tf_op jit(solution)/shard_map/ppermute | solution.py:137
  22.2 2.4 %collective-permute-start.4 = (f32[3,256]{1,0:T(4,128)S(1)}, f32[3,256]{1,0:T(4,128)S(1)}, u32[]{:S(2)}, u32[]{:S(2)}) collective-permute-start(f32[3,256]{1,0:T(4,128)S(1)} %get-tuple-element.67), channel_id=1, source_target_pairs={{0,32},{32,64},{64,96},{96,128},{128,160},{160,192},{192,224},{224... | collective-permute-start | bytes 9224 | tf_op jit(solution)/shard_map/ppermute | solution.py:136
  24.6 1.1 %fusion.24 = (bf16[6,3,2048]{2,1,0:T(4,128)(2,1)S(1)}, bf16[6,3,2048]{2,1,0:T(4,128)(2,1)S(1)}) fusion(bf16[6,128,2048]{2,1,0:T(8,128)(2,1)} %param.19), kind=kLoop, calls=%fused_computation.52 | loop fusion | bytes 294912 | tf_op jit(solution)/shard_map/slice | solution.py:137
  25.7 3.2 %collective-permute-start = (bf16[6,3,2048]{2,1,0:T(4,128)(2,1)S(1)}, bf16[6,3,2048]{2,1,0:T(4,128)(2,1)S(1)}, u32[]{:S(2)}, u32[]{:S(2)}) collective-permute-start(bf16[6,3,2048]{2,1,0:T(4,128)(2,1)S(1)} %get-tuple-element.54), channel_id=1, source_target_pairs={{32,0},{64,32},{96,64},{128,96},{160,128},{192,160},{224,192},{256... | collective-permute-start | bytes 221192 | tf_op jit(solution)/shard_map/ppermute | solution.py:137
  28.9 3.9 %collective-permute-start.1 = (bf16[6,3,2048]{2,1,0:T(4,128)(2,1)S(1)}, bf16[6,3,2048]{2,1,0:T(4,128)(2,1)S(1)}, u32[]{:S(2)}, u32[]{:S(2)}) collective-permute-start(bf16[6,3,2048]{2,1,0:T(4,128)(2,1)S(1)} %get-tuple-element.55), channel_id=1, source_target_pairs={{0,32},{32,64},{64,96},{96,128},{128,160},{160,192},{192,224},{224... | collective-permute-start | bytes 221192 | tf_op jit(solution)/shard_map/ppermute | solution.py:136
  33.4 0.9 convert_reduce_fusion
  34.3 0.0 all-to-all-done
  34.4 0.9 broadcast_in_dim.116
  35.2 9.8 %all-to-all-start.1 = ((bf16[32,32,256]{2,1,0:T(8,128)(2,1)}), bf16[32,32,256]{2,1,0:T(8,128)(2,1)S(1)}, u32[]{:S(2)}, u32[]{:S(2)}) async-start(bf16[32,32,256]{2,1,0:T(8,128)(2,1)} %broadcast_in_dim.116), calls=%async_computation.1 | async-start | bytes 1048576 | tf_op jit(solution)/shard_map/all_to_all | solution.py:21
  45.0 0.0 copy-done.5
  45.0 0.0 copy-done.6
  45.0 0.1 select_reduce_fusion.rows_ref
  45.2 0.7 gather_fusion
  45.8 0.1 broadcast_select_fusion.2
  45.9 14.4 %all-to-all-done.1 = bf16[32,32,256]{2,1,0:T(8,128)(2,1)S(1)} async-done(((bf16[32,32,256]{2,1,0:T(8,128)(2,1)}), bf16[32,32,256]{2,1,0:T(8,128)(2,1)S(1)}, u32[]{:S(2)}, u32[]{:S(2)}) %all-to-all-start.1) | async-done | bytes 524320 | tf_op jit(solution)/shard_map/all_to_all | solution.py:21
  60.3 5.1 %collective-permute-start.2 = (bf16[1024,256]{1,0:T(8,128)(2,1)S(1)}, bf16[1024,256]{1,0:T(8,128)(2,1)S(1)}, u32[]{:S(2)}, u32[]{:S(2)}) collective-permute-start(bf16[1024,256]{1,0:T(8,128)(2,1)S(1)} %bitcast.73), channel_id=1, source_target_pairs={{0,32},{32,0},{64,96},{96,64},{128,160},{160,128},{192,224},{224,1... | collective-permute-start | bytes 1572872 | tf_op jit(solution)/shard_map/ppermute | solution.py:31
  65.4 0.1 fusion.19
  65.5 0.1 pad.19.clone
  65.6 0.1 pad.11.clone
  65.6 0.1 pad.25.clone
  65.7 0.0 collective-permute-done.3
  65.7 0.0 collective-permute-done.4
  65.7 0.1 fusion.30
  65.8 0.1 fusion.27
  65.9 0.1 copy.40
  66.0 0.1 copy.44
  66.1 0.8 collective-permute-done.2
  66.9 0.1 broadcast_select_fusion.1
  67.0 0.0 collective-permute-done
  67.0 0.0 collective-permute-done.1
  67.0 3.0 %fusion.loading_ref = f32[6,136,256]{2,1,0:T(8,128)S(1)} fusion(bf16[6,3,2048]{2,1,0:T(4,128)(2,1)S(1)} %collective-permute-done.1, bf16[6,3,2048]{2,1,0:T(4,128)(2,1)S(1)} %collective-permute-done, bf16[6,128,2048]{2,1,0:T(8,128)(2,1)} %param.19, bf16[136]{0:T(256)(128)(2,1)S(1)} %pad.25.clone, bf16[1024,256]{1,0:T(8,128)(2,1)S(1)} %get-tuple-element.57, ...), kind=kOutput, calls=%fused_computation.1 | convolution fusion | flops 871104512 | bytes 5177616 | tf_op jit(solution)/shard_map/dot_general | solution.py:224
  70.1 0.0 copy-done.4
  70.1 0.0 copy-start.1
  70.1 0.2 fusion.25
  70.3 0.3 copy.39
  70.7 0.3 copy.43
  71.1 4.1 %collective-permute-start.6 = (f32[21,136]{1,0:T(8,128)S(1)}, f32[21,136]{1,0:T(8,128)S(1)}, u32[]{:S(2)}, u32[]{:S(2)}) collective-permute-start(f32[21,136]{1,0:T(8,128)S(1)} %reshape.93), channel_id=1, source_target_pairs={{0,1},{1,2},{2,3},{3,4},{4,5},{5,6},{6,7},{7,8},{8,9},{9,10},{10,1... | collective-permute-start | bytes 34280 | tf_op jit(solution)/shard_map/ppermute | solution.py:158
  75.2 1.3 %collective-permute-start.5 = (f32[21,136]{1,0:T(8,128)S(1)}, f32[21,136]{1,0:T(8,128)S(1)}, u32[]{:S(2)}, u32[]{:S(2)}) collective-permute-start(f32[21,136]{1,0:T(8,128)S(1)} %reshape.91), channel_id=1, source_target_pairs={{1,0},{2,1},{3,2},{4,3},{5,4},{6,5},{7,6},{8,7},{9,8},{10,9},{11,1... | collective-permute-start | bytes 34280 | tf_op jit(solution)/shard_map/ppermute | solution.py:159
  76.5 0.7 pad_maximum_fusion.1.stiff_ref
  77.2 3.7 %collective-permute-done.5 = f32[21,136]{1,0:T(8,128)S(1)} collective-permute-done((f32[21,136]{1,0:T(8,128)S(1)}, f32[21,136]{1,0:T(8,128)S(1)}, u32[]{:S(2)}, u32[]{:S(2)}) %collective-permute-start.5) | collective-permute-done | bytes 11456 | tf_op jit(solution)/shard_map/ppermute | solution.py:159
  80.9 0.2 copy.42
  81.1 0.0 collective-permute-done.6
  81.2 0.2 copy.46
  81.4 0.0 copy-start.2
  81.4 1.0 pad_maximum_fusion.side_ref
  82.4 6.8 %shard_map.122 = (f32[6,128,256]{2,1,0:T(8,128)}, f32[6,64,256]{2,1,0:T(8,128)}) custom-call(s32[64]{0:T(128)} %copy-done.4, f32[6,6]{1,0:T(8,128)} %coupling_ref.1, f32[6,136,256]{2,1,0:T(8,128)} %copy-done.1, f32[7,136,128]{2,1,0:T(8,128)} %pad_maximum_fusion.side_ref, f32[136,256]{1,0:T(8,128)} %pad_maximum_fusion.1.stiff_ref), custom_call_target="tpu_custom_call" | custom-call | tf_op jit(solution)/shard_map/pallas_call | solution.py:114
  89.3 1.8 %fusion.8 = f32[64,4,256]{2,1,0:T(4,128)S(1)} fusion(f32[6,64,256]{2,1,0:T(8,128)} %get-tuple-element.9, f32[64,256]{1,0:T(8,128)S(1)} %broadcast_select_fusion.2, f32[4,6]{1,0:T(4,128)S(1)} %copy-done.3), kind=kOutput, calls=%fused_computation.10 | convolution fusion | flops 4784128 | bytes 720992 | tf_op jit(solution)/shard_map/ka,aij->ikj/dot_general | solution.py:228
  91.1 0.2 fusion.26
  91.3 0.1 maximum_select_fusion
  91.4 0.1 copy.51
  91.5 0.8 select_n.115
  92.2 6.0 %all-to-all-start.2 = ((f32[32,8,128]{2,1,0:T(8,128)}), f32[32,8,128]{2,1,0:T(8,128)S(1)}, u32[]{:S(2)}, u32[]{:S(2)}) async-start(f32[32,8,128]{2,1,0:T(8,128)} %select_n.115), calls=%async_computation.2 | async-start | bytes 262144 | tf_op jit(solution)/shard_map/all_to_all | solution.py:234
  98.9 9.7 %all-to-all-done.2 = f32[32,8,128]{2,1,0:T(8,128)S(1)} async-done(((f32[32,8,128]{2,1,0:T(8,128)}), f32[32,8,128]{2,1,0:T(8,128)S(1)}, u32[]{:S(2)}, u32[]{:S(2)}) %all-to-all-start.2) | async-done | bytes 131104 | tf_op jit(solution)/shard_map/all_to_all | solution.py:234
  108.6 0.1 mul.64
  108.7 0.0 copy-done.2
  108.7 0.7 add.90
  (23 shorter events, 0.2 us)
Async XLA Ops:
  0.6 1.2 %copy-start = (bf16[2048,256]{1,0:T(8,128)(2,1)S(1)}, bf16[2048,256]{1,0:T(8,128)(2,1)}, u32[]{:S(2)}) copy-start(bf16[2048,256]{1,0:T(8,128)(2,1)} %param.20) | copy-start | bytes 3145732
  0.6 44.4 %copy-start.5 = (s32[1,32,1]{1,2,0:T(1,128)S(1)}, s32[1,32,1]{1,2,0:T(1,128)}, u32[]{:S(2)}) copy-start(s32[1,32,1]{1,2,0:T(1,128)} %param.28) | copy-start | bytes 388
  0.7 44.4 %copy-start.6 = (s32[1,32]{1,0:T(1,128)S(1)}, s32[1,32]{1,0:T(1,128)}, u32[]{:S(2)}) copy-start(s32[1,32]{1,0:T(1,128)} %param.27) | copy-start | bytes 388
  2.7 31.6 %all-to-all-start = ((bf16[32,32,256]{2,1,0:T(8,128)(2,1)}), bf16[32,32,256]{2,1,0:T(8,128)(2,1)S(1)}, u32[]{:S(2)}, u32[]{:S(2)}) async-start(bf16[32,32,256]{2,1,0:T(8,128)(2,1)} %bitcast.2), calls=%async_computation | async-start | bytes 1048576 | tf_op jit(solution)/shard_map/all_to_all | solution.py:18
  20.3 45.5 %collective-permute-start.3 = (f32[3,256]{1,0:T(4,128)S(1)}, f32[3,256]{1,0:T(4,128)S(1)}, u32[]{:S(2)}, u32[]{:S(2)}) collective-permute-start(f32[3,256]{1,0:T(4,128)S(1)} %get-tuple-element.66), channel_id=1, source_target_pairs={{32,0},{64,32},{96,64},{128,96},{160,128},{192,160},{224,192},{256... | collective-permute-start | bytes 9224 | tf_op jit(solution)/shard_map/ppermute | solution.py:137
  22.2 43.5 %collective-permute-start.4 = (f32[3,256]{1,0:T(4,128)S(1)}, f32[3,256]{1,0:T(4,128)S(1)}, u32[]{:S(2)}, u32[]{:S(2)}) collective-permute-start(f32[3,256]{1,0:T(4,128)S(1)} %get-tuple-element.67), channel_id=1, source_target_pairs={{0,32},{32,64},{64,96},{96,128},{128,160},{160,192},{192,224},{224... | collective-permute-start | bytes 9224 | tf_op jit(solution)/shard_map/ppermute | solution.py:136
  25.7 41.3 %collective-permute-start = (bf16[6,3,2048]{2,1,0:T(4,128)(2,1)S(1)}, bf16[6,3,2048]{2,1,0:T(4,128)(2,1)S(1)}, u32[]{:S(2)}, u32[]{:S(2)}) collective-permute-start(bf16[6,3,2048]{2,1,0:T(4,128)(2,1)S(1)} %get-tuple-element.54), channel_id=1, source_target_pairs={{32,0},{64,32},{96,64},{128,96},{160,128},{192,160},{224,192},{256... | collective-permute-start | bytes 221192 | tf_op jit(solution)/shard_map/ppermute | solution.py:137
  28.9 38.1 %collective-permute-start.1 = (bf16[6,3,2048]{2,1,0:T(4,128)(2,1)S(1)}, bf16[6,3,2048]{2,1,0:T(4,128)(2,1)S(1)}, u32[]{:S(2)}, u32[]{:S(2)}) collective-permute-start(bf16[6,3,2048]{2,1,0:T(4,128)(2,1)S(1)} %get-tuple-element.55), channel_id=1, source_target_pairs={{0,32},{32,64},{64,96},{96,128},{128,160},{160,192},{192,224},{224... | collective-permute-start | bytes 221192 | tf_op jit(solution)/shard_map/ppermute | solution.py:136
  35.2 25.1 %all-to-all-start.1 = ((bf16[32,32,256]{2,1,0:T(8,128)(2,1)}), bf16[32,32,256]{2,1,0:T(8,128)(2,1)S(1)}, u32[]{:S(2)}, u32[]{:S(2)}) async-start(bf16[32,32,256]{2,1,0:T(8,128)(2,1)} %broadcast_in_dim.116), calls=%async_computation.1 | async-start | bytes 1048576 | tf_op jit(solution)/shard_map/all_to_all | solution.py:21
  45.1 24.9 %copy-start.4 = (s32[64]{0:T(128)}, s32[64]{0:T(128)S(1)}, u32[]{:S(2)}) copy-start(s32[64]{0:T(128)S(1)} %select_reduce_fusion.rows_ref) | copy-start | bytes 772
  60.3 6.6 %collective-permute-start.2 = (bf16[1024,256]{1,0:T(8,128)(2,1)S(1)}, bf16[1024,256]{1,0:T(8,128)(2,1)S(1)}, u32[]{:S(2)}, u32[]{:S(2)}) collective-permute-start(bf16[1024,256]{1,0:T(8,128)(2,1)S(1)} %bitcast.73), channel_id=1, source_target_pairs={{0,32},{32,0},{64,96},{96,64},{128,160},{160,128},{192,224},{224,1... | collective-permute-start | bytes 1572872 | tf_op jit(solution)/shard_map/ppermute | solution.py:31
  70.1 12.4 %copy-start.1 = (f32[6,136,256]{2,1,0:T(8,128)}, f32[6,136,256]{2,1,0:T(8,128)S(1)}, u32[]{:S(2)}) copy-start(f32[6,136,256]{2,1,0:T(8,128)S(1)} %fusion.loading_ref) | copy-start | bytes 2506756
  70.3 19.0 %copy-start.3 = (f32[4,6]{1,0:T(4,128)S(1)}, f32[4,6]{1,0:T(4,128)}, u32[]{:S(2)}) copy-start(f32[4,6]{1,0:T(4,128)} %param.25) | copy-start | bytes 292
  71.1 10.1 %collective-permute-start.6 = (f32[21,136]{1,0:T(8,128)S(1)}, f32[21,136]{1,0:T(8,128)S(1)}, u32[]{:S(2)}, u32[]{:S(2)}) collective-permute-start(f32[21,136]{1,0:T(8,128)S(1)} %reshape.93), channel_id=1, source_target_pairs={{0,1},{1,2},{2,3},{3,4},{4,5},{5,6},{6,7},{7,8},{8,9},{9,10},{10,1... | collective-permute-start | bytes 34280 | tf_op jit(solution)/shard_map/ppermute | solution.py:158
  75.2 5.7 %collective-permute-start.5 = (f32[21,136]{1,0:T(8,128)S(1)}, f32[21,136]{1,0:T(8,128)S(1)}, u32[]{:S(2)}, u32[]{:S(2)}) collective-permute-start(f32[21,136]{1,0:T(8,128)S(1)} %reshape.91), channel_id=1, source_target_pairs={{1,0},{2,1},{3,2},{4,3},{5,4},{6,5},{7,6},{8,7},{9,8},{10,9},{11,1... | collective-permute-start | bytes 34280 | tf_op jit(solution)/shard_map/ppermute | solution.py:159
  81.4 27.3 %copy-start.2 = (f32[1,1,32,2,2,256]{5,4,3,2,1,0:T(2,128)S(1)}, f32[1,1,32,2,2,256]{5,4,3,2,1,0:T(2,128)}, u32[]{:S(2)}) copy-start(f32[1,1,32,2,2,256]{5,4,3,2,1,0:T(2,128)} %param.29) | copy-start | bytes 393220
  92.2 16.3 %all-to-all-start.2 = ((f32[32,8,128]{2,1,0:T(8,128)}), f32[32,8,128]{2,1,0:T(8,128)S(1)}, u32[]{:S(2)}, u32[]{:S(2)}) async-start(f32[32,8,128]{2,1,0:T(8,128)} %select_n.115), calls=%async_computation.2 | async-start | bytes 262144 | tf_op jit(solution)/shard_map/all_to_all | solution.py:234

commit v9 on v6

--- a/solution.py
+++ b/solution.py
@@ -64,13 +64,13 @@
     return jnp.concatenate([low, block, high], axis=2)
 
 
-def sweeps_kernel(coupling_ref, packed_ref, out_ref, motion_ref, next_ref):
+def sweeps_kernel(rows_ref, coupling_ref, packed_ref, out_ref, picked_ref, motion_ref, next_ref):
     fields = out_ref.shape[0]
     rows, cols = packed_ref.shape[1], packed_ref.shape[2]
     width = SWEEPS - 1
     stiffness = packed_ref[fields]
     for a in range(fields):
-        diagonal = 4.0 * stiffness + coupling_ref[a * fields + a]
+        diagonal = 4.0 * stiffness + coupling_ref[a, a]
         motion_ref[a] = chebyshev_weight(0) * (packed_ref[a] / diagonal)
     source, target = motion_ref, next_ref
     for sweep in range(1, SWEEPS):
@@ -82,31 +82,40 @@
                 + pltpu.roll(centre, cols - 1, 1)
                 + pltpu.roll(centre, 1, 1)
             )
-            mixing = coupling_ref[a * fields] * source[0]
+            mixing = coupling_ref[a, 0] * source[0]
             for b in range(1, fields):
-                mixing = mixing + coupling_ref[a * fields + b] * source[b]
+                mixing = mixing + coupling_ref[a, b] * source[b]
             applied = stiffness * (4.0 * centre - beside) + mixing
-            diagonal = 4.0 * stiffness + coupling_ref[a * fields + a]
+            diagonal = 4.0 * stiffness + coupling_ref[a, a]
             target[a] = centre + chebyshev_weight(sweep) * ((packed_ref[a] - applied) / diagonal)
         source, target = target, source
     out_rows, out_cols = out_ref.shape[1], out_ref.shape[2]
     for a in range(fields):
         moved = pltpu.roll(pltpu.roll(source[a], rows - width, 0), cols - width, 1)
         out_ref[a] = moved[:out_rows, :out_cols]
-
-
-def run_sweeps(packed, coupling, out_rows, out_cols):
+    for slot in range(picked_ref.shape[1]):
+        row = rows_ref[slot] + width
+        for a in range(fields):
+            line = source[a, pl.ds(row, 1), :]
+            picked_ref[a, pl.ds(slot, 1), :] = pltpu.roll(line, cols - width, 1)[:, :out_cols]
+
+
+def run_sweeps(slot_row, packed, coupling, out_rows, out_cols):
     fields = packed.shape[0] - 1
     return pl.pallas_call(
         sweeps_kernel,
-        out_shape=jax.ShapeDtypeStruct((fields, out_rows, out_cols), jnp.float32),
+        out_shape=(
+            jax.ShapeDtypeStruct((fields, out_rows, out_cols), jnp.float32),
+            jax.ShapeDtypeStruct((fields, slot_row.shape[0], out_cols), jnp.float32),
+        ),
         in_specs=[
+            pl.BlockSpec(memory_space=pltpu.SMEM),
             pl.BlockSpec(memory_space=pltpu.SMEM),
             pl.BlockSpec(memory_space=pltpu.VMEM),
         ],
-        out_specs=pl.BlockSpec(memory_space=pltpu.VMEM),
+        out_specs=(pl.BlockSpec(memory_space=pltpu.VMEM), pl.BlockSpec(memory_space=pltpu.VMEM)),
         scratch_shapes=[pltpu.VMEM((fields,) + packed.shape[1:], jnp.float32)] * 2,
-    )(coupling.reshape(-1), packed)
+    )(slot_row, coupling, packed)
 
 
 def chebyshev_weight(sweep):
@@ -160,9 +169,6 @@
     coupling_diag = jnp.diagonal(coupling)[:, None, None]
     packed = jnp.concatenate([loading, stiffness_rows[None]], axis=0)
     packed = padded_last(packed, "girth", width)
-    ext_cols = packed.shape[2]
-    packed = jnp.pad(packed, ((0, 0), (0, -ext_rows % 8), (0, -ext_cols % 128)))
-    motion = run_sweeps(packed, coupling, row_count, girth_cells)
     girth_count = lax.axis_size("girth")
     tile_ids = hotspot_tile[0]
     owner_ids = hotspot_owner[0, :, 0]
@@ -177,7 +183,9 @@
     filled = jnp.any(hit, axis=1)
     slot_row = jnp.sum(jnp.where(hit, tile_ids[None, :], 0), axis=1)
     stiffness_at = jnp.take(stiffness, slot_row, axis=0)
-    motion_at = jnp.take(motion, slot_row, axis=1)
+    ext_cols = packed.shape[2]
+    packed = jnp.pad(packed, ((0, 0), (0, -ext_rows % 8), (0, -ext_cols % 128)))
+    motion, motion_at = run_sweeps(slot_row, packed, coupling, row_count, girth_cells)
     stress_rows = stiffness_at[:, None, :] * jnp.einsum(
         "ka,aij->ikj", stress_map, motion_at, precision=lax.Precision.HIGHEST
     )

time: 105 us -> 105 us (level)
  local copies, waits for them, and re-layouts: 10.5 us -> 7.63 us
  Pallas kernels: 6.92 us -> 8.34 us
  matrix products: 3.67 us -> 4.78 us
    pallas_call x1 -> x0, local copies, waits for them, and re-layouts: 1.62 us -> none  [run_sweeps(): pl.pallas_call(sweeps_kernel, out_shape=jax.ShapeDtypeStruct((fields, out...]
    pallas_call x1, Pallas kernels: 6.92 us -> 8.34 us  [run_sweeps(): pl.pallas_call(sweeps_kernel, out_shape=(jax.ShapeDtypeStruct((fields, ou...]
    dot_general x1, matrix products: 0.67 us -> 1.78 us  [on_device(): jnp.einsum('ka,aij->ikj', stress_map, motion_at, precision=lax.Precision....]
  transfers between devices with their start and end apart: 10 -> 10, of which waited for: 5 -> 5; matrix products, arithmetic and copies ran while one was open for 10% -> 9% of each run, Pallas kernels for 0% -> 0%
where the time goes in v9:
time: 105 us; the launch traced here: 104 us
  starting transfers between devices  45.1 us (43%)
  waiting for transfers between devices  27.6 us (26%)
  other arithmetic  8.43 us (8%)
  Pallas kernels  8.34 us (8%)
  local copies, waits for them, and re-layouts  7.63 us (7%)
  matrix products  4.78 us (5%)
  between operations  2.3 us (2%)
    all_to_all x1, waiting for transfers between devices, scatter_gather(): full = lax.all_to_all(send, axis, 0, 0, tiled=True)  10.1 us
    all_to_all x1, starting transfers between devices, scatter_gather(): got = lax.all_to_all(send, axis, 0, 0, tiled=True)  10.1 us
    all_to_all x1, waiting for transfers between devices, on_device(): lax.all_to_all(outbox, 'girth', split_axis=0, concat_axis=0, tiled=True)  9.72 us
    all_to_all x1, starting transfers between devices, on_device(): lax.all_to_all(outbox, 'girth', split_axis=0, concat_axis=0, tiled=True)  9.6 us
    pallas_call x1, Pallas kernels, run_sweeps(): pl.pallas_call(sweeps_kernel, out_shape=(jax.ShapeDtypeStruct((fields, ou...  8.34 us
    ppermute x2, starting transfers between devices, padded_2(): lax.ppermute(lax.slice_in_dim(block, 0, width, axis=dim), axis, backward)  6.28 us
    all_to_all x1, starting transfers between devices, scatter_gather(): full = lax.all_to_all(send, axis, 0, 0, tiled=True)  5.62 us
    ppermute x1, starting transfers between devices, padded_last(): lax.ppermute(pack(block[:, :, block.shape[2] - width:]), axis, forward)  5.36 us
  transfers between devices with their start and end apart: 10, of which 5 were waited for; matrix products, arithmetic and copies ran while one was open for 9% of the time, Pallas kernels for 0%

profile of v9, /device:TPU:192, one launch (start us, length us, event | category | flops | bytes accessed | tf_op | source)
XLA Modules:
  0.0 104.2 jit_solution(5105319085119690933)
XLA Ops:
  0.6 0.0 copy-start
  0.6 0.0 copy-start.3
  0.7 0.0 copy-start.2
  0.7 1.2 %copy-done = bf16[2048,256]{1,0:T(8,128)(2,1)S(1)} copy-done((bf16[2048,256]{1,0:T(8,128)(2,1)S(1)}, bf16[2048,256]{1,0:T(8,128)(2,1)}, u32[]{:S(2)}) %copy-start) | copy-done | bytes 1048600
  1.9 0.8 constant_dynamic-slice_fusion
  2.7 0.0 copy-start.6
  2.7 0.0 copy-start.7
  2.7 10.1 %all-to-all-start = ((bf16[32,32,256]{2,1,0:T(8,128)(2,1)}), bf16[32,32,256]{2,1,0:T(8,128)(2,1)S(1)}, u32[]{:S(2)}, u32[]{:S(2)}) async-start(bf16[32,32,256]{2,1,0:T(8,128)(2,1)} %bitcast.2), calls=%async_computation | async-start | bytes 1048576 | tf_op jit(solution)/shard_map/all_to_all | solution.py:18
  12.8 0.0 copy-done.3
  12.8 0.7 fusion.34
  13.5 0.0 copy-done.2
  13.5 5.1 %select_add_fusion = f32[128,256]{1,0:T(8,128)S(1)} fusion(s32[128,256]{1,0:T(8,128)S(1)} %copy-done.2, f32[]{:T(128)} %bitcast.14, f32[]{:T(128)} %bitcast.13, f32[]{:T(128)} %bitcast.12, f32[]{:T(128)} %bitcast.11, f32[]{:T(128)} %bitcast.10, f32[]{:T(128)} %bitcast.9, f32[]{:T(128)} %bitcast.8, f32[]{:T(128)} %bitcast.7), kind=kLoop, calls=%fused_computation.33 | loop fusion | flops 753664 | bytes 262176 | tf_op jit(solution)/shard_map/add | solution.py:162
  18.6 1.9 %collective-permute-start.3 = (f32[3,256]{1,0:T(4,128)S(1)}, f32[3,256]{1,0:T(4,128)S(1)}, u32[]{:S(2)}, u32[]{:S(2)}) collective-permute-start(f32[3,256]{1,0:T(4,128)S(1)} %get-tuple-element.64), channel_id=1, source_target_pairs={{0,32},{32,64},{64,96},{96,128},{128,160},{160,192},{192,224},{224... | collective-permute-start | bytes 9224 | tf_op jit(solution)/shard_map/ppermute | solution.py:42
  20.5 3.6 %collective-permute-start.4 = (f32[3,256]{1,0:T(4,128)S(1)}, f32[3,256]{1,0:T(4,128)S(1)}, u32[]{:S(2)}, u32[]{:S(2)}) collective-permute-start(f32[3,256]{1,0:T(4,128)S(1)} %get-tuple-element.65), channel_id=1, source_target_pairs={{32,0},{64,32},{96,64},{128,96},{160,128},{192,160},{224,192},{256... | collective-permute-start | bytes 9224 | tf_op jit(solution)/shard_map/ppermute | solution.py:45
  24.8 4.9 %all-to-all-done = bf16[32,32,256]{2,1,0:T(8,128)(2,1)S(1)} async-done(((bf16[32,32,256]{2,1,0:T(8,128)(2,1)}), bf16[32,32,256]{2,1,0:T(8,128)(2,1)S(1)}, u32[]{:S(2)}, u32[]{:S(2)}) %all-to-all-start) | async-done | bytes 524320 | tf_op jit(solution)/shard_map/all_to_all | solution.py:18
  29.6 0.9 broadcast_in_dim.106
  30.5 5.6 %all-to-all-start.1 = ((bf16[32,32,256]{2,1,0:T(8,128)(2,1)}), bf16[32,32,256]{2,1,0:T(8,128)(2,1)S(1)}, u32[]{:S(2)}, u32[]{:S(2)}) async-start(bf16[32,32,256]{2,1,0:T(8,128)(2,1)} %broadcast_in_dim.106), calls=%async_computation.1 | async-start | bytes 1048576 | tf_op jit(solution)/shard_map/all_to_all | solution.py:21
  36.1 1.1 %fusion.31 = (bf16[6,3,2048]{2,1,0:T(4,128)(2,1)S(1)}, bf16[6,3,2048]{2,1,0:T(4,128)(2,1)S(1)}) fusion(bf16[6,128,2048]{2,1,0:T(8,128)(2,1)} %param.19), kind=kLoop, calls=%fused_computation.63 | loop fusion | bytes 294912 | tf_op jit(solution)/shard_map/slice | solution.py:43
  37.2 2.9 %collective-permute-start = (bf16[6,3,2048]{2,1,0:T(4,128)(2,1)S(1)}, bf16[6,3,2048]{2,1,0:T(4,128)(2,1)S(1)}, u32[]{:S(2)}, u32[]{:S(2)}) collective-permute-start(bf16[6,3,2048]{2,1,0:T(4,128)(2,1)S(1)} %get-tuple-element.54), channel_id=1, source_target_pairs={{0,32},{32,64},{64,96},{96,128},{128,160},{160,192},{192,224},{224... | collective-permute-start | bytes 221192 | tf_op jit(solution)/shard_map/ppermute | solution.py:42
  40.2 2.6 %collective-permute-start.1 = (bf16[6,3,2048]{2,1,0:T(4,128)(2,1)S(1)}, bf16[6,3,2048]{2,1,0:T(4,128)(2,1)S(1)}, u32[]{:S(2)}, u32[]{:S(2)}) collective-permute-start(bf16[6,3,2048]{2,1,0:T(4,128)(2,1)S(1)} %get-tuple-element.55), channel_id=1, source_target_pairs={{32,0},{64,32},{96,64},{128,96},{160,128},{192,160},{224,192},{256... | collective-permute-start | bytes 221192 | tf_op jit(solution)/shard_map/ppermute | solution.py:45
  42.8 0.0 copy-done.6
  42.8 0.2 convert_reduce_fusion
  43.0 0.0 copy-done.7
  43.0 0.1 select_reduce_fusion.rows_ref
  43.1 0.0 copy-start.5
  43.2 0.7 gather_fusion
  43.8 10.1 %all-to-all-done.1 = bf16[32,32,256]{2,1,0:T(8,128)(2,1)S(1)} async-done(((bf16[32,32,256]{2,1,0:T(8,128)(2,1)}), bf16[32,32,256]{2,1,0:T(8,128)(2,1)S(1)}, u32[]{:S(2)}, u32[]{:S(2)}) %all-to-all-start.1) | async-done | bytes 524320 | tf_op jit(solution)/shard_map/all_to_all | solution.py:21
  53.9 2.0 %collective-permute-start.2 = (bf16[1024,256]{1,0:T(8,128)(2,1)S(1)}, bf16[1024,256]{1,0:T(8,128)(2,1)S(1)}, u32[]{:S(2)}, u32[]{:S(2)}) collective-permute-start(bf16[1024,256]{1,0:T(8,128)(2,1)S(1)} %bitcast.73), channel_id=1, source_target_pairs={{0,32},{32,0},{64,96},{96,64},{128,160},{160,128},{192,224},{224,1... | collective-permute-start | bytes 1572872 | tf_op jit(solution)/shard_map/ppermute | solution.py:31
  56.0 0.1 broadcast_select_fusion.2
  56.1 0.0 collective-permute-done.3
  56.1 0.0 collective-permute-done.4
  56.1 1.6 %collective-permute-done.2 = bf16[1024,256]{1,0:T(8,128)(2,1)S(1)} collective-permute-done((bf16[1024,256]{1,0:T(8,128)(2,1)S(1)}, bf16[1024,256]{1,0:T(8,128)(2,1)S(1)}, u32[]{:S(2)}, u32[]{:S(2)}) %collective-permute-start.2) | collective-permute-done | bytes 524320 | tf_op jit(solution)/shard_map/ppermute | solution.py:31
  57.7 0.1 broadcast_select_fusion.1
  57.8 0.0 copy-done.5
  57.9 0.0 collective-permute-done
  57.9 0.0 collective-permute-done.1
  57.9 3.0 %fusion = f32[6,134,256]{2,1,0:T(8,128)S(1)} fusion(bf16[6,3,2048]{2,1,0:T(4,128)(2,1)S(1)} %collective-permute-done.1, bf16[6,128,2048]{2,1,0:T(8,128)(2,1)} %param.19, bf16[6,3,2048]{2,1,0:T(4,128)(2,1)S(1)} %collective-permute-done, bf16[1024,256]{1,0:T(8,128)(2,1)S(1)} %get-tuple-element.57, bf16[1024,256]{1,0:T(8,128)(2,1)S(1)} %get-tuple-element.56), kind=kOutput, calls=%fused_computation.1 | convolution fusion | flops 855031808 | bytes 5165056 | tf_op jit(solution)/shard_map/dot_general | solution.py:167
  60.9 0.2 fusion.17
  61.1 0.3 copy.26
  61.4 0.3 copy.28
  61.8 1.3 %collective-permute-start.6 = (f32[21,134]{1,0:T(8,128)S(1)}, f32[21,134]{1,0:T(8,128)S(1)}, u32[]{:S(2)}, u32[]{:S(2)}) collective-permute-start(f32[21,134]{1,0:T(8,128)S(1)} %reshape.93), channel_id=1, source_target_pairs={{1,0},{2,1},{3,2},{4,3},{5,4},{6,5},{7,6},{8,7},{9,8},{10,9},{11,1... | collective-permute-start | bytes 33776 | tf_op jit(solution)/shard_map/ppermute | solution.py:63
  63.1 5.4 %collective-permute-start.5 = (f32[21,134]{1,0:T(8,128)S(1)}, f32[21,134]{1,0:T(8,128)S(1)}, u32[]{:S(2)}, u32[]{:S(2)}) collective-permute-start(f32[21,134]{1,0:T(8,128)S(1)} %reshape.91), channel_id=1, source_target_pairs={{0,1},{1,2},{2,3},{3,4},{4,5},{5,6},{6,7},{7,8},{8,9},{9,10},{10,1... | collective-permute-start | bytes 33776 | tf_op jit(solution)/shard_map/ppermute | solution.py:62
  68.4 0.1 fusion.26
  68.5 1.2 %collective-permute-done.5 = f32[21,134]{1,0:T(8,128)S(1)} collective-permute-done((f32[21,134]{1,0:T(8,128)S(1)}, f32[21,134]{1,0:T(8,128)S(1)}, u32[]{:S(2)}, u32[]{:S(2)}) %collective-permute-start.5) | collective-permute-done | bytes 11288 | tf_op jit(solution)/shard_map/ppermute | solution.py:62
  69.8 0.2 copy.27
  70.0 0.0 collective-permute-done.6
  70.0 0.2 copy.29
  70.3 1.7 %select_maximum_fusion.packed_ref = f32[7,136,384]{2,1,0:T(8,128)} fusion(f32[7,134,3]{2,1,0:T(8,128)S(1)} %bitcast.75, f32[7,134,3]{2,1,0:T(8,128)S(1)} %bitcast.74, f32[1,134,256]{2,1,0:T(8,128)S(1)} %maximum_bitcast_fusion.2, f32[6,134,256]{2,1,0:T(8,128)S(1)} %fusion), kind=kLoop, calls=%fused_computation.7 | loop fusion | flops 5117952 | bytes 2445296 | tf_op jit(solution)/shard_map/concatenate | solution.py:64
  72.0 0.0 copy-start.4
  72.0 8.3 %shard_map.122 = (f32[6,128,256]{2,1,0:T(8,128)}, f32[6,64,256]{2,1,0:T(8,128)}) custom-call(s32[64]{0:T(128)} %copy-done.5, f32[6,6]{1,0:T(8,128)} %coupling_ref.1, f32[7,136,384]{2,1,0:T(8,128)} %select_maximum_fusion.packed_ref), custom_call_target="tpu_custom_call" | custom-call | tf_op jit(solution)/shard_map/pallas_call | solution.py:105
  80.4 0.0 copy-done.4
  80.4 1.8 %fusion.12 = f32[64,4,256]{2,1,0:T(4,128)S(1)} fusion(f32[6,64,256]{2,1,0:T(8,128)} %get-tuple-element.9, f32[64,256]{1,0:T(8,128)S(1)} %broadcast_select_fusion.2, f32[4,6]{1,0:T(4,128)S(1)} %copy-done.4), kind=kOutput, calls=%fused_computation.18 | convolution fusion | flops 4784128 | bytes 720992 | tf_op jit(solution)/shard_map/ka,aij->ikj/dot_general | solution.py:189
  82.1 0.0 copy-start.1
  82.2 0.2 fusion.32
  82.4 0.1 maximum_select_fusion
  82.5 0.1 copy.34
  82.6 0.8 select_n.115
  83.3 9.6 %all-to-all-start.2 = ((f32[32,8,128]{2,1,0:T(8,128)}), f32[32,8,128]{2,1,0:T(8,128)S(1)}, u32[]{:S(2)}, u32[]{:S(2)}) async-start(f32[32,8,128]{2,1,0:T(8,128)} %select_n.115), calls=%async_computation.2 | async-start | bytes 262144 | tf_op jit(solution)/shard_map/all_to_all | solution.py:195
  93.6 9.7 %all-to-all-done.2 = f32[32,8,128]{2,1,0:T(8,128)S(1)} async-done(((f32[32,8,128]{2,1,0:T(8,128)}), f32[32,8,128]{2,1,0:T(8,128)S(1)}, u32[]{:S(2)}, u32[]{:S(2)}) %all-to-all-start.2) | async-done | bytes 131104 | tf_op jit(solution)/shard_map/all_to_all | solution.py:195
  103.3 0.1 mul.64
  103.4 0.0 copy-done.1
  103.4 0.7 add.92
  (13 shorter events, 0.2 us)
Async XLA Ops:
  0.6 1.2 %copy-start = (bf16[2048,256]{1,0:T(8,128)(2,1)S(1)}, bf16[2048,256]{1,0:T(8,128)(2,1)}, u32[]{:S(2)}) copy-start(bf16[2048,256]{1,0:T(8,128)(2,1)} %param.20) | copy-start | bytes 3145732
  0.6 12.1 %copy-start.3 = (f32[8]{0:T(128)S(1)}, f32[8]{0:T(128)}, u32[]{:S(2)}) copy-start(f32[8]{0:T(128)} %param.23) | copy-start | bytes 100
  0.7 12.8 %copy-start.2 = (s32[128,256]{1,0:T(8,128)S(1)}, s32[128,256]{1,0:T(8,128)}, u32[]{:S(2)}) copy-start(s32[128,256]{1,0:T(8,128)} %param.22) | copy-start | bytes 393220
  2.7 40.1 %copy-start.6 = (s32[1,32,1]{1,2,0:T(1,128)S(1)}, s32[1,32,1]{1,2,0:T(1,128)}, u32[]{:S(2)}) copy-start(s32[1,32,1]{1,2,0:T(1,128)} %param.28) | copy-start | bytes 388
  2.7 40.3 %copy-start.7 = (s32[1,32]{1,0:T(1,128)S(1)}, s32[1,32]{1,0:T(1,128)}, u32[]{:S(2)}) copy-start(s32[1,32]{1,0:T(1,128)} %param.27) | copy-start | bytes 388
  2.7 27.0 %all-to-all-start = ((bf16[32,32,256]{2,1,0:T(8,128)(2,1)}), bf16[32,32,256]{2,1,0:T(8,128)(2,1)S(1)}, u32[]{:S(2)}, u32[]{:S(2)}) async-start(bf16[32,32,256]{2,1,0:T(8,128)(2,1)} %bitcast.2), calls=%async_computation | async-start | bytes 1048576 | tf_op jit(solution)/shard_map/all_to_all | solution.py:18
  18.6 37.5 %collective-permute-start.3 = (f32[3,256]{1,0:T(4,128)S(1)}, f32[3,256]{1,0:T(4,128)S(1)}, u32[]{:S(2)}, u32[]{:S(2)}) collective-permute-start(f32[3,256]{1,0:T(4,128)S(1)} %get-tuple-element.64), channel_id=1, source_target_pairs={{0,32},{32,64},{64,96},{96,128},{128,160},{160,192},{192,224},{224... | collective-permute-start | bytes 9224 | tf_op jit(solution)/shard_map/ppermute | solution.py:42
  20.5 35.6 %collective-permute-start.4 = (f32[3,256]{1,0:T(4,128)S(1)}, f32[3,256]{1,0:T(4,128)S(1)}, u32[]{:S(2)}, u32[]{:S(2)}) collective-permute-start(f32[3,256]{1,0:T(4,128)S(1)} %get-tuple-element.65), channel_id=1, source_target_pairs={{32,0},{64,32},{96,64},{128,96},{160,128},{192,160},{224,192},{256... | collective-permute-start | bytes 9224 | tf_op jit(solution)/shard_map/ppermute | solution.py:45
  30.5 23.4 %all-to-all-start.1 = ((bf16[32,32,256]{2,1,0:T(8,128)(2,1)}), bf16[32,32,256]{2,1,0:T(8,128)(2,1)S(1)}, u32[]{:S(2)}, u32[]{:S(2)}) async-start(bf16[32,32,256]{2,1,0:T(8,128)(2,1)} %broadcast_in_dim.106), calls=%async_computation.1 | async-start | bytes 1048576 | tf_op jit(solution)/shard_map/all_to_all | solution.py:21
  37.2 20.6 %collective-permute-start = (bf16[6,3,2048]{2,1,0:T(4,128)(2,1)S(1)}, bf16[6,3,2048]{2,1,0:T(4,128)(2,1)S(1)}, u32[]{:S(2)}, u32[]{:S(2)}) collective-permute-start(bf16[6,3,2048]{2,1,0:T(4,128)(2,1)S(1)} %get-tuple-element.54), channel_id=1, source_target_pairs={{0,32},{32,64},{64,96},{96,128},{128,160},{160,192},{192,224},{224... | collective-permute-start | bytes 221192 | tf_op jit(solution)/shard_map/ppermute | solution.py:42
  40.2 17.7 %collective-permute-start.1 = (bf16[6,3,2048]{2,1,0:T(4,128)(2,1)S(1)}, bf16[6,3,2048]{2,1,0:T(4,128)(2,1)S(1)}, u32[]{:S(2)}, u32[]{:S(2)}) collective-permute-start(bf16[6,3,2048]{2,1,0:T(4,128)(2,1)S(1)} %get-tuple-element.55), channel_id=1, source_target_pairs={{32,0},{64,32},{96,64},{128,96},{160,128},{192,160},{224,192},{256... | collective-permute-start | bytes 221192 | tf_op jit(solution)/shard_map/ppermute | solution.py:45
  43.1 14.7 %copy-start.5 = (s32[64]{0:T(128)}, s32[64]{0:T(128)S(1)}, u32[]{:S(2)}) copy-start(s32[64]{0:T(128)S(1)} %select_reduce_fusion.rows_ref) | copy-start | bytes 772
  53.9 3.8 %collective-permute-start.2 = (bf16[1024,256]{1,0:T(8,128)(2,1)S(1)}, bf16[1024,256]{1,0:T(8,128)(2,1)S(1)}, u32[]{:S(2)}, u32[]{:S(2)}) collective-permute-start(bf16[1024,256]{1,0:T(8,128)(2,1)S(1)} %bitcast.73), channel_id=1, source_target_pairs={{0,32},{32,0},{64,96},{96,64},{128,160},{160,128},{192,224},{224,1... | collective-permute-start | bytes 1572872 | tf_op jit(solution)/shard_map/ppermute | solution.py:31
  61.8 8.2 %collective-permute-start.6 = (f32[21,134]{1,0:T(8,128)S(1)}, f32[21,134]{1,0:T(8,128)S(1)}, u32[]{:S(2)}, u32[]{:S(2)}) collective-permute-start(f32[21,134]{1,0:T(8,128)S(1)} %reshape.93), channel_id=1, source_target_pairs={{1,0},{2,1},{3,2},{4,3},{5,4},{6,5},{7,6},{8,7},{9,8},{10,9},{11,1... | collective-permute-start | bytes 33776 | tf_op jit(solution)/shard_map/ppermute | solution.py:63
  63.1 6.7 %collective-permute-start.5 = (f32[21,134]{1,0:T(8,128)S(1)}, f32[21,134]{1,0:T(8,128)S(1)}, u32[]{:S(2)}, u32[]{:S(2)}) collective-permute-start(f32[21,134]{1,0:T(8,128)S(1)} %reshape.91), channel_id=1, source_target_pairs={{0,1},{1,2},{2,3},{3,4},{4,5},{5,6},{6,7},{7,8},{8,9},{9,10},{10,1... | collective-permute-start | bytes 33776 | tf_op jit(solution)/shard_map/ppermute | solution.py:62
  72.0 8.3 %copy-start.4 = (f32[4,6]{1,0:T(4,128)S(1)}, f32[4,6]{1,0:T(4,128)}, u32[]{:S(2)}) copy-start(f32[4,6]{1,0:T(4,128)} %param.25) | copy-start | bytes 292
  82.1 21.3 %copy-start.1 = (f32[1,1,32,2,2,256]{5,4,3,2,1,0:T(2,128)S(1)}, f32[1,1,32,2,2,256]{5,4,3,2,1,0:T(2,128)}, u32[]{:S(2)}) copy-start(f32[1,1,32,2,2,256]{5,4,3,2,1,0:T(2,128)} %param.29) | copy-start | bytes 393220
  83.3 20.0 %all-to-all-start.2 = ((f32[32,8,128]{2,1,0:T(8,128)}), f32[32,8,128]{2,1,0:T(8,128)S(1)}, u32[]{:S(2)}, u32[]{:S(2)}) async-start(f32[32,8,128]{2,1,0:T(8,128)} %select_n.115), calls=%async_computation.2 | async-start | bytes 262144 | tf_op jit(solution)/shard_map/all_to_all | solution.py:195

commit v10 on v8

--- a/solution.py
+++ b/solution.py
@@ -64,19 +64,17 @@
     return jnp.concatenate([low, block, high], axis=2)
 
 
-def sweeps_kernel(
-    rows_ref, coupling_ref, loading_ref, side_ref, stiff_ref,
-    out_ref, picked_ref, load_scr, stiff_scr, motion_ref, next_ref,
-):
+def sweeps_kernel(rows_ref, coupling_ref, loading_ref, stiff_ref, side_ref, out_ref, picked_ref, load_scr, motion_ref, next_ref):
     fields = out_ref.shape[0]
-    cells = loading_ref.shape[2]
+    ext_rows, cells = loading_ref.shape[1], loading_ref.shape[2]
     rows, cols = load_scr.shape[1], load_scr.shape[2]
-    stiff_scr[:, :cells] = stiff_ref[...]
-    stiff_scr[:, cells:] = side_ref[fields]
+    width = SWEEPS - 1
+    load_scr[:, ext_rows:, :] = jnp.zeros((fields + 1, rows - ext_rows, cols), jnp.float32)
     for a in range(fields):
-        load_scr[a, :, :cells] = loading_ref[a]
-        load_scr[a, :, cells:] = side_ref[a]
-    stiffness = stiff_scr[...]
+        load_scr[a, :ext_rows, :cells] = loading_ref[a]
+    load_scr[fields, :ext_rows, :cells] = stiff_ref[...]
+    load_scr[:, :ext_rows, cells:] = side_ref[...]
+    stiffness = load_scr[fields]
     for a in range(fields):
         diagonal = 4.0 * stiffness + coupling_ref[a, a]
         motion_ref[a] = chebyshev_weight(0) * (load_scr[a] / diagonal)
@@ -99,15 +97,16 @@
         source, target = target, source
     out_rows = out_ref.shape[1]
     for a in range(fields):
-        out_ref[a] = source[a, :out_rows, :cells]
+        out_ref[a] = pltpu.roll(source[a], rows - width, 0)[:out_rows, :cells]
     for slot in range(picked_ref.shape[1]):
-        row = rows_ref[slot]
+        row = rows_ref[slot] + width
         for a in range(fields):
             picked_ref[a, pl.ds(slot, 1), :] = source[a, pl.ds(row, 1), pl.ds(0, cells)]
 
 
-def run_sweeps(slot_row, coupling, loading, side, stiffness, out_rows):
-    fields, rows, cells = loading.shape
+def run_sweeps(slot_row, coupling, loading, stiffness, side, out_rows):
+    fields, ext_rows, cells = loading.shape
+    rows = -(-ext_rows // 8) * 8
     cols = cells + side.shape[2]
     smem = pl.BlockSpec(memory_space=pltpu.SMEM)
     vmem = pl.BlockSpec(memory_space=pltpu.VMEM)
@@ -120,27 +119,14 @@
         in_specs=[smem, smem, vmem, vmem, vmem],
         out_specs=(vmem, vmem),
         scratch_shapes=[
-            pltpu.VMEM((fields, rows, cols), jnp.float32),
-            pltpu.VMEM((rows, cols), jnp.float32),
+            pltpu.VMEM((fields + 1, rows, cols), jnp.float32),
             pltpu.VMEM((fields, rows, cols), jnp.float32),
             pltpu.VMEM((fields, rows, cols), jnp.float32),
         ],
-    )(slot_row, coupling, loading, side, stiffness)
-
-
-def cyclic_rows(block, axis, dim, width, rows):
-    count = lax.axis_size(axis)
-    forward = [(i, i + 1) for i in range(count - 1)]
-    backward = [(target, source) for source, target in forward]
-    size = block.shape[dim]
-    before = lax.ppermute(lax.slice_in_dim(block, size - width, None, axis=dim), axis, forward)
-    after = lax.ppermute(lax.slice_in_dim(block, 0, width, axis=dim), axis, backward)
-    gap_shape = list(block.shape)
-    gap_shape[dim] = rows - size - 2 * width
-    return jnp.concatenate([block, after, jnp.zeros(gap_shape, block.dtype), before], axis=dim)
-
-
-def cyclic_side(blocks, axis, width, lanes):
+    )(slot_row, coupling, loading, stiffness, side)
+
+
+def girth_side(blocks, axis, width, lanes):
     count = lax.axis_size(axis)
     forward = [(i, i + 1) for i in range(count - 1)]
     backward = [(target, source) for source, target in forward]
@@ -203,9 +189,12 @@
     stiffness = jnp.zeros((row_count, girth_cells), jnp.float32)
     for level in range(class_stiffness.shape[0]):
         stiffness = stiffness + jnp.where(thickness_class == level, class_stiffness[level], 0.0)
-    ring_rows = -(-(row_count + 2 * width) // 8) * 8
-    amplitude_ext = cyclic_rows(wave_amplitude, "length", 1, width, ring_rows)
-    stiffness_ext = cyclic_rows(stiffness, "length", 0, width, ring_rows)
+    amplitude_ext = padded_2(wave_amplitude, (("length", 1),), width)
+    stiffness_rows = padded_2(stiffness, (("length", 0),), width)
+    factors = spread(load_bank, "girth", root, "length")
+    ext_rows = row_count + 2 * width
+    loading = jnp.dot(amplitude_ext.reshape(6 * ext_rows, mode_count), factors, preferred_element_type=jnp.float32)
+    loading = loading.reshape(6, ext_rows, girth_cells)
     girth_count = lax.axis_size("girth")
     tile_ids = hotspot_tile[0]
     owner_ids = hotspot_owner[0, :, 0]
@@ -220,11 +209,8 @@
     filled = jnp.any(hit, axis=1)
     slot_row = jnp.sum(jnp.where(hit, tile_ids[None, :], 0), axis=1)
     stiffness_at = jnp.take(stiffness, slot_row, axis=0)
-    factors = spread(load_bank, "girth", root, "length")
-    loading = jnp.dot(amplitude_ext.reshape(6 * ring_rows, mode_count), factors, preferred_element_type=jnp.float32)
-    loading = loading.reshape(6, ring_rows, girth_cells)
-    side = cyclic_side([loading, stiffness_ext[None]], "girth", width, 128)
-    motion, motion_at = run_sweeps(slot_row, coupling, loading, side, stiffness_ext, row_count)
+    side = girth_side([loading, stiffness_rows[None]], "girth", width, 128)
+    motion, motion_at = run_sweeps(slot_row, coupling, loading, stiffness_rows, side, row_count)
     stress_rows = stiffness_at[:, None, :] * jnp.einsum(
         "ka,aij->ikj", stress_map, motion_at, precision=lax.Precision.HIGHEST
     )

time: 110 us -> 102 us (0.927)
  starting transfers between devices: 47.6 us -> 43.7 us
  waiting for transfers between devices: 28.6 us -> 25.6 us
    all_to_all x1, waiting for transfers between devices: 14.4 us -> 8.21 us  [scatter_gather(): full = lax.all_to_all(send, axis, 0, 0, tiled=True)]
    all_to_all x1, waiting for transfers between devices: 0.01 us -> 2.92 us  [scatter_gather(): got = lax.all_to_all(send, axis, 0, 0, tiled=True)]
    all_to_all x1, starting transfers between devices: 9.78 us -> 6.88 us  [scatter_gather(): full = lax.all_to_all(send, axis, 0, 0, tiled=True)]
    ppermute x1, starting transfers between devices: 5.1 us -> 3.95 us  [spread(): other = lax.ppermute(got, pair_axis, pairs)]
  transfers between devices with their start and end apart: 10 -> 10, of which waited for: 4 -> 5; matrix products, arithmetic and copies ran while one was open for 12% -> 12% of each run, Pallas kernels for 0% -> 0%
where the time goes in v10:
time: 102 us
  starting transfers between devices  43.7 us (43%)
  waiting for transfers between devices  25.6 us (25%)
  other arithmetic  9.21 us (9%)
  local copies, waits for them, and re-layouts  9.13 us (9%)
  Pallas kernels  7 us (7%)
  matrix products  4.79 us (5%)
  between operations  2.32 us (2%)
    all_to_all x1, starting transfers between devices, scatter_gather(): got = lax.all_to_all(send, axis, 0, 0, tiled=True)  9.95 us
    all_to_all x1, waiting for transfers between devices, on_device(): lax.all_to_all(outbox, 'girth', split_axis=0, concat_axis=0, tiled=True)  9.71 us
    all_to_all x1, waiting for transfers between devices, scatter_gather(): full = lax.all_to_all(send, axis, 0, 0, tiled=True)  8.21 us
    pallas_call x1, Pallas kernels, run_sweeps(): pl.pallas_call(sweeps_kernel, out_shape=(jax.ShapeDtypeStruct((fields, ou...  7 us
    all_to_all x1, starting transfers between devices, scatter_gather(): full = lax.all_to_all(send, axis, 0, 0, tiled=True)  6.88 us
    add x1, other arithmetic, on_device(): stiffness + jnp.where(thickness_class == level, class_stiffness[level], 0.0)  6.08 us
    all_to_all x1, starting transfers between devices, on_device(): lax.all_to_all(outbox, 'girth', split_axis=0, concat_axis=0, tiled=True)  5.79 us
    ppermute x2, starting transfers between devices, padded_2(): lax.ppermute(lax.slice_in_dim(block, 0, width, axis=dim), axis, backward)  5.61 us
  transfers between devices with their start and end apart: 10, of which 5 were waited for; matrix products, arithmetic and copies ran while one was open for 12% of the time, Pallas kernels for 0%

profile of v10, /device:TPU:192, one launch (start us, length us, event | category | flops | bytes accessed | tf_op | source)
XLA Modules:
  0.0 101.7 jit_solution(3514197848156056245)
XLA Ops:
  0.6 0.0 copy-start
  0.6 0.0 copy-start.5
  0.7 0.0 copy-start.6
  0.7 1.2 %copy-done = bf16[2048,256]{1,0:T(8,128)(2,1)S(1)} copy-done((bf16[2048,256]{1,0:T(8,128)(2,1)S(1)}, bf16[2048,256]{1,0:T(8,128)(2,1)}, u32[]{:S(2)}) %copy-start) | copy-done | bytes 1048600
  1.9 0.8 constant_dynamic-slice_fusion
  2.7 10.0 %all-to-all-start = ((bf16[32,32,256]{2,1,0:T(8,128)(2,1)}), bf16[32,32,256]{2,1,0:T(8,128)(2,1)S(1)}, u32[]{:S(2)}, u32[]{:S(2)}) async-start(bf16[32,32,256]{2,1,0:T(8,128)(2,1)} %bitcast.2), calls=%async_computation | async-start | bytes 1048576 | tf_op jit(solution)/shard_map/all_to_all | solution.py:18
  12.6 1.6 %fusion.28 = (f32[1]{0:T(128)}, f32[1]{0:T(128)}, f32[1]{0:T(128)}, f32[1]{0:T(128)}, f32[1]{0:T(128)}, /*index=5*/f32[1]{0:T(128)}, f32[1]{0:T(128)}, f32[1]{0:T(128)}) fusion(f32[8]{0:T(128)} %param.23), kind=kLoop, calls=%fused_computation.56 | loop fusion | bytes 64 | tf_op jit(solution)/shard_map/slice | solution.py:191
  14.3 6.1 %select_add_fusion = f32[128,256]{1,0:T(8,128)S(1)} fusion(s32[128,256]{1,0:T(8,128)} %param.22, f32[]{:T(128)} %bitcast.14, f32[]{:T(128)} %bitcast.13, f32[]{:T(128)} %bitcast.12, f32[]{:T(128)} %bitcast.11, f32[]{:T(128)} %bitcast.10, f32[]{:T(128)} %bitcast.9, f32[]{:T(128)} %bitcast.8, f32[]{:T(128)} %bitcast.7), kind=kLoop, calls=%fused_computation.18 | loop fusion | flops 753664 | bytes 262176 | tf_op jit(solution)/shard_map/add | solution.py:191
  20.4 1.9 %collective-permute-start.3 = (f32[3,256]{1,0:T(4,128)S(1)}, f32[3,256]{1,0:T(4,128)S(1)}, u32[]{:S(2)}, u32[]{:S(2)}) collective-permute-start(f32[3,256]{1,0:T(4,128)S(1)} %get-tuple-element.68), channel_id=1, source_target_pairs={{0,32},{32,64},{64,96},{96,128},{128,160},{160,192},{192,224},{224... | collective-permute-start | bytes 9224 | tf_op jit(solution)/shard_map/ppermute | solution.py:42
  22.3 3.6 %collective-permute-start.4 = (f32[3,256]{1,0:T(4,128)S(1)}, f32[3,256]{1,0:T(4,128)S(1)}, u32[]{:S(2)}, u32[]{:S(2)}) collective-permute-start(f32[3,256]{1,0:T(4,128)S(1)} %get-tuple-element.69), channel_id=1, source_target_pairs={{32,0},{64,32},{96,64},{128,96},{160,128},{192,160},{224,192},{256... | collective-permute-start | bytes 9224 | tf_op jit(solution)/shard_map/ppermute | solution.py:45
  26.6 2.9 %all-to-all-done = bf16[32,32,256]{2,1,0:T(8,128)(2,1)S(1)} async-done(((bf16[32,32,256]{2,1,0:T(8,128)(2,1)}), bf16[32,32,256]{2,1,0:T(8,128)(2,1)S(1)}, u32[]{:S(2)}, u32[]{:S(2)}) %all-to-all-start) | async-done | bytes 524320 | tf_op jit(solution)/shard_map/all_to_all | solution.py:18
  29.5 0.9 broadcast_in_dim.109
  30.4 6.9 %all-to-all-start.1 = ((bf16[32,32,256]{2,1,0:T(8,128)(2,1)}), bf16[32,32,256]{2,1,0:T(8,128)(2,1)S(1)}, u32[]{:S(2)}, u32[]{:S(2)}) async-start(bf16[32,32,256]{2,1,0:T(8,128)(2,1)} %broadcast_in_dim.109), calls=%async_computation.1 | async-start | bytes 1048576 | tf_op jit(solution)/shard_map/all_to_all | solution.py:21
  37.3 1.1 %fusion.23 = (bf16[6,3,2048]{2,1,0:T(4,128)(2,1)S(1)}, bf16[6,3,2048]{2,1,0:T(4,128)(2,1)S(1)}) fusion(bf16[6,128,2048]{2,1,0:T(8,128)(2,1)} %param.19), kind=kLoop, calls=%fused_computation.51 | loop fusion | bytes 294912 | tf_op jit(solution)/shard_map/slice | solution.py:43
  38.4 3.6 %collective-permute-start = (bf16[6,3,2048]{2,1,0:T(4,128)(2,1)S(1)}, bf16[6,3,2048]{2,1,0:T(4,128)(2,1)S(1)}, u32[]{:S(2)}, u32[]{:S(2)}) collective-permute-start(bf16[6,3,2048]{2,1,0:T(4,128)(2,1)S(1)} %get-tuple-element.54), channel_id=1, source_target_pairs={{0,32},{32,64},{64,96},{96,128},{128,160},{160,192},{192,224},{224... | collective-permute-start | bytes 221192 | tf_op jit(solution)/shard_map/ppermute | solution.py:42
  42.0 2.0 %collective-permute-start.1 = (bf16[6,3,2048]{2,1,0:T(4,128)(2,1)S(1)}, bf16[6,3,2048]{2,1,0:T(4,128)(2,1)S(1)}, u32[]{:S(2)}, u32[]{:S(2)}) collective-permute-start(bf16[6,3,2048]{2,1,0:T(4,128)(2,1)S(1)} %get-tuple-element.55), channel_id=1, source_target_pairs={{32,0},{64,32},{96,64},{128,96},{160,128},{192,160},{224,192},{256... | collective-permute-start | bytes 221192 | tf_op jit(solution)/shard_map/ppermute | solution.py:45
  44.0 0.0 copy-done.5
  44.0 0.2 convert_reduce_fusion
  44.2 0.0 copy-done.6
  44.2 0.1 select_reduce_fusion.rows_ref
  44.3 0.7 gather_fusion
  45.0 8.2 %all-to-all-done.1 = bf16[32,32,256]{2,1,0:T(8,128)(2,1)S(1)} async-done(((bf16[32,32,256]{2,1,0:T(8,128)(2,1)}), bf16[32,32,256]{2,1,0:T(8,128)(2,1)S(1)}, u32[]{:S(2)}, u32[]{:S(2)}) %all-to-all-start.1) | async-done | bytes 524320 | tf_op jit(solution)/shard_map/all_to_all | solution.py:21
  53.2 4.0 %collective-permute-start.2 = (bf16[1024,256]{1,0:T(8,128)(2,1)S(1)}, bf16[1024,256]{1,0:T(8,128)(2,1)S(1)}, u32[]{:S(2)}, u32[]{:S(2)}) collective-permute-start(bf16[1024,256]{1,0:T(8,128)(2,1)S(1)} %bitcast.73), channel_id=1, source_target_pairs={{0,32},{32,0},{64,96},{96,64},{128,160},{160,128},{192,224},{224,1... | collective-permute-start | bytes 1572872 | tf_op jit(solution)/shard_map/ppermute | solution.py:31
  57.1 0.1 broadcast_select_fusion.2
  57.2 0.0 collective-permute-done.3
  57.2 0.0 collective-permute-done.4
  57.2 0.7 fusion.22
  57.9 0.1 fusion.26
  58.0 0.1 copy.40
  58.1 0.1 copy.44
  58.2 0.5 collective-permute-done.2
  58.7 0.1 broadcast_select_fusion.1
  58.8 0.0 collective-permute-done
  58.8 0.0 collective-permute-done.1
  58.8 3.0 %fusion.loading_ref = f32[6,134,256]{2,1,0:T(8,128)S(1)} fusion(bf16[6,3,2048]{2,1,0:T(4,128)(2,1)S(1)} %collective-permute-done.1, bf16[6,128,2048]{2,1,0:T(8,128)(2,1)} %param.19, bf16[6,3,2048]{2,1,0:T(4,128)(2,1)S(1)} %collective-permute-done, bf16[1024,256]{1,0:T(8,128)(2,1)S(1)} %get-tuple-element.57, bf16[1024,256]{1,0:T(8,128)(2,1)S(1)} %get-tuple-element.56), kind=kOutput, calls=%fused_computation.1 | convolution fusion | flops 855031808 | bytes 5165056 | tf_op jit(solution)/shard_map/dot_general | solution.py:196
  61.8 0.0 copy-done.4
  61.8 0.0 copy-start.1
  61.8 0.0 copy-start.3
  61.8 0.2 fusion.24
  62.0 0.3 copy.39
  62.4 0.3 copy.43
  62.8 4.7 %collective-permute-start.6 = (f32[21,134]{1,0:T(8,128)S(1)}, f32[21,134]{1,0:T(8,128)S(1)}, u32[]{:S(2)}, u32[]{:S(2)}) collective-permute-start(f32[21,134]{1,0:T(8,128)S(1)} %reshape.93), channel_id=1, source_target_pairs={{0,1},{1,2},{2,3},{3,4},{4,5},{5,6},{6,7},{7,8},{8,9},{9,10},{10,1... | collective-permute-start | bytes 33776 | tf_op jit(solution)/shard_map/ppermute | solution.py:144
  67.5 1.3 %collective-permute-start.5 = (f32[21,134]{1,0:T(8,128)S(1)}, f32[21,134]{1,0:T(8,128)S(1)}, u32[]{:S(2)}, u32[]{:S(2)}) collective-permute-start(f32[21,134]{1,0:T(8,128)S(1)} %reshape.91), channel_id=1, source_target_pairs={{1,0},{2,1},{3,2},{4,3},{5,4},{6,5},{7,6},{8,7},{9,8},{10,9},{11,1... | collective-permute-start | bytes 33776 | tf_op jit(solution)/shard_map/ppermute | solution.py:145
  68.8 0.1 fusion.17
  68.9 0.1 pad.11.clone
  69.0 4.2 %collective-permute-done.5 = f32[21,134]{1,0:T(8,128)S(1)} collective-permute-done((f32[21,134]{1,0:T(8,128)S(1)}, f32[21,134]{1,0:T(8,128)S(1)}, u32[]{:S(2)}, u32[]{:S(2)}) %collective-permute-start.5) | collective-permute-done | bytes 11288 | tf_op jit(solution)/shard_map/ppermute | solution.py:145
  73.2 0.2 copy.42
  73.5 0.0 collective-permute-done.6
  73.5 0.2 copy.46
  73.7 0.0 copy-start.2
  73.7 1.0 pad_maximum_fusion.side_ref
  74.7 0.0 copy-done.1
  74.7 7.0 %shard_map.122 = (f32[6,128,256]{2,1,0:T(8,128)}, f32[6,64,256]{2,1,0:T(8,128)}) custom-call(s32[64]{0:T(128)} %copy-done.4, f32[6,6]{1,0:T(8,128)} %coupling_ref.1, f32[6,134,256]{2,1,0:T(8,128)} %copy-done.1, f32[134,256]{1,0:T(8,128)} %get-tuple-element.67.stiff_ref, f32[7,134,128]{2,1,0:T(8,128)} %pad_maximum_fusion.side_ref), custom_call_target="tpu_custom_call" | custom-call | tf_op jit(solution)/shard_map/pallas_call | solution.py:113
  81.7 0.0 copy-done.3
  81.7 1.8 %fusion.6 = f32[64,4,256]{2,1,0:T(4,128)S(1)} fusion(f32[6,64,256]{2,1,0:T(8,128)} %get-tuple-element.9, f32[64,256]{1,0:T(8,128)S(1)} %broadcast_select_fusion.2, f32[4,6]{1,0:T(4,128)S(1)} %copy-done.3), kind=kOutput, calls=%fused_computation.8 | convolution fusion | flops 4784128 | bytes 720992 | tf_op jit(solution)/shard_map/ka,aij->ikj/dot_general | solution.py:214
  83.5 0.2 fusion.25
  83.7 0.1 maximum_select_fusion
  83.8 0.1 copy.51
  83.9 0.8 select_n.115
  84.7 5.8 %all-to-all-start.2 = ((f32[32,8,128]{2,1,0:T(8,128)}), f32[32,8,128]{2,1,0:T(8,128)S(1)}, u32[]{:S(2)}, u32[]{:S(2)}) async-start(f32[32,8,128]{2,1,0:T(8,128)} %select_n.115), calls=%async_computation.2 | async-start | bytes 262144 | tf_op jit(solution)/shard_map/all_to_all | solution.py:220
  91.1 9.7 %all-to-all-done.2 = f32[32,8,128]{2,1,0:T(8,128)S(1)} async-done(((f32[32,8,128]{2,1,0:T(8,128)}), f32[32,8,128]{2,1,0:T(8,128)S(1)}, u32[]{:S(2)}, u32[]{:S(2)}) %all-to-all-start.2) | async-done | bytes 131104 | tf_op jit(solution)/shard_map/all_to_all | solution.py:220
  100.9 0.1 mul.64
  101.0 0.0 copy-done.2
  101.0 0.7 add.90
  (18 shorter events, 0.2 us)
Async XLA Ops:
  0.6 1.2 %copy-start = (bf16[2048,256]{1,0:T(8,128)(2,1)S(1)}, bf16[2048,256]{1,0:T(8,128)(2,1)}, u32[]{:S(2)}) copy-start(bf16[2048,256]{1,0:T(8,128)(2,1)} %param.20) | copy-start | bytes 3145732
  0.6 43.3 %copy-start.5 = (s32[1,32,1]{1,2,0:T(1,128)S(1)}, s32[1,32,1]{1,2,0:T(1,128)}, u32[]{:S(2)}) copy-start(s32[1,32,1]{1,2,0:T(1,128)} %param.28) | copy-start | bytes 388
  0.7 43.5 %copy-start.6 = (s32[1,32]{1,0:T(1,128)S(1)}, s32[1,32]{1,0:T(1,128)}, u32[]{:S(2)}) copy-start(s32[1,32]{1,0:T(1,128)} %param.27) | copy-start | bytes 388
  2.7 26.8 %all-to-all-start = ((bf16[32,32,256]{2,1,0:T(8,128)(2,1)}), bf16[32,32,256]{2,1,0:T(8,128)(2,1)S(1)}, u32[]{:S(2)}, u32[]{:S(2)}) async-start(bf16[32,32,256]{2,1,0:T(8,128)(2,1)} %bitcast.2), calls=%async_computation | async-start | bytes 1048576 | tf_op jit(solution)/shard_map/all_to_all | solution.py:18
  20.4 36.9 %collective-permute-start.3 = (f32[3,256]{1,0:T(4,128)S(1)}, f32[3,256]{1,0:T(4,128)S(1)}, u32[]{:S(2)}, u32[]{:S(2)}) collective-permute-start(f32[3,256]{1,0:T(4,128)S(1)} %get-tuple-element.68), channel_id=1, source_target_pairs={{0,32},{32,64},{64,96},{96,128},{128,160},{160,192},{192,224},{224... | collective-permute-start | bytes 9224 | tf_op jit(solution)/shard_map/ppermute | solution.py:42
  22.3 34.9 %collective-permute-start.4 = (f32[3,256]{1,0:T(4,128)S(1)}, f32[3,256]{1,0:T(4,128)S(1)}, u32[]{:S(2)}, u32[]{:S(2)}) collective-permute-start(f32[3,256]{1,0:T(4,128)S(1)} %get-tuple-element.69), channel_id=1, source_target_pairs={{32,0},{64,32},{96,64},{128,96},{160,128},{192,160},{224,192},{256... | collective-permute-start | bytes 9224 | tf_op jit(solution)/shard_map/ppermute | solution.py:45
  30.4 22.8 %all-to-all-start.1 = ((bf16[32,32,256]{2,1,0:T(8,128)(2,1)}), bf16[32,32,256]{2,1,0:T(8,128)(2,1)S(1)}, u32[]{:S(2)}, u32[]{:S(2)}) async-start(bf16[32,32,256]{2,1,0:T(8,128)(2,1)} %broadcast_in_dim.109), calls=%async_computation.1 | async-start | bytes 1048576 | tf_op jit(solution)/shard_map/all_to_all | solution.py:21
  38.4 20.4 %collective-permute-start = (bf16[6,3,2048]{2,1,0:T(4,128)(2,1)S(1)}, bf16[6,3,2048]{2,1,0:T(4,128)(2,1)S(1)}, u32[]{:S(2)}, u32[]{:S(2)}) collective-permute-start(bf16[6,3,2048]{2,1,0:T(4,128)(2,1)S(1)} %get-tuple-element.54), channel_id=1, source_target_pairs={{0,32},{32,64},{64,96},{96,128},{128,160},{160,192},{192,224},{224... | collective-permute-start | bytes 221192 | tf_op jit(solution)/shard_map/ppermute | solution.py:42
  42.0 16.8 %collective-permute-start.1 = (bf16[6,3,2048]{2,1,0:T(4,128)(2,1)S(1)}, bf16[6,3,2048]{2,1,0:T(4,128)(2,1)S(1)}, u32[]{:S(2)}, u32[]{:S(2)}) collective-permute-start(bf16[6,3,2048]{2,1,0:T(4,128)(2,1)S(1)} %get-tuple-element.55), channel_id=1, source_target_pairs={{32,0},{64,32},{96,64},{128,96},{160,128},{192,160},{224,192},{256... | collective-permute-start | bytes 221192 | tf_op jit(solution)/shard_map/ppermute | solution.py:45
  44.3 17.5 %copy-start.4 = (s32[64]{0:T(128)}, s32[64]{0:T(128)S(1)}, u32[]{:S(2)}) copy-start(s32[64]{0:T(128)S(1)} %select_reduce_fusion.rows_ref) | copy-start | bytes 772
  53.2 5.5 %collective-permute-start.2 = (bf16[1024,256]{1,0:T(8,128)(2,1)S(1)}, bf16[1024,256]{1,0:T(8,128)(2,1)S(1)}, u32[]{:S(2)}, u32[]{:S(2)}) collective-permute-start(bf16[1024,256]{1,0:T(8,128)(2,1)S(1)} %bitcast.73), channel_id=1, source_target_pairs={{0,32},{32,0},{64,96},{96,64},{128,160},{160,128},{192,224},{224,1... | collective-permute-start | bytes 1572872 | tf_op jit(solution)/shard_map/ppermute | solution.py:31
  61.8 12.9 %copy-start.1 = (f32[6,134,256]{2,1,0:T(8,128)}, f32[6,134,256]{2,1,0:T(8,128)S(1)}, u32[]{:S(2)}) copy-start(f32[6,134,256]{2,1,0:T(8,128)S(1)} %fusion.loading_ref) | copy-start | bytes 2469892
  61.8 19.9 %copy-start.3 = (f32[4,6]{1,0:T(4,128)S(1)}, f32[4,6]{1,0:T(4,128)}, u32[]{:S(2)}) copy-start(f32[4,6]{1,0:T(4,128)} %param.25) | copy-start | bytes 292
  62.8 10.6 %collective-permute-start.6 = (f32[21,134]{1,0:T(8,128)S(1)}, f32[21,134]{1,0:T(8,128)S(1)}, u32[]{:S(2)}, u32[]{:S(2)}) collective-permute-start(f32[21,134]{1,0:T(8,128)S(1)} %reshape.93), channel_id=1, source_target_pairs={{0,1},{1,2},{2,3},{3,4},{4,5},{5,6},{6,7},{7,8},{8,9},{9,10},{10,1... | collective-permute-start | bytes 33776 | tf_op jit(solution)/shard_map/ppermute | solution.py:144
  67.5 5.7 %collective-permute-start.5 = (f32[21,134]{1,0:T(8,128)S(1)}, f32[21,134]{1,0:T(8,128)S(1)}, u32[]{:S(2)}, u32[]{:S(2)}) collective-permute-start(f32[21,134]{1,0:T(8,128)S(1)} %reshape.91), channel_id=1, source_target_pairs={{1,0},{2,1},{3,2},{4,3},{5,4},{6,5},{7,6},{8,7},{9,8},{10,9},{11,1... | collective-permute-start | bytes 33776 | tf_op jit(solution)/shard_map/ppermute | solution.py:145
  73.7 27.2 %copy-start.2 = (f32[1,1,32,2,2,256]{5,4,3,2,1,0:T(2,128)S(1)}, f32[1,1,32,2,2,256]{5,4,3,2,1,0:T(2,128)}, u32[]{:S(2)}) copy-start(f32[1,1,32,2,2,256]{5,4,3,2,1,0:T(2,128)} %param.29) | copy-start | bytes 393220
  84.7 16.2 %all-to-all-start.2 = ((f32[32,8,128]{2,1,0:T(8,128)}), f32[32,8,128]{2,1,0:T(8,128)S(1)}, u32[]{:S(2)}, u32[]{:S(2)}) async-start(f32[32,8,128]{2,1,0:T(8,128)} %select_n.115), calls=%async_computation.2 | async-start | bytes 262144 | tf_op jit(solution)/shard_map/all_to_all | solution.py:220

commit v11 on v10

--- a/solution.py
+++ b/solution.py
@@ -22,16 +22,18 @@
     return full.reshape(rows, block.shape[1])
 
 
-def spread(block, axis, source, pair_axis):
+def spread_product(amplitude, block, axis, source, pair_axis):
     core = lax.axis_index(pair_axis) % 2
     half = block.shape[0] // 2
     mine = lax.dynamic_slice_in_dim(block, core * half, half, 0)
     got = scatter_gather(mine, axis, source)
     pairs = [(i, i ^ 1) for i in range(lax.axis_size(pair_axis))]
     other = lax.ppermute(got, pair_axis, pairs)
-    low = jnp.where(core == 0, got, other)
-    high = jnp.where(core == 0, other, got)
-    return jnp.concatenate([low, high], axis=0)
+    low, high = amplitude[:, :half], amplitude[:, half:]
+    own_part = jnp.dot(jnp.where(core == 0, low, high), got, preferred_element_type=jnp.float32)
+    own_part, other = lax.optimization_barrier((own_part, other))
+    other_part = jnp.dot(jnp.where(core == 0, high, low), other, preferred_element_type=jnp.float32)
+    return own_part + other_part
 
 
 def padded_2(block, sides, width):
@@ -191,9 +193,8 @@
         stiffness = stiffness + jnp.where(thickness_class == level, class_stiffness[level], 0.0)
     amplitude_ext = padded_2(wave_amplitude, (("length", 1),), width)
     stiffness_rows = padded_2(stiffness, (("length", 0),), width)
-    factors = spread(load_bank, "girth", root, "length")
     ext_rows = row_count + 2 * width
-    loading = jnp.dot(amplitude_ext.reshape(6 * ext_rows, mode_count), factors, preferred_element_type=jnp.float32)
+    loading = spread_product(amplitude_ext.reshape(6 * ext_rows, mode_count), load_bank, "girth", root, "length")
     loading = loading.reshape(6, ext_rows, girth_cells)
     girth_count = lax.axis_size("girth")
     tile_ids = hotspot_tile[0]

time: 102 us -> 120 us (1.18)
  starting transfers between devices: 43.7 us -> 51.6 us
  other arithmetic: 9.21 us -> 16 us
  local copies, waits for them, and re-layouts: 9.13 us -> 13.4 us
  waiting for transfers between devices: 25.6 us -> 24.2 us
    all_to_all x1, waiting for transfers between devices: 8.21 us -> 13.5 us  [scatter_gather(): full = lax.all_to_all(send, axis, 0, 0, tiled=True)]
    concatenate x0 -> x1, other arithmetic: none -> 4.75 us  [padded_2(): block = jnp.concatenate([low, block, high], axis=dim)]
    ppermute x1, waiting for transfers between devices: 4.25 us -> 0.01 us  [girth_side(): after = unpack(lax.ppermute(pack(0), axis, backward))]
    reshape x0 -> x2, local copies, waits for them, and re-layouts: none -> 4.04 us  [the longest x1 3.95 us: on_device(): amplitude_ext.reshape(6 * ext_rows, mode_count)]
    all_to_all x1, starting transfers between devices: 5.79 us -> 9.23 us  [on_device(): lax.all_to_all(outbox, 'girth', split_axis=0, concat_axis=0, tiled=True)]
    all_to_all x1, waiting for transfers between devices: 2.92 us -> 0.01 us  [scatter_gather(): got = lax.all_to_all(send, axis, 0, 0, tiled=True)]
    all_to_all x1, starting transfers between devices: 6.88 us -> 9.78 us  [scatter_gather(): full = lax.all_to_all(send, axis, 0, 0, tiled=True)]
    dot_general x1 -> x2, matrix products: 3.01 us -> 3.28 us  [the longest x1 2.68 us: spread_product(): jnp.dot(jnp.where(core == 0, low, high), got, preferred_element_type=jnp....]
  transfers between devices with their start and end apart: 10 -> 10, of which waited for: 5 -> 3; matrix products, arithmetic and copies ran while one was open for 12% -> 22% of each run, Pallas kernels for 0% -> 0%
where the time goes in v11:
time: 120 us
  starting transfers between devices  51.6 us (43%)
  waiting for transfers between devices  24.2 us (20%)
  other arithmetic  16 us (13%)
  local copies, waits for them, and re-layouts  13.4 us (11%)
  Pallas kernels  6.98 us (6%)
  matrix products  5.08 us (4%)
  between operations  2.3 us (2%)
    all_to_all x1, waiting for transfers between devices, scatter_gather(): full = lax.all_to_all(send, axis, 0, 0, tiled=True)  13.5 us
    all_to_all x1, starting transfers between devices, scatter_gather(): got = lax.all_to_all(send, axis, 0, 0, tiled=True)  9.95 us
    all_to_all x1, starting transfers between devices, scatter_gather(): full = lax.all_to_all(send, axis, 0, 0, tiled=True)  9.78 us
    all_to_all x1, waiting for transfers between devices, on_device(): lax.all_to_all(outbox, 'girth', split_axis=0, concat_axis=0, tiled=True)  9.71 us
    all_to_all x1, starting transfers between devices, on_device(): lax.all_to_all(outbox, 'girth', split_axis=0, concat_axis=0, tiled=True)  9.23 us
    pallas_call x1, Pallas kernels, run_sweeps(): pl.pallas_call(sweeps_kernel, out_shape=(jax.ShapeDtypeStruct((fields, ou...  6.98 us
    add x1, other arithmetic, on_device(): stiffness + jnp.where(thickness_class == level, class_stiffness[level], 0.0)  6.08 us
    ppermute x2, starting transfers between devices, padded_2(): lax.ppermute(lax.slice_in_dim(block, block.shape[dim] - width, None, axis...  5.79 us
  transfers between devices with their start and end apart: 10, of which 3 were waited for; matrix products, arithmetic and copies ran while one was open for 22% of the time, Pallas kernels for 0%

profile of v11, /device:TPU:192, one launch (start us, length us, event | category | flops | bytes accessed | tf_op | source)
XLA Modules:
  0.0 119.6 jit_solution(3890876822582585721)
XLA Ops:
  0.6 0.0 copy-start
  0.7 1.2 %copy-done = bf16[2048,256]{1,0:T(8,128)(2,1)S(1)} copy-done((bf16[2048,256]{1,0:T(8,128)(2,1)S(1)}, bf16[2048,256]{1,0:T(8,128)(2,1)}, u32[]{:S(2)}) %copy-start) | copy-done | bytes 1048600
  1.9 0.8 constant_dynamic-slice_fusion
  2.7 9.9 %all-to-all-start = ((bf16[32,32,256]{2,1,0:T(8,128)(2,1)}), bf16[32,32,256]{2,1,0:T(8,128)(2,1)S(1)}, u32[]{:S(2)}, u32[]{:S(2)}) async-start(bf16[32,32,256]{2,1,0:T(8,128)(2,1)} %bitcast.2), calls=%async_computation | async-start | bytes 1048576 | tf_op jit(solution)/shard_map/all_to_all | solution.py:18
  12.6 1.1 fusion.24
  13.8 1.9 %collective-permute-start = (bf16[6,3,2048]{2,1,0:T(4,128)(2,1)S(1)}, bf16[6,3,2048]{2,1,0:T(4,128)(2,1)S(1)}, u32[]{:S(2)}, u32[]{:S(2)}) collective-permute-start(bf16[6,3,2048]{2,1,0:T(4,128)(2,1)S(1)} %get-tuple-element.58), channel_id=1, source_target_pairs={{0,32},{32,64},{64,96},{96,128},{128,160},{160,192},{192,224},{224... | collective-permute-start | bytes 221192 | tf_op jit(solution)/shard_map/ppermute | solution.py:44
  15.7 3.6 %collective-permute-start.1 = (bf16[6,3,2048]{2,1,0:T(4,128)(2,1)S(1)}, bf16[6,3,2048]{2,1,0:T(4,128)(2,1)S(1)}, u32[]{:S(2)}, u32[]{:S(2)}) collective-permute-start(bf16[6,3,2048]{2,1,0:T(4,128)(2,1)S(1)} %get-tuple-element.59), channel_id=1, source_target_pairs={{32,0},{64,32},{96,64},{128,96},{160,128},{192,160},{224,192},{256... | collective-permute-start | bytes 221192 | tf_op jit(solution)/shard_map/ppermute | solution.py:47
  19.3 1.6 %fusion.29 = (f32[1]{0:T(128)}, f32[1]{0:T(128)}, f32[1]{0:T(128)}, f32[1]{0:T(128)}, f32[1]{0:T(128)}, /*index=5*/f32[1]{0:T(128)}, f32[1]{0:T(128)}, f32[1]{0:T(128)}) fusion(f32[8]{0:T(128)} %param.23), kind=kLoop, calls=%fused_computation.55 | loop fusion | bytes 64 | tf_op jit(solution)/shard_map/slice | solution.py:193
  21.0 6.1 %select_add_fusion = f32[128,256]{1,0:T(8,128)S(1)} fusion(s32[128,256]{1,0:T(8,128)} %param.22, f32[]{:T(128)} %bitcast.13, f32[]{:T(128)} %bitcast.12, f32[]{:T(128)} %bitcast.11, f32[]{:T(128)} %bitcast.10, f32[]{:T(128)} %bitcast.9, f32[]{:T(128)} %bitcast.8, f32[]{:T(128)} %bitcast.7, f32[]{:T(128)} %bitcast.6), kind=kLoop, calls=%fused_computation.18 | loop fusion | flops 753664 | bytes 262176 | tf_op jit(solution)/shard_map/add | solution.py:193
  27.1 3.9 %collective-permute-start.3 = (f32[3,256]{1,0:T(4,128)S(1)}, f32[3,256]{1,0:T(4,128)S(1)}, u32[]{:S(2)}, u32[]{:S(2)}) collective-permute-start(f32[3,256]{1,0:T(4,128)S(1)} %get-tuple-element.70), channel_id=1, source_target_pairs={{0,32},{32,64},{64,96},{96,128},{128,160},{160,192},{192,224},{224... | collective-permute-start | bytes 9224 | tf_op jit(solution)/shard_map/ppermute | solution.py:44
  31.0 1.9 %collective-permute-start.4 = (f32[3,256]{1,0:T(4,128)S(1)}, f32[3,256]{1,0:T(4,128)S(1)}, u32[]{:S(2)}, u32[]{:S(2)}) collective-permute-start(f32[3,256]{1,0:T(4,128)S(1)} %get-tuple-element.71), channel_id=1, source_target_pairs={{32,0},{64,32},{96,64},{128,96},{160,128},{192,160},{224,192},{256... | collective-permute-start | bytes 9224 | tf_op jit(solution)/shard_map/ppermute | solution.py:47
  33.5 0.9 convert_reduce_fusion
  34.5 0.7 multiply_add_fusion
  35.1 0.7 select_reduce_fusion.rows_ref
  35.9 0.0 all-to-all-done
  35.9 0.9 broadcast_in_dim.109
  36.8 9.8 %all-to-all-start.1 = ((bf16[32,32,256]{2,1,0:T(8,128)(2,1)}), bf16[32,32,256]{2,1,0:T(8,128)(2,1)S(1)}, u32[]{:S(2)}, u32[]{:S(2)}) async-start(bf16[32,32,256]{2,1,0:T(8,128)(2,1)} %broadcast_in_dim.109), calls=%async_computation.1 | async-start | bytes 1048576 | tf_op jit(solution)/shard_map/all_to_all | solution.py:21
  46.6 0.7 gather_fusion
  47.2 0.1 broadcast_select_fusion
  47.3 0.0 collective-permute-done.3
  47.3 0.0 collective-permute-done.4
  47.3 0.7 fusion.23
  48.0 0.1 fusion.27
  48.1 0.1 copy.40
  48.2 0.1 copy.44
  48.3 13.5 %all-to-all-done.1 = bf16[32,32,256]{2,1,0:T(8,128)(2,1)S(1)} async-done(((bf16[32,32,256]{2,1,0:T(8,128)(2,1)}), bf16[32,32,256]{2,1,0:T(8,128)(2,1)S(1)}, u32[]{:S(2)}, u32[]{:S(2)}) %all-to-all-start.1) | async-done | bytes 524320 | tf_op jit(solution)/shard_map/all_to_all | solution.py:21
  61.8 5.1 %collective-permute-start.2 = (bf16[1024,256]{1,0:T(8,128)(2,1)S(1)}, bf16[1024,256]{1,0:T(8,128)(2,1)S(1)}, u32[]{:S(2)}, u32[]{:S(2)}) collective-permute-start(bf16[1024,256]{1,0:T(8,128)(2,1)S(1)} %bitcast.72), channel_id=1, source_target_pairs={{0,32},{32,0},{64,96},{96,64},{128,160},{160,128},{192,224},{224,1... | collective-permute-start | bytes 1572872 | tf_op jit(solution)/shard_map/ppermute | solution.py:31
  66.9 0.0 collective-permute-done
  66.9 0.0 collective-permute-done.1
  66.9 4.7 %pad_maximum_fusion = bf16[6,134,2048]{2,1,0:T(8,128)(2,1)} fusion(bf16[6,3,2048]{2,1,0:T(4,128)(2,1)S(1)} %collective-permute-done.1, bf16[6,128,2048]{2,1,0:T(8,128)(2,1)} %param.19, bf16[6,3,2048]{2,1,0:T(4,128)(2,1)S(1)} %collective-permute-done), kind=kLoop, calls=%fused_computation.1 | loop fusion | flops 9879552 | bytes 6586368 | tf_op jit(solution)/shard_map/concatenate | solution.py:48
  71.7 0.0 copy-done.5
  71.7 4.0 %reshape.91 = bf16[804,2048]{1,0:T(8,128)(2,1)} reshape(bf16[6,134,2048]{2,1,0:T(8,128)(2,1)} %pad_maximum_fusion) | data formatting | bytes 6586368 | tf_op jit(solution)/shard_map/reshape | solution.py:197
  75.7 2.7 %fusion.2 = f32[804,256]{1,0:T(8,128)S(1)} fusion(bf16[1024,256]{1,0:T(8,128)(2,1)S(1)} %bitcast.73, pred[]{:T(512)S(6)} %eq.86, bf16[804,2048]{1,0:T(8,128)(2,1)} %reshape.91), kind=kOutput, calls=%fused_computation.4 | convolution fusion | flops 422350848 | bytes 4640769 | tf_op jit(solution)/shard_map/dot_general | solution.py:33
  78.3 0.0 collective-permute-done.2
  78.3 0.2 copy-done.2
  78.6 0.6 fusion
  79.2 0.2 add.80
  79.3 0.1 reshape.94.loading_ref
  79.4 0.0 copy-start.1
  79.5 0.0 copy-start.4
  79.5 0.2 fusion.25
  79.6 0.3 copy.39
  80.0 1.3 %collective-permute-start.5 = (f32[21,134]{1,0:T(8,128)S(1)}, f32[21,134]{1,0:T(8,128)S(1)}, u32[]{:S(2)}, u32[]{:S(2)}) collective-permute-start(f32[21,134]{1,0:T(8,128)S(1)} %reshape.95), channel_id=1, source_target_pairs={{1,0},{2,1},{3,2},{4,3},{5,4},{6,5},{7,6},{8,7},{9,8},{10,9},{11,1... | collective-permute-start | bytes 33776 | tf_op jit(solution)/shard_map/ppermute | solution.py:147
  81.3 0.3 copy.43
  81.7 4.9 %collective-permute-start.6 = (f32[21,134]{1,0:T(8,128)S(1)}, f32[21,134]{1,0:T(8,128)S(1)}, u32[]{:S(2)}, u32[]{:S(2)}) collective-permute-start(f32[21,134]{1,0:T(8,128)S(1)} %reshape.97), channel_id=1, source_target_pairs={{0,1},{1,2},{2,3},{3,4},{4,5},{5,6},{6,7},{7,8},{8,9},{9,10},{10,1... | collective-permute-start | bytes 33776 | tf_op jit(solution)/shard_map/ppermute | solution.py:146
  86.6 0.1 fusion.19
  86.7 0.1 pad.11.clone
  86.8 0.0 collective-permute-done.5
  86.8 0.2 copy.42
  87.1 0.9 collective-permute-done.6
  88.0 0.0 copy-start.3
  88.0 0.2 copy.46
  88.2 1.0 pad_maximum_fusion.1.side_ref
  89.2 7.0 %shard_map.122 = (f32[6,128,256]{2,1,0:T(8,128)}, f32[6,64,256]{2,1,0:T(8,128)}) custom-call(s32[64]{0:T(128)} %copy-done.5, f32[6,6]{1,0:T(8,128)} %coupling_ref.1, f32[6,134,256]{2,1,0:T(8,128)} %copy-done.1, f32[134,256]{1,0:T(8,128)} %get-tuple-element.69.stiff_ref, f32[7,134,128]{2,1,0:T(8,128)} %pad_maximum_fusion.1.side_ref), custom_call_target="tpu_custom_call" | custom-call | tf_op jit(solution)/shard_map/pallas_call | solution.py:115
  96.2 0.0 copy-done.4
  96.2 1.8 %fusion.10 = f32[64,4,256]{2,1,0:T(4,128)S(1)} fusion(f32[6,64,256]{2,1,0:T(8,128)} %get-tuple-element.13, f32[64,256]{1,0:T(8,128)S(1)} %broadcast_select_fusion, f32[4,6]{1,0:T(4,128)S(1)} %copy-done.4), kind=kOutput, calls=%fused_computation.13 | convolution fusion | flops 4784128 | bytes 720992 | tf_op jit(solution)/shard_map/ka,aij->ikj/dot_general | solution.py:215
  98.0 0.2 fusion.26
  98.2 0.1 maximum_select_fusion
  98.3 0.1 copy.51
  98.4 0.8 select_n.115
  99.2 9.2 %all-to-all-start.2 = ((f32[32,8,128]{2,1,0:T(8,128)}), f32[32,8,128]{2,1,0:T(8,128)S(1)}, u32[]{:S(2)}, u32[]{:S(2)}) async-start(f32[32,8,128]{2,1,0:T(8,128)} %select_n.115), calls=%async_computation.2 | async-start | bytes 262144 | tf_op jit(solution)/shard_map/all_to_all | solution.py:221
  109.1 9.7 %all-to-all-done.2 = f32[32,8,128]{2,1,0:T(8,128)S(1)} async-done(((f32[32,8,128]{2,1,0:T(8,128)}), f32[32,8,128]{2,1,0:T(8,128)S(1)}, u32[]{:S(2)}, u32[]{:S(2)}) %all-to-all-start.2) | async-done | bytes 131104 | tf_op jit(solution)/shard_map/all_to_all | solution.py:221
  118.8 0.1 mul.64
  118.9 0.7 add.94
  (20 shorter events, 0.2 us)
Async XLA Ops:
  0.6 1.2 %copy-start = (bf16[2048,256]{1,0:T(8,128)(2,1)S(1)}, bf16[2048,256]{1,0:T(8,128)(2,1)}, u32[]{:S(2)}) copy-start(bf16[2048,256]{1,0:T(8,128)(2,1)} %param.20) | copy-start | bytes 3145732
  2.7 33.2 %all-to-all-start = ((bf16[32,32,256]{2,1,0:T(8,128)(2,1)}), bf16[32,32,256]{2,1,0:T(8,128)(2,1)S(1)}, u32[]{:S(2)}, u32[]{:S(2)}) async-start(bf16[32,32,256]{2,1,0:T(8,128)(2,1)} %bitcast.2), calls=%async_computation | async-start | bytes 1048576 | tf_op jit(solution)/shard_map/all_to_all | solution.py:18
  13.8 53.2 %collective-permute-start = (bf16[6,3,2048]{2,1,0:T(4,128)(2,1)S(1)}, bf16[6,3,2048]{2,1,0:T(4,128)(2,1)S(1)}, u32[]{:S(2)}, u32[]{:S(2)}) collective-permute-start(bf16[6,3,2048]{2,1,0:T(4,128)(2,1)S(1)} %get-tuple-element.58), channel_id=1, source_target_pairs={{0,32},{32,64},{64,96},{96,128},{128,160},{160,192},{192,224},{224... | collective-permute-start | bytes 221192 | tf_op jit(solution)/shard_map/ppermute | solution.py:44
  15.7 51.2 %collective-permute-start.1 = (bf16[6,3,2048]{2,1,0:T(4,128)(2,1)S(1)}, bf16[6,3,2048]{2,1,0:T(4,128)(2,1)S(1)}, u32[]{:S(2)}, u32[]{:S(2)}) collective-permute-start(bf16[6,3,2048]{2,1,0:T(4,128)(2,1)S(1)} %get-tuple-element.59), channel_id=1, source_target_pairs={{32,0},{64,32},{96,64},{128,96},{160,128},{192,160},{224,192},{256... | collective-permute-start | bytes 221192 | tf_op jit(solution)/shard_map/ppermute | solution.py:47
  27.1 20.2 %collective-permute-start.3 = (f32[3,256]{1,0:T(4,128)S(1)}, f32[3,256]{1,0:T(4,128)S(1)}, u32[]{:S(2)}, u32[]{:S(2)}) collective-permute-start(f32[3,256]{1,0:T(4,128)S(1)} %get-tuple-element.70), channel_id=1, source_target_pairs={{0,32},{32,64},{64,96},{96,128},{128,160},{160,192},{192,224},{224... | collective-permute-start | bytes 9224 | tf_op jit(solution)/shard_map/ppermute | solution.py:44
  31.0 16.4 %collective-permute-start.4 = (f32[3,256]{1,0:T(4,128)S(1)}, f32[3,256]{1,0:T(4,128)S(1)}, u32[]{:S(2)}, u32[]{:S(2)}) collective-permute-start(f32[3,256]{1,0:T(4,128)S(1)} %get-tuple-element.71), channel_id=1, source_target_pairs={{32,0},{64,32},{96,64},{128,96},{160,128},{192,160},{224,192},{256... | collective-permute-start | bytes 9224 | tf_op jit(solution)/shard_map/ppermute | solution.py:47
  35.9 35.8 %copy-start.5 = (s32[64]{0:T(128)}, s32[64]{0:T(128)S(1)}, u32[]{:S(2)}) copy-start(s32[64]{0:T(128)S(1)} %select_reduce_fusion.rows_ref) | copy-start | bytes 772
  36.8 25.1 %all-to-all-start.1 = ((bf16[32,32,256]{2,1,0:T(8,128)(2,1)}), bf16[32,32,256]{2,1,0:T(8,128)(2,1)S(1)}, u32[]{:S(2)}, u32[]{:S(2)}) async-start(bf16[32,32,256]{2,1,0:T(8,128)(2,1)} %broadcast_in_dim.109), calls=%async_computation.1 | async-start | bytes 1048576 | tf_op jit(solution)/shard_map/all_to_all | solution.py:21
  61.8 16.5 %collective-permute-start.2 = (bf16[1024,256]{1,0:T(8,128)(2,1)S(1)}, bf16[1024,256]{1,0:T(8,128)(2,1)S(1)}, u32[]{:S(2)}, u32[]{:S(2)}) collective-permute-start(bf16[1024,256]{1,0:T(8,128)(2,1)S(1)} %bitcast.72), channel_id=1, source_target_pairs={{0,32},{32,0},{64,96},{96,64},{128,160},{160,128},{192,224},{224,1... | collective-permute-start | bytes 1572872 | tf_op jit(solution)/shard_map/ppermute | solution.py:31
  75.6 2.9 %copy-start.2 = (bf16[804,2048]{1,0:T(8,128)(2,1)S(1)}, bf16[804,2048]{1,0:T(8,128)(2,1)}, u32[]{:S(2)}) copy-start(bf16[804,2048]{1,0:T(8,128)(2,1)} %reshape.91) | copy-start | bytes 9879556
  79.4 9.8 %copy-start.1 = (f32[6,134,256]{2,1,0:T(8,128)}, f32[6,134,256]{2,1,0:T(8,128)S(1)}, u32[]{:S(2)}) copy-start(f32[6,134,256]{2,1,0:T(8,128)S(1)} %reshape.94.loading_ref) | copy-start | bytes 2469892
  79.5 16.8 %copy-start.4 = (f32[4,6]{1,0:T(4,128)S(1)}, f32[4,6]{1,0:T(4,128)}, u32[]{:S(2)}) copy-start(f32[4,6]{1,0:T(4,128)} %param.25) | copy-start | bytes 292
  80.0 6.8 %collective-permute-start.5 = (f32[21,134]{1,0:T(8,128)S(1)}, f32[21,134]{1,0:T(8,128)S(1)}, u32[]{:S(2)}, u32[]{:S(2)}) collective-permute-start(f32[21,134]{1,0:T(8,128)S(1)} %reshape.95), channel_id=1, source_target_pairs={{1,0},{2,1},{3,2},{4,3},{5,4},{6,5},{7,6},{8,7},{9,8},{10,9},{11,1... | collective-permute-start | bytes 33776 | tf_op jit(solution)/shard_map/ppermute | solution.py:147
  81.7 6.2 %collective-permute-start.6 = (f32[21,134]{1,0:T(8,128)S(1)}, f32[21,134]{1,0:T(8,128)S(1)}, u32[]{:S(2)}, u32[]{:S(2)}) collective-permute-start(f32[21,134]{1,0:T(8,128)S(1)} %reshape.97), channel_id=1, source_target_pairs={{0,1},{1,2},{2,3},{3,4},{4,5},{5,6},{6,7},{7,8},{8,9},{9,10},{10,1... | collective-permute-start | bytes 33776 | tf_op jit(solution)/shard_map/ppermute | solution.py:146
  88.0 30.9 %copy-start.3 = (f32[1,1,32,2,2,256]{5,4,3,2,1,0:T(2,128)S(1)}, f32[1,1,32,2,2,256]{5,4,3,2,1,0:T(2,128)}, u32[]{:S(2)}) copy-start(f32[1,1,32,2,2,256]{5,4,3,2,1,0:T(2,128)} %param.29) | copy-start | bytes 393220
  99.2 19.6 %all-to-all-start.2 = ((f32[32,8,128]{2,1,0:T(8,128)}), f32[32,8,128]{2,1,0:T(8,128)S(1)}, u32[]{:S(2)}, u32[]{:S(2)}) async-start(f32[32,8,128]{2,1,0:T(8,128)} %select_n.115), calls=%async_computation.2 | async-start | bytes 262144 | tf_op jit(solution)/shard_map/all_to_all | solution.py:221

commit v12 on v10

--- a/solution.py
+++ b/solution.py
@@ -64,7 +64,10 @@
     return jnp.concatenate([low, block, high], axis=2)
 
 
-def sweeps_kernel(rows_ref, coupling_ref, loading_ref, stiff_ref, side_ref, out_ref, picked_ref, load_scr, motion_ref, next_ref):
+def sweeps_kernel(
+    rows_ref, filled_ref, coupling_ref, stress_ref, loading_ref, stiff_ref, side_ref,
+    out_ref, outbox_ref, load_scr, motion_ref, next_ref,
+):
     fields = out_ref.shape[0]
     ext_rows, cells = loading_ref.shape[1], loading_ref.shape[2]
     rows, cols = load_scr.shape[1], load_scr.shape[2]
@@ -98,13 +101,27 @@
     out_rows = out_ref.shape[1]
     for a in range(fields):
         out_ref[a] = pltpu.roll(source[a], rows - width, 0)[:out_rows, :cells]
-    for slot in range(picked_ref.shape[1]):
+    per_owner = outbox_ref.shape[1] // (2 * CAP)
+    for slot in range(rows_ref.shape[0]):
         row = rows_ref[slot] + width
-        for a in range(fields):
-            picked_ref[a, pl.ds(slot, 1), :] = source[a, pl.ds(row, 1), pl.ds(0, cells)]
-
-
-def run_sweeps(slot_row, coupling, loading, stiffness, side, out_rows):
+        lines = [source[a, pl.ds(row, 1), pl.ds(0, cells)] for a in range(fields)]
+        stiff_line = load_scr[fields, pl.ds(row, 1), pl.ds(0, cells)]
+        stress = []
+        for k in range(stress_ref.shape[0]):
+            mapped = stress_ref[k, 0] * lines[0]
+            for a in range(1, fields):
+                mapped = mapped + stress_ref[k, a] * lines[a]
+            stress.append(stiff_line * mapped)
+        keep = filled_ref[slot] != 0
+        for d in range(2):
+            spectrum = stress[2 * d] * stress[2 * d] + stress[2 * d + 1] * stress[2 * d + 1]
+            spectrum = jnp.where(keep, spectrum, 0.0)
+            for h in range(per_owner):
+                place = ((slot % CAP) * 2 + d) * per_owner + h
+                outbox_ref[slot // CAP, pl.ds(place, 1), :] = spectrum[:, h * 128 : (h + 1) * 128]
+
+
+def run_sweeps(slot_row, filled, coupling, stress_map, loading, stiffness, side, out_rows):
     fields, ext_rows, cells = loading.shape
     rows = -(-ext_rows // 8) * 8
     cols = cells + side.shape[2]
@@ -114,16 +131,16 @@
         sweeps_kernel,
         out_shape=(
             jax.ShapeDtypeStruct((fields, out_rows, cells), jnp.float32),
-            jax.ShapeDtypeStruct((fields, slot_row.shape[0], cells), jnp.float32),
+            jax.ShapeDtypeStruct((slot_row.shape[0] // CAP, CAP * 2 * cells // 128, 128), jnp.float32),
         ),
-        in_specs=[smem, smem, vmem, vmem, vmem],
+        in_specs=[smem, smem, smem, smem, vmem, vmem, vmem],
         out_specs=(vmem, vmem),
         scratch_shapes=[
             pltpu.VMEM((fields + 1, rows, cols), jnp.float32),
             pltpu.VMEM((fields, rows, cols), jnp.float32),
             pltpu.VMEM((fields, rows, cols), jnp.float32),
         ],
-    )(slot_row, coupling, loading, stiffness, side)
+    )(slot_row, filled, coupling, stress_map, loading, stiffness, side)
 
 
 def girth_side(blocks, axis, width, lanes):
@@ -208,15 +225,10 @@
     hit = target[None, :] == slots[:, None]
     filled = jnp.any(hit, axis=1)
     slot_row = jnp.sum(jnp.where(hit, tile_ids[None, :], 0), axis=1)
-    stiffness_at = jnp.take(stiffness, slot_row, axis=0)
     side = girth_side([loading, stiffness_rows[None]], "girth", width, 128)
-    motion, motion_at = run_sweeps(slot_row, coupling, loading, stiffness_rows, side, row_count)
-    stress_rows = stiffness_at[:, None, :] * jnp.einsum(
-        "ka,aij->ikj", stress_map, motion_at, precision=lax.Precision.HIGHEST
+    motion, outbox = run_sweeps(
+        slot_row, filled.astype(jnp.int32), coupling, stress_map, loading, stiffness_rows, side, row_count
     )
-    spectra = square_pairs(stress_rows, 1)
-    outbox = jnp.where(filled[:, None, None], spectra, 0.0)
-    outbox = outbox.reshape(girth_count, CAP * 2 * girth_cells // 128, 128)
     received = lax.all_to_all(outbox, "girth", split_axis=0, concat_axis=0, tiled=True)
     received = received.reshape(girth_count, CAP, 2, girth_cells)
     hotspot_moments = prior_moments + (psd_weight[0] * received)[None, None]

time: 102 us -> 105 us (1.029)
  starting transfers between devices: 43.7 us -> 49.6 us
  local copies, waits for them, and re-layouts: 9.13 us -> 6.47 us
  matrix products: 4.79 us -> 3 us
  waiting for transfers between devices: 25.6 us -> 26.7 us
    all_to_all x1, waiting for transfers between devices: 2.92 us -> 16.2 us  [scatter_gather(): got = lax.all_to_all(send, axis, 0, 0, tiled=True)]
    all_to_all x1, waiting for transfers between devices: 8.21 us -> 0.01 us  [scatter_gather(): full = lax.all_to_all(send, axis, 0, 0, tiled=True)]
    all_to_all x1, starting transfers between devices: 5.79 us -> 12 us  [on_device(): lax.all_to_all(outbox, 'girth', split_axis=0, concat_axis=0, tiled=True)]
    ppermute x1, waiting for transfers between devices: 4.25 us -> 0.01 us  [girth_side(): after = unpack(lax.ppermute(pack(0), axis, backward))]
    dot_general x1 -> x0, matrix products: 1.78 us -> none  [on_device(): jnp.einsum('ka,aij->ikj', stress_map, motion_at, precision=lax.Precision....]
    all_to_all x1, starting transfers between devices: 6.88 us -> 5.62 us  [scatter_gather(): full = lax.all_to_all(send, axis, 0, 0, tiled=True)]
  transfers between devices with their start and end apart: 10 -> 10, of which waited for: 5 -> 3; matrix products, arithmetic and copies ran while one was open for 12% -> 10% of each run, Pallas kernels for 0% -> 0%
where the time goes in v12:
time: 105 us; the launch traced here: 104 us
  starting transfers between devices  49.6 us (47%)
  waiting for transfers between devices  26.7 us (25%)
  other arithmetic  9.23 us (9%)
  Pallas kernels  7.17 us (7%)
  local copies, waits for them, and re-layouts  6.47 us (6%)
  matrix products  3 us (3%)
  between operations  2.25 us (2%)
    all_to_all x1, waiting for transfers between devices, scatter_gather(): got = lax.all_to_all(send, axis, 0, 0, tiled=True)  16.2 us
    all_to_all x1, starting transfers between devices, on_device(): lax.all_to_all(outbox, 'girth', split_axis=0, concat_axis=0, tiled=True)  12 us
    all_to_all x1, starting transfers between devices, scatter_gather(): got = lax.all_to_all(send, axis, 0, 0, tiled=True)  9.95 us
    all_to_all x1, waiting for transfers between devices, on_device(): lax.all_to_all(outbox, 'girth', split_axis=0, concat_axis=0, tiled=True)  9.93 us
    pallas_call x1, Pallas kernels, run_sweeps(): pl.pallas_call(sweeps_kernel, out_shape=(jax.ShapeDtypeStruct((fields, ou...  7.17 us
    ppermute x2, starting transfers between devices, padded_2(): lax.ppermute(lax.slice_in_dim(block, block.shape[dim] - width, None, axis...  5.79 us
    all_to_all x1, starting transfers between devices, scatter_gather(): full = lax.all_to_all(send, axis, 0, 0, tiled=True)  5.62 us
    ppermute x2, starting transfers between devices, padded_2(): lax.ppermute(lax.slice_in_dim(block, 0, width, axis=dim), axis, backward)  5.56 us
  transfers between devices with their start and end apart: 10, of which 3 were waited for; matrix products, arithmetic and copies ran while one was open for 10% of the time, Pallas kernels for 0%

profile of v12, /device:TPU:192, one launch (start us, length us, event | category | flops | bytes accessed | tf_op | source)
XLA Modules:
  0.0 104.4 jit_solution(1641646398284384648)
XLA Ops:
  0.6 0.0 copy-start
  0.6 0.0 copy-start.4
  0.7 0.0 copy-start.3
  0.7 0.0 copy-start.5
  0.7 0.0 copy-start.6
  0.7 1.2 %copy-done = bf16[2048,256]{1,0:T(8,128)(2,1)S(1)} copy-done((bf16[2048,256]{1,0:T(8,128)(2,1)S(1)}, bf16[2048,256]{1,0:T(8,128)(2,1)}, u32[]{:S(2)}) %copy-start) | copy-done | bytes 1048600
  1.9 0.8 constant_dynamic-slice_fusion
  2.7 9.9 %all-to-all-start = ((bf16[32,32,256]{2,1,0:T(8,128)(2,1)}), bf16[32,32,256]{2,1,0:T(8,128)(2,1)S(1)}, u32[]{:S(2)}, u32[]{:S(2)}) async-start(bf16[32,32,256]{2,1,0:T(8,128)(2,1)} %bitcast.2), calls=%async_computation | async-start | bytes 1048576 | tf_op jit(solution)/shard_map/all_to_all | solution.py:18
  13.3 16.2 %all-to-all-done = bf16[32,32,256]{2,1,0:T(8,128)(2,1)S(1)} async-done(((bf16[32,32,256]{2,1,0:T(8,128)(2,1)}), bf16[32,32,256]{2,1,0:T(8,128)(2,1)S(1)}, u32[]{:S(2)}, u32[]{:S(2)}) %all-to-all-start) | async-done | bytes 524320 | tf_op jit(solution)/shard_map/all_to_all | solution.py:18
  29.5 0.9 broadcast_in_dim.73
  30.4 5.6 %all-to-all-start.1 = ((bf16[32,32,256]{2,1,0:T(8,128)(2,1)}), bf16[32,32,256]{2,1,0:T(8,128)(2,1)S(1)}, u32[]{:S(2)}, u32[]{:S(2)}) async-start(bf16[32,32,256]{2,1,0:T(8,128)(2,1)} %broadcast_in_dim.73), calls=%async_computation.1 | async-start | bytes 1048576 | tf_op jit(solution)/shard_map/all_to_all | solution.py:21
  36.0 1.1 %fusion.12 = (bf16[6,3,2048]{2,1,0:T(4,128)(2,1)S(1)}, bf16[6,3,2048]{2,1,0:T(4,128)(2,1)S(1)}) fusion(bf16[6,128,2048]{2,1,0:T(8,128)(2,1)} %param.11), kind=kLoop, calls=%fused_computation.28 | loop fusion | bytes 294912 | tf_op jit(solution)/shard_map/slice | solution.py:43
  37.1 1.9 %collective-permute-start = (bf16[6,3,2048]{2,1,0:T(4,128)(2,1)S(1)}, bf16[6,3,2048]{2,1,0:T(4,128)(2,1)S(1)}, u32[]{:S(2)}, u32[]{:S(2)}) collective-permute-start(bf16[6,3,2048]{2,1,0:T(4,128)(2,1)S(1)} %get-tuple-element.6), channel_id=1, source_target_pairs={{0,32},{32,64},{64,96},{96,128},{128,160},{160,192},{192,224},{224... | collective-permute-start | bytes 221192 | tf_op jit(solution)/shard_map/ppermute | solution.py:42
  39.0 3.6 %collective-permute-start.1 = (bf16[6,3,2048]{2,1,0:T(4,128)(2,1)S(1)}, bf16[6,3,2048]{2,1,0:T(4,128)(2,1)S(1)}, u32[]{:S(2)}, u32[]{:S(2)}) collective-permute-start(bf16[6,3,2048]{2,1,0:T(4,128)(2,1)S(1)} %get-tuple-element.7), channel_id=1, source_target_pairs={{32,0},{64,32},{96,64},{128,96},{160,128},{192,160},{224,192},{256... | collective-permute-start | bytes 221192 | tf_op jit(solution)/shard_map/ppermute | solution.py:45
  42.7 0.0 copy-done.4
  42.7 0.7 fusion.16
  43.4 0.0 copy-done.3
  43.4 5.2 %select_add_fusion = f32[128,256]{1,0:T(8,128)S(1)} fusion(s32[128,256]{1,0:T(8,128)S(1)} %copy-done.3, f32[]{:T(128)} %bitcast.14, f32[]{:T(128)} %bitcast.13, f32[]{:T(128)} %bitcast.12, f32[]{:T(128)} %bitcast.11, f32[]{:T(128)} %bitcast.10, f32[]{:T(128)} %bitcast.9, f32[]{:T(128)} %bitcast.8, f32[]{:T(128)} %bitcast.7), kind=kLoop, calls=%fused_computation.13 | loop fusion | flops 753664 | bytes 262176 | tf_op jit(solution)/shard_map/add | solution.py:208
  48.6 3.9 %collective-permute-start.3 = (f32[3,256]{1,0:T(4,128)S(1)}, f32[3,256]{1,0:T(4,128)S(1)}, u32[]{:S(2)}, u32[]{:S(2)}) collective-permute-start(f32[3,256]{1,0:T(4,128)S(1)} %get-tuple-element.16), channel_id=1, source_target_pairs={{0,32},{32,64},{64,96},{96,128},{128,160},{160,192},{192,224},{224... | collective-permute-start | bytes 9224 | tf_op jit(solution)/shard_map/ppermute | solution.py:42
  52.5 1.9 %collective-permute-start.4 = (f32[3,256]{1,0:T(4,128)S(1)}, f32[3,256]{1,0:T(4,128)S(1)}, u32[]{:S(2)}, u32[]{:S(2)}) collective-permute-start(f32[3,256]{1,0:T(4,128)S(1)} %get-tuple-element.17), channel_id=1, source_target_pairs={{32,0},{64,32},{96,64},{128,96},{160,128},{192,160},{224,192},{256... | collective-permute-start | bytes 9224 | tf_op jit(solution)/shard_map/ppermute | solution.py:45
  54.4 0.0 copy-done.5
  54.4 0.2 convert_reduce_fusion
  54.6 0.0 all-to-all-done.1
  54.6 4.9 %collective-permute-start.2 = (bf16[1024,256]{1,0:T(8,128)(2,1)S(1)}, bf16[1024,256]{1,0:T(8,128)(2,1)S(1)}, u32[]{:S(2)}, u32[]{:S(2)}) collective-permute-start(bf16[1024,256]{1,0:T(8,128)(2,1)S(1)} %bitcast.34), channel_id=1, source_target_pairs={{0,32},{32,0},{64,96},{96,64},{128,160},{160,128},{192,224},{224,1... | collective-permute-start | bytes 1572872 | tf_op jit(solution)/shard_map/ppermute | solution.py:31
  59.5 0.0 copy-done.6
  59.5 0.7 select_reduce_fusion.rows_ref
  60.2 0.0 collective-permute-done.3
  60.2 0.0 collective-permute-done.4
  60.2 0.7 fusion.11
  60.8 0.1 fusion.14
  60.9 0.1 copy.26
  61.0 0.1 copy.30
  61.1 0.0 collective-permute-done.2
  61.1 0.1 broadcast_select_fusion.1
  61.2 0.0 collective-permute-done
  61.2 0.0 collective-permute-done.1
  61.2 3.0 %fusion.loading_ref = f32[6,134,256]{2,1,0:T(8,128)S(1)} fusion(bf16[6,3,2048]{2,1,0:T(4,128)(2,1)S(1)} %collective-permute-done.1, bf16[6,128,2048]{2,1,0:T(8,128)(2,1)} %param.11, bf16[6,3,2048]{2,1,0:T(4,128)(2,1)S(1)} %collective-permute-done, bf16[1024,256]{1,0:T(8,128)(2,1)S(1)} %get-tuple-element.9, bf16[1024,256]{1,0:T(8,128)(2,1)S(1)} %get-tuple-element.8), kind=kOutput, calls=%fused_computation | convolution fusion | flops 855031808 | bytes 5165056 | tf_op jit(solution)/shard_map/dot_general | solution.py:213
  64.2 0.0 copy-start.1
  64.3 0.2 fusion.13
  64.4 0.0 copy-start.2
  64.4 0.3 copy.25
  64.8 1.3 %collective-permute-start.5 = (f32[21,134]{1,0:T(8,128)S(1)}, f32[21,134]{1,0:T(8,128)S(1)}, u32[]{:S(2)}, u32[]{:S(2)}) collective-permute-start(f32[21,134]{1,0:T(8,128)S(1)} %reshape.51), channel_id=1, source_target_pairs={{1,0},{2,1},{3,2},{4,3},{5,4},{6,5},{7,6},{8,7},{9,8},{10,9},{11,1... | collective-permute-start | bytes 33776 | tf_op jit(solution)/shard_map/ppermute | solution.py:162
  66.1 0.3 copy.29
  66.5 4.5 %collective-permute-start.6 = (f32[21,134]{1,0:T(8,128)S(1)}, f32[21,134]{1,0:T(8,128)S(1)}, u32[]{:S(2)}, u32[]{:S(2)}) collective-permute-start(f32[21,134]{1,0:T(8,128)S(1)} %reshape.53), channel_id=1, source_target_pairs={{0,1},{1,2},{2,3},{3,4},{4,5},{5,6},{6,7},{7,8},{8,9},{9,10},{10,1... | collective-permute-start | bytes 33776 | tf_op jit(solution)/shard_map/ppermute | solution.py:161
  71.1 0.1 fusion.8
  71.2 0.5 convert_element_type.7.filled_ref
  71.7 0.1 pad.1.clone
  71.8 0.0 collective-permute-done.5
  71.8 0.2 copy.28
  72.0 0.6 collective-permute-done.6
  72.6 0.2 copy.32
  72.8 1.0 pad_maximum_fusion.side_ref
  73.8 0.0 copy-done.1
  73.8 7.2 %shard_map.122 = (f32[6,128,256]{2,1,0:T(8,128)}, f32[32,8,128]{2,1,0:T(8,128)}) custom-call(s32[64]{0:T(128)} %select_reduce_fusion.rows_ref, s32[64]{0:T(128)} %convert_element_type.7.filled_ref, f32[6,6]{1,0:T(8,128)} %coupling_ref.1, f32[4,6]{1,0:T(4,128)} %stress_ref.1, f32[6,134,256]{2,1,0:T(8,128)} %copy-done.1, ...), custom_call_target="tpu_custom_call" | custom-call | tf_op jit(solution)/shard_map/pallas_call | solution.py:130
  81.0 12.0 %all-to-all-start.2 = ((f32[32,8,128]{2,1,0:T(8,128)}), f32[32,8,128]{2,1,0:T(8,128)S(1)}, u32[]{:S(2)}, u32[]{:S(2)}) async-start(f32[32,8,128]{2,1,0:T(8,128)} %get-tuple-element.5), calls=%async_computation.2 | async-start | bytes 262144 | tf_op jit(solution)/shard_map/all_to_all | solution.py:232
  93.6 9.9 %all-to-all-done.2 = f32[32,8,128]{2,1,0:T(8,128)S(1)} async-done(((f32[32,8,128]{2,1,0:T(8,128)}), f32[32,8,128]{2,1,0:T(8,128)S(1)}, u32[]{:S(2)}, u32[]{:S(2)}) %all-to-all-start.2) | async-done | bytes 131104 | tf_op jit(solution)/shard_map/all_to_all | solution.py:232
  103.6 0.1 mul.34
  103.7 0.0 copy-done.2
  103.7 0.7 add.53
  (13 shorter events, 0.2 us)
Async XLA Ops:
  0.6 1.2 %copy-start = (bf16[2048,256]{1,0:T(8,128)(2,1)S(1)}, bf16[2048,256]{1,0:T(8,128)(2,1)}, u32[]{:S(2)}) copy-start(bf16[2048,256]{1,0:T(8,128)(2,1)} %param.12) | copy-start | bytes 3145732
  0.6 42.0 %copy-start.4 = (f32[8]{0:T(128)S(1)}, f32[8]{0:T(128)}, u32[]{:S(2)}) copy-start(f32[8]{0:T(128)} %param.15) | copy-start | bytes 100
  0.7 42.7 %copy-start.3 = (s32[128,256]{1,0:T(8,128)S(1)}, s32[128,256]{1,0:T(8,128)}, u32[]{:S(2)}) copy-start(s32[128,256]{1,0:T(8,128)} %param.14) | copy-start | bytes 393220
  0.7 53.7 %copy-start.5 = (s32[1,32,1]{1,2,0:T(1,128)S(1)}, s32[1,32,1]{1,2,0:T(1,128)}, u32[]{:S(2)}) copy-start(s32[1,32,1]{1,2,0:T(1,128)} %param.20) | copy-start | bytes 388
  0.7 58.8 %copy-start.6 = (s32[1,32]{1,0:T(1,128)S(1)}, s32[1,32]{1,0:T(1,128)}, u32[]{:S(2)}) copy-start(s32[1,32]{1,0:T(1,128)} %param.19) | copy-start | bytes 388
  2.7 26.8 %all-to-all-start = ((bf16[32,32,256]{2,1,0:T(8,128)(2,1)}), bf16[32,32,256]{2,1,0:T(8,128)(2,1)S(1)}, u32[]{:S(2)}, u32[]{:S(2)}) async-start(bf16[32,32,256]{2,1,0:T(8,128)(2,1)} %bitcast.2), calls=%async_computation | async-start | bytes 1048576 | tf_op jit(solution)/shard_map/all_to_all | solution.py:18
  30.4 24.2 %all-to-all-start.1 = ((bf16[32,32,256]{2,1,0:T(8,128)(2,1)}), bf16[32,32,256]{2,1,0:T(8,128)(2,1)S(1)}, u32[]{:S(2)}, u32[]{:S(2)}) async-start(bf16[32,32,256]{2,1,0:T(8,128)(2,1)} %broadcast_in_dim.73), calls=%async_computation.1 | async-start | bytes 1048576 | tf_op jit(solution)/shard_map/all_to_all | solution.py:21
  37.1 24.1 %collective-permute-start = (bf16[6,3,2048]{2,1,0:T(4,128)(2,1)S(1)}, bf16[6,3,2048]{2,1,0:T(4,128)(2,1)S(1)}, u32[]{:S(2)}, u32[]{:S(2)}) collective-permute-start(bf16[6,3,2048]{2,1,0:T(4,128)(2,1)S(1)} %get-tuple-element.6), channel_id=1, source_target_pairs={{0,32},{32,64},{64,96},{96,128},{128,160},{160,192},{192,224},{224... | collective-permute-start | bytes 221192 | tf_op jit(solution)/shard_map/ppermute | solution.py:42
  39.0 22.2 %collective-permute-start.1 = (bf16[6,3,2048]{2,1,0:T(4,128)(2,1)S(1)}, bf16[6,3,2048]{2,1,0:T(4,128)(2,1)S(1)}, u32[]{:S(2)}, u32[]{:S(2)}) collective-permute-start(bf16[6,3,2048]{2,1,0:T(4,128)(2,1)S(1)} %get-tuple-element.7), channel_id=1, source_target_pairs={{32,0},{64,32},{96,64},{128,96},{160,128},{192,160},{224,192},{256... | collective-permute-start | bytes 221192 | tf_op jit(solution)/shard_map/ppermute | solution.py:45
  48.6 11.6 %collective-permute-start.3 = (f32[3,256]{1,0:T(4,128)S(1)}, f32[3,256]{1,0:T(4,128)S(1)}, u32[]{:S(2)}, u32[]{:S(2)}) collective-permute-start(f32[3,256]{1,0:T(4,128)S(1)} %get-tuple-element.16), channel_id=1, source_target_pairs={{0,32},{32,64},{64,96},{96,128},{128,160},{160,192},{192,224},{224... | collective-permute-start | bytes 9224 | tf_op jit(solution)/shard_map/ppermute | solution.py:42
  52.5 7.7 %collective-permute-start.4 = (f32[3,256]{1,0:T(4,128)S(1)}, f32[3,256]{1,0:T(4,128)S(1)}, u32[]{:S(2)}, u32[]{:S(2)}) collective-permute-start(f32[3,256]{1,0:T(4,128)S(1)} %get-tuple-element.17), channel_id=1, source_target_pairs={{32,0},{64,32},{96,64},{128,96},{160,128},{192,160},{224,192},{256... | collective-permute-start | bytes 9224 | tf_op jit(solution)/shard_map/ppermute | solution.py:45
  54.6 6.5 %collective-permute-start.2 = (bf16[1024,256]{1,0:T(8,128)(2,1)S(1)}, bf16[1024,256]{1,0:T(8,128)(2,1)S(1)}, u32[]{:S(2)}, u32[]{:S(2)}) collective-permute-start(bf16[1024,256]{1,0:T(8,128)(2,1)S(1)} %bitcast.34), channel_id=1, source_target_pairs={{0,32},{32,0},{64,96},{96,64},{128,160},{160,128},{192,224},{224,1... | collective-permute-start | bytes 1572872 | tf_op jit(solution)/shard_map/ppermute | solution.py:31
  64.2 9.6 %copy-start.1 = (f32[6,134,256]{2,1,0:T(8,128)}, f32[6,134,256]{2,1,0:T(8,128)S(1)}, u32[]{:S(2)}) copy-start(f32[6,134,256]{2,1,0:T(8,128)S(1)} %fusion.loading_ref) | copy-start | bytes 2469892
  64.4 39.2 %copy-start.2 = (f32[1,1,32,2,2,256]{5,4,3,2,1,0:T(2,128)S(1)}, f32[1,1,32,2,2,256]{5,4,3,2,1,0:T(2,128)}, u32[]{:S(2)}) copy-start(f32[1,1,32,2,2,256]{5,4,3,2,1,0:T(2,128)} %param.21) | copy-start | bytes 393220
  64.8 6.9 %collective-permute-start.5 = (f32[21,134]{1,0:T(8,128)S(1)}, f32[21,134]{1,0:T(8,128)S(1)}, u32[]{:S(2)}, u32[]{:S(2)}) collective-permute-start(f32[21,134]{1,0:T(8,128)S(1)} %reshape.51), channel_id=1, source_target_pairs={{1,0},{2,1},{3,2},{4,3},{5,4},{6,5},{7,6},{8,7},{9,8},{10,9},{11,1... | collective-permute-start | bytes 33776 | tf_op jit(solution)/shard_map/ppermute | solution.py:162
  66.5 6.1 %collective-permute-start.6 = (f32[21,134]{1,0:T(8,128)S(1)}, f32[21,134]{1,0:T(8,128)S(1)}, u32[]{:S(2)}, u32[]{:S(2)}) collective-permute-start(f32[21,134]{1,0:T(8,128)S(1)} %reshape.53), channel_id=1, source_target_pairs={{0,1},{1,2},{2,3},{3,4},{4,5},{5,6},{6,7},{7,8},{8,9},{9,10},{10,1... | collective-permute-start | bytes 33776 | tf_op jit(solution)/shard_map/ppermute | solution.py:161
  81.0 22.5 %all-to-all-start.2 = ((f32[32,8,128]{2,1,0:T(8,128)}), f32[32,8,128]{2,1,0:T(8,128)S(1)}, u32[]{:S(2)}, u32[]{:S(2)}) async-start(f32[32,8,128]{2,1,0:T(8,128)} %get-tuple-element.5), calls=%async_computation.2 | async-start | bytes 262144 | tf_op jit(solution)/shard_map/all_to_all | solution.py:232

commit v13 on v10

--- a/solution.py
+++ b/solution.py
@@ -211,10 +211,13 @@
     stiffness_at = jnp.take(stiffness, slot_row, axis=0)
     side = girth_side([loading, stiffness_rows[None]], "girth", width, 128)
     motion, motion_at = run_sweeps(slot_row, coupling, loading, stiffness_rows, side, row_count)
-    stress_rows = stiffness_at[:, None, :] * jnp.einsum(
-        "ka,aij->ikj", stress_map, motion_at, precision=lax.Precision.HIGHEST
+    stress = [
+        stiffness_at * sum(stress_map[k, a] * motion_at[a] for a in range(motion_at.shape[0]))
+        for k in range(stress_map.shape[0])
+    ]
+    spectra = jnp.stack(
+        [stress[0] * stress[0] + stress[1] * stress[1], stress[2] * stress[2] + stress[3] * stress[3]], axis=1
     )
-    spectra = square_pairs(stress_rows, 1)
     outbox = jnp.where(filled[:, None, None], spectra, 0.0)
     outbox = outbox.reshape(girth_count, CAP * 2 * girth_cells // 128, 128)
     received = lax.all_to_all(outbox, "girth", split_axis=0, concat_axis=0, tiled=True)

time: 102 us -> 119 us (1.17)
  other arithmetic: 9.21 us -> 26.3 us
  matrix products: 4.79 us -> 3 us
    add x0 -> x2, other arithmetic: none -> 17.2 us  [the longest x1 8.63 us: on_device(): stress[2] * stress[2] + stress[3] * stress[3]]
    dot_general x1 -> x0, matrix products: 1.78 us -> none  [on_device(): jnp.einsum('ka,aij->ikj', stress_map, motion_at, precision=lax.Precision....]
    slice x0 -> x2, local copies, waits for them, and re-layouts: none -> 1.41 us  [on_device(): stress_map[k, a] * motion_at[a]]
  transfers between devices with their start and end apart: 10 -> 10, of which waited for: 5 -> 4; matrix products, arithmetic and copies ran while one was open for 12% -> 11% of each run, Pallas kernels for 0% -> 0%
where the time goes in v13:
time: 119 us; the launch traced here: 118 us
  starting transfers between devices  43.6 us (37%)
  other arithmetic  26.3 us (22%)
  waiting for transfers between devices  25.1 us (21%)
  local copies, waits for them, and re-layouts  10.3 us (9%)
  Pallas kernels  7 us (6%)
  matrix products  3 us (3%)
  between operations  2.31 us (2%)
    all_to_all x1, starting transfers between devices, scatter_gather(): got = lax.all_to_all(send, axis, 0, 0, tiled=True)  9.95 us
    all_to_all x1, waiting for transfers between devices, on_device(): lax.all_to_all(outbox, 'girth', split_axis=0, concat_axis=0, tiled=True)  9.71 us
    all_to_all x1, waiting for transfers between devices, scatter_gather(): full = lax.all_to_all(send, axis, 0, 0, tiled=True)  8.79 us
    add x1, other arithmetic, on_device(): stress[2] * stress[2] + stress[3] * stress[3]  8.63 us
    add x1, other arithmetic, on_device(): stress[0] * stress[0] + stress[1] * stress[1]  8.57 us
    pallas_call x1, Pallas kernels, run_sweeps(): pl.pallas_call(sweeps_kernel, out_shape=(jax.ShapeDtypeStruct((fields, ou...  7 us
    all_to_all x1, starting transfers between devices, scatter_gather(): full = lax.all_to_all(send, axis, 0, 0, tiled=True)  6.88 us
    add x1, other arithmetic, on_device(): stiffness + jnp.where(thickness_class == level, class_stiffness[level], 0.0)  6.08 us
  transfers between devices with their start and end apart: 10, of which 4 were waited for; matrix products, arithmetic and copies ran while one was open for 11% of the time, Pallas kernels for 0%

profile of v13, /device:TPU:192, one launch (start us, length us, event | category | flops | bytes accessed | tf_op | source)
XLA Modules:
  0.0 117.7 jit_solution(6740739542430951386)
XLA Ops:
  0.6 0.0 copy-start
  0.6 0.0 copy-start.5
  0.7 0.0 copy-start.6
  0.7 0.0 copy-start.3
  0.7 1.2 copy-done
  1.9 0.8 constant_dynamic-slice_fusion
  2.7 10.0 %all-to-all-start = ((bf16[32,32,256]{2,1,0:T(8,128)(2,1)}), bf16[32,32,256]{2,1,0:T(8,128)(2,1)S(1)}, u32[]{:S(2)}, u32[]{:S(2)}) async-start(bf16[32,32,256]{2,1,0:T(8,128)(2,1)} %bitcast.2), calls=%async_computation | async-start | bytes 1048576 | tf_op jit(solution)/shard_map/all_to_all | solution.py:18
  12.6 1.6 %fusion.25 = (f32[1]{0:T(128)}, f32[1]{0:T(128)}, f32[1]{0:T(128)}, f32[1]{0:T(128)}, f32[1]{0:T(128)}, /*index=5*/f32[1]{0:T(128)}, f32[1]{0:T(128)}, f32[1]{0:T(128)}) fusion(f32[8]{0:T(128)} %param.15), kind=kLoop, calls=%fused_computation.52 | loop fusion | bytes 64 | tf_op jit(solution)/shard_map/slice | solution.py:191
  14.3 6.1 %select_add_fusion = f32[128,256]{1,0:T(8,128)S(1)} fusion(s32[128,256]{1,0:T(8,128)} %param.14, f32[]{:T(128)} %bitcast.14, f32[]{:T(128)} %bitcast.13, f32[]{:T(128)} %bitcast.12, f32[]{:T(128)} %bitcast.11, f32[]{:T(128)} %bitcast.10, f32[]{:T(128)} %bitcast.9, f32[]{:T(128)} %bitcast.8, f32[]{:T(128)} %bitcast.7), kind=kLoop, calls=%fused_computation.15 | loop fusion | flops 753664 | bytes 262176 | tf_op jit(solution)/shard_map/add | solution.py:191
  20.4 1.9 %collective-permute-start.3 = (f32[3,256]{1,0:T(4,128)S(1)}, f32[3,256]{1,0:T(4,128)S(1)}, u32[]{:S(2)}, u32[]{:S(2)}) collective-permute-start(f32[3,256]{1,0:T(4,128)S(1)} %get-tuple-element.16), channel_id=1, source_target_pairs={{0,32},{32,64},{64,96},{96,128},{128,160},{160,192},{192,224},{224... | collective-permute-start | bytes 9224 | tf_op jit(solution)/shard_map/ppermute | solution.py:42
  22.3 3.6 %collective-permute-start.4 = (f32[3,256]{1,0:T(4,128)S(1)}, f32[3,256]{1,0:T(4,128)S(1)}, u32[]{:S(2)}, u32[]{:S(2)}) collective-permute-start(f32[3,256]{1,0:T(4,128)S(1)} %get-tuple-element.17), channel_id=1, source_target_pairs={{32,0},{64,32},{96,64},{128,96},{160,128},{192,160},{224,192},{256... | collective-permute-start | bytes 9224 | tf_op jit(solution)/shard_map/ppermute | solution.py:45
  26.6 2.9 %all-to-all-done = bf16[32,32,256]{2,1,0:T(8,128)(2,1)S(1)} async-done(((bf16[32,32,256]{2,1,0:T(8,128)(2,1)}), bf16[32,32,256]{2,1,0:T(8,128)(2,1)S(1)}, u32[]{:S(2)}, u32[]{:S(2)}) %all-to-all-start) | async-done | bytes 524320 | tf_op jit(solution)/shard_map/all_to_all | solution.py:18
  29.5 0.9 broadcast_in_dim.96
  30.4 6.9 %all-to-all-start.1 = ((bf16[32,32,256]{2,1,0:T(8,128)(2,1)}), bf16[32,32,256]{2,1,0:T(8,128)(2,1)S(1)}, u32[]{:S(2)}, u32[]{:S(2)}) async-start(bf16[32,32,256]{2,1,0:T(8,128)(2,1)} %broadcast_in_dim.96), calls=%async_computation.1 | async-start | bytes 1048576 | tf_op jit(solution)/shard_map/all_to_all | solution.py:21
  37.3 1.1 fusion.19
  38.4 3.6 %collective-permute-start = (bf16[6,3,2048]{2,1,0:T(4,128)(2,1)S(1)}, bf16[6,3,2048]{2,1,0:T(4,128)(2,1)S(1)}, u32[]{:S(2)}, u32[]{:S(2)}) collective-permute-start(bf16[6,3,2048]{2,1,0:T(4,128)(2,1)S(1)} %get-tuple-element.6), channel_id=1, source_target_pairs={{0,32},{32,64},{64,96},{96,128},{128,160},{160,192},{192,224},{224... | collective-permute-start | bytes 221192 | tf_op jit(solution)/shard_map/ppermute | solution.py:42
  42.0 2.0 %collective-permute-start.1 = (bf16[6,3,2048]{2,1,0:T(4,128)(2,1)S(1)}, bf16[6,3,2048]{2,1,0:T(4,128)(2,1)S(1)}, u32[]{:S(2)}, u32[]{:S(2)}) collective-permute-start(bf16[6,3,2048]{2,1,0:T(4,128)(2,1)S(1)} %get-tuple-element.7), channel_id=1, source_target_pairs={{32,0},{64,32},{96,64},{128,96},{160,128},{192,160},{224,192},{256... | collective-permute-start | bytes 221192 | tf_op jit(solution)/shard_map/ppermute | solution.py:45
  44.0 0.0 copy-done.5
  44.0 0.2 convert_reduce_fusion
  44.2 0.1 fusion.14
  44.3 0.0 copy-done.6
  44.3 0.1 select_reduce_fusion.rows_ref
  44.4 8.8 %all-to-all-done.1 = bf16[32,32,256]{2,1,0:T(8,128)(2,1)S(1)} async-done(((bf16[32,32,256]{2,1,0:T(8,128)(2,1)}), bf16[32,32,256]{2,1,0:T(8,128)(2,1)S(1)}, u32[]{:S(2)}, u32[]{:S(2)}) %all-to-all-start.1) | async-done | bytes 524320 | tf_op jit(solution)/shard_map/all_to_all | solution.py:21
  53.2 4.0 %collective-permute-start.2 = (bf16[1024,256]{1,0:T(8,128)(2,1)S(1)}, bf16[1024,256]{1,0:T(8,128)(2,1)S(1)}, u32[]{:S(2)}, u32[]{:S(2)}) collective-permute-start(bf16[1024,256]{1,0:T(8,128)(2,1)S(1)} %bitcast.92), channel_id=1, source_target_pairs={{0,32},{32,0},{64,96},{96,64},{128,160},{160,128},{192,224},{224,1... | collective-permute-start | bytes 1572872 | tf_op jit(solution)/shard_map/ppermute | solution.py:31
  57.1 0.0 copy-done.3
  57.1 0.7 fusion.23
  57.9 0.7 fusion.24
  58.6 0.0 collective-permute-done.3
  58.6 0.0 collective-permute-done.4
  58.6 0.7 fusion.18
  59.3 0.1 fusion.21
  59.3 0.1 copy.28
  59.4 0.1 copy.32
  59.5 0.0 collective-permute-done.2
  59.5 0.1 broadcast_select_fusion.1
  59.6 0.0 collective-permute-done
  59.6 0.0 collective-permute-done.1
  59.7 3.0 %fusion.loading_ref = f32[6,134,256]{2,1,0:T(8,128)S(1)} fusion(bf16[6,3,2048]{2,1,0:T(4,128)(2,1)S(1)} %collective-permute-done.1, bf16[6,128,2048]{2,1,0:T(8,128)(2,1)} %param.11, bf16[6,3,2048]{2,1,0:T(4,128)(2,1)S(1)} %collective-permute-done, bf16[1024,256]{1,0:T(8,128)(2,1)S(1)} %get-tuple-element.9, bf16[1024,256]{1,0:T(8,128)(2,1)S(1)} %get-tuple-element.8), kind=kOutput, calls=%fused_computation.1 | convolution fusion | flops 855031808 | bytes 5165056 | tf_op jit(solution)/shard_map/dot_general | solution.py:196
  62.7 0.0 copy-done.4
  62.7 0.0 copy-start.1
  62.7 0.2 fusion.20
  62.9 0.3 copy.27
  63.3 0.3 copy.31
  63.7 4.7 %collective-permute-start.6 = (f32[21,134]{1,0:T(8,128)S(1)}, f32[21,134]{1,0:T(8,128)S(1)}, u32[]{:S(2)}, u32[]{:S(2)}) collective-permute-start(f32[21,134]{1,0:T(8,128)S(1)} %reshape.498), channel_id=1, source_target_pairs={{0,1},{1,2},{2,3},{3,4},{4,5},{5,6},{6,7},{7,8},{8,9},{9,10},{10,1... | collective-permute-start | bytes 33776 | tf_op jit(solution)/shard_map/ppermute | solution.py:144
  68.3 1.3 %collective-permute-start.5 = (f32[21,134]{1,0:T(8,128)S(1)}, f32[21,134]{1,0:T(8,128)S(1)}, u32[]{:S(2)}, u32[]{:S(2)}) collective-permute-start(f32[21,134]{1,0:T(8,128)S(1)} %reshape.496), channel_id=1, source_target_pairs={{1,0},{2,1},{3,2},{4,3},{5,4},{6,5},{7,6},{8,7},{9,8},{10,9},{11,1... | collective-permute-start | bytes 33776 | tf_op jit(solution)/shard_map/ppermute | solution.py:145
  69.6 0.7 gather_fusion
  70.3 0.1 pad.3.clone
  70.4 3.7 %collective-permute-done.5 = f32[21,134]{1,0:T(8,128)S(1)} collective-permute-done((f32[21,134]{1,0:T(8,128)S(1)}, f32[21,134]{1,0:T(8,128)S(1)}, u32[]{:S(2)}, u32[]{:S(2)}) %collective-permute-start.5) | collective-permute-done | bytes 11288 | tf_op jit(solution)/shard_map/ppermute | solution.py:145
  74.1 0.2 copy.30
  74.3 0.0 copy-start.2
  74.3 0.0 collective-permute-done.6
  74.3 0.2 copy.34
  74.6 1.0 pad_maximum_fusion.side_ref
  75.6 0.0 copy-done.1
  75.6 7.0 %shard_map.122 = (f32[6,128,256]{2,1,0:T(8,128)}, f32[6,64,256]{2,1,0:T(8,128)}) custom-call(s32[64]{0:T(128)} %copy-done.4, f32[6,6]{1,0:T(8,128)} %coupling_ref.1, f32[6,134,256]{2,1,0:T(8,128)} %copy-done.1, f32[134,256]{1,0:T(8,128)} %get-tuple-element.15.stiff_ref, f32[7,134,128]{2,1,0:T(8,128)} %pad_maximum_fusion.side_ref), custom_call_target="tpu_custom_call" | custom-call | tf_op jit(solution)/shard_map/pallas_call | solution.py:113
  82.6 8.6 %fusion.9 = f32[64,1,256]{2,0,1:T(8,128)S(1)} fusion(f32[64,256]{1,0:T(8,128)S(1)} %gather_fusion, f32[6,64,256]{2,1,0:T(8,128)} %get-tuple-element.5, f32[]{:T(128)} %bitcast.50, f32[]{:T(128)} %bitcast.49, f32[]{:T(128)} %bitcast.48, f32[]{:T(128)} %bitcast.47, f32[]{:T(128)} %bitcast.46, f32[]{:T(128)} %bitcast.45, f32[]{:T(128)} %bitcast.43, ...), kind=kLoop, calls=%fused_computation.18 | loop fusion | flops 458752 | bytes 524400 | tf_op jit(solution)/shard_map/add | solution.py:219
  91.2 8.6 %fusion.12 = f32[64,1,256]{2,0,1:T(8,128)S(1)} fusion(f32[64,256]{1,0:T(8,128)S(1)} %gather_fusion, f32[6,64,256]{2,1,0:T(8,128)} %get-tuple-element.5, f32[]{:T(128)} %bitcast.36, f32[]{:T(128)} %bitcast.35, f32[]{:T(128)} %bitcast.34, f32[]{:T(128)} %bitcast.33, f32[]{:T(128)} %bitcast.32, f32[]{:T(128)} %bitcast.31, f32[]{:T(128)} %bitcast.29, ...), kind=kLoop, calls=%fused_computation.23 | loop fusion | flops 458752 | bytes 524400 | tf_op jit(solution)/shard_map/add | solution.py:219
  99.8 0.1 maximum_select_fusion
  99.8 0.1 copy.35
  100.0 0.8 select_n.113
  100.7 5.8 %all-to-all-start.2 = ((f32[32,8,128]{2,1,0:T(8,128)}), f32[32,8,128]{2,1,0:T(8,128)S(1)}, u32[]{:S(2)}, u32[]{:S(2)}) async-start(f32[32,8,128]{2,1,0:T(8,128)} %select_n.113), calls=%async_computation.2 | async-start | bytes 262144 | tf_op jit(solution)/shard_map/all_to_all | solution.py:223
  107.2 9.7 %all-to-all-done.2 = f32[32,8,128]{2,1,0:T(8,128)S(1)} async-done(((f32[32,8,128]{2,1,0:T(8,128)}), f32[32,8,128]{2,1,0:T(8,128)S(1)}, u32[]{:S(2)}, u32[]{:S(2)}) %all-to-all-start.2) | async-done | bytes 131104 | tf_op jit(solution)/shard_map/all_to_all | solution.py:223
  116.9 0.1 mul.530
  117.0 0.7 add.344
  (18 shorter events, 0.2 us)
Async XLA Ops:
  0.6 1.2 %copy-start = (bf16[2048,256]{1,0:T(8,128)(2,1)S(1)}, bf16[2048,256]{1,0:T(8,128)(2,1)}, u32[]{:S(2)}) copy-start(bf16[2048,256]{1,0:T(8,128)(2,1)} %param.12) | copy-start | bytes 3145732
  0.6 43.3 %copy-start.5 = (s32[1,32,1]{1,2,0:T(1,128)S(1)}, s32[1,32,1]{1,2,0:T(1,128)}, u32[]{:S(2)}) copy-start(s32[1,32,1]{1,2,0:T(1,128)} %param.20) | copy-start | bytes 388
  0.7 43.6 %copy-start.6 = (s32[1,32]{1,0:T(1,128)S(1)}, s32[1,32]{1,0:T(1,128)}, u32[]{:S(2)}) copy-start(s32[1,32]{1,0:T(1,128)} %param.19) | copy-start | bytes 388
  0.7 56.5 %copy-start.3 = (f32[4,6]{1,0:T(4,128)S(1)}, f32[4,6]{1,0:T(4,128)}, u32[]{:S(2)}) copy-start(f32[4,6]{1,0:T(4,128)} %param.17) | copy-start | bytes 292
  2.7 26.8 %all-to-all-start = ((bf16[32,32,256]{2,1,0:T(8,128)(2,1)}), bf16[32,32,256]{2,1,0:T(8,128)(2,1)S(1)}, u32[]{:S(2)}, u32[]{:S(2)}) async-start(bf16[32,32,256]{2,1,0:T(8,128)(2,1)} %bitcast.2), calls=%async_computation | async-start | bytes 1048576 | tf_op jit(solution)/shard_map/all_to_all | solution.py:18
  20.4 38.2 %collective-permute-start.3 = (f32[3,256]{1,0:T(4,128)S(1)}, f32[3,256]{1,0:T(4,128)S(1)}, u32[]{:S(2)}, u32[]{:S(2)}) collective-permute-start(f32[3,256]{1,0:T(4,128)S(1)} %get-tuple-element.16), channel_id=1, source_target_pairs={{0,32},{32,64},{64,96},{96,128},{128,160},{160,192},{192,224},{224... | collective-permute-start | bytes 9224 | tf_op jit(solution)/shard_map/ppermute | solution.py:42
  22.3 36.3 %collective-permute-start.4 = (f32[3,256]{1,0:T(4,128)S(1)}, f32[3,256]{1,0:T(4,128)S(1)}, u32[]{:S(2)}, u32[]{:S(2)}) collective-permute-start(f32[3,256]{1,0:T(4,128)S(1)} %get-tuple-element.17), channel_id=1, source_target_pairs={{32,0},{64,32},{96,64},{128,96},{160,128},{192,160},{224,192},{256... | collective-permute-start | bytes 9224 | tf_op jit(solution)/shard_map/ppermute | solution.py:45
  30.4 22.8 %all-to-all-start.1 = ((bf16[32,32,256]{2,1,0:T(8,128)(2,1)}), bf16[32,32,256]{2,1,0:T(8,128)(2,1)S(1)}, u32[]{:S(2)}, u32[]{:S(2)}) async-start(bf16[32,32,256]{2,1,0:T(8,128)(2,1)} %broadcast_in_dim.96), calls=%async_computation.1 | async-start | bytes 1048576 | tf_op jit(solution)/shard_map/all_to_all | solution.py:21
  38.4 21.2 %collective-permute-start = (bf16[6,3,2048]{2,1,0:T(4,128)(2,1)S(1)}, bf16[6,3,2048]{2,1,0:T(4,128)(2,1)S(1)}, u32[]{:S(2)}, u32[]{:S(2)}) collective-permute-start(bf16[6,3,2048]{2,1,0:T(4,128)(2,1)S(1)} %get-tuple-element.6), channel_id=1, source_target_pairs={{0,32},{32,64},{64,96},{96,128},{128,160},{160,192},{192,224},{224... | collective-permute-start | bytes 221192 | tf_op jit(solution)/shard_map/ppermute | solution.py:42
  42.0 17.7 %collective-permute-start.1 = (bf16[6,3,2048]{2,1,0:T(4,128)(2,1)S(1)}, bf16[6,3,2048]{2,1,0:T(4,128)(2,1)S(1)}, u32[]{:S(2)}, u32[]{:S(2)}) collective-permute-start(bf16[6,3,2048]{2,1,0:T(4,128)(2,1)S(1)} %get-tuple-element.7), channel_id=1, source_target_pairs={{32,0},{64,32},{96,64},{128,96},{160,128},{192,160},{224,192},{256... | collective-permute-start | bytes 221192 | tf_op jit(solution)/shard_map/ppermute | solution.py:45
  44.4 18.3 %copy-start.4 = (s32[64]{0:T(128)}, s32[64]{0:T(128)S(1)}, u32[]{:S(2)}) copy-start(s32[64]{0:T(128)S(1)} %select_reduce_fusion.rows_ref) | copy-start | bytes 772
  53.2 6.3 %collective-permute-start.2 = (bf16[1024,256]{1,0:T(8,128)(2,1)S(1)}, bf16[1024,256]{1,0:T(8,128)(2,1)S(1)}, u32[]{:S(2)}, u32[]{:S(2)}) collective-permute-start(bf16[1024,256]{1,0:T(8,128)(2,1)S(1)} %bitcast.92), channel_id=1, source_target_pairs={{0,32},{32,0},{64,96},{96,64},{128,160},{160,128},{192,224},{224,1... | collective-permute-start | bytes 1572872 | tf_op jit(solution)/shard_map/ppermute | solution.py:31
  62.7 12.9 %copy-start.1 = (f32[6,134,256]{2,1,0:T(8,128)}, f32[6,134,256]{2,1,0:T(8,128)S(1)}, u32[]{:S(2)}) copy-start(f32[6,134,256]{2,1,0:T(8,128)S(1)} %fusion.loading_ref) | copy-start | bytes 2469892
  63.7 10.6 %collective-permute-start.6 = (f32[21,134]{1,0:T(8,128)S(1)}, f32[21,134]{1,0:T(8,128)S(1)}, u32[]{:S(2)}, u32[]{:S(2)}) collective-permute-start(f32[21,134]{1,0:T(8,128)S(1)} %reshape.498), channel_id=1, source_target_pairs={{0,1},{1,2},{2,3},{3,4},{4,5},{5,6},{6,7},{7,8},{8,9},{9,10},{10,1... | collective-permute-start | bytes 33776 | tf_op jit(solution)/shard_map/ppermute | solution.py:144
  68.3 5.7 %collective-permute-start.5 = (f32[21,134]{1,0:T(8,128)S(1)}, f32[21,134]{1,0:T(8,128)S(1)}, u32[]{:S(2)}, u32[]{:S(2)}) collective-permute-start(f32[21,134]{1,0:T(8,128)S(1)} %reshape.496), channel_id=1, source_target_pairs={{1,0},{2,1},{3,2},{4,3},{5,4},{6,5},{7,6},{8,7},{9,8},{10,9},{11,1... | collective-permute-start | bytes 33776 | tf_op jit(solution)/shard_map/ppermute | solution.py:145
  74.3 42.7 %copy-start.2 = (f32[1,1,32,2,2,256]{5,4,3,2,1,0:T(2,128)S(1)}, f32[1,1,32,2,2,256]{5,4,3,2,1,0:T(2,128)}, u32[]{:S(2)}) copy-start(f32[1,1,32,2,2,256]{5,4,3,2,1,0:T(2,128)} %param.21) | copy-start | bytes 393220
  100.7 16.2 %all-to-all-start.2 = ((f32[32,8,128]{2,1,0:T(8,128)}), f32[32,8,128]{2,1,0:T(8,128)S(1)}, u32[]{:S(2)}, u32[]{:S(2)}) async-start(f32[32,8,128]{2,1,0:T(8,128)} %select_n.113), calls=%async_computation.2 | async-start | bytes 262144 | tf_op jit(solution)/shard_map/all_to_all | solution.py:223

commit v14 on v10

--- a/solution.py
+++ b/solution.py
@@ -75,9 +75,10 @@
     load_scr[fields, :ext_rows, :cells] = stiff_ref[...]
     load_scr[:, :ext_rows, cells:] = side_ref[...]
     stiffness = load_scr[fields]
+    inverse = []
     for a in range(fields):
-        diagonal = 4.0 * stiffness + coupling_ref[a, a]
-        motion_ref[a] = chebyshev_weight(0) * (load_scr[a] / diagonal)
+        inverse.append(1.0 / (4.0 * stiffness + coupling_ref[a, a]))
+        motion_ref[a] = chebyshev_weight(0) * (load_scr[a] * inverse[a])
     source, target = motion_ref, next_ref
     for sweep in range(1, SWEEPS):
         for a in range(fields):
@@ -92,8 +93,7 @@
             for b in range(1, fields):
                 mixing = mixing + coupling_ref[a, b] * source[b]
             applied = stiffness * (4.0 * centre - beside) + mixing
-            diagonal = 4.0 * stiffness + coupling_ref[a, a]
-            target[a] = centre + chebyshev_weight(sweep) * ((load_scr[a] - applied) / diagonal)
+            target[a] = centre + chebyshev_weight(sweep) * ((load_scr[a] - applied) * inverse[a])
         source, target = target, source
     out_rows = out_ref.shape[1]
     for a in range(fields):

time: 102 us -> 102 us (level)
  the two profiles are of different devices: /device:TPU:192 before, /device:TPU:64 now
where the time goes in v14:
time: 102 us; the launch traced here: 101 us
  starting transfers between devices  41.6 us (41%)
  waiting for transfers between devices  27.7 us (27%)
  other arithmetic  9.21 us (9%)
  local copies, waits for them, and re-layouts  9.13 us (9%)
  Pallas kernels  6.68 us (7%)
  matrix products  4.79 us (5%)
  between operations  2.32 us (2%)
    all_to_all x1, waiting for transfers between devices, scatter_gather(): full = lax.all_to_all(send, axis, 0, 0, tiled=True)  9.97 us
    all_to_all x1, starting transfers between devices, scatter_gather(): got = lax.all_to_all(send, axis, 0, 0, tiled=True)  9.95 us
    all_to_all x1, waiting for transfers between devices, on_device(): lax.all_to_all(outbox, 'girth', split_axis=0, concat_axis=0, tiled=True)  9.72 us
    all_to_all x1, starting transfers between devices, scatter_gather(): full = lax.all_to_all(send, axis, 0, 0, tiled=True)  6.88 us
    ppermute x2, starting transfers between devices, padded_2(): lax.ppermute(lax.slice_in_dim(block, 0, width, axis=dim), axis, backward)  6.82 us
    pallas_call x1, Pallas kernels, run_sweeps(): pl.pallas_call(sweeps_kernel, out_shape=(jax.ShapeDtypeStruct((fields, ou...  6.68 us
    add x1, other arithmetic, on_device(): stiffness + jnp.where(thickness_class == level, class_stiffness[level], 0.0)  6.08 us
    all_to_all x1, starting transfers between devices, on_device(): lax.all_to_all(outbox, 'girth', split_axis=0, concat_axis=0, tiled=True)  5.99 us
  transfers between devices with their start and end apart: 10, of which 5 were waited for; matrix products, arithmetic and copies ran while one was open for 12% of the time, Pallas kernels for 0%

profile of v14, /device:TPU:64, one launch (start us, length us, event | category | flops | bytes accessed | tf_op | source)
XLA Modules:
  0.0 101.4 jit_solution(5743106511776970906)
XLA Ops:
  0.6 0.0 copy-start
  0.6 0.0 copy-start.5
  0.7 0.0 copy-start.6
  0.7 1.2 %copy-done = bf16[2048,256]{1,0:T(8,128)(2,1)S(1)} copy-done((bf16[2048,256]{1,0:T(8,128)(2,1)S(1)}, bf16[2048,256]{1,0:T(8,128)(2,1)}, u32[]{:S(2)}) %copy-start) | copy-done | bytes 1048600
  1.9 0.8 constant_dynamic-slice_fusion
  2.7 10.0 %all-to-all-start = ((bf16[32,32,256]{2,1,0:T(8,128)(2,1)}), bf16[32,32,256]{2,1,0:T(8,128)(2,1)S(1)}, u32[]{:S(2)}, u32[]{:S(2)}) async-start(bf16[32,32,256]{2,1,0:T(8,128)(2,1)} %bitcast.2), calls=%async_computation | async-start | bytes 1048576 | tf_op jit(solution)/shard_map/all_to_all | solution.py:18
  12.6 1.6 %fusion.28 = (f32[1]{0:T(128)}, f32[1]{0:T(128)}, f32[1]{0:T(128)}, f32[1]{0:T(128)}, f32[1]{0:T(128)}, /*index=5*/f32[1]{0:T(128)}, f32[1]{0:T(128)}, f32[1]{0:T(128)}) fusion(f32[8]{0:T(128)} %param.23), kind=kLoop, calls=%fused_computation.56 | loop fusion | bytes 64 | tf_op jit(solution)/shard_map/slice | solution.py:191
  14.3 6.1 %select_add_fusion = f32[128,256]{1,0:T(8,128)S(1)} fusion(s32[128,256]{1,0:T(8,128)} %param.22, f32[]{:T(128)} %bitcast.14, f32[]{:T(128)} %bitcast.13, f32[]{:T(128)} %bitcast.12, f32[]{:T(128)} %bitcast.11, f32[]{:T(128)} %bitcast.10, f32[]{:T(128)} %bitcast.9, f32[]{:T(128)} %bitcast.8, f32[]{:T(128)} %bitcast.7), kind=kLoop, calls=%fused_computation.18 | loop fusion | flops 753664 | bytes 262176 | tf_op jit(solution)/shard_map/add | solution.py:191
  20.4 1.9 %collective-permute-start.3 = (f32[3,256]{1,0:T(4,128)S(1)}, f32[3,256]{1,0:T(4,128)S(1)}, u32[]{:S(2)}, u32[]{:S(2)}) collective-permute-start(f32[3,256]{1,0:T(4,128)S(1)} %get-tuple-element.68), channel_id=1, source_target_pairs={{0,32},{32,64},{64,96},{96,128},{128,160},{160,192},{192,224},{224... | collective-permute-start | bytes 9224 | tf_op jit(solution)/shard_map/ppermute | solution.py:42
  22.3 3.6 %collective-permute-start.4 = (f32[3,256]{1,0:T(4,128)S(1)}, f32[3,256]{1,0:T(4,128)S(1)}, u32[]{:S(2)}, u32[]{:S(2)}) collective-permute-start(f32[3,256]{1,0:T(4,128)S(1)} %get-tuple-element.69), channel_id=1, source_target_pairs={{32,0},{64,32},{96,64},{128,96},{160,128},{192,160},{224,192},{256... | collective-permute-start | bytes 9224 | tf_op jit(solution)/shard_map/ppermute | solution.py:45
  26.6 2.9 %all-to-all-done = bf16[32,32,256]{2,1,0:T(8,128)(2,1)S(1)} async-done(((bf16[32,32,256]{2,1,0:T(8,128)(2,1)}), bf16[32,32,256]{2,1,0:T(8,128)(2,1)S(1)}, u32[]{:S(2)}, u32[]{:S(2)}) %all-to-all-start) | async-done | bytes 524320 | tf_op jit(solution)/shard_map/all_to_all | solution.py:18
  29.5 0.9 broadcast_in_dim.109
  30.4 6.9 %all-to-all-start.1 = ((bf16[32,32,256]{2,1,0:T(8,128)(2,1)}), bf16[32,32,256]{2,1,0:T(8,128)(2,1)S(1)}, u32[]{:S(2)}, u32[]{:S(2)}) async-start(bf16[32,32,256]{2,1,0:T(8,128)(2,1)} %broadcast_in_dim.109), calls=%async_computation.1 | async-start | bytes 1048576 | tf_op jit(solution)/shard_map/all_to_all | solution.py:21
  37.3 1.1 %fusion.23 = (bf16[6,3,2048]{2,1,0:T(4,128)(2,1)S(1)}, bf16[6,3,2048]{2,1,0:T(4,128)(2,1)S(1)}) fusion(bf16[6,128,2048]{2,1,0:T(8,128)(2,1)} %param.19), kind=kLoop, calls=%fused_computation.51 | loop fusion | bytes 294912 | tf_op jit(solution)/shard_map/slice | solution.py:43
  38.4 2.4 %collective-permute-start = (bf16[6,3,2048]{2,1,0:T(4,128)(2,1)S(1)}, bf16[6,3,2048]{2,1,0:T(4,128)(2,1)S(1)}, u32[]{:S(2)}, u32[]{:S(2)}) collective-permute-start(bf16[6,3,2048]{2,1,0:T(4,128)(2,1)S(1)} %get-tuple-element.54), channel_id=1, source_target_pairs={{0,32},{32,64},{64,96},{96,128},{128,160},{160,192},{192,224},{224... | collective-permute-start | bytes 221192 | tf_op jit(solution)/shard_map/ppermute | solution.py:42
  40.8 3.2 %collective-permute-start.1 = (bf16[6,3,2048]{2,1,0:T(4,128)(2,1)S(1)}, bf16[6,3,2048]{2,1,0:T(4,128)(2,1)S(1)}, u32[]{:S(2)}, u32[]{:S(2)}) collective-permute-start(bf16[6,3,2048]{2,1,0:T(4,128)(2,1)S(1)} %get-tuple-element.55), channel_id=1, source_target_pairs={{32,0},{64,32},{96,64},{128,96},{160,128},{192,160},{224,192},{256... | collective-permute-start | bytes 221192 | tf_op jit(solution)/shard_map/ppermute | solution.py:45
  44.0 0.0 copy-done.5
  44.0 0.2 convert_reduce_fusion
  44.2 0.0 copy-done.6
  44.2 0.1 select_reduce_fusion.rows_ref
  44.3 0.7 gather_fusion
  45.0 10.0 %all-to-all-done.1 = bf16[32,32,256]{2,1,0:T(8,128)(2,1)S(1)} async-done(((bf16[32,32,256]{2,1,0:T(8,128)(2,1)}), bf16[32,32,256]{2,1,0:T(8,128)(2,1)S(1)}, u32[]{:S(2)}, u32[]{:S(2)}) %all-to-all-start.1) | async-done | bytes 524320 | tf_op jit(solution)/shard_map/all_to_all | solution.py:21
  54.9 1.9 %collective-permute-start.2 = (bf16[1024,256]{1,0:T(8,128)(2,1)S(1)}, bf16[1024,256]{1,0:T(8,128)(2,1)S(1)}, u32[]{:S(2)}, u32[]{:S(2)}) collective-permute-start(bf16[1024,256]{1,0:T(8,128)(2,1)S(1)} %bitcast.73), channel_id=1, source_target_pairs={{0,32},{32,0},{64,96},{96,64},{128,160},{160,128},{192,224},{224,1... | collective-permute-start | bytes 1572872 | tf_op jit(solution)/shard_map/ppermute | solution.py:31
  56.9 0.1 broadcast_select_fusion.2
  56.9 0.0 collective-permute-done.3
  56.9 0.0 collective-permute-done.4
  56.9 0.7 fusion.22
  57.6 0.1 fusion.26
  57.7 0.1 copy.40
  57.8 0.1 copy.44
  57.9 0.8 collective-permute-done.2
  58.7 0.1 broadcast_select_fusion.1
  58.8 0.0 collective-permute-done
  58.8 0.0 collective-permute-done.1
  58.9 3.0 %fusion.loading_ref = f32[6,134,256]{2,1,0:T(8,128)S(1)} fusion(bf16[6,3,2048]{2,1,0:T(4,128)(2,1)S(1)} %collective-permute-done.1, bf16[6,128,2048]{2,1,0:T(8,128)(2,1)} %param.19, bf16[6,3,2048]{2,1,0:T(4,128)(2,1)S(1)} %collective-permute-done, bf16[1024,256]{1,0:T(8,128)(2,1)S(1)} %get-tuple-element.57, bf16[1024,256]{1,0:T(8,128)(2,1)S(1)} %get-tuple-element.56), kind=kOutput, calls=%fused_computation.1 | convolution fusion | flops 855031808 | bytes 5165056 | tf_op jit(solution)/shard_map/dot_general | solution.py:196
  61.9 0.0 copy-done.4
  61.9 0.0 copy-start.1
  61.9 0.0 copy-start.3
  61.9 0.2 fusion.24
  62.1 0.3 copy.39
  62.5 0.3 copy.43
  62.9 4.4 %collective-permute-start.6 = (f32[21,134]{1,0:T(8,128)S(1)}, f32[21,134]{1,0:T(8,128)S(1)}, u32[]{:S(2)}, u32[]{:S(2)}) collective-permute-start(f32[21,134]{1,0:T(8,128)S(1)} %reshape.93), channel_id=1, source_target_pairs={{0,1},{1,2},{2,3},{3,4},{4,5},{5,6},{6,7},{7,8},{8,9},{9,10},{10,1... | collective-permute-start | bytes 33776 | tf_op jit(solution)/shard_map/ppermute | solution.py:144
  67.3 1.3 %collective-permute-start.5 = (f32[21,134]{1,0:T(8,128)S(1)}, f32[21,134]{1,0:T(8,128)S(1)}, u32[]{:S(2)}, u32[]{:S(2)}) collective-permute-start(f32[21,134]{1,0:T(8,128)S(1)} %reshape.91), channel_id=1, source_target_pairs={{1,0},{2,1},{3,2},{4,3},{5,4},{6,5},{7,6},{8,7},{9,8},{10,9},{11,1... | collective-permute-start | bytes 33776 | tf_op jit(solution)/shard_map/ppermute | solution.py:145
  68.6 0.1 fusion.17
  68.7 0.1 pad.11.clone
  68.8 4.2 %collective-permute-done.5 = f32[21,134]{1,0:T(8,128)S(1)} collective-permute-done((f32[21,134]{1,0:T(8,128)S(1)}, f32[21,134]{1,0:T(8,128)S(1)}, u32[]{:S(2)}, u32[]{:S(2)}) %collective-permute-start.5) | collective-permute-done | bytes 11288 | tf_op jit(solution)/shard_map/ppermute | solution.py:145
  73.0 0.2 copy.42
  73.3 0.0 collective-permute-done.6
  73.3 0.2 copy.46
  73.5 0.0 copy-start.2
  73.5 1.0 pad_maximum_fusion.side_ref
  74.5 0.0 copy-done.1
  74.5 6.7 %shard_map.122 = (f32[6,128,256]{2,1,0:T(8,128)}, f32[6,64,256]{2,1,0:T(8,128)}) custom-call(s32[64]{0:T(128)} %copy-done.4, f32[6,6]{1,0:T(8,128)} %coupling_ref.1, f32[6,134,256]{2,1,0:T(8,128)} %copy-done.1, f32[134,256]{1,0:T(8,128)} %get-tuple-element.67.stiff_ref, f32[7,134,128]{2,1,0:T(8,128)} %pad_maximum_fusion.side_ref), custom_call_target="tpu_custom_call" | custom-call | tf_op jit(solution)/shard_map/pallas_call | solution.py:113
  81.2 0.0 copy-done.3
  81.2 1.8 %fusion.6 = f32[64,4,256]{2,1,0:T(4,128)S(1)} fusion(f32[6,64,256]{2,1,0:T(8,128)} %get-tuple-element.9, f32[64,256]{1,0:T(8,128)S(1)} %broadcast_select_fusion.2, f32[4,6]{1,0:T(4,128)S(1)} %copy-done.3), kind=kOutput, calls=%fused_computation.8 | convolution fusion | flops 4784128 | bytes 720992 | tf_op jit(solution)/shard_map/ka,aij->ikj/dot_general | solution.py:214
  83.0 0.2 fusion.25
  83.2 0.1 maximum_select_fusion
  83.3 0.1 copy.51
  83.4 0.8 select_n.115
  84.2 6.0 %all-to-all-start.2 = ((f32[32,8,128]{2,1,0:T(8,128)}), f32[32,8,128]{2,1,0:T(8,128)S(1)}, u32[]{:S(2)}, u32[]{:S(2)}) async-start(f32[32,8,128]{2,1,0:T(8,128)} %select_n.115), calls=%async_computation.2 | async-start | bytes 262144 | tf_op jit(solution)/shard_map/all_to_all | solution.py:220
  90.8 9.7 %all-to-all-done.2 = f32[32,8,128]{2,1,0:T(8,128)S(1)} async-done(((f32[32,8,128]{2,1,0:T(8,128)}), f32[32,8,128]{2,1,0:T(8,128)S(1)}, u32[]{:S(2)}, u32[]{:S(2)}) %all-to-all-start.2) | async-done | bytes 131104 | tf_op jit(solution)/shard_map/all_to_all | solution.py:220
  100.6 0.1 mul.64
  100.7 0.0 copy-done.2
  100.7 0.7 add.90
  (18 shorter events, 0.2 us)
Async XLA Ops:
  0.6 1.2 %copy-start = (bf16[2048,256]{1,0:T(8,128)(2,1)S(1)}, bf16[2048,256]{1,0:T(8,128)(2,1)}, u32[]{:S(2)}) copy-start(bf16[2048,256]{1,0:T(8,128)(2,1)} %param.20) | copy-start | bytes 3145732
  0.6 43.3 %copy-start.5 = (s32[1,32,1]{1,2,0:T(1,128)S(1)}, s32[1,32,1]{1,2,0:T(1,128)}, u32[]{:S(2)}) copy-start(s32[1,32,1]{1,2,0:T(1,128)} %param.28) | copy-start | bytes 388
  0.7 43.5 %copy-start.6 = (s32[1,32]{1,0:T(1,128)S(1)}, s32[1,32]{1,0:T(1,128)}, u32[]{:S(2)}) copy-start(s32[1,32]{1,0:T(1,128)} %param.27) | copy-start | bytes 388
  2.7 26.8 %all-to-all-start = ((bf16[32,32,256]{2,1,0:T(8,128)(2,1)}), bf16[32,32,256]{2,1,0:T(8,128)(2,1)S(1)}, u32[]{:S(2)}, u32[]{:S(2)}) async-start(bf16[32,32,256]{2,1,0:T(8,128)(2,1)} %bitcast.2), calls=%async_computation | async-start | bytes 1048576 | tf_op jit(solution)/shard_map/all_to_all | solution.py:18
  20.4 36.6 %collective-permute-start.3 = (f32[3,256]{1,0:T(4,128)S(1)}, f32[3,256]{1,0:T(4,128)S(1)}, u32[]{:S(2)}, u32[]{:S(2)}) collective-permute-start(f32[3,256]{1,0:T(4,128)S(1)} %get-tuple-element.68), channel_id=1, source_target_pairs={{0,32},{32,64},{64,96},{96,128},{128,160},{160,192},{192,224},{224... | collective-permute-start | bytes 9224 | tf_op jit(solution)/shard_map/ppermute | solution.py:42
  22.3 34.6 %collective-permute-start.4 = (f32[3,256]{1,0:T(4,128)S(1)}, f32[3,256]{1,0:T(4,128)S(1)}, u32[]{:S(2)}, u32[]{:S(2)}) collective-permute-start(f32[3,256]{1,0:T(4,128)S(1)} %get-tuple-element.69), channel_id=1, source_target_pairs={{32,0},{64,32},{96,64},{128,96},{160,128},{192,160},{224,192},{256... | collective-permute-start | bytes 9224 | tf_op jit(solution)/shard_map/ppermute | solution.py:45
  30.4 24.6 %all-to-all-start.1 = ((bf16[32,32,256]{2,1,0:T(8,128)(2,1)}), bf16[32,32,256]{2,1,0:T(8,128)(2,1)S(1)}, u32[]{:S(2)}, u32[]{:S(2)}) async-start(bf16[32,32,256]{2,1,0:T(8,128)(2,1)} %broadcast_in_dim.109), calls=%async_computation.1 | async-start | bytes 1048576 | tf_op jit(solution)/shard_map/all_to_all | solution.py:21
  38.4 20.5 %collective-permute-start = (bf16[6,3,2048]{2,1,0:T(4,128)(2,1)S(1)}, bf16[6,3,2048]{2,1,0:T(4,128)(2,1)S(1)}, u32[]{:S(2)}, u32[]{:S(2)}) collective-permute-start(bf16[6,3,2048]{2,1,0:T(4,128)(2,1)S(1)} %get-tuple-element.54), channel_id=1, source_target_pairs={{0,32},{32,64},{64,96},{96,128},{128,160},{160,192},{192,224},{224... | collective-permute-start | bytes 221192 | tf_op jit(solution)/shard_map/ppermute | solution.py:42
  40.8 18.1 %collective-permute-start.1 = (bf16[6,3,2048]{2,1,0:T(4,128)(2,1)S(1)}, bf16[6,3,2048]{2,1,0:T(4,128)(2,1)S(1)}, u32[]{:S(2)}, u32[]{:S(2)}) collective-permute-start(bf16[6,3,2048]{2,1,0:T(4,128)(2,1)S(1)} %get-tuple-element.55), channel_id=1, source_target_pairs={{32,0},{64,32},{96,64},{128,96},{160,128},{192,160},{224,192},{256... | collective-permute-start | bytes 221192 | tf_op jit(solution)/shard_map/ppermute | solution.py:45
  44.3 17.6 %copy-start.4 = (s32[64]{0:T(128)}, s32[64]{0:T(128)S(1)}, u32[]{:S(2)}) copy-start(s32[64]{0:T(128)S(1)} %select_reduce_fusion.rows_ref) | copy-start | bytes 772
  54.9 3.8 %collective-permute-start.2 = (bf16[1024,256]{1,0:T(8,128)(2,1)S(1)}, bf16[1024,256]{1,0:T(8,128)(2,1)S(1)}, u32[]{:S(2)}, u32[]{:S(2)}) collective-permute-start(bf16[1024,256]{1,0:T(8,128)(2,1)S(1)} %bitcast.73), channel_id=1, source_target_pairs={{0,32},{32,0},{64,96},{96,64},{128,160},{160,128},{192,224},{224,1... | collective-permute-start | bytes 1572872 | tf_op jit(solution)/shard_map/ppermute | solution.py:31
  61.9 12.7 %copy-start.1 = (f32[6,134,256]{2,1,0:T(8,128)}, f32[6,134,256]{2,1,0:T(8,128)S(1)}, u32[]{:S(2)}) copy-start(f32[6,134,256]{2,1,0:T(8,128)S(1)} %fusion.loading_ref) | copy-start | bytes 2469892
  61.9 19.3 %copy-start.3 = (f32[4,6]{1,0:T(4,128)S(1)}, f32[4,6]{1,0:T(4,128)}, u32[]{:S(2)}) copy-start(f32[4,6]{1,0:T(4,128)} %param.25) | copy-start | bytes 292
  62.9 10.4 %collective-permute-start.6 = (f32[21,134]{1,0:T(8,128)S(1)}, f32[21,134]{1,0:T(8,128)S(1)}, u32[]{:S(2)}, u32[]{:S(2)}) collective-permute-start(f32[21,134]{1,0:T(8,128)S(1)} %reshape.93), channel_id=1, source_target_pairs={{0,1},{1,2},{2,3},{3,4},{4,5},{5,6},{6,7},{7,8},{8,9},{9,10},{10,1... | collective-permute-start | bytes 33776 | tf_op jit(solution)/shard_map/ppermute | solution.py:144
  67.3 5.7 %collective-permute-start.5 = (f32[21,134]{1,0:T(8,128)S(1)}, f32[21,134]{1,0:T(8,128)S(1)}, u32[]{:S(2)}, u32[]{:S(2)}) collective-permute-start(f32[21,134]{1,0:T(8,128)S(1)} %reshape.91), channel_id=1, source_target_pairs={{1,0},{2,1},{3,2},{4,3},{5,4},{6,5},{7,6},{8,7},{9,8},{10,9},{11,1... | collective-permute-start | bytes 33776 | tf_op jit(solution)/shard_map/ppermute | solution.py:145
  73.5 27.1 %copy-start.2 = (f32[1,1,32,2,2,256]{5,4,3,2,1,0:T(2,128)S(1)}, f32[1,1,32,2,2,256]{5,4,3,2,1,0:T(2,128)}, u32[]{:S(2)}) copy-start(f32[1,1,32,2,2,256]{5,4,3,2,1,0:T(2,128)} %param.29) | copy-start | bytes 393220
  84.2 16.4 %all-to-all-start.2 = ((f32[32,8,128]{2,1,0:T(8,128)}), f32[32,8,128]{2,1,0:T(8,128)S(1)}, u32[]{:S(2)}, u32[]{:S(2)}) async-start(f32[32,8,128]{2,1,0:T(8,128)} %select_n.115), calls=%async_computation.2 | async-start | bytes 262144 | tf_op jit(solution)/shard_map/all_to_all | solution.py:220
